TPU v7x, 32 devices: a whole 2x2x4 slice. The times are simulated.
32 devices in a mesh: rot: 16 (over z, x, core), term: 2 (over y).
Axes of the slice: x: 2, y: 2, z: 4, core: 2. Of those that a mesh axis runs over, the one named last changes fastest.
Arguments:
- receptor_grids: bfloat16 [22, 128, 1024], P('term', 'rot'), may hold values from -6 to 6
- term_weights: float32 [22], P('term'), may hold values from 0.5 to 2
- atom_weights: float32 [22, 256], P('term'), may hold values from -0.125 to 0.125
- ligand_cells: int32 [3, 32, 256], P(None, 'rot'), may hold values from 0 to 15
Outputs:
- best_scores: float32 [4, 32], P(None, 'rot')
- best_overall: float32 [4], replicated
All inputs are finite; a program needn't handle non-finite values.
Results may differ from a plain program's by a relative error of at most 0.0017.
Values may be sent and summed in bfloat16 or wider, within the bound.
No kernel may reach another device: no remote copies, remote signals or barrier semaphores. Data moves between devices by JAX's collectives and lax.ppermute only.
A program may use at most 128 MiB of HBM per device.

v0:
```python
import math

import numpy as np

import jax
import jax.numpy as jnp
from jax import lax
from jax.sharding import PartitionSpec as P

G = 32
HZ = G // 2 + 1
LB = 16

HIGH = lax.Precision.HIGH
HIGHEST = lax.Precision.HIGHEST


def line_table(freq_count, cell_count):
    freq = np.arange(freq_count)[:, None]
    cell = np.arange(cell_count)[None, :]
    phase = (freq * cell % G).astype(np.float64) * (2.0 * math.pi / G)
    return np.cos(phase).astype(np.float32), np.sin(phase).astype(np.float32)


def plane_tables(side):
    cy, sy = line_table(G, side)
    cz, sz = line_table(HZ, side)
    cy = jnp.asarray(cy.T)[:, None, :, None]
    sy = jnp.asarray(sy.T)[:, None, :, None]
    cz = jnp.asarray(cz.T)[None, :, None, :]
    sz = jnp.asarray(sz.T)[None, :, None, :]
    cos_t = (cy * cz - sy * sz).reshape(side * side, G * HZ)
    sin_t = (sy * cz + cy * sz).reshape(side * side, G * HZ)
    return cos_t, sin_t


def split_bf16(table):
    upper = table.astype(jnp.bfloat16)
    lower = (table - upper.astype(jnp.float32)).astype(jnp.bfloat16)
    return upper, lower


def mix_table(cell_count):
    cos_x, sin_x = line_table(G, cell_count)
    return jnp.asarray(np.concatenate([cos_x, sin_x], axis=0))


def dot2(rows, upper, lower):
    first = jnp.dot(rows, upper, preferred_element_type=jnp.float32)
    second = jnp.dot(rows, lower, preferred_element_type=jnp.float32)
    return first + second


def receptor_spectra(grids, cos_hi, cos_lo, sin_hi, sin_lo):
    terms, rows, cells = grids.shape
    receptors = rows // G
    flat = grids.reshape(terms * rows, cells)
    plane_re = dot2(flat, cos_hi, cos_lo).reshape(terms, receptors, G, G * HZ)
    plane_ims = dot2(flat, sin_hi, sin_lo).reshape(terms, receptors, G, G * HZ)
    mix = mix_table(G)
    mixed_re = jnp.einsum("px,trxq->trpq", mix, plane_re, precision=HIGH)
    mixed_ims = jnp.einsum("px,trxq->trpq", mix, plane_ims, precision=HIGH)
    spec_re = mixed_re[:, :, :G] - mixed_ims[:, :, G:]
    spec_im = -mixed_ims[:, :, :G] - mixed_re[:, :, G:]
    return spec_re, spec_im


def ligand_spectra(voxels, coefficients, box_cos, box_sin):
    rot_count = voxels.shape[1]
    terms = coefficients.shape[0]
    flat_index = (voxels[0] * LB + voxels[1]) * LB + voxels[2]
    cells = jnp.arange(LB**3, dtype=jnp.int32)
    onehot = (flat_index[:, :, None] == cells[None, None, :]).astype(jnp.float32)
    grid = jnp.einsum("ta,nac->tnc", coefficients, onehot, precision=HIGHEST)
    grid = grid.reshape(terms, rot_count, LB, LB * LB)
    plane_re = jnp.einsum("tnxc,cq->tnxq", grid, box_cos, precision=HIGH)
    plane_ims = jnp.einsum("tnxc,cq->tnxq", grid, box_sin, precision=HIGH)
    mix = mix_table(LB)
    mixed_re = jnp.einsum("px,tnxq->tnpq", mix, plane_re, precision=HIGH)
    mixed_ims = jnp.einsum("px,tnxq->tnpq", mix, plane_ims, precision=HIGH)
    lig_re = mixed_re[:, :, :G] - mixed_ims[:, :, G:]
    lig_im = -mixed_ims[:, :, :G] - mixed_re[:, :, G:]
    return lig_re, lig_im


def correlate(lig_re, lig_im, rec_re, rec_im):
    lr = lig_re[:, None]
    li = lig_im[:, None]
    rr = rec_re[:, :, None]
    ri = rec_im[:, :, None]
    prod_re = jnp.sum(lr * rr + li * ri, axis=0)
    prod_im = jnp.sum(lr * ri - li * rr, axis=0)
    return jnp.stack([prod_re, prod_im], axis=0)


def inverse_scores(products, cos_t, sin_t):
    mix = mix_table(G)
    mixed = jnp.einsum("xp,srnpq->srnxq", mix, products, precision=HIGH)
    inv_re = mixed[0, :, :, :G] - mixed[1, :, :, G:]
    inv_im = mixed[1, :, :, :G] + mixed[0, :, :, G:]
    freq_z = np.arange(G * HZ) % HZ
    fold = np.where((freq_z == 0) | (freq_z == G // 2), 1.0, 2.0) / float(G**3)
    fold = jnp.asarray(fold.astype(np.float32))
    scores = jnp.einsum("rnxq,cq->rnxc", inv_re * fold, cos_t, precision=HIGH)
    scores = scores - jnp.einsum("rnxq,cq->rnxc", inv_im * fold, sin_t, precision=HIGH)
    return scores


def body(receptor_grids, term_weights, atom_weights, ligand_cells):
    gathered = lax.all_gather(receptor_grids, "rot", axis=1, tiled=True)
    with jax.named_scope("twiddle_tables"):
        cos_t, sin_t = plane_tables(G)
        box_cos, box_sin = plane_tables(LB)
        cos_hi, cos_lo = split_bf16(cos_t)
        sin_hi, sin_lo = split_bf16(sin_t)
        tables = lax.optimization_barrier(
            (cos_t, sin_t, box_cos, box_sin, cos_hi, cos_lo, sin_hi, sin_lo)
        )
        cos_t, sin_t, box_cos, box_sin, cos_hi, cos_lo, sin_hi, sin_lo = tables
    with jax.named_scope("ligand_spectra"):
        coefficients = atom_weights * term_weights[:, None]
        lig_re, lig_im = ligand_spectra(ligand_cells, coefficients, box_cos, box_sin)
    with jax.named_scope("receptor_spectra"):
        rec_re, rec_im = receptor_spectra(gathered, cos_hi, cos_lo, sin_hi, sin_lo)
    with jax.named_scope("correlate"):
        products = correlate(lig_re, lig_im, rec_re, rec_im)
    products = lax.psum_scatter(products, "term", scatter_dimension=2, tiled=True)
    with jax.named_scope("inverse_scores"):
        scores = inverse_scores(products, cos_t, sin_t)
        best_here = jnp.max(scores, axis=(2, 3))
    best_all = lax.all_gather(best_here, ("rot", "term"), axis=1, tiled=True)
    rot_local = ligand_cells.shape[1]
    start = lax.axis_index("rot") * rot_local
    best_scores = lax.dynamic_slice_in_dim(best_all, start, rot_local, axis=1)
    best_overall = jnp.max(best_all, axis=1)
    return (best_scores, best_overall)


def solution(mesh):
    placed = (P("term", "rot", None), P("term"), P("term", None), P(None, "rot", None))
    return jax.shard_map(
        body, mesh=mesh, in_specs=placed, out_specs=(P(None, "rot"), P()), check_vma=False
    )
```

profile of v0, /device:TPU:0, one launch (start us, length us, event | category | flops | bytes accessed | tf_op | source)
XLA Modules:
  0.0 238.6 jit_solution(8877241703728081015)
XLA Ops:
  7.2 0.7 all-gather.3.cloned.1.call-update
  7.9 8.2 %multiply_add_fusion = (f32[32,32,32,17]{1,0,3,2:T(8,128)}, f32[32,32,32,17]{1,0,3,2:T(8,128)}) fusion(f32[32,17]{0,1:T(8,128)} %constant.43.clone, f32[32,32]{0,1:T(8,128)} %constant.41.clone, f32[32,17]{0,1:T(8,128)} %constant.42.clone, f32[32,32]{0,1:T(8,128)} %constant.40.clone), kind=kLoop, calls=%fused_computation | loop fusion | flops 3342336 | bytes 4468992 | tf_op jit(solution)/shard_map/twiddle_tables/add | solution.py:33
  16.2 7.0 %add.65 = f32[1024,544]{0,1:T(8,128)S(1)} reshape(f32[32,32,32,17]{1,0,3,2:T(8,128)} %get-tuple-element.28) | data formatting | bytes 4456448 | tf_op jit(solution)/shard_map/twiddle_tables/add | solution.py:33
  23.2 7.9 %sub.49 = f32[1024,544]{0,1:T(8,128)} reshape(f32[32,32,32,17]{1,0,3,2:T(8,128)} %get-tuple-element.29) | data formatting | bytes 4456448 | tf_op jit(solution)/shard_map/twiddle_tables/sub | solution.py:32
  31.2 4.5 %multiply_add_fusion.1 = (f32[16,16,32,17]{3,2,1,0:T(8,128)}, f32[16,16,32,17]{3,2,1,0:T(8,128)}) fusion(f32[16,17]{1,0:T(8,128)S(1)} %copy-done.12, f32[16,32]{1,0:T(8,128)S(1)} %copy-done.10, f32[16,17]{1,0:T(8,128)S(1)} %copy-done.11, f32[16,32]{1,0:T(8,128)S(1)} %copy-done.9), kind=kLoop, calls=%fused_computation.6 | loop fusion | flops 835584 | bytes 1120384 | tf_op jit(solution)/shard_map/twiddle_tables/add | solution.py:33
  35.7 4.5 %add.67 = f32[256,544]{1,0:T(8,128)S(1)} reshape(f32[16,16,32,17]{3,2,1,0:T(8,128)} %get-tuple-element.30) | data formatting | bytes 1114112 | tf_op jit(solution)/shard_map/twiddle_tables/add | solution.py:33
  40.1 5.1 %sub.51 = f32[256,544]{1,0:T(8,128)} reshape(f32[16,16,32,17]{3,2,1,0:T(8,128)} %get-tuple-element.31) | data formatting | bytes 1114112 | tf_op jit(solution)/shard_map/twiddle_tables/sub | solution.py:32
  45.3 5.1 %subtract_convert_fusion = (bf16[1024,544]{0,1:T(8,128)(2,1)}, bf16[1024,544]{0,1:T(8,128)(2,1)}, bf16[1024,544]{0,1:T(8,128)(2,1)}, bf16[1024,544]{0,1:T(8,128)(2,1)}) fusion(f32[1024,544]{0,1:T(8,128)S(1)} %add.65, f32[1024,544]{0,1:T(8,128)} %sub.49), kind=kLoop, calls=%fused_computation.22 | loop fusion | flops 4456448 | bytes 8912896 | tf_op jit(solution)/shard_map/twiddle_tables/convert_element_type | solution.py:39
  50.4 3.6 %fusion = f32[11,2,4096]{2,0,1:T(8,128)} fusion(s32[2,256]{1,0:T(2,128)S(1)} %add_bitcast_fusion, f32[11,256]{1,0:T(8,128)S(1)} %copy-done.16, f32[11]{0:T(128)S(1)} %copy-done.17), kind=kOutput, calls=%fused_computation.3 | convolution fusion | flops 278924032 | bytes 373804 | tf_op jit(solution)/shard_map/ligand_spectra/ta,nac->tnc/dot_general | solution.py:74
  54.0 1.1 reshape.132
  55.2 0.6 fusion.15
  55.8 1.7 fusion.17
  57.5 1.6 convolution_bitcast_fusion.2
  59.1 1.6 convolution_bitcast_fusion.3
  60.7 2.3 slice_subtract_fusion.3
  63.1 3.9 %fusion.35 = f32[544,1408]{1,0:T(8,128)S(1)} fusion(bf16[1024,544]{0,1:T(8,128)(2,1)S(1)} %copy-done.5, bf16[1408,1024]{1,0:T(8,128)(2,1)} %bitcast.113), kind=kOutput, calls=%fused_computation.56 | convolution fusion | flops 1568669696 | bytes 7061504 | tf_op jit(solution)/shard_map/receptor_spectra/dot_general | solution.py:49
  67.0 3.6 %fusion.3 = f32[1408,544]{0,1:T(8,128)} fusion(f32[544,1408]{1,0:T(8,128)S(1)} %fusion.35, bf16[1024,544]{0,1:T(8,128)(2,1)S(1)} %copy-done.4, bf16[1408,1024]{1,0:T(8,128)(2,1)S(1)} %bitcast.115), kind=kOutput, calls=%fused_computation.15 | convolution fusion | flops 1569435648 | bytes 10125312 | tf_op jit(solution)/shard_map/receptor_spectra/dot_general | solution.py:50
  70.6 4.9 %copy.44 = f32[1408,544]{1,0:T(8,128)} copy(f32[1408,544]{0,1:T(8,128)} %fusion.3) | data formatting | bytes 6127616 | tf_op jit(solution)/shard_map/receptor_spectra/add | solution.py:51
  75.5 3.9 %fusion.36 = f32[544,1408]{1,0:T(8,128)S(1)} fusion(bf16[1024,544]{0,1:T(8,128)(2,1)S(1)} %copy-done.3, bf16[1408,1024]{1,0:T(8,128)(2,1)} %bitcast.114), kind=kOutput, calls=%fused_computation.57 | convolution fusion | flops 1568669696 | bytes 7061504 | tf_op jit(solution)/shard_map/receptor_spectra/dot_general | solution.py:49
  79.4 3.6 %fusion.2 = f32[1408,544]{0,1:T(8,128)} fusion(f32[544,1408]{1,0:T(8,128)S(1)} %fusion.36, bf16[1024,544]{0,1:T(8,128)(2,1)S(1)} %copy-done.2, bf16[1408,1024]{1,0:T(8,128)(2,1)S(1)} %bitcast.116), kind=kOutput, calls=%fused_computation.13 | convolution fusion | flops 1569435648 | bytes 10125312 | tf_op jit(solution)/shard_map/receptor_spectra/dot_general | solution.py:50
  83.0 4.8 %copy.45 = f32[1408,544]{1,0:T(8,128)} copy(f32[1408,544]{0,1:T(8,128)} %fusion.2) | data formatting | bytes 6127616 | tf_op jit(solution)/shard_map/receptor_spectra/add | solution.py:51
  87.9 5.2 %convolution_bitcast_fusion.1 = f32[11,4,64,544]{3,2,1,0:T(8,128)S(1)} fusion(f32[11,4,32,544]{3,2,1,0:T(8,128)} %bitcast.105, f32[64,32,1,1]{0,1,3,2:T(8,128)S(1)} %copy-done.6), kind=kOutput, calls=%fused_computation.17 | convolution fusion | flops 294125568 | bytes 9199616 | tf_op jit(solution)/shard_map/receptor_spectra/px,trxq->trpq/dot_general | solution.py:61
  93.1 5.1 %convolution_bitcast_fusion = f32[11,4,64,544]{3,2,1,0:T(8,128)} fusion(f32[11,4,32,544]{3,2,1,0:T(8,128)S(1)} %bitcast.106, f32[64,32,1,1]{0,1,3,2:T(8,128)S(1)} %copy-done.6), kind=kOutput, calls=%fused_computation.16 | convolution fusion | flops 294125568 | bytes 9199616 | tf_op jit(solution)/shard_map/receptor_spectra/px,trxq->trpq/dot_general | solution.py:62
  98.2 6.6 %slice_subtract_fusion.1 = (f32[11,4,32,544]{3,2,1,0:T(8,128)S(1)}, f32[11,4,32,544]{3,2,1,0:T(8,128)}) fusion(f32[11,4,64,544]{3,2,1,0:T(8,128)} %convolution_bitcast_fusion, f32[11,4,64,544]{3,2,1,0:T(8,128)S(1)} %convolution_bitcast_fusion.1), kind=kLoop, calls=%fused_computation.11 | loop fusion | flops 2297856 | bytes 18382848 | tf_op jit(solution)/shard_map/receptor_spectra/sub | solution.py:63
  104.8 4.6 %add_reduce_fusion = (f32[4,2,32,544]{3,2,1,0:T(8,128)S(1)}, f32[4,2,32,544]{3,2,1,0:T(8,128)S(1)}) fusion(f32[11,4,32,544]{3,2,1,0:T(8,128)} %get-tuple-element.25, f32[11,2,32,544]{3,2,1,0:T(8,128)} %get-tuple-element.27, f32[11,4,32,544]{3,2,1,0:T(8,128)S(1)} %get-tuple-element.24, f32[11,2,32,544]{3,2,1,0:T(8,128)} %get-tuple-element.26), kind=kLoop, calls=%fused_computation.5 | loop fusion | flops 11976704 | bytes 10305536 | tf_op jit(solution)/shard_map/correlate/reduce_sum | solution.py:91
  109.5 1.2 pad_maximum_fusion
  110.7 0.6 dynamic-slice.2
  111.3 48.1 %all-reduce.3.cloned.1.call-done = f32[2,4,2,32,544]{4,3,2,1,0:T(8,128)} async-done(((f32[2,4,2,32,544]{4,3,2,1,0:T(8,128)}), f32[2,4,2,32,544]{4,3,2,1,0:T(8,128)}) %all-reduce.3.cloned.1.call-update) | async-done | bytes 1114128
  159.4 2.6 %fusion.14 = f32[2,4,544,64]{2,3,1,0:T(8,128)S(1)} fusion(f32[64,32,1,1]{0,1,3,2:T(8,128)S(1)} %copy-done.6, f32[2,4,2,32,544]{4,3,2,1,0:T(8,128)} %all-reduce.3.cloned.1.call-done, u32[]{:T(128)} %bitcast.40), kind=kOutput, calls=%fused_computation.33 | convolution fusion | flops 53477376 | bytes 1778176 | tf_op jit(solution)/shard_map/inverse_scores/xp,srnpq->srnxq/dot_general | solution.py:98
  162.0 0.9 fusion.4
  163.0 1.1 fusion.11
  164.1 66.6 %all-gather = f32[32,1,4]{2,1,0:T(1,128)S(1)} all-gather(f32[1,1,4]{2,1,0:T(1,128)S(1)} %bitcast.111), channel_id=1, replica_groups=mesh['rot'=16,'term'=2] {'rot','term'}, dimensions={0}, use_global_device_ids=true | all-gather | bytes 528 | tf_op jit(solution)/shard_map/all_gather | solution.py:131
  (45 shorter events, 1.3 us)
Async XLA Ops:
  7.2 55.9 %all-gather.3.cloned.1.call-start = ((), (), s32[]{:S(2)}) async-start(), calls=%async_computation | async-start | bytes 3063808 | tf_op jit(solution)/shard_map/all_gather | solution.py:110
  7.9 151.5 %all-reduce.3.cloned.1.call-start = ((), (), s32[]{:S(2)}) async-start(), calls=%async_computation.1 | async-start | bytes 2621440
  23.2 8.0 %copy-start.9 = (f32[16,32]{1,0:T(8,128)S(1)}, f32[16,32]{1,0:T(8,128)}, u32[]{:S(2)}) copy-start(f32[16,32]{1,0:T(8,128)} %constant.44.clone) | copy-start | bytes 6148
  23.2 8.0 %copy-start.10 = (f32[16,32]{1,0:T(8,128)S(1)}, f32[16,32]{1,0:T(8,128)}, u32[]{:S(2)}) copy-start(f32[16,32]{1,0:T(8,128)} %constant.45.clone) | copy-start | bytes 6148
  23.2 7.9 %copy-start.11 = (f32[16,17]{1,0:T(8,128)S(1)}, f32[16,17]{1,0:T(8,128)}, u32[]{:S(2)}) copy-start(f32[16,17]{1,0:T(8,128)} %constant.46.clone) | copy-start | bytes 3268
  23.2 7.9 %copy-start.12 = (f32[16,17]{1,0:T(8,128)S(1)}, f32[16,17]{1,0:T(8,128)}, u32[]{:S(2)}) copy-start(f32[16,17]{1,0:T(8,128)} %constant.47.clone) | copy-start | bytes 3268
  45.3 5.1 %copy-start.13 = (s32[3,2,256]{2,1,0:T(2,128)S(1)}, s32[3,2,256]{2,1,0:T(2,128)}, u32[]{:S(2)}) copy-start(s32[3,2,256]{2,1,0:T(2,128)} %param.19) | copy-start | bytes 18436
  45.3 5.1 %copy-start.16 = (f32[11,256]{1,0:T(8,128)S(1)}, f32[11,256]{1,0:T(8,128)}, u32[]{:S(2)}) copy-start(f32[11,256]{1,0:T(8,128)} %param.18) | copy-start | bytes 33796
  45.3 5.2 %copy-start.17 = (f32[11]{0:T(128)S(1)}, f32[11]{0:T(128)}, u32[]{:S(2)}) copy-start(f32[11]{0:T(128)} %param.17) | copy-start | bytes 136
  50.4 7.1 %copy-start.7 = (f32[64,16,1,1]{0,1,3,2:T(8,128)S(1)}, f32[64,16,1,1]{0,1,3,2:T(8,128)}, u32[]{:S(2)}) copy-start(f32[64,16,1,1]{0,1,3,2:T(8,128)} %constant.60) | copy-start | bytes 12292
  60.7 2.3 copy-start.5
  63.1 3.9 %copy-start.4 = (bf16[1024,544]{0,1:T(8,128)(2,1)S(1)}, bf16[1024,544]{0,1:T(8,128)(2,1)}, u32[]{:S(2)}) copy-start(bf16[1024,544]{0,1:T(8,128)(2,1)} %get-tuple-element.13) | copy-start | bytes 3342340
  63.1 3.9 %copy-start.14 = (bf16[11,128,1024]{2,1,0:T(8,128)(2,1)S(1)}, bf16[11,128,1024]{2,1,0:T(8,128)(2,1)}, u32[]{:S(2)}) copy-start(bf16[11,128,1024]{2,1,0:T(8,128)(2,1)} %all-gather.3.cloned.1.call-done) | copy-start | bytes 8650756
  70.6 4.9 %copy-start.3 = (bf16[1024,544]{0,1:T(8,128)(2,1)S(1)}, bf16[1024,544]{0,1:T(8,128)(2,1)}, u32[]{:S(2)}) copy-start(bf16[1024,544]{0,1:T(8,128)(2,1)} %get-tuple-element.14) | copy-start | bytes 3342340
  75.5 3.9 %copy-start.2 = (bf16[1024,544]{0,1:T(8,128)(2,1)S(1)}, bf16[1024,544]{0,1:T(8,128)(2,1)}, u32[]{:S(2)}) copy-start(bf16[1024,544]{0,1:T(8,128)(2,1)} %get-tuple-element.15) | copy-start | bytes 3342340
  75.5 3.9 %copy-start.15 = (bf16[11,128,1024]{2,1,0:T(8,128)(2,1)S(1)}, bf16[11,128,1024]{2,1,0:T(8,128)(2,1)}, u32[]{:S(2)}) copy-start(bf16[11,128,1024]{2,1,0:T(8,128)(2,1)} %all-gather.3.cloned.1.call-done) | copy-start | bytes 8650756
  83.0 4.8 %copy-start.6 = (f32[64,32,1,1]{0,1,3,2:T(8,128)S(1)}, f32[64,32,1,1]{0,1,3,2:T(8,128)}, u32[]{:S(2)}) copy-start(f32[64,32,1,1]{0,1,3,2:T(8,128)} %constant.61) | copy-start | bytes 24580
  87.9 5.2 %copy-start.1 = (f32[1408,544]{1,0:T(8,128)S(1)}, f32[1408,544]{1,0:T(8,128)}, u32[]{:S(2)}) copy-start(f32[1408,544]{1,0:T(8,128)} %copy.45) | copy-start | bytes 9191428
  109.5 1.3 copy-start.18
  109.5 52.6 %copy-start.8 = (f32[544]{0:T(1024)S(1)}, f32[544]{0:T(1024)}, u32[]{:S(2)}) copy-start(f32[544]{0:T(1024)} %constant.50.clone) | copy-start | bytes 6532
  159.4 3.6 %copy-start = (f32[1024,544]{0,1:T(8,128)S(1)}, f32[1024,544]{0,1:T(8,128)}, u32[]{:S(2)}) copy-start(f32[1024,544]{0,1:T(8,128)} %sub.49) | copy-start | bytes 6684676
Sparse Core Ops, SparseCore 0:
  10.2 47.0 all-gather.2
  110.8 48.5 all-reduce.2
where the time goes:
time: 239 us
  blocking collectives  66.6 us (28%)
  waiting for transfers between devices  48.8 us (20%)
  matrix products  39.1 us (16%)
  local copies, waits for them, and re-layouts  36.6 us (15%)
  other arithmetic  33.2 us (14%)
  between operations  14.3 us (6%)
    all_gather x1, blocking collectives, body(): best_all = lax.all_gather(best_here, ('rot', 'term'), axis=1, tiled=True)  66.6 us
    unnamed x3, waiting for transfers between devices  48.8 us
    sub x2, local copies, waits for them, and re-layouts, plane_tables(): cos_t = (cy * cz - sy * sz).reshape(side * side, G * HZ)  13 us
    add x2, other arithmetic, plane_tables(): sin_t = (sy * cz + cy * sz).reshape(side * side, G * HZ)  12.7 us
    add x2, local copies, waits for them, and re-layouts, plane_tables(): sin_t = (sy * cz + cy * sz).reshape(side * side, G * HZ)  11.5 us
    add x2, local copies, waits for them, and re-layouts, dot2(): return first + second  9.7 us
    dot_general x2, matrix products, dot2(): first = jnp.dot(rows, upper, preferred_element_type=jnp.float32)  7.78 us
    dot_general x2, matrix products, dot2(): second = jnp.dot(rows, lower, preferred_element_type=jnp.float32)  7.23 us
  transfers between devices with their start and end apart: 2, of which 1 were waited for; matrix products, arithmetic and copies ran while one was open for 23% of the time, Pallas kernels for 0%

commit v1 on v0

--- a/solution.py
+++ b/solution.py
@@ -23,12 +23,14 @@
 
 
 def plane_tables(side):
-    cy, sy = line_table(G, side)
-    cz, sz = line_table(HZ, side)
-    cy = jnp.asarray(cy.T)[:, None, :, None]
-    sy = jnp.asarray(sy.T)[:, None, :, None]
-    cz = jnp.asarray(cz.T)[None, :, None, :]
-    sz = jnp.asarray(sz.T)[None, :, None, :]
+    column = np.arange(G * HZ)
+    cell = np.arange(side)[:, None]
+    phase_y = (cell * (column // HZ)[None, :] % G) * (2.0 * math.pi / G)
+    phase_z = (cell * (column % HZ)[None, :] % G) * (2.0 * math.pi / G)
+    cy = jnp.asarray(np.cos(phase_y).astype(np.float32))[:, None, :]
+    sy = jnp.asarray(np.sin(phase_y).astype(np.float32))[:, None, :]
+    cz = jnp.asarray(np.cos(phase_z).astype(np.float32))[None, :, :]
+    sz = jnp.asarray(np.sin(phase_z).astype(np.float32))[None, :, :]
     cos_t = (cy * cz - sy * sz).reshape(side * side, G * HZ)
     sin_t = (sy * cz + cy * sz).reshape(side * side, G * HZ)
     return cos_t, sin_t
@@ -106,38 +108,55 @@
     return scores
 
 
-def body(receptor_grids, term_weights, atom_weights, ligand_cells):
-    gathered = lax.all_gather(receptor_grids, "rot", axis=1, tiled=True)
-    with jax.named_scope("twiddle_tables"):
-        cos_t, sin_t = plane_tables(G)
-        box_cos, box_sin = plane_tables(LB)
-        cos_hi, cos_lo = split_bf16(cos_t)
-        sin_hi, sin_lo = split_bf16(sin_t)
-        tables = lax.optimization_barrier(
-            (cos_t, sin_t, box_cos, box_sin, cos_hi, cos_lo, sin_hi, sin_lo)
-        )
-        cos_t, sin_t, box_cos, box_sin, cos_hi, cos_lo, sin_hi, sin_lo = tables
-    with jax.named_scope("ligand_spectra"):
-        coefficients = atom_weights * term_weights[:, None]
-        lig_re, lig_im = ligand_spectra(ligand_cells, coefficients, box_cos, box_sin)
-    with jax.named_scope("receptor_spectra"):
-        rec_re, rec_im = receptor_spectra(gathered, cos_hi, cos_lo, sin_hi, sin_lo)
-    with jax.named_scope("correlate"):
-        products = correlate(lig_re, lig_im, rec_re, rec_im)
-    products = lax.psum_scatter(products, "term", scatter_dimension=2, tiled=True)
-    with jax.named_scope("inverse_scores"):
-        scores = inverse_scores(products, cos_t, sin_t)
-        best_here = jnp.max(scores, axis=(2, 3))
-    best_all = lax.all_gather(best_here, ("rot", "term"), axis=1, tiled=True)
-    rot_local = ligand_cells.shape[1]
-    start = lax.axis_index("rot") * rot_local
-    best_scores = lax.dynamic_slice_in_dim(best_all, start, rot_local, axis=1)
-    best_overall = jnp.max(best_all, axis=1)
-    return (best_scores, best_overall)
+def reduce_scatter_terms(products, term_count):
+    share = products.shape[2] // term_count
+    here = lax.axis_index("term")
+    total = lax.dynamic_slice_in_dim(products, here * share, share, axis=2)
+    for shift in range(1, term_count):
+        target = (here + shift) % term_count
+        outgoing = lax.dynamic_slice_in_dim(products, target * share, share, axis=2)
+        pairs = [(k, (k + shift) % term_count) for k in range(term_count)]
+        total = total + lax.ppermute(outgoing, "term", pairs)
+    return total
+
+
+def make_body(term_count):
+    def body(receptor_grids, term_weights, atom_weights, ligand_cells):
+        gathered = lax.all_gather(receptor_grids, "rot", axis=1, tiled=True)
+        with jax.named_scope("twiddle_tables"):
+            cos_t, sin_t = plane_tables(G)
+            box_cos, box_sin = plane_tables(LB)
+            cos_hi, cos_lo = split_bf16(cos_t)
+            sin_hi, sin_lo = split_bf16(sin_t)
+            tables = lax.optimization_barrier(
+                (cos_t, sin_t, box_cos, box_sin, cos_hi, cos_lo, sin_hi, sin_lo)
+            )
+            cos_t, sin_t, box_cos, box_sin, cos_hi, cos_lo, sin_hi, sin_lo = tables
+        with jax.named_scope("ligand_spectra"):
+            coefficients = atom_weights * term_weights[:, None]
+            lig_re, lig_im = ligand_spectra(ligand_cells, coefficients, box_cos, box_sin)
+        with jax.named_scope("receptor_spectra"):
+            rec_re, rec_im = receptor_spectra(gathered, cos_hi, cos_lo, sin_hi, sin_lo)
+        with jax.named_scope("correlate"):
+            products = correlate(lig_re, lig_im, rec_re, rec_im)
+        products = reduce_scatter_terms(products, term_count)
+        with jax.named_scope("inverse_scores"):
+            scores = inverse_scores(products, cos_t, sin_t)
+            best_here = jnp.max(scores, axis=(2, 3))
+        best_scores = lax.all_gather(best_here, "term", axis=1, tiled=True)
+        best_all = lax.all_gather(best_scores, "rot", axis=1, tiled=True)
+        best_overall = jnp.max(best_all, axis=1)
+        return (best_scores, best_overall)
+
+    return body
 
 
 def solution(mesh):
     placed = (P("term", "rot", None), P("term"), P("term", None), P(None, "rot", None))
     return jax.shard_map(
-        body, mesh=mesh, in_specs=placed, out_specs=(P(None, "rot"), P()), check_vma=False
+        make_body(mesh.shape["term"]),
+        mesh=mesh,
+        in_specs=placed,
+        out_specs=(P(None, "rot"), P()),
+        check_vma=False,
     )

time: 239 us -> 163 us (0.68)
  blocking collectives: 66.6 us -> 22.9 us
  local copies, waits for them, and re-layouts: 36.6 us -> 11.2 us
  other arithmetic: 33.2 us -> 24.7 us
  waiting for transfers between devices: 48.8 us -> 45.9 us
  matrix products: 39.1 us -> 41.9 us
    unnamed x3 -> x1, waiting for transfers between devices: 48.8 us -> 0.68 us
    all_gather x1 -> x2, blocking collectives: 66.6 us -> 22.9 us  [the longest x1 18.7 us: body(): best_all = lax.all_gather(best_scores, 'rot', axis=1, tiled=True)]
    all_gather x1, waiting for transfers between devices: 0.01 us -> 29.5 us  [body(): gathered = lax.all_gather(receptor_grids, 'rot', axis=1, tiled=True)]
    ppermute x0 -> x1, waiting for transfers between devices: none -> 15.7 us  [reduce_scatter_terms(): total = total + lax.ppermute(outgoing, 'term', pairs)]
    sub x2 -> x0, local copies, waits for them, and re-layouts: 13 us -> none  [plane_tables(): cos_t = (cy * cz - sy * sz).reshape(side * side, G * HZ)]
    add x2 -> x0, local copies, waits for them, and re-layouts: 11.5 us -> none  [plane_tables(): sin_t = (sy * cz + cy * sz).reshape(side * side, G * HZ)]
    add x2, other arithmetic: 12.7 us -> 3.86 us  [plane_tables(): sin_t = (sy * cz + cy * sz).reshape(side * side, G * HZ)]
    convert_element_type x1, other arithmetic: 5.12 us -> 2.3 us  [split_bf16(): lower = (table - upper.astype(jnp.float32)).astype(jnp.bfloat16)]
  transfers between devices with their start and end apart: 2 -> 2, of which waited for: 1 -> 2; matrix products, arithmetic and copies ran while one was open for 23% -> 12% of each run, Pallas kernels for 0% -> 0%
where the time goes in v1:
time: 163 us; the launch traced here: 162 us
  waiting for transfers between devices  45.9 us (28%)
  matrix products  41.9 us (26%)
  other arithmetic  24.7 us (15%)
  blocking collectives  22.9 us (14%)
  between operations  14.2 us (9%)
  local copies, waits for them, and re-layouts  11.2 us (7%)
    all_gather x1, waiting for transfers between devices, body(): gathered = lax.all_gather(receptor_grids, 'rot', axis=1, tiled=True)  29.5 us
    all_gather x1, blocking collectives, body(): best_all = lax.all_gather(best_scores, 'rot', axis=1, tiled=True)  18.7 us
    ppermute x1, waiting for transfers between devices, reduce_scatter_terms(): total = total + lax.ppermute(outgoing, 'term', pairs)  15.7 us
    add x2, local copies, waits for them, and re-layouts, dot2(): return first + second  9.61 us
    dot_general x2, matrix products, dot2(): first = jnp.dot(rows, upper, preferred_element_type=jnp.float32)  9.15 us
    dot_general x2, matrix products, dot2(): second = jnp.dot(rows, lower, preferred_element_type=jnp.float32)  8.2 us
    sub x1, other arithmetic, receptor_spectra(): spec_re = mixed_re[:, :, :G] - mixed_ims[:, :, G:]  7.84 us
    dot_general x1, matrix products, receptor_spectra(): mixed_re = jnp.einsum('px,trxq->trpq', mix, plane_re, precision=HIGH)  5.18 us
  transfers between devices with their start and end apart: 2, of which 2 were waited for; matrix products, arithmetic and copies ran while one was open for 12% of the time, Pallas kernels for 0%

profile of v1, /device:TPU:0, one launch (start us, length us, event | category | flops | bytes accessed | tf_op | source)
XLA Modules:
  0.0 162.3 jit_solution(9747538450186945429)
XLA Ops:
  7.2 0.7 all-gather.4.cloned.1.call-update
  7.9 2.1 %multiply_add_fusion.1 = (f32[16,16,544]{2,1,0:T(8,128)}, f32[16,16,544]{2,1,0:T(8,128)}) fusion(f32[16,544]{1,0:T(8,128)} %constant.54.clone, f32[16,544]{1,0:T(8,128)} %constant.52.clone, f32[16,544]{1,0:T(8,128)} %constant.53.clone, f32[16,544]{1,0:T(8,128)} %constant.51.clone), kind=kLoop, calls=%fused_computation.42 | loop fusion | flops 835584 | bytes 1253376 | tf_op jit(solution)/shard_map/twiddle_tables/add | solution.py:35
  10.0 1.8 %multiply_add_fusion = (f32[32,32,544]{2,1,0:T(8,128)S(1)}, f32[32,32,544]{2,1,0:T(8,128)S(1)}) fusion(f32[32,544]{1,0:T(8,128)} %constant.50.clone, f32[32,544]{1,0:T(8,128)} %constant.48.clone, f32[32,544]{1,0:T(8,128)} %constant.49.clone, f32[32,544]{1,0:T(8,128)} %constant.47.clone), kind=kLoop, calls=%fused_computation.20 | loop fusion | flops 3342336 | bytes 4734976 | tf_op jit(solution)/shard_map/twiddle_tables/add | solution.py:35
  11.8 2.3 %subtract_convert_fusion = (bf16[1024,544]{1,0:T(8,128)(2,1)}, bf16[1024,544]{1,0:T(8,128)(2,1)}) fusion(f32[32,32,544]{2,1,0:T(8,128)S(1)} %get-tuple-element.24, f32[32,32,544]{2,1,0:T(8,128)S(1)} %get-tuple-element.25), kind=kLoop, calls=%fused_computation.18 | loop fusion | flops 4456448 | bytes 6684672 | tf_op jit(solution)/shard_map/twiddle_tables/convert_element_type | solution.py:41
  14.1 1.8 %bitcast_convert_fusion = (bf16[1024,544]{1,0:T(8,128)(2,1)}, bf16[1024,544]{1,0:T(8,128)(2,1)}) fusion(f32[32,32,544]{2,1,0:T(8,128)S(1)} %get-tuple-element.24, f32[32,32,544]{2,1,0:T(8,128)S(1)} %get-tuple-element.25), kind=kLoop, calls=%fused_computation.61 | loop fusion | flops 1114112 | bytes 6684672 | tf_op jit(solution)/shard_map/twiddle_tables/convert_element_type | solution.py:40
  15.9 2.8 %fusion = f32[11,2,4096]{2,0,1:T(8,128)S(1)} fusion(s32[2,256]{1,0:T(2,128)S(1)} %add_bitcast_fusion, f32[11,256]{1,0:T(8,128)S(1)} %copy-done.13, f32[11]{0:T(128)S(1)} %copy-done.14), kind=kOutput, calls=%fused_computation.1 | convolution fusion | flops 278924032 | bytes 373804 | tf_op jit(solution)/shard_map/ligand_spectra/ta,nac->tnc/dot_general | solution.py:76
  18.8 1.7 %fusion.20 = f32[11,2,16,544]{3,2,1,0:T(8,128)S(1)} fusion(f32[256,544]{1,0:T(8,128)} %bitcast.110, f32[11,2,16,256]{3,2,0,1:T(8,128)S(1)} %reshape.134), kind=kOutput, calls=%fused_computation.38 | convolution fusion | flops 294125568 | bytes 1683456 | tf_op jit(solution)/shard_map/ligand_spectra/tnxc,cq->tnxq/dot_general | solution.py:79
  20.5 1.7 %fusion.22 = f32[11,2,16,544]{3,2,1,0:T(8,128)S(1)} fusion(f32[256,544]{1,0:T(8,128)} %bitcast.109, f32[11,2,16,256]{3,2,0,1:T(8,128)S(1)} %reshape.134), kind=kOutput, calls=%fused_computation.40 | convolution fusion | flops 294125568 | bytes 1683456 | tf_op jit(solution)/shard_map/ligand_spectra/tnxc,cq->tnxq/dot_general | solution.py:78
  22.3 1.6 convolution_bitcast_fusion.2
  23.9 1.6 convolution_bitcast_fusion.3
  25.5 2.3 %slice_subtract_fusion.3 = (f32[11,2,32,544]{3,2,1,0:T(8,128)}, f32[11,2,32,544]{3,2,1,0:T(8,128)}) fusion(f32[11,2,64,544]{3,2,1,0:T(8,128)S(1)} %convolution_bitcast_fusion.2, f32[11,2,64,544]{3,2,1,0:T(8,128)S(1)} %convolution_bitcast_fusion.3), kind=kLoop, calls=%fused_computation.26 | loop fusion | flops 1148928 | bytes 9191424 | tf_op jit(solution)/shard_map/ligand_spectra/sub | solution.py:83
  27.8 29.5 %all-gather.4.cloned.1.call-done = bf16[11,128,1024]{2,1,0:T(8,128)(2,1)} async-done(((bf16[11,8,1024]{2,1,0:T(8,128)(2,1)}), bf16[11,128,1024]{2,1,0:T(8,128)(2,1)}) %all-gather.4.cloned.1.call-update) | async-done | bytes 2883600 | tf_op jit(solution)/shard_map/all_gather | solution.py:125
  57.3 4.6 %fusion.41 = f32[544,1408]{1,0:T(8,128)S(1)} fusion(bf16[1024,544]{1,0:T(8,128)(2,1)} %get-tuple-element.12, bf16[1408,1024]{1,0:T(8,128)(2,1)} %bitcast.114), kind=kOutput, calls=%fused_computation.64 | convolution fusion | flops 1568669696 | bytes 7061504 | tf_op jit(solution)/shard_map/receptor_spectra/dot_general | solution.py:51
  61.9 4.2 %fusion.3 = f32[1408,544]{0,1:T(8,128)} fusion(f32[544,1408]{1,0:T(8,128)S(1)} %fusion.41, bf16[1024,544]{1,0:T(8,128)(2,1)S(1)} %copy-done.6, bf16[1408,1024]{1,0:T(8,128)(2,1)S(1)} %bitcast.116), kind=kOutput, calls=%fused_computation.11 | convolution fusion | flops 1569435648 | bytes 10125312 | tf_op jit(solution)/shard_map/receptor_spectra/dot_general | solution.py:52
  66.1 4.8 %copy.48 = f32[1408,544]{1,0:T(8,128)} copy(f32[1408,544]{0,1:T(8,128)} %fusion.3) | data formatting | bytes 6127616 | tf_op jit(solution)/shard_map/receptor_spectra/add | solution.py:53
  70.9 4.6 %fusion.42 = f32[544,1408]{1,0:T(8,128)S(1)} fusion(bf16[1024,544]{1,0:T(8,128)(2,1)} %get-tuple-element.14, bf16[1408,1024]{1,0:T(8,128)(2,1)} %bitcast.115), kind=kOutput, calls=%fused_computation.65 | convolution fusion | flops 1568669696 | bytes 7061504 | tf_op jit(solution)/shard_map/receptor_spectra/dot_general | solution.py:51
  75.5 4.0 %fusion.2 = f32[1408,544]{0,1:T(8,128)} fusion(f32[544,1408]{1,0:T(8,128)S(1)} %fusion.42, bf16[1024,544]{1,0:T(8,128)(2,1)S(1)} %copy-done.5, bf16[1408,1024]{1,0:T(8,128)(2,1)S(1)} %bitcast.117), kind=kOutput, calls=%fused_computation.9 | convolution fusion | flops 1569435648 | bytes 10125312 | tf_op jit(solution)/shard_map/receptor_spectra/dot_general | solution.py:52
  79.5 4.8 %copy.49 = f32[1408,544]{1,0:T(8,128)} copy(f32[1408,544]{0,1:T(8,128)} %fusion.2) | data formatting | bytes 6127616 | tf_op jit(solution)/shard_map/receptor_spectra/add | solution.py:53
  84.3 5.2 %convolution_bitcast_fusion.1 = f32[11,4,64,544]{3,2,1,0:T(8,128)S(1)} fusion(f32[11,4,32,544]{3,2,1,0:T(8,128)} %bitcast.101, f32[64,32,1,1]{0,1,3,2:T(8,128)S(1)} %copy-done.7), kind=kOutput, calls=%fused_computation.13 | convolution fusion | flops 294125568 | bytes 9199616 | tf_op jit(solution)/shard_map/receptor_spectra/px,trxq->trpq/dot_general | solution.py:63
  89.5 5.1 %convolution_bitcast_fusion = f32[11,4,64,544]{3,2,1,0:T(8,128)} fusion(f32[11,4,32,544]{3,2,1,0:T(8,128)S(1)} %bitcast.102, f32[64,32,1,1]{0,1,3,2:T(8,128)S(1)} %copy-done.7), kind=kOutput, calls=%fused_computation.12 | convolution fusion | flops 294125568 | bytes 9199616 | tf_op jit(solution)/shard_map/receptor_spectra/px,trxq->trpq/dot_general | solution.py:64
  94.6 7.8 %slice_subtract_fusion.1 = (f32[11,4,32,544]{3,2,1,0:T(8,128)}, f32[11,4,32,544]{3,2,1,0:T(8,128)}) fusion(f32[11,4,64,544]{3,2,1,0:T(8,128)} %convolution_bitcast_fusion, f32[11,4,64,544]{3,2,1,0:T(8,128)S(1)} %convolution_bitcast_fusion.1), kind=kLoop, calls=%fused_computation.7 | loop fusion | flops 2297856 | bytes 18382848 | tf_op jit(solution)/shard_map/receptor_spectra/sub | solution.py:65
  102.5 5.1 %subtract_reduce_fusion = (f32[4,2,32,544]{3,2,1,0:T(8,128)S(1)}, f32[4,2,32,544]{3,2,1,0:T(8,128)S(1)}) fusion(f32[11,4,32,544]{3,2,1,0:T(8,128)} %get-tuple-element.21, f32[11,2,32,544]{3,2,1,0:T(8,128)} %get-tuple-element.23, f32[11,4,32,544]{3,2,1,0:T(8,128)} %get-tuple-element.20, f32[11,2,32,544]{3,2,1,0:T(8,128)S(1)} %copy-done.3), kind=kLoop, calls=%fused_computation.2 | loop fusion | flops 11976704 | bytes 10305536 | tf_op jit(solution)/shard_map/correlate/reduce_sum | solution.py:94
  107.6 0.8 copy-done.4
  108.4 0.9 fusion.14
  109.3 1.5 collective-permute-start
  110.8 15.7 %collective-permute-done = f32[2,4,1,32,544]{4,3,2,1,0:T(8,128)} collective-permute-done((f32[2,4,1,32,544]{4,3,2,1,0:T(8,128)}, f32[2,4,1,32,544]{4,3,2,1,0:T(8,128)}, u32[]{:S(2)}, u32[]{:S(2)}) %collective-permute-start) | collective-permute-done | bytes 557088 | tf_op jit(solution)/shard_map/ppermute | solution.py:119
  126.5 1.9 %fusion.18 = f32[2,4,544,64]{2,3,1,0:T(8,128)S(1)} fusion(f32[64,32,1,1]{0,1,3,2:T(8,128)S(1)} %copy-done.7, f32[2,4,1,32,544]{4,3,2,1,0:T(8,128)} %collective-permute-done, s32[]{:T(128)S(6)} %select_n.13, f32[1,4,2,32,544]{4,3,2,1,0:T(8,128)} %bitcast.106, f32[1,4,2,32,544]{4,3,2,1,0:T(8,128)S(1)} %bitcast.104), kind=kOutput, calls=%fused_computation.37 | convolution fusion | flops 53755904 | bytes 2793476 | tf_op jit(solution)/shard_map/inverse_scores/xp,srnpq->srnxq/dot_general | solution.py:100
  128.5 1.5 fusion.4
  129.9 1.5 fusion.11
  131.5 4.2 %all-gather = f32[2,1,4]{2,1,0:T(1,128)S(1)} all-gather(f32[1,1,4]{2,1,0:T(1,128)S(1)} %bitcast.113), channel_id=1, replica_groups=mesh['rot'=16,'term'=2] {'term'}, dimensions={0}, use_global_device_ids=true | all-gather | bytes 48 | tf_op jit(solution)/shard_map/all_gather | solution.py:146
  135.7 18.7 %all-gather.1 = f32[16,2,4]{2,1,0:T(2,128)S(1)} all-gather(f32[1,2,4]{2,1,0:T(2,128)S(1)} %bitcast.111), channel_id=1, replica_groups=mesh['rot'=16,'term'=2] {'rot'}, dimensions={0}, use_global_device_ids=true | all-gather | bytes 544 | tf_op jit(solution)/shard_map/all_gather | solution.py:147
  154.9 0.6 copy.70
  (33 shorter events, 0.8 us)
Async XLA Ops:
  7.2 50.1 %all-gather.4.cloned.1.call-start = ((), (), s32[]{:S(2)}) async-start(), calls=%async_computation | async-start | bytes 3063808 | tf_op jit(solution)/shard_map/all_gather | solution.py:125
  11.8 2.4 %copy-start = (f32[32,32,544]{2,1,0:T(8,128)}, f32[32,32,544]{2,1,0:T(8,128)S(1)}, u32[]{:S(2)}) copy-start(f32[32,32,544]{2,1,0:T(8,128)S(1)} %get-tuple-element.24) | copy-start | bytes 6684676
  14.1 1.8 %copy-start.10 = (s32[3,2,256]{2,1,0:T(2,128)S(1)}, s32[3,2,256]{2,1,0:T(2,128)}, u32[]{:S(2)}) copy-start(s32[3,2,256]{2,1,0:T(2,128)} %param.19) | copy-start | bytes 18436
  14.1 1.8 %copy-start.13 = (f32[11,256]{1,0:T(8,128)S(1)}, f32[11,256]{1,0:T(8,128)}, u32[]{:S(2)}) copy-start(f32[11,256]{1,0:T(8,128)} %param.18) | copy-start | bytes 33796
  14.1 1.8 %copy-start.14 = (f32[11]{0:T(128)S(1)}, f32[11]{0:T(128)}, u32[]{:S(2)}) copy-start(f32[11]{0:T(128)} %param.17) | copy-start | bytes 136
  18.7 3.5 %copy-start.8 = (f32[64,16,1,1]{0,1,3,2:T(8,128)S(1)}, f32[64,16,1,1]{0,1,3,2:T(8,128)}, u32[]{:S(2)}) copy-start(f32[64,16,1,1]{0,1,3,2:T(8,128)} %constant.62) | copy-start | bytes 12292
  57.3 4.6 %copy-start.6 = (bf16[1024,544]{1,0:T(8,128)(2,1)S(1)}, bf16[1024,544]{1,0:T(8,128)(2,1)}, u32[]{:S(2)}) copy-start(bf16[1024,544]{1,0:T(8,128)(2,1)} %get-tuple-element.13) | copy-start | bytes 3342340
  57.3 4.6 %copy-start.11 = (bf16[11,128,1024]{2,1,0:T(8,128)(2,1)S(1)}, bf16[11,128,1024]{2,1,0:T(8,128)(2,1)}, u32[]{:S(2)}) copy-start(bf16[11,128,1024]{2,1,0:T(8,128)(2,1)} %all-gather.4.cloned.1.call-done) | copy-start | bytes 8650756
  70.9 4.6 %copy-start.5 = (bf16[1024,544]{1,0:T(8,128)(2,1)S(1)}, bf16[1024,544]{1,0:T(8,128)(2,1)}, u32[]{:S(2)}) copy-start(bf16[1024,544]{1,0:T(8,128)(2,1)} %get-tuple-element.15) | copy-start | bytes 3342340
  70.9 4.6 %copy-start.12 = (bf16[11,128,1024]{2,1,0:T(8,128)(2,1)S(1)}, bf16[11,128,1024]{2,1,0:T(8,128)(2,1)}, u32[]{:S(2)}) copy-start(bf16[11,128,1024]{2,1,0:T(8,128)(2,1)} %all-gather.4.cloned.1.call-done) | copy-start | bytes 8650756
  79.5 4.8 %copy-start.7 = (f32[64,32,1,1]{0,1,3,2:T(8,128)S(1)}, f32[64,32,1,1]{0,1,3,2:T(8,128)}, u32[]{:S(2)}) copy-start(f32[64,32,1,1]{0,1,3,2:T(8,128)} %constant.63) | copy-start | bytes 24580
  84.3 5.2 %copy-start.2 = (f32[1408,544]{1,0:T(8,128)S(1)}, f32[1408,544]{1,0:T(8,128)}, u32[]{:S(2)}) copy-start(f32[1408,544]{1,0:T(8,128)} %copy.49) | copy-start | bytes 9191428
  94.6 7.8 %copy-start.3 = (f32[11,2,32,544]{3,2,1,0:T(8,128)S(1)}, f32[11,2,32,544]{3,2,1,0:T(8,128)}, u32[]{:S(2)}) copy-start(f32[11,2,32,544]{3,2,1,0:T(8,128)} %get-tuple-element.22) | copy-start | bytes 4595716
  107.6 0.8 copy-start.4
  108.4 20.0 %copy-start.9 = (f32[544]{0:T(1024)S(1)}, f32[544]{0:T(1024)}, u32[]{:S(2)}) copy-start(f32[544]{0:T(1024)} %constant.57.clone) | copy-start | bytes 6532
  109.3 17.2 %collective-permute-start = (f32[2,4,1,32,544]{4,3,2,1,0:T(8,128)}, f32[2,4,1,32,544]{4,3,2,1,0:T(8,128)}, u32[]{:S(2)}, u32[]{:S(2)}) collective-permute-start(f32[2,4,1,32,544]{4,3,2,1,0:T(8,128)} %fusion.14), channel_id=1, source_target_pairs={{0,1},{1,0},{2,3},{3,2},{4,5},{5,4},{6,7},{7,6},{8,9},{9,8},{10,11... | collective-permute-start | bytes 1671176 | tf_op jit(solution)/shard_map/ppermute | solution.py:119
  110.8 17.6 %copy-start.1 = (f32[32,32,544]{2,1,0:T(8,128)S(1)}, f32[32,32,544]{2,1,0:T(8,128)}, u32[]{:S(2)}) copy-start(f32[32,32,544]{2,1,0:T(8,128)} %copy-done) | copy-start | bytes 6684676
Sparse Core Ops, SparseCore 0:
  10.2 47.0 all-gather.3

commit v2 on v1

v2 whole, which is shorter than its diff:
```python
import math

import numpy as np

import jax
import jax.numpy as jnp
from jax import lax
from jax.sharding import PartitionSpec as P

G = 32
HZ = G // 2 + 1
LB = 16

HIGH = lax.Precision.HIGH
HIGHEST = lax.Precision.HIGHEST


def line_table(freq_count, cell_count):
    freq = np.arange(freq_count)[:, None]
    cell = np.arange(cell_count)[None, :]
    phase = (freq * cell % G).astype(np.float64) * (2.0 * math.pi / G)
    return np.cos(phase).astype(np.float32), np.sin(phase).astype(np.float32)


def plane_tables(side):
    column = np.arange(G * HZ)
    cell = np.arange(side)[:, None]
    phase_y = (cell * (column // HZ)[None, :] % G) * (2.0 * math.pi / G)
    phase_z = (cell * (column % HZ)[None, :] % G) * (2.0 * math.pi / G)
    cy = jnp.asarray(np.cos(phase_y).astype(np.float32))[:, None, :]
    sy = jnp.asarray(np.sin(phase_y).astype(np.float32))[:, None, :]
    cz = jnp.asarray(np.cos(phase_z).astype(np.float32))[None, :, :]
    sz = jnp.asarray(np.sin(phase_z).astype(np.float32))[None, :, :]
    cos_t = cy * cz - sy * sz
    sin_t = sy * cz + cy * sz
    return jnp.concatenate([cos_t, sin_t], axis=-1).reshape(side * side, 2 * G * HZ)


def split_bf16(table):
    upper = table.astype(jnp.bfloat16)
    lower = (table - upper.astype(jnp.float32)).astype(jnp.bfloat16)
    return upper, lower


def mix_table(cell_count):
    cos_x, sin_x = line_table(G, cell_count)
    return jnp.asarray(np.concatenate([cos_x, sin_x], axis=0))


def receptor_mixed(grids, table_hi, table_lo):
    terms, rows, cells = grids.shape
    receptors = rows // G
    flat = grids.reshape(terms * rows, cells)
    plane = jnp.dot(flat, table_hi, preferred_element_type=jnp.float32)
    plane = plane + jnp.dot(flat, table_lo, preferred_element_type=jnp.float32)
    plane = plane.reshape(terms, receptors, G, 2 * G * HZ)
    return jnp.einsum("px,trxq->trpq", mix_table(G), plane, precision=HIGH)


def ligand_coefficients(voxels, coefficients, box_table):
    rot_count = voxels.shape[1]
    terms = coefficients.shape[0]
    width = G * HZ
    flat_index = (voxels[0] * LB + voxels[1]) * LB + voxels[2]
    cells = jnp.arange(LB**3, dtype=jnp.int32)
    onehot = (flat_index[:, :, None] == cells[None, None, :]).astype(jnp.float32)
    grid = jnp.einsum("ta,nac->tnc", coefficients, onehot, precision=HIGHEST)
    grid = grid.reshape(terms, rot_count, LB, LB * LB)
    plane = jnp.einsum("tnxc,cq->tnxq", grid, box_table, precision=HIGH)
    mixed = jnp.einsum("px,tnxq->tnpq", mix_table(LB), plane, precision=HIGH)
    lig_re = mixed[:, :, :G, :width] - mixed[:, :, G:, width:]
    lig_im = -mixed[:, :, :G, width:] - mixed[:, :, G:, :width]
    first = jnp.concatenate([lig_re, -lig_im], axis=-1)
    second = jnp.concatenate([-lig_im, -lig_re], axis=-1)
    third = jnp.concatenate([-lig_re, lig_im], axis=-1)
    return first, second, third


def correlate(mixed, first, second, third):
    rec_cos = mixed[:, :, None, :G]
    rec_sin = mixed[:, :, None, G:]
    a = first[:, None]
    b = second[:, None]
    d = third[:, None]
    part_re = jnp.sum(rec_cos * a + rec_sin * b, axis=0)
    part_im = jnp.sum(rec_cos * b + rec_sin * d, axis=0)
    return part_re, part_im


def inverse_scores(products, full_table):
    width = G * HZ
    mixed = jnp.einsum("xp,srnpq->srnxq", mix_table(G), products, precision=HIGH)
    inv_re = mixed[0, :, :, :G] - mixed[1, :, :, G:]
    inv_im = mixed[1, :, :, :G] + mixed[0, :, :, G:]
    freq_z = np.arange(width) % HZ
    fold = np.where((freq_z == 0) | (freq_z == G // 2), 1.0, 2.0) / float(G**3)
    fold = jnp.asarray(fold.astype(np.float32))
    joined = jnp.concatenate([inv_re * fold, -inv_im * fold], axis=-1)
    return jnp.einsum("rnxq,cq->rnxc", joined, full_table, precision=HIGH)


def reduce_scatter_terms(products, term_count):
    share = products.shape[2] // term_count
    here = lax.axis_index("term")
    total = lax.dynamic_slice_in_dim(products, here * share, share, axis=2)
    for shift in range(1, term_count):
        target = (here + shift) % term_count
        outgoing = lax.dynamic_slice_in_dim(products, target * share, share, axis=2)
        pairs = [(k, (k + shift) % term_count) for k in range(term_count)]
        total = total + lax.ppermute(outgoing, "term", pairs)
    return total


def max_over_rot(values, rot_count):
    if rot_count & (rot_count - 1):
        gathered = lax.all_gather(values, "rot", axis=0, tiled=True)
        return jnp.max(gathered, axis=0, keepdims=True)
    shift = 1
    while shift < rot_count:
        pairs = [(k, k ^ shift) for k in range(rot_count)]
        values = jnp.maximum(values, lax.ppermute(values, "rot", pairs))
        shift *= 2
    return values


def make_body(term_count, rot_count):
    def body(receptor_grids, term_weights, atom_weights, ligand_cells):
        terms_here = receptor_grids.shape[0]
        cut = (terms_here + 1) // 2
        chunks = [(0, cut), (cut, terms_here)]
        gathered = [
            lax.all_gather(receptor_grids[lo:hi], "rot", axis=1, tiled=True) for lo, hi in chunks
        ]
        with jax.named_scope("twiddle_tables"):
            full_table = plane_tables(G)
            box_table = plane_tables(LB)
            table_hi, table_lo = split_bf16(full_table)
            tables = lax.optimization_barrier((full_table, box_table, table_hi, table_lo))
            full_table, box_table, table_hi, table_lo = tables
        with jax.named_scope("ligand_spectra"):
            coefficients = atom_weights * term_weights[:, None]
            first, second, third = ligand_coefficients(ligand_cells, coefficients, box_table)
        part_re = 0.0
        part_im = 0.0
        for (lo, hi), grids in zip(chunks, gathered):
            with jax.named_scope("receptor_spectra"):
                mixed = receptor_mixed(grids, table_hi, table_lo)
            with jax.named_scope("correlate"):
                add_re, add_im = correlate(mixed, first[lo:hi], second[lo:hi], third[lo:hi])
            part_re = part_re + add_re
            part_im = part_im + add_im
        width = G * HZ
        prod_re = part_re[..., :width] + part_re[..., width:]
        prod_im = part_im[..., :width] + part_im[..., width:]
        products = jnp.stack([prod_re, prod_im], axis=0)
        products = reduce_scatter_terms(products, term_count)
        with jax.named_scope("inverse_scores"):
            scores = inverse_scores(products, full_table)
            best_here = jnp.max(scores, axis=(2, 3))
        best_scores = lax.all_gather(best_here, "term", axis=1, tiled=True)
        best_overall = max_over_rot(jnp.max(best_scores, axis=1)[None], rot_count)[0]
        return (best_scores, best_overall)

    return body


def solution(mesh):
    placed = (P("term", "rot", None), P("term"), P("term", None), P(None, "rot", None))
    return jax.shard_map(
        make_body(mesh.shape["term"], mesh.shape["rot"]),
        mesh=mesh,
        in_specs=placed,
        out_specs=(P(None, "rot"), P()),
        check_vma=False,
    )
```

time: 163 us -> 162 us (level)
  waiting for transfers between devices: 45.9 us -> 64.9 us
  blocking collectives: 22.9 us -> 4.21 us
  local copies, waits for them, and re-layouts: 11.2 us -> 18.4 us
  matrix products: 41.9 us -> 35 us
  other arithmetic: 24.7 us -> 20.8 us
  starting transfers between devices: 1.51 us -> 3.53 us
    all_gather x1 -> x0, blocking collectives: 18.7 us -> none  [body(): best_all = lax.all_gather(best_scores, 'rot', axis=1, tiled=True)]
    ppermute x0 -> x4, waiting for transfers between devices: none -> 10.8 us  [max_over_rot(): values = jnp.maximum(values, lax.ppermute(values, 'rot', pairs))]
    all_gather x1 -> x2, waiting for transfers between devices: 29.5 us -> 38.6 us  [body(): lax.all_gather(receptor_grids[lo:hi], 'rot', axis=1, tiled=True)]
    sub x2, other arithmetic: 10.2 us -> 1.91 us  [plane_tables(): cos_t = cy * cz - sy * sz]
    dot_general x14 -> x11, matrix products: 41.9 us -> 35 us  [the longest x2 8.08 us: receptor_mixed(): plane = jnp.dot(flat, table_hi, preferred_element_type=jnp.float32)]
    concatenate x0 -> x3, other arithmetic: none -> 6.23 us  [the longest x2 5.99 us: ligand_coefficients(): first = jnp.concatenate([lig_re, -lig_im], axis=-1)]
    unnamed x31 -> x47, local copies, waits for them, and re-layouts: 1.5 us -> 5.76 us
    slice x0 -> x4, local copies, waits for them, and re-layouts: none -> 4.2 us  [the longest x2 3.07 us: body(): receptor_grids[lo:hi]]
  transfers between devices with their start and end apart: 2 -> 7, of which waited for: 2 -> 7; matrix products, arithmetic and copies ran while one was open for 12% -> 26% of each run, Pallas kernels for 0% -> 0%
where the time goes in v2:
time: 162 us; the launch traced here: 161 us
  waiting for transfers between devices  64.9 us (40%)
  matrix products  35 us (22%)
  other arithmetic  20.8 us (13%)
  local copies, waits for them, and re-layouts  18.4 us (11%)
  between operations  14.4 us (9%)
  blocking collectives  4.21 us (3%)
  starting transfers between devices  3.53 us (2%)
    all_gather x2, waiting for transfers between devices, body(): lax.all_gather(receptor_grids[lo:hi], 'rot', axis=1, tiled=True)  38.6 us
    ppermute x1, waiting for transfers between devices, reduce_scatter_terms(): total = total + lax.ppermute(outgoing, 'term', pairs)  15.4 us
    ppermute x4, waiting for transfers between devices, max_over_rot(): values = jnp.maximum(values, lax.ppermute(values, 'rot', pairs))  10.8 us
    dot_general x2, matrix products, receptor_mixed(): plane = jnp.dot(flat, table_hi, preferred_element_type=jnp.float32)  8.08 us
    dot_general x2, matrix products, receptor_mixed(): plane = plane + jnp.dot(flat, table_lo, preferred_element_type=jnp.float32)  7.55 us
    add x2, local copies, waits for them, and re-layouts, receptor_mixed(): plane = plane + jnp.dot(flat, table_lo, preferred_element_type=jnp.float32)  6.53 us
    reduce_sum x2, other arithmetic, correlate(): part_im = jnp.sum(rec_cos * b + rec_sin * d, axis=0)  6.04 us
    concatenate x2, other arithmetic, ligand_coefficients(): first = jnp.concatenate([lig_re, -lig_im], axis=-1)  5.99 us
  transfers between devices with their start and end apart: 7, of which 7 were waited for; matrix products, arithmetic and copies ran while one was open for 26% of the time, Pallas kernels for 0%

profile of v2, /device:TPU:0, one launch (start us, length us, event | category | flops | bytes accessed | tf_op | source)
XLA Modules:
  0.0 161.2 jit_solution(17769088742113290178)
XLA Ops:
  7.2 1.5 slice.93
  8.8 1.5 slice.81
  10.4 1.8 %multiply_subtract_fusion = (f32[32,32,544]{2,1,0:T(8,128)S(1)}, f32[32,32,544]{2,1,0:T(8,128)S(1)}) fusion(f32[32,544]{1,0:T(8,128)} %constant.50.clone, f32[32,544]{1,0:T(8,128)} %constant.48.clone, f32[32,544]{1,0:T(8,128)} %constant.49.clone, f32[32,544]{1,0:T(8,128)} %constant.47.clone), kind=kLoop, calls=%fused_computation.25 | loop fusion | flops 3342336 | bytes 4734976 | tf_op jit(solution)/shard_map/twiddle_tables/sub | solution.py:34
  12.2 4.1 %subtract_convert_fusion = (bf16[1024,1088]{1,0:T(8,128)(2,1)S(1)}, bf16[1024,1088]{1,0:T(8,128)(2,1)}, f32[1024,1088]{1,0:T(8,128)}) fusion(f32[1024,544]{1,0:T(8,128)S(1)} %bitcast.89, f32[1024,544]{1,0:T(8,128)S(1)} %bitcast.88), kind=kLoop, calls=%fused_computation.12 | loop fusion | flops 5570560 | bytes 13369344 | tf_op jit(solution)/shard_map/twiddle_tables/convert_element_type | solution.py:41
  17.1 3.6 %fusion = f32[11,2,4096]{2,0,1:T(8,128)} fusion(s32[2,256]{1,0:T(2,128)S(1)} %add_bitcast_fusion, f32[11,256]{1,0:T(8,128)S(1)} %copy-done.21, f32[11]{0:T(128)S(1)} %copy-done.22), kind=kOutput, calls=%fused_computation.1 | convolution fusion | flops 278924032 | bytes 373804 | tf_op jit(solution)/shard_map/ligand_spectra/ta,nac->tnc/dot_general | solution.py:67
  20.7 1.9 %reshape.178 = f32[11,2,16,256]{3,2,0,1:T(8,128)} reshape(f32[11,2,4096]{2,0,1:T(8,128)} %fusion) | data formatting | bytes 720896 | tf_op jit(solution)/shard_map/ligand_spectra/reshape | solution.py:68
  22.6 1.9 %fusion.9 = f32[11,2,16,1088]{3,2,1,0:T(8,128)S(1)} fusion(f32[256,1088]{1,0:T(8,128)S(1)} %pad_maximum_fusion.4, f32[11,2,16,256]{3,2,0,1:T(8,128)} %reshape.178), kind=kOutput, calls=%fused_computation.40 | convolution fusion | flops 588251136 | bytes 3006464 | tf_op jit(solution)/shard_map/ligand_spectra/tnxc,cq->tnxq/dot_general | solution.py:69
  24.5 2.7 %convolution_bitcast_fusion.1 = f32[11,2,64,1088]{3,2,1,0:T(8,128)S(1)} fusion(f32[11,2,16,1088]{3,2,1,0:T(8,128)S(1)} %fusion.9, f32[64,16,1,1]{0,1,3,2:T(8,128)S(1)} %copy-done.16), kind=kOutput, calls=%fused_computation.7 | convolution fusion | flops 147062784 | bytes 7663616 | tf_op jit(solution)/shard_map/ligand_spectra/px,tnxq->tnpq/dot_general | solution.py:70
  27.3 1.1 fusion.36
  28.4 3.2 %fusion.8 = (f32[6,2,32,1088]{3,2,1,0:T(8,128)}, f32[6,2,32,1088]{3,2,1,0:T(8,128)}, f32[6,2,32,1088]{3,2,1,0:T(8,128)}) fusion(f32[11,2,32,544]{3,2,1,0:T(8,128)S(1)} %get-tuple-element.24, f32[11,2,32,544]{3,2,1,0:T(8,128)S(1)} %get-tuple-element.14, f32[11,2,32,544]{3,2,1,0:T(8,128)S(1)} %get-tuple-element.23, f32[11,2,32,544]{3,2,1,0:T(8,128)S(1)} %get-tuple-element.15), kind=kLoop, calls=%fused_computation.31 | loop fusion | flops 1253376 | bytes 11141120 | tf_op jit(solution)/shard_map/ligand_spectra/concatenate | solution.py:73
  31.6 2.8 %pad_maximum_fusion.3 = (f32[5,2,32,1088]{3,2,1,0:T(8,128)}, f32[5,2,32,1088]{3,2,1,0:T(8,128)}, f32[5,2,32,1088]{3,2,1,0:T(8,128)}) fusion(f32[11,2,32,544]{3,2,1,0:T(8,128)S(1)} %get-tuple-element.14, f32[11,2,32,544]{3,2,1,0:T(8,128)S(1)} %get-tuple-element.24, f32[11,2,32,544]{3,2,1,0:T(8,128)S(1)} %get-tuple-element.23, ...), kind=kLoop, calls=%fused_computation.38 | loop fusion | flops 1044480 | bytes 10305536 | tf_op jit(solution)/shard_map/ligand_spectra/concatenate | solution.py:73
  34.4 17.3 %all-gather.6.cloned.1.call-done = bf16[5,128,1024]{2,1,0:T(8,128)(2,1)} async-done(((bf16[5,8,1024]{2,1,0:T(8,128)(2,1)}), bf16[5,128,1024]{2,1,0:T(8,128)(2,1)}) %all-gather.6.cloned.1.call-update) | async-done | bytes 1310736 | tf_op jit(solution)/shard_map/all_gather | solution.py:132
  51.8 4.4 %fusion.41 = f32[1088,640]{1,0:T(8,128)S(1)} fusion(bf16[1024,1088]{1,0:T(8,128)(2,1)} %get-tuple-element.6, bf16[640,1024]{1,0:T(8,128)(2,1)} %bitcast.99), kind=kOutput, calls=%fused_computation.79 | convolution fusion | flops 1426063360 | bytes 6324224 | tf_op jit(solution)/shard_map/receptor_spectra/dot_general | solution.py:54
  56.1 3.7 %fusion.5 = f32[640,1088]{0,1:T(8,128)} fusion(f32[1088,640]{1,0:T(8,128)S(1)} %fusion.41, bf16[1024,1088]{1,0:T(8,128)(2,1)S(1)} %get-tuple-element.7, bf16[640,1024]{1,0:T(8,128)(2,1)S(1)} %bitcast.100), kind=kOutput, calls=%fused_computation.17 | convolution fusion | flops 1426759680 | bytes 9109504 | tf_op jit(solution)/shard_map/receptor_spectra/dot_general | solution.py:55
  59.8 3.1 %copy.45 = f32[640,1088]{1,0:T(8,128)S(1)} copy(f32[640,1088]{0,1:T(8,128)} %fusion.5) | data formatting | bytes 5570560 | tf_op jit(solution)/shard_map/receptor_spectra/add | solution.py:55
  62.9 2.6 %convolution_bitcast_fusion.2 = f32[5,4,64,1088]{3,2,1,0:T(8,128)S(1)} fusion(f32[5,4,32,1088]{3,2,1,0:T(8,128)S(1)} %bitcast.87, f32[64,32,1,1]{0,1,3,2:T(8,128)S(1)} %copy-done.11), kind=kOutput, calls=%fused_computation.8 | convolution fusion | flops 267386880 | bytes 8364032 | tf_op jit(solution)/shard_map/receptor_spectra/px,trxq->trpq/dot_general | solution.py:57
  67.7 3.5 %add_reduce_fusion.2 = (f32[4,2,32,1088]{3,2,1,0:T(8,128)}, f32[4,2,32,1088]{3,2,1,0:T(8,128)}) fusion(f32[5,2,32,1088]{3,2,1,0:T(8,128)S(1)} %copy-done.5, f32[5,2,32,1088]{3,2,1,0:T(8,128)S(1)} %copy-done.4, f32[5,4,32,1088]{3,2,1,0:T(8,128)S(1)} %get-tuple-element.26, f32[5,4,32,1088]{3,2,1,0:T(8,128)S(1)} %get-tuple-element.25, ...), kind=kLoop, calls=%fused_computation.4 | loop fusion | flops 10584064 | bytes 11976704 | tf_op jit(solution)/shard_map/correlate/reduce_sum | solution.py:86
  71.2 21.3 %all-gather.4.cloned.1.call-done = bf16[6,128,1024]{2,1,0:T(8,128)(2,1)} async-done(((bf16[6,8,1024]{2,1,0:T(8,128)(2,1)}), bf16[6,128,1024]{2,1,0:T(8,128)(2,1)}) %all-gather.4.cloned.1.call-update) | async-done | bytes 1572880 | tf_op jit(solution)/shard_map/all_gather | solution.py:132
  92.5 3.7 %fusion.40 = f32[1088,768]{1,0:T(8,128)S(1)} fusion(bf16[1024,1088]{1,0:T(8,128)(2,1)S(1)} %copy-done.10, bf16[768,1024]{1,0:T(8,128)(2,1)} %bitcast.97), kind=kOutput, calls=%fused_computation.78 | convolution fusion | flops 1711276032 | bytes 7143424 | tf_op jit(solution)/shard_map/receptor_spectra/dot_general | solution.py:54
  96.3 3.9 %fusion.4 = f32[768,1088]{0,1:T(8,128)} fusion(f32[1088,768]{1,0:T(8,128)S(1)} %fusion.40, bf16[1024,1088]{1,0:T(8,128)(2,1)S(1)} %copy-done.9, bf16[768,1024]{1,0:T(8,128)(2,1)S(1)} %bitcast.98), kind=kOutput, calls=%fused_computation.15 | convolution fusion | flops 1712111616 | bytes 10485760 | tf_op jit(solution)/shard_map/receptor_spectra/dot_general | solution.py:55
  100.2 3.5 %copy.42 = f32[768,1088]{1,0:T(8,128)S(1)} copy(f32[768,1088]{0,1:T(8,128)} %fusion.4) | data formatting | bytes 6684672 | tf_op jit(solution)/shard_map/receptor_spectra/add | solution.py:55
  103.6 3.0 %convolution_bitcast_fusion = f32[6,4,64,1088]{3,2,1,0:T(8,128)S(1)} fusion(f32[6,4,32,1088]{3,2,1,0:T(8,128)S(1)} %bitcast.86, f32[64,32,1,1]{0,1,3,2:T(8,128)S(1)} %copy-done.11), kind=kOutput, calls=%fused_computation.6 | convolution fusion | flops 320864256 | bytes 10035200 | tf_op jit(solution)/shard_map/receptor_spectra/px,trxq->trpq/dot_general | solution.py:57
  109.2 2.5 %add_reduce_fusion = (f32[4,2,32,1088]{3,2,1,0:T(8,128)S(1)}, f32[4,2,32,1088]{3,2,1,0:T(8,128)S(1)}) fusion(f32[6,2,32,1088]{3,2,1,0:T(8,128)S(1)} %copy-done.2, f32[6,2,32,1088]{3,2,1,0:T(8,128)S(1)} %copy-done.1, f32[6,4,32,1088]{3,2,1,0:T(8,128)S(1)} %get-tuple-element.22, f32[6,4,32,1088]{3,2,1,0:T(8,128)S(1)} %get-tuple-element.21, ...), kind=kLoop, calls=%fused_computation.2 | loop fusion | flops 12812288 | bytes 13926400 | tf_op jit(solution)/shard_map/correlate/reduce_sum | solution.py:86
  111.9 1.1 copy-done.6
  113.7 1.5 collective-permute-start
  115.2 15.4 %collective-permute-done = f32[2,4,1,32,544]{4,3,2,1,0:T(8,128)S(1)} collective-permute-done((f32[2,4,1,32,544]{4,3,2,1,0:T(8,128)S(1)}, f32[2,4,1,32,544]{4,3,2,1,0:T(8,128)S(1)}, u32[]{:S(2)}, u32[]{:S(2)}) %collective-permute-start) | collective-permute-done | bytes 557088 | tf_op jit(solution)/shard_map/ppermute | solution.py:110
  131.5 4.9 %fusion.11 = f32[4]{0:T(128)S(1)} fusion(f32[1024,1088]{1,0:T(8,128)} %get-tuple-element.9, f32[4,1,32,544]{3,2,0,1:T(8,128)S(1)} %get-tuple-element.38, f32[4,1,32,544]{3,2,0,1:T(8,128)S(1)} %get-tuple-element.37), kind=kOutput, calls=%fused_computation.42 | convolution fusion | flops 855908352 | bytes 5013520 | tf_op jit(solution)/shard_map/inverse_scores/rnxq,cq->rnxc/dot_general | solution.py:99
  136.3 4.2 %all-gather = f32[2,1,4]{2,1,0:T(1,128)S(1)} all-gather(f32[1,1,4]{2,1,0:T(1,128)S(1)} %bitcast.95), channel_id=1, replica_groups=mesh['rot'=16,'term'=2] {'term'}, dimensions={0}, use_global_device_ids=true | all-gather | bytes 48 | tf_op jit(solution)/shard_map/all_gather | solution.py:160
  140.6 1.1 collective-permute-done.1
  142.4 2.9 %collective-permute-done.2 = f32[1,4]{1,0:T(1,128)S(1)} collective-permute-done((f32[1,4]{1,0:T(1,128)S(1)}, f32[1,4]{1,0:T(1,128)S(1)}, u32[]{:S(2)}, u32[]{:S(2)}) %collective-permute-start.2) | collective-permute-done | bytes 48 | tf_op jit(solution)/shard_map/ppermute | solution.py:121
  145.7 3.1 %collective-permute-done.3 = f32[1,4]{1,0:T(1,128)S(1)} collective-permute-done((f32[1,4]{1,0:T(1,128)S(1)}, f32[1,4]{1,0:T(1,128)S(1)}, u32[]{:S(2)}, u32[]{:S(2)}) %collective-permute-start.3) | collective-permute-done | bytes 48 | tf_op jit(solution)/shard_map/ppermute | solution.py:121
  149.6 3.7 %collective-permute-done.4 = f32[1,4]{1,0:T(1,128)S(1)} collective-permute-done((f32[1,4]{1,0:T(1,128)S(1)}, f32[1,4]{1,0:T(1,128)S(1)}, u32[]{:S(2)}, u32[]{:S(2)}) %collective-permute-start.4) | collective-permute-done | bytes 48 | tf_op jit(solution)/shard_map/ppermute | solution.py:121
  (70 shorter events, 10.3 us)
Async XLA Ops:
  7.2 44.6 %all-gather.6.cloned.1.call-start = ((), (), s32[]{:S(2)}) async-start(), calls=%async_computation.1 | async-start | bytes 1392640 | tf_op jit(solution)/shard_map/all_gather | solution.py:132
  8.8 83.7 %all-gather.4.cloned.1.call-start = ((), (), s32[]{:S(2)}) async-start(), calls=%async_computation | async-start | bytes 1671168 | tf_op jit(solution)/shard_map/all_gather | solution.py:132
  12.2 4.1 %copy-start.12 = (f32[16,544]{1,0:T(8,128)S(1)}, f32[16,544]{1,0:T(8,128)}, u32[]{:S(2)}) copy-start(f32[16,544]{1,0:T(8,128)} %constant.51.clone) | copy-start | bytes 104452
  12.2 4.1 %copy-start.13 = (f32[16,544]{1,0:T(8,128)S(1)}, f32[16,544]{1,0:T(8,128)}, u32[]{:S(2)}) copy-start(f32[16,544]{1,0:T(8,128)} %constant.52.clone) | copy-start | bytes 104452
  12.2 4.1 %copy-start.14 = (f32[16,544]{1,0:T(8,128)S(1)}, f32[16,544]{1,0:T(8,128)}, u32[]{:S(2)}) copy-start(f32[16,544]{1,0:T(8,128)} %constant.53.clone) | copy-start | bytes 104452
  12.2 4.1 %copy-start.15 = (f32[16,544]{1,0:T(8,128)S(1)}, f32[16,544]{1,0:T(8,128)}, u32[]{:S(2)}) copy-start(f32[16,544]{1,0:T(8,128)} %constant.54.clone) | copy-start | bytes 104452
  16.3 39.8 %copy-start.8 = (bf16[1024,1088]{1,0:T(8,128)(2,1)}, bf16[1024,1088]{1,0:T(8,128)(2,1)S(1)}, u32[]{:S(2)}) copy-start(bf16[1024,1088]{1,0:T(8,128)(2,1)S(1)} %get-tuple-element.7) | copy-start | bytes 6684676
  16.3 0.7 copy-start.17
  16.3 0.8 copy-start.21
  16.4 0.8 copy-start.22
  20.7 3.8 %copy-start.16 = (f32[64,16,1,1]{0,1,3,2:T(8,128)S(1)}, f32[64,16,1,1]{0,1,3,2:T(8,128)}, u32[]{:S(2)}) copy-start(f32[64,16,1,1]{0,1,3,2:T(8,128)} %constant.63) | copy-start | bytes 12292
  51.8 4.4 %copy-start.20 = (bf16[5,128,1024]{2,1,0:T(8,128)(2,1)S(1)}, bf16[5,128,1024]{2,1,0:T(8,128)(2,1)}, u32[]{:S(2)}) copy-start(bf16[5,128,1024]{2,1,0:T(8,128)(2,1)} %all-gather.6.cloned.1.call-done) | copy-start | bytes 3932164
  59.8 3.1 %copy-start.11 = (f32[64,32,1,1]{0,1,3,2:T(8,128)S(1)}, f32[64,32,1,1]{0,1,3,2:T(8,128)}, u32[]{:S(2)}) copy-start(f32[64,32,1,1]{0,1,3,2:T(8,128)} %constant.62) | copy-start | bytes 24580
  65.4 1.4 copy-start.3
  65.5 1.8 %copy-start.4 = (f32[5,2,32,1088]{3,2,1,0:T(8,128)S(1)}, f32[5,2,32,1088]{3,2,1,0:T(8,128)}, u32[]{:S(2)}) copy-start(f32[5,2,32,1088]{3,2,1,0:T(8,128)} %get-tuple-element.28) | copy-start | bytes 4177924
  65.5 2.3 %copy-start.5 = (f32[5,2,32,1088]{3,2,1,0:T(8,128)S(1)}, f32[5,2,32,1088]{3,2,1,0:T(8,128)}, u32[]{:S(2)}) copy-start(f32[5,2,32,1088]{3,2,1,0:T(8,128)} %get-tuple-element.29) | copy-start | bytes 4177924
  67.7 24.8 %copy-start.10 = (bf16[1024,1088]{1,0:T(8,128)(2,1)S(1)}, bf16[1024,1088]{1,0:T(8,128)(2,1)}, u32[]{:S(2)}) copy-start(bf16[1024,1088]{1,0:T(8,128)(2,1)} %get-tuple-element.6) | copy-start | bytes 6684676
  92.5 3.7 %copy-start.9 = (bf16[1024,1088]{1,0:T(8,128)(2,1)S(1)}, bf16[1024,1088]{1,0:T(8,128)(2,1)}, u32[]{:S(2)}) copy-start(bf16[1024,1088]{1,0:T(8,128)(2,1)} %copy-done.8) | copy-start | bytes 6684676
  92.5 3.7 %copy-start.19 = (bf16[6,128,1024]{2,1,0:T(8,128)(2,1)S(1)}, bf16[6,128,1024]{2,1,0:T(8,128)(2,1)}, u32[]{:S(2)}) copy-start(bf16[6,128,1024]{2,1,0:T(8,128)(2,1)} %all-gather.4.cloned.1.call-done) | copy-start | bytes 4718596
  106.7 1.5 copy-start
  106.7 2.0 %copy-start.1 = (f32[6,2,32,1088]{3,2,1,0:T(8,128)S(1)}, f32[6,2,32,1088]{3,2,1,0:T(8,128)}, u32[]{:S(2)}) copy-start(f32[6,2,32,1088]{3,2,1,0:T(8,128)} %get-tuple-element.31) | copy-start | bytes 5013508
  106.7 2.5 %copy-start.2 = (f32[6,2,32,1088]{3,2,1,0:T(8,128)S(1)}, f32[6,2,32,1088]{3,2,1,0:T(8,128)}, u32[]{:S(2)}) copy-start(f32[6,2,32,1088]{3,2,1,0:T(8,128)} %get-tuple-element.32) | copy-start | bytes 5013508
  109.2 2.5 %copy-start.7 = (f32[4,2,32,1088]{3,2,1,0:T(8,128)S(1)}, f32[4,2,32,1088]{3,2,1,0:T(8,128)}, u32[]{:S(2)}) copy-start(f32[4,2,32,1088]{3,2,1,0:T(8,128)} %get-tuple-element.13) | copy-start | bytes 3342340
  111.8 1.3 copy-start.6
  113.6 17.8 %copy-start.18 = (f32[544]{0:T(1024)S(1)}, f32[544]{0:T(1024)}, u32[]{:S(2)}) copy-start(f32[544]{0:T(1024)} %constant.57.clone) | copy-start | bytes 6532
  113.7 17.0 %collective-permute-start = (f32[2,4,1,32,544]{4,3,2,1,0:T(8,128)S(1)}, f32[2,4,1,32,544]{4,3,2,1,0:T(8,128)S(1)}, u32[]{:S(2)}, u32[]{:S(2)}) collective-permute-start(f32[2,4,1,32,544]{4,3,2,1,0:T(8,128)S(1)} %fusion.14), channel_id=1, source_target_pairs={{0,1},{1,0},{2,3},{3,2},{4,5},{5,4},{6,7},{7,6},{8,9},{9,8},{10,11... | collective-permute-start | bytes 1671176 | tf_op jit(solution)/shard_map/ppermute | solution.py:110
  140.6 1.2 collective-permute-start.1
  141.7 3.5 %collective-permute-start.2 = (f32[1,4]{1,0:T(1,128)S(1)}, f32[1,4]{1,0:T(1,128)S(1)}, u32[]{:S(2)}, u32[]{:S(2)}) collective-permute-start(f32[1,4]{1,0:T(1,128)S(1)} %bitcast_maximum_fusion), channel_id=1, source_target_pairs={{0,4},{2,6},{4,0},{6,2},{8,12},{10,14},{12,8},{14,10},{16,20},{18,... | collective-permute-start | bytes 56 | tf_op jit(solution)/shard_map/ppermute | solution.py:121
  145.3 3.5 %collective-permute-start.3 = (f32[1,4]{1,0:T(1,128)S(1)}, f32[1,4]{1,0:T(1,128)S(1)}, u32[]{:S(2)}, u32[]{:S(2)}) collective-permute-start(f32[1,4]{1,0:T(1,128)S(1)} %max.13), channel_id=1, source_target_pairs={{0,8},{2,10},{4,12},{6,14},{8,0},{10,2},{12,4},{14,6},{16,24},{18,... | collective-permute-start | bytes 56 | tf_op jit(solution)/shard_map/ppermute | solution.py:121
  148.8 4.4 %collective-permute-start.4 = (f32[1,4]{1,0:T(1,128)S(1)}, f32[1,4]{1,0:T(1,128)S(1)}, u32[]{:S(2)}, u32[]{:S(2)}) collective-permute-start(f32[1,4]{1,0:T(1,128)S(1)} %max.14), channel_id=1, source_target_pairs={{0,16},{2,18},{4,20},{6,22},{8,24},{10,26},{12,28},{14,30},{16,0},... | collective-permute-start | bytes 56 | tf_op jit(solution)/shard_map/ppermute | solution.py:121
Sparse Core Ops, SparseCore 0:
  10.2 41.5 all-gather.5
  53.9 38.5 all-gather.3

commit v3 on v2

--- a/solution.py
+++ b/solution.py
@@ -99,38 +99,36 @@
     return jnp.einsum("rnxq,cq->rnxc", joined, full_table, precision=HIGH)
 
 
-def reduce_scatter_terms(products, term_count):
-    share = products.shape[2] // term_count
-    here = lax.axis_index("term")
-    total = lax.dynamic_slice_in_dim(products, here * share, share, axis=2)
-    for shift in range(1, term_count):
-        target = (here + shift) % term_count
-        outgoing = lax.dynamic_slice_in_dim(products, target * share, share, axis=2)
-        pairs = [(k, (k + shift) % term_count) for k in range(term_count)]
-        total = total + lax.ppermute(outgoing, "term", pairs)
-    return total
-
-
-def max_over_rot(values, rot_count):
-    if rot_count & (rot_count - 1):
-        gathered = lax.all_gather(values, "rot", axis=0, tiled=True)
-        return jnp.max(gathered, axis=0, keepdims=True)
+def butterfly_max(values, axes, device_count):
     shift = 1
-    while shift < rot_count:
-        pairs = [(k, k ^ shift) for k in range(rot_count)]
-        values = jnp.maximum(values, lax.ppermute(values, "rot", pairs))
+    while shift < device_count:
+        pairs = [(k, k ^ shift) for k in range(device_count)]
+        values = jnp.maximum(values, lax.ppermute(values, axes, pairs))
         shift *= 2
     return values
 
 
-def make_body(term_count, rot_count):
+def make_body(plane_count, inner_count, term_count):
+    all_axes = ("plane", "inner", "term")
+
     def body(receptor_grids, term_weights, atom_weights, ligand_cells):
-        terms_here = receptor_grids.shape[0]
-        cut = (terms_here + 1) // 2
-        chunks = [(0, cut), (cut, terms_here)]
-        gathered = [
-            lax.all_gather(receptor_grids[lo:hi], "rot", axis=1, tiled=True) for lo, hi in chunks
-        ]
+        terms_here, rows_here, cells = receptor_grids.shape
+        rot_here = ligand_cells.shape[1]
+        rot_total = rot_here * plane_count * inner_count
+        plane = lax.axis_index("plane")
+        inner = lax.axis_index("inner")
+        term = lax.axis_index("term")
+        gathered = lax.all_gather(receptor_grids, ("term", "inner"), axis=0, tiled=False)
+        gathered = gathered.reshape(term_count, inner_count, terms_here, rows_here, cells)
+        gathered = jnp.transpose(gathered, (0, 2, 1, 3, 4))
+        gathered = gathered.reshape(term_count * terms_here, inner_count * rows_here, cells)
+        cells_here = lax.all_gather(ligand_cells, "plane", axis=1, tiled=True)
+        share = cells_here.shape[1] // term_count
+        voxels = lax.dynamic_slice_in_dim(cells_here, term * share, share, axis=1)
+        local = term * share + jnp.arange(share, dtype=jnp.int32)
+        rot_ids = ((local // rot_here) * inner_count + inner) * rot_here + local % rot_here
+        coefficients = atom_weights * term_weights[:, None]
+        coefficients = lax.all_gather(coefficients, "term", axis=0, tiled=True)
         with jax.named_scope("twiddle_tables"):
             full_table = plane_tables(G)
             box_table = plane_tables(LB)
@@ -138,38 +136,51 @@
             tables = lax.optimization_barrier((full_table, box_table, table_hi, table_lo))
             full_table, box_table, table_hi, table_lo = tables
         with jax.named_scope("ligand_spectra"):
-            coefficients = atom_weights * term_weights[:, None]
-            first, second, third = ligand_coefficients(ligand_cells, coefficients, box_table)
-        part_re = 0.0
-        part_im = 0.0
-        for (lo, hi), grids in zip(chunks, gathered):
-            with jax.named_scope("receptor_spectra"):
-                mixed = receptor_mixed(grids, table_hi, table_lo)
-            with jax.named_scope("correlate"):
-                add_re, add_im = correlate(mixed, first[lo:hi], second[lo:hi], third[lo:hi])
-            part_re = part_re + add_re
-            part_im = part_im + add_im
+            first, second, third = ligand_coefficients(voxels, coefficients, box_table)
+        with jax.named_scope("receptor_spectra"):
+            mixed = receptor_mixed(gathered, table_hi, table_lo)
+        with jax.named_scope("correlate"):
+            part_re, part_im = correlate(mixed, first, second, third)
         width = G * HZ
         prod_re = part_re[..., :width] + part_re[..., width:]
         prod_im = part_im[..., :width] + part_im[..., width:]
         products = jnp.stack([prod_re, prod_im], axis=0)
-        products = reduce_scatter_terms(products, term_count)
         with jax.named_scope("inverse_scores"):
             scores = inverse_scores(products, full_table)
-            best_here = jnp.max(scores, axis=(2, 3))
-        best_scores = lax.all_gather(best_here, "term", axis=1, tiled=True)
-        best_overall = max_over_rot(jnp.max(best_scores, axis=1)[None], rot_count)[0]
+            best_here = jnp.max(scores, axis=(2, 3))[0]
+        receptors = plane_count
+        columns = jnp.arange(rot_total, dtype=jnp.int32)
+        hit = rot_ids[:, None] == columns[None, :]
+        row = jnp.max(jnp.where(hit, best_here[:, None], -jnp.inf), axis=0)
+        mine = jnp.arange(receptors, dtype=jnp.int32)[:, None] == plane
+        placed = jnp.where(mine, row[None, :], -jnp.inf)
+        placed = butterfly_max(placed, all_axes, plane_count * inner_count * term_count)
+        start = (plane * inner_count + inner) * rot_here
+        best_scores = lax.dynamic_slice_in_dim(placed, start, rot_here, axis=1)
+        best_overall = jnp.max(placed, axis=1)
         return (best_scores, best_overall)
 
     return body
 
 
 def solution(mesh):
-    placed = (P("term", "rot", None), P("term"), P("term", None), P(None, "rot", None))
-    return jax.shard_map(
-        make_body(mesh.shape["term"], mesh.shape["rot"]),
-        mesh=mesh,
-        in_specs=placed,
-        out_specs=(P(None, "rot"), P()),
-        check_vma=False,
-    )
+    rot_count = mesh.shape["rot"]
+    term_count = mesh.shape["term"]
+
+    def run(receptor_grids, term_weights, atom_weights, ligand_cells):
+        receptors = receptor_grids.shape[1] // G
+        inner_count = rot_count // receptors
+        devices = np.asarray(mesh.devices).reshape(receptors, inner_count, term_count)
+        fine = jax.sharding.Mesh(devices, ("plane", "inner", "term"))
+        rows = ("plane", "inner")
+        placed = (P("term", rows, None), P("term"), P("term", None), P(None, rows, None))
+        mapped = jax.shard_map(
+            make_body(receptors, inner_count, term_count),
+            mesh=fine,
+            in_specs=placed,
+            out_specs=(P(None, rows), P()),
+            check_vma=False,
+        )
+        return mapped(receptor_grids, term_weights, atom_weights, ligand_cells)
+
+    return run

time: 162 us -> 140 us (0.86)
  waiting for transfers between devices: 64.9 us -> 11.3 us
  other arithmetic: 20.8 us -> 43 us
  blocking collectives: 4.21 us -> 19.2 us
  local copies, waits for them, and re-layouts: 18.4 us -> 9.3 us
  starting transfers between devices: 3.53 us -> 6.46 us
    all_gather x2 -> x1, waiting for transfers between devices: 38.6 us -> 0.01 us  [body(): lax.all_gather(receptor_grids, ('term', 'inner'), axis=0, tiled=False)]
    ppermute x5, waiting for transfers between devices: 26.2 us -> 10.6 us  [butterfly_max(): values = jnp.maximum(values, lax.ppermute(values, axes, pairs))]
    all_gather x1 -> x2, blocking collectives: 4.21 us -> 19.2 us  [the longest x1 13.9 us: body(): cells_here = lax.all_gather(ligand_cells, 'plane', axis=1, tiled=True)]
    concatenate x2 -> x1, other arithmetic: 5.99 us -> 19.2 us  [ligand_coefficients(): third = jnp.concatenate([-lig_re, lig_im], axis=-1)]
    dot_general x1, matrix products: 2.72 us -> 13.6 us  [ligand_coefficients(): mixed = jnp.einsum('px,tnxq->tnpq', mix_table(LB), plane, precision=HIGH)]
    reduce_sum x2 -> x1, other arithmetic: 6.04 us -> 14.4 us  [correlate(): part_re = jnp.sum(rec_cos * a + rec_sin * b, axis=0)]
    add x2 -> x0, local copies, waits for them, and re-layouts: 6.53 us -> none  [receptor_mixed(): plane = plane + jnp.dot(flat, table_lo, preferred_element_type=jnp.float32)]
    dot_general x2 -> x1, matrix products: 8.08 us -> 2.03 us  [receptor_mixed(): plane = jnp.dot(flat, table_hi, preferred_element_type=jnp.float32)]
  transfers between devices with their start and end apart: 7 -> 6, of which waited for: 7 -> 5; matrix products, arithmetic and copies ran while one was open for 26% -> 37% of each run, Pallas kernels for 0% -> 0%
where the time goes in v3:
time: 140 us; the launch traced here: 139 us
  other arithmetic  43 us (31%)
  matrix products  35.8 us (26%)
  blocking collectives  19.2 us (14%)
  between operations  14.4 us (10%)
  waiting for transfers between devices  11.3 us (8%)
  local copies, waits for them, and re-layouts  9.3 us (7%)
  starting transfers between devices  6.46 us (5%)
    concatenate x1, other arithmetic, ligand_coefficients(): third = jnp.concatenate([-lig_re, lig_im], axis=-1)  19.2 us
    reduce_sum x1, other arithmetic, correlate(): part_re = jnp.sum(rec_cos * a + rec_sin * b, axis=0)  14.4 us
    all_gather x1, blocking collectives, body(): cells_here = lax.all_gather(ligand_cells, 'plane', axis=1, tiled=True)  13.9 us
    dot_general x1, matrix products, ligand_coefficients(): mixed = jnp.einsum('px,tnxq->tnpq', mix_table(LB), plane, precision=HIGH)  13.6 us
    ppermute x5, waiting for transfers between devices, butterfly_max(): values = jnp.maximum(values, lax.ppermute(values, axes, pairs))  10.6 us
    dot_general x1, matrix products, ligand_coefficients(): grid = jnp.einsum('ta,nac->tnc', coefficients, onehot, precision=HIGHEST)  6.53 us
    ppermute x5, starting transfers between devices, butterfly_max(): values = jnp.maximum(values, lax.ppermute(values, axes, pairs))  6.43 us
    all_gather x1, blocking collectives, body(): coefficients = lax.all_gather(coefficients, 'term', axis=0, tiled=True)  5.32 us
  transfers between devices with their start and end apart: 6, of which 5 were waited for; matrix products, arithmetic and copies ran while one was open for 37% of the time, Pallas kernels for 0%

profile of v3, /device:TPU:0, one launch (start us, length us, event | category | flops | bytes accessed | tf_op | source)
XLA Modules:
  0.0 139.4 jit_solution(8370256144591692725)
XLA Ops:
  7.2 0.7 all-gather.4.cloned.1.call-update
  7.9 1.8 %multiply_subtract_fusion = (f32[32,32,544]{2,1,0:T(8,128)S(1)}, f32[32,32,544]{2,1,0:T(8,128)S(1)}) fusion(f32[32,544]{1,0:T(8,128)} %constant.77.clone, f32[32,544]{1,0:T(8,128)} %constant.75.clone, f32[32,544]{1,0:T(8,128)} %constant.76.clone, f32[32,544]{1,0:T(8,128)} %constant.74.clone), kind=kLoop, calls=%fused_computation.25 | loop fusion | flops 3342336 | bytes 4734976 | tf_op jit(solution)/shard_map/twiddle_tables/sub | solution.py:34
  9.7 4.7 %subtract_convert_fusion = (bf16[1024,1088]{1,0:T(8,128)(2,1)}, bf16[1024,1088]{1,0:T(8,128)(2,1)}, f32[1024,1088]{1,0:T(8,128)}) fusion(f32[1024,544]{1,0:T(8,128)S(1)} %bitcast.92, f32[1024,544]{1,0:T(8,128)S(1)} %bitcast.91), kind=kLoop, calls=%fused_computation.20 | loop fusion | flops 5570560 | bytes 13369344 | tf_op jit(solution)/shard_map/twiddle_tables/convert_element_type | solution.py:41
  14.8 0.3 copy-done.8
  15.2 5.3 %all-gather.1 = f32[2,11,256]{2,1,0:T(8,128)S(1)} all-gather(f32[1,11,256]{2,1,0:T(8,128)S(1)} %multiply_bitcast_fusion), channel_id=1, replica_groups=mesh['plane'=4,'inner'=4,'term'=2] {'term'}, dimensions={0}, use_global_device_ids=true | all-gather | bytes 33792 | tf_op jit(solution)/shard_map/all_gather | solution.py:131
  20.5 13.9 %all_gather.15 = s32[3,8,256]{2,0,1:T(4,128)S(1)} all-gather(s32[3,2,256]{2,0,1:T(4,128)S(1)} %copy.36), channel_id=1, replica_groups=mesh['plane'=4,'inner'=4,'term'=2] {'plane'}, dimensions={1}, use_global_device_ids=true | all-gather | bytes 30720 | tf_op jit(solution)/shard_map/all_gather | solution.py:125
  34.5 6.5 %fusion = f32[22,4,4096]{2,0,1:T(8,128)} fusion(f32[22,256,1]{1,0,2:T(8,128)S(1)} %reshape.336, s32[4,256]{1,0:T(4,128)S(1)} %bitcast.103), kind=kOutput, calls=%fused_computation.2 | convolution fusion | flops 1111490560 | bytes 1468416 | tf_op jit(solution)/shard_map/ligand_spectra/ta,nac->tnc/dot_general | solution.py:67
  41.0 1.7 %reshape.342 = f32[22,4,16,256]{3,2,0,1:T(8,128)S(1)} reshape(f32[22,4,4096]{2,0,1:T(8,128)} %fusion) | data formatting | bytes 2883584 | tf_op jit(solution)/shard_map/ligand_spectra/reshape | solution.py:68
  42.7 3.1 %fusion.10 = f32[22,4,16,1088]{3,2,1,0:T(8,128)S(1)} fusion(f32[22,4,16,256]{3,2,0,1:T(8,128)S(1)} %reshape.342, f32[256,1088]{1,0:T(8,128)S(1)} %pad_maximum_fusion.2), kind=kOutput, calls=%fused_computation.28 | convolution fusion | flops 2353004544 | bytes 8683520 | tf_op jit(solution)/shard_map/ligand_spectra/tnxc,cq->tnxq/dot_general | solution.py:69
  45.9 13.6 %convolution_bitcast_fusion = f32[22,4,64,1088]{3,2,1,0:T(8,128)} fusion(f32[22,4,16,1088]{3,2,1,0:T(8,128)S(1)} %fusion.10, f32[64,16,1,1]{0,1,3,2:T(8,128)S(1)} %copy-done.9), kind=kOutput, calls=%fused_computation | convolution fusion | flops 588251136 | bytes 30642176 | tf_op jit(solution)/shard_map/ligand_spectra/px,tnxq->tnpq/dot_general | solution.py:70
  59.5 19.2 %fusion.9 = (f32[22,1,4,32,544]{4,3,2,0,1:T(8,128)}, f32[22,1,4,32,544]{4,3,2,0,1:T(8,128)}, f32[22,1,4,32,544]{4,3,2,0,1:T(8,128)}, f32[22,1,4,32,544]{4,3,2,0,1:T(8,128)}) fusion(f32[22,4,64,1088]{3,2,1,0:T(8,128)} %convolution_bitcast_fusion), kind=kLoop, calls=%fused_computation.27 | loop fusion | flops 7659520 | bytes 49020928 | tf_op jit(solution)/shard_map/ligand_spectra/concatenate | solution.py:75
  78.7 1.5 %copy.35 = bf16[2,11,4,8,1024]{4,3,2,1,0:T(8,128)(2,1)S(1)} copy(bf16[2,11,4,8,1024]{4,3,1,2,0:T(8,128)(2,1)} %bitcast.100) | data formatting | bytes 2883584 | tf_op jit(solution)/shard_map/transpose | solution.py:123
  80.2 2.0 %fusion.34 = f32[1088,704]{0,1:T(8,128)S(1)} fusion(bf16[704,1024]{1,0:T(8,128)(2,1)S(1)} %bitcast.101, bf16[1024,1088]{1,0:T(8,128)(2,1)S(1)} %copy-done.1), kind=kOutput, calls=%fused_computation.74 | convolution fusion | flops 1568669696 | bytes 6733824 | tf_op jit(solution)/shard_map/receptor_spectra/dot_general | solution.py:54
  82.3 2.1 %convolution_add_fusion = f32[1088,704]{0,1:T(8,128)S(1)} fusion(f32[1088,704]{0,1:T(8,128)S(1)} %fusion.34, bf16[704,1024]{1,0:T(8,128)(2,1)S(1)} %bitcast.102, bf16[1024,1088]{1,0:T(8,128)(2,1)S(1)} %copy-done), kind=kOutput, calls=%fused_computation.21 | convolution fusion | flops 1569435648 | bytes 9797632 | tf_op jit(solution)/shard_map/receptor_spectra/dot_general | solution.py:55
  84.4 2.8 %convolution_bitcast_fusion.1 = f32[22,1,64,1088]{3,2,0,1:T(8,128)S(1)} fusion(f32[22,32,1088]{2,1,0:T(8,128)S(1)} %bitcast.95, f32[64,32,1]{0,1,2:T(8,128)S(1)} %copy-done.7), kind=kOutput, calls=%fused_computation.16 | convolution fusion | flops 294125568 | bytes 9199616 | tf_op jit(solution)/shard_map/receptor_spectra/px,trxq->trpq/dot_general | solution.py:57
  87.2 3.8 %slice_bitcast_fusion.1 = (f32[22,32,1088]{2,1,0:T(8,128)}, f32[22,32,1088]{2,1,0:T(8,128)}) fusion(f32[22,1,64,1088]{3,2,0,1:T(8,128)S(1)} %convolution_bitcast_fusion.1), kind=kLoop, calls=%fused_computation.23 | loop fusion | bytes 12255232 | tf_op jit(solution)/shard_map/correlate/mul | solution.py:85
  91.0 1.4 %slice-done.3 = s8[3014656]{0:T(1024)(128)(4,1)S(1)} async-done(((s8[7208960]{0:T(1024)(128)(4,1)}), s8[3014656]{0:T(1024)(128)(4,1)S(1)}, s32[]{:S(2)}) %slice-start.3) | async-done | bytes 3014680
  92.4 14.4 %fusion.2 = (f32[4,32,1088]{2,1,0:T(8,128)}, f32[4,32,1088]{2,1,0:T(8,128)}) fusion(f32[22,1,4,32,544]{4,3,2,0,1:T(8,128)} %get-tuple-element.20, f32[22,1,4,32,544]{4,3,2,0,1:T(8,128)} %get-tuple-element.19, f32[22,1,4,32,544]{4,3,2,0,1:T(8,128)S(1)} %bitcast.90, f32[22,32,1088]{2,1,0:T(8,128)} %get-tuple-element.22, f32[22,32,1088]{2,1,0:T(8,128)} %get-tuple-element.21, ...), kind=kLoop, calls=%fused_computation.5 | loop fusion | flops 33423360 | bytes 31752192 | tf_op jit(solution)/shard_map/correlate/reduce_sum | solution.py:85
  106.8 1.5 %fusion.26 = (f32[1,1,4,32,544]{4,3,2,0,1:T(8,128)S(1)}, f32[1,1,4,32,544]{4,3,2,0,1:T(8,128)S(1)}) fusion(f32[1,4,32,1088]{3,2,1,0:T(8,128)} %bitcast.97, f32[1,4,32,1088]{3,2,1,0:T(8,128)} %bitcast.96), kind=kLoop, calls=%fused_computation.50 | loop fusion | flops 139264 | bytes 1671168 | tf_op jit(solution)/shard_map/stack | solution.py:147
  108.4 0.7 fusion.16
  109.2 4.9 %fusion.13 = f32[4]{0:T(128)S(1)} fusion(f32[1024,1088]{1,0:T(8,128)} %get-tuple-element.9, f32[1,4,32,544]{3,2,1,0:T(8,128)S(1)} %get-tuple-element.28, f32[1,4,32,544]{3,2,1,0:T(8,128)S(1)} %get-tuple-element.27), kind=kOutput, calls=%fused_computation.32 | convolution fusion | flops 855908352 | bytes 5013520 | tf_op jit(solution)/shard_map/inverse_scores/rnxq,cq->rnxc/dot_general | solution.py:99
  114.2 1.5 %collective-permute-start = (f32[4,32]{0,1:T(8,128)S(1)}, f32[4,32]{0,1:T(8,128)S(1)}, u32[]{:S(2)}, u32[]{:S(2)}) collective-permute-start(f32[4,32]{0,1:T(8,128)S(1)} %broadcast_select_fusion), channel_id=1, source_target_pairs={{0,1},{1,0},{2,3},{3,2},{4,5},{5,4},{6,7},{7,6},{8,9},{9,8},{10,11... | collective-permute-start | bytes 1544 | tf_op jit(solution)/shard_map/ppermute | solution.py:106
  115.8 2.2 %collective-permute-done = f32[4,32]{0,1:T(8,128)S(1)} collective-permute-done((f32[4,32]{0,1:T(8,128)S(1)}, f32[4,32]{0,1:T(8,128)S(1)}, u32[]{:S(2)}, u32[]{:S(2)}) %collective-permute-start) | collective-permute-done | bytes 544 | tf_op jit(solution)/shard_map/ppermute | solution.py:106
  118.1 1.2 collective-permute-done.1
  119.3 1.5 %collective-permute-start.2 = (f32[4,32]{0,1:T(8,128)S(1)}, f32[4,32]{0,1:T(8,128)S(1)}, u32[]{:S(2)}, u32[]{:S(2)}) collective-permute-start(f32[4,32]{0,1:T(8,128)S(1)} %fusion.45), channel_id=1, source_target_pairs={{0,4},{1,5},{2,6},{3,7},{4,0},{5,1},{6,2},{7,3},{8,12},{9,13},{10,... | collective-permute-start | bytes 1544 | tf_op jit(solution)/shard_map/ppermute | solution.py:106
  120.8 2.3 %collective-permute-done.2 = f32[4,32]{0,1:T(8,128)S(1)} collective-permute-done((f32[4,32]{0,1:T(8,128)S(1)}, f32[4,32]{0,1:T(8,128)S(1)}, u32[]{:S(2)}, u32[]{:S(2)}) %collective-permute-start.2) | collective-permute-done | bytes 544 | tf_op jit(solution)/shard_map/ppermute | solution.py:106
  123.1 1.6 %collective-permute-start.3 = (f32[4,32]{0,1:T(8,128)S(1)}, f32[4,32]{0,1:T(8,128)S(1)}, u32[]{:S(2)}, u32[]{:S(2)}) collective-permute-start(f32[4,32]{0,1:T(8,128)S(1)} %max.17), channel_id=1, source_target_pairs={{0,8},{1,9},{2,10},{3,11},{4,12},{5,13},{6,14},{7,15},{8,0},{9,1},... | collective-permute-start | bytes 1544 | tf_op jit(solution)/shard_map/ppermute | solution.py:106
  124.6 2.2 %collective-permute-done.3 = f32[4,32]{0,1:T(8,128)S(1)} collective-permute-done((f32[4,32]{0,1:T(8,128)S(1)}, f32[4,32]{0,1:T(8,128)S(1)}, u32[]{:S(2)}, u32[]{:S(2)}) %collective-permute-start.3) | collective-permute-done | bytes 544 | tf_op jit(solution)/shard_map/ppermute | solution.py:106
  126.8 1.9 %collective-permute-start.4 = (f32[4,32]{0,1:T(8,128)S(1)}, f32[4,32]{0,1:T(8,128)S(1)}, u32[]{:S(2)}, u32[]{:S(2)}) collective-permute-start(f32[4,32]{0,1:T(8,128)S(1)} %max.18), channel_id=1, source_target_pairs={{0,16},{1,17},{2,18},{3,19},{4,20},{5,21},{6,22},{7,23},{8,24},{9,... | collective-permute-start | bytes 1544 | tf_op jit(solution)/shard_map/ppermute | solution.py:106
  128.7 2.7 %collective-permute-done.4 = f32[4,32]{0,1:T(8,128)S(1)} collective-permute-done((f32[4,32]{0,1:T(8,128)S(1)}, f32[4,32]{0,1:T(8,128)S(1)}, u32[]{:S(2)}, u32[]{:S(2)}) %collective-permute-start.4) | collective-permute-done | bytes 544 | tf_op jit(solution)/shard_map/ppermute | solution.py:106
  131.5 0.5 fusion.33
  132.0 0.6 constant_dynamic-slice_fusion
  (53 shorter events, 1.1 us)
Async XLA Ops:
  7.2 71.5 %all-gather.4.cloned.1.call-start = ((), (), s32[]{:S(2)}) async-start(), calls=%async_computation | async-start | bytes 1622016 | tf_op jit(solution)/shard_map/all_gather | solution.py:121
  9.7 4.7 %copy-start.2 = (f32[16,544]{1,0:T(8,128)S(1)}, f32[16,544]{1,0:T(8,128)}, u32[]{:S(2)}) copy-start(f32[16,544]{1,0:T(8,128)} %constant.81.clone) | copy-start | bytes 104452
  9.7 4.7 %copy-start.3 = (f32[16,544]{1,0:T(8,128)S(1)}, f32[16,544]{1,0:T(8,128)}, u32[]{:S(2)}) copy-start(f32[16,544]{1,0:T(8,128)} %constant.79.clone) | copy-start | bytes 104452
  9.7 4.7 %copy-start.4 = (f32[16,544]{1,0:T(8,128)S(1)}, f32[16,544]{1,0:T(8,128)}, u32[]{:S(2)}) copy-start(f32[16,544]{1,0:T(8,128)} %constant.80.clone) | copy-start | bytes 104452
  9.7 4.7 %copy-start.5 = (f32[16,544]{1,0:T(8,128)S(1)}, f32[16,544]{1,0:T(8,128)}, u32[]{:S(2)}) copy-start(f32[16,544]{1,0:T(8,128)} %constant.78.clone) | copy-start | bytes 104452
  14.4 0.7 copy-start.8
  14.4 0.7 copy-start.12
  14.4 6.1 %copy-start.10 = (s32[3,2,256]{2,1,0:T(2,128)S(1)}, s32[3,2,256]{2,1,0:T(2,128)}, u32[]{:S(2)}) copy-start(s32[3,2,256]{2,1,0:T(2,128)} %param.19) | copy-start | bytes 18436
  42.7 3.2 %copy-start.9 = (f32[64,16,1,1]{0,1,3,2:T(8,128)S(1)}, f32[64,16,1,1]{0,1,3,2:T(8,128)}, u32[]{:S(2)}) copy-start(f32[64,16,1,1]{0,1,3,2:T(8,128)} %constant.90) | copy-start | bytes 12292
  59.5 20.7 %copy-start.1 = (bf16[1024,1088]{1,0:T(8,128)(2,1)S(1)}, bf16[1024,1088]{1,0:T(8,128)(2,1)}, u32[]{:S(2)}) copy-start(bf16[1024,1088]{1,0:T(8,128)(2,1)} %get-tuple-element.6) | copy-start | bytes 6684676
  80.2 2.0 %copy-start = (bf16[1024,1088]{1,0:T(8,128)(2,1)S(1)}, bf16[1024,1088]{1,0:T(8,128)(2,1)}, u32[]{:S(2)}) copy-start(bf16[1024,1088]{1,0:T(8,128)(2,1)} %get-tuple-element.7) | copy-start | bytes 6684676
  82.2 2.1 %copy-start.7 = (f32[64,32,1]{0,1,2:T(8,128)S(1)}, f32[64,32,1]{0,1,2:T(8,128)}, u32[]{:S(2)}) copy-start(f32[64,32,1]{0,1,2:T(8,128)} %constant.89) | copy-start | bytes 24580
  84.4 6.6 %slice-start = ((s8[7208960]{0:T(1024)(128)(4,1)}), s8[4194304]{0:T(1024)(128)(4,1)S(1)}, s32[]{:S(2)}) async-start(s8[7208960]{0:T(1024)(128)(4,1)} %bitcast.87), calls=%async_computation.1 | async-start | bytes 8388608
  84.4 6.6 %slice-start.2 = ((s8[7208960]{0:T(1024)(128)(4,1)}), s8[4194304]{0:T(1024)(128)(4,1)S(1)}, s32[]{:S(2)}) async-start(s8[7208960]{0:T(1024)(128)(4,1)} %bitcast.89), calls=%async_computation.3 | async-start | bytes 8388608
  87.2 3.8 %slice-start.1 = ((s8[7208960]{0:T(1024)(128)(4,1)}), s8[3014656]{0:T(1024)(128)(4,1)S(1)}, s32[]{:S(2)}) async-start(s8[7208960]{0:T(1024)(128)(4,1)} %bitcast.87), calls=%async_computation.2 | async-start | bytes 6029312
  87.2 5.2 %slice-start.3 = ((s8[7208960]{0:T(1024)(128)(4,1)}), s8[3014656]{0:T(1024)(128)(4,1)S(1)}, s32[]{:S(2)}) async-start(s8[7208960]{0:T(1024)(128)(4,1)} %bitcast.89), calls=%async_computation.4 | async-start | bytes 6029312
  92.4 16.0 %copy-start.6 = (f32[64,32,1,1]{0,1,3,2:T(8,128)S(1)}, f32[64,32,1,1]{0,1,3,2:T(8,128)}, u32[]{:S(2)}) copy-start(f32[64,32,1,1]{0,1,3,2:T(8,128)} %constant.91) | copy-start | bytes 24580
  106.8 2.3 %copy-start.11 = (f32[544]{0:T(1024)S(1)}, f32[544]{0:T(1024)}, u32[]{:S(2)}) copy-start(f32[544]{0:T(1024)} %constant.84.clone) | copy-start | bytes 6532
  114.2 3.7 %collective-permute-start = (f32[4,32]{0,1:T(8,128)S(1)}, f32[4,32]{0,1:T(8,128)S(1)}, u32[]{:S(2)}, u32[]{:S(2)}) collective-permute-start(f32[4,32]{0,1:T(8,128)S(1)} %broadcast_select_fusion), channel_id=1, source_target_pairs={{0,1},{1,0},{2,3},{3,2},{4,5},{5,4},{6,7},{7,6},{8,9},{9,8},{10,11... | collective-permute-start | bytes 1544 | tf_op jit(solution)/shard_map/ppermute | solution.py:106
  118.1 1.2 collective-permute-start.1
  119.3 3.7 %collective-permute-start.2 = (f32[4,32]{0,1:T(8,128)S(1)}, f32[4,32]{0,1:T(8,128)S(1)}, u32[]{:S(2)}, u32[]{:S(2)}) collective-permute-start(f32[4,32]{0,1:T(8,128)S(1)} %fusion.45), channel_id=1, source_target_pairs={{0,4},{1,5},{2,6},{3,7},{4,0},{5,1},{6,2},{7,3},{8,12},{9,13},{10,... | collective-permute-start | bytes 1544 | tf_op jit(solution)/shard_map/ppermute | solution.py:106
  123.1 3.7 %collective-permute-start.3 = (f32[4,32]{0,1:T(8,128)S(1)}, f32[4,32]{0,1:T(8,128)S(1)}, u32[]{:S(2)}, u32[]{:S(2)}) collective-permute-start(f32[4,32]{0,1:T(8,128)S(1)} %max.17), channel_id=1, source_target_pairs={{0,8},{1,9},{2,10},{3,11},{4,12},{5,13},{6,14},{7,15},{8,0},{9,1},... | collective-permute-start | bytes 1544 | tf_op jit(solution)/shard_map/ppermute | solution.py:106
  126.8 4.6 %collective-permute-start.4 = (f32[4,32]{0,1:T(8,128)S(1)}, f32[4,32]{0,1:T(8,128)S(1)}, u32[]{:S(2)}, u32[]{:S(2)}) collective-permute-start(f32[4,32]{0,1:T(8,128)S(1)} %max.18), channel_id=1, source_target_pairs={{0,16},{1,17},{2,18},{3,19},{4,20},{5,21},{6,22},{7,23},{8,24},{9,... | collective-permute-start | bytes 1544 | tf_op jit(solution)/shard_map/ppermute | solution.py:106
Sparse Core Ops, SparseCore 0:
  9.9 27.8 all-gather.3

commit v4 on v3

--- a/solution.py
+++ b/solution.py
@@ -10,6 +10,7 @@
 G = 32
 HZ = G // 2 + 1
 LB = 16
+WIDTH = 640
 
 HIGH = lax.Precision.HIGH
 HIGHEST = lax.Precision.HIGHEST
@@ -33,7 +34,9 @@
     sz = jnp.asarray(np.sin(phase_z).astype(np.float32))[None, :, :]
     cos_t = cy * cz - sy * sz
     sin_t = sy * cz + cy * sz
-    return jnp.concatenate([cos_t, sin_t], axis=-1).reshape(side * side, 2 * G * HZ)
+    pad = jnp.zeros((side, side, WIDTH - G * HZ), jnp.float32)
+    joined = jnp.concatenate([cos_t, pad, sin_t, pad], axis=-1)
+    return joined.reshape(side * side, 2 * WIDTH)
 
 
 def split_bf16(table):
@@ -53,50 +56,54 @@
     flat = grids.reshape(terms * rows, cells)
     plane = jnp.dot(flat, table_hi, preferred_element_type=jnp.float32)
     plane = plane + jnp.dot(flat, table_lo, preferred_element_type=jnp.float32)
-    plane = plane.reshape(terms, receptors, G, 2 * G * HZ)
+    plane = plane.reshape(terms, receptors, G, 2 * WIDTH)
     return jnp.einsum("px,trxq->trpq", mix_table(G), plane, precision=HIGH)
 
 
-def ligand_coefficients(voxels, coefficients, box_table):
-    rot_count = voxels.shape[1]
-    terms = coefficients.shape[0]
-    width = G * HZ
-    flat_index = (voxels[0] * LB + voxels[1]) * LB + voxels[2]
-    cells = jnp.arange(LB**3, dtype=jnp.int32)
-    onehot = (flat_index[:, :, None] == cells[None, None, :]).astype(jnp.float32)
-    grid = jnp.einsum("ta,nac->tnc", coefficients, onehot, precision=HIGHEST)
-    grid = grid.reshape(terms, rot_count, LB, LB * LB)
-    plane = jnp.einsum("tnxc,cq->tnxq", grid, box_table, precision=HIGH)
+def ligand_spectra(voxels, coefficients, box_table):
+    yz_index = voxels[1] * LB + voxels[2]
+    rows = jnp.take(box_table, yz_index, axis=0)
+    x_cells = jnp.arange(LB, dtype=jnp.int32)
+    in_x = (voxels[0][:, None, :] == x_cells[None, :, None]).astype(jnp.float32)
+    weights = coefficients[None, :, None, :] * in_x[:, None, :, :]
+    plane = jnp.einsum("ntxa,naq->tnxq", weights, rows, precision=HIGH)
     mixed = jnp.einsum("px,tnxq->tnpq", mix_table(LB), plane, precision=HIGH)
-    lig_re = mixed[:, :, :G, :width] - mixed[:, :, G:, width:]
-    lig_im = -mixed[:, :, :G, width:] - mixed[:, :, G:, :width]
-    first = jnp.concatenate([lig_re, -lig_im], axis=-1)
-    second = jnp.concatenate([-lig_im, -lig_re], axis=-1)
-    third = jnp.concatenate([-lig_re, lig_im], axis=-1)
-    return first, second, third
+    lig_re = mixed[:, :, :G, :WIDTH] - mixed[:, :, G:, WIDTH:]
+    lig_im = -mixed[:, :, :G, WIDTH:] - mixed[:, :, G:, :WIDTH]
+    return lig_re, lig_im
 
 
-def correlate(mixed, first, second, third):
-    rec_cos = mixed[:, :, None, :G]
-    rec_sin = mixed[:, :, None, G:]
-    a = first[:, None]
-    b = second[:, None]
-    d = third[:, None]
-    part_re = jnp.sum(rec_cos * a + rec_sin * b, axis=0)
-    part_im = jnp.sum(rec_cos * b + rec_sin * d, axis=0)
-    return part_re, part_im
+def correlate(mixed, lig_re, lig_im):
+    re_cos = mixed[:, :, None, :G, :WIDTH]
+    re_sin = mixed[:, :, None, G:, :WIDTH]
+    ims_cos = mixed[:, :, None, :G, WIDTH:]
+    ims_sin = mixed[:, :, None, G:, WIDTH:]
+    lr = lig_re[:, None]
+    li = lig_im[:, None]
+    prod_re = jnp.sum(re_cos * lr - re_sin * li - ims_sin * lr - ims_cos * li, axis=0)
+    prod_im = jnp.sum(-ims_cos * lr - re_sin * lr - re_cos * li + ims_sin * li, axis=0)
+    return jnp.stack([prod_re, prod_im], axis=0)
 
 
 def inverse_scores(products, full_table):
-    width = G * HZ
     mixed = jnp.einsum("xp,srnpq->srnxq", mix_table(G), products, precision=HIGH)
     inv_re = mixed[0, :, :, :G] - mixed[1, :, :, G:]
     inv_im = mixed[1, :, :, :G] + mixed[0, :, :, G:]
-    freq_z = np.arange(width) % HZ
+    column = np.arange(WIDTH)
+    freq_z = column % HZ
     fold = np.where((freq_z == 0) | (freq_z == G // 2), 1.0, 2.0) / float(G**3)
+    fold = np.where(column < G * HZ, fold, 0.0)
     fold = jnp.asarray(fold.astype(np.float32))
     joined = jnp.concatenate([inv_re * fold, -inv_im * fold], axis=-1)
     return jnp.einsum("rnxq,cq->rnxc", joined, full_table, precision=HIGH)
+
+
+def gather_by_permutes(values, axis_name, count, here):
+    blocks = [values]
+    for shift in range(1, count):
+        pairs = [(k, (k + shift) % count) for k in range(count)]
+        blocks.append(lax.ppermute(values, axis_name, pairs))
+    return blocks
 
 
 def butterfly_max(values, axes, device_count):
@@ -122,13 +129,17 @@
         gathered = gathered.reshape(term_count, inner_count, terms_here, rows_here, cells)
         gathered = jnp.transpose(gathered, (0, 2, 1, 3, 4))
         gathered = gathered.reshape(term_count * terms_here, inner_count * rows_here, cells)
-        cells_here = lax.all_gather(ligand_cells, "plane", axis=1, tiled=True)
+        cell_blocks = gather_by_permutes(ligand_cells, "plane", plane_count, plane)
+        cells_here = jnp.concatenate(cell_blocks, axis=1)
         share = cells_here.shape[1] // term_count
         voxels = lax.dynamic_slice_in_dim(cells_here, term * share, share, axis=1)
         local = term * share + jnp.arange(share, dtype=jnp.int32)
-        rot_ids = ((local // rot_here) * inner_count + inner) * rot_here + local % rot_here
+        source_plane = (plane - local // rot_here) % plane_count
+        rot_ids = (source_plane * inner_count + inner) * rot_here + local % rot_here
         coefficients = atom_weights * term_weights[:, None]
-        coefficients = lax.all_gather(coefficients, "term", axis=0, tiled=True)
+        term_blocks = jnp.stack(gather_by_permutes(coefficients, "term", term_count, term))
+        order = (term - jnp.arange(term_count, dtype=jnp.int32)) % term_count
+        coefficients = jnp.take(term_blocks, order, axis=0).reshape(-1, coefficients.shape[1])
         with jax.named_scope("twiddle_tables"):
             full_table = plane_tables(G)
             box_table = plane_tables(LB)
@@ -136,15 +147,11 @@
             tables = lax.optimization_barrier((full_table, box_table, table_hi, table_lo))
             full_table, box_table, table_hi, table_lo = tables
         with jax.named_scope("ligand_spectra"):
-            first, second, third = ligand_coefficients(voxels, coefficients, box_table)
+            lig_re, lig_im = ligand_spectra(voxels, coefficients, box_table)
         with jax.named_scope("receptor_spectra"):
             mixed = receptor_mixed(gathered, table_hi, table_lo)
         with jax.named_scope("correlate"):
-            part_re, part_im = correlate(mixed, first, second, third)
-        width = G * HZ
-        prod_re = part_re[..., :width] + part_re[..., width:]
-        prod_im = part_im[..., :width] + part_im[..., width:]
-        products = jnp.stack([prod_re, prod_im], axis=0)
+            products = correlate(mixed, lig_re, lig_im)
         with jax.named_scope("inverse_scores"):
             scores = inverse_scores(products, full_table)
             best_here = jnp.max(scores, axis=(2, 3))[0]

time: 140 us -> 118 us (0.84)
  blocking collectives: 19.2 us -> 0 us
  other arithmetic: 43 us -> 28.9 us
  local copies, waits for them, and re-layouts: 9.3 us -> 17.1 us
  starting transfers between devices: 6.46 us -> 11.8 us
  matrix products: 35.8 us -> 31.6 us
  waiting for transfers between devices: 11.3 us -> 13.9 us
    concatenate x2 -> x1, other arithmetic: 19.4 us -> 0.04 us  [body(): cells_here = jnp.concatenate(cell_blocks, axis=1)]
    all_gather x2 -> x0, blocking collectives: 19.2 us -> none  [the longest x1 13.9 us: body(): cells_here = lax.all_gather(ligand_cells, 'plane', axis=1, tiled=True)]
    ppermute x0 -> x4, starting transfers between devices: none -> 8.53 us  [gather_by_permutes(): blocks.append(lax.ppermute(values, axis_name, pairs))]
    gather x0 -> x3, local copies, waits for them, and re-layouts: none -> 6.32 us  [the longest x1 5.76 us: ligand_spectra(): rows = jnp.take(box_table, yz_index, axis=0)]
    concatenate x0 -> x2, local copies, waits for them, and re-layouts: none -> 5.99 us  [plane_tables(): joined = jnp.concatenate([cos_t, pad, sin_t, pad], axis=-1)]
    add x2 -> x3, other arithmetic: 0.03 us -> 3.44 us  [the longest x2 3.41 us: plane_tables(): sin_t = sy * cz + cy * sz]
    ppermute x5, waiting for transfers between devices: 10.6 us -> 13.9 us  [butterfly_max(): values = jnp.maximum(values, lax.ppermute(values, axes, pairs))]
    ppermute x5, starting transfers between devices: 6.43 us -> 3.19 us  [butterfly_max(): values = jnp.maximum(values, lax.ppermute(values, axes, pairs))]
  transfers between devices with their start and end apart: 6 -> 10, of which waited for: 5 -> 5; matrix products, arithmetic and copies ran while one was open for 37% -> 39% of each run, Pallas kernels for 0% -> 0%
where the time goes in v4:
time: 118 us
  matrix products  31.6 us (27%)
  other arithmetic  28.9 us (24%)
  local copies, waits for them, and re-layouts  17.1 us (14%)
  between operations  14.4 us (12%)
  waiting for transfers between devices  13.9 us (12%)
  starting transfers between devices  11.8 us (10%)
    dot_general x1, matrix products, ligand_spectra(): mixed = jnp.einsum('px,tnxq->tnpq', mix_table(LB), plane, precision=HIGH)  15.2 us
    reduce_sum x1, other arithmetic, correlate(): jnp.sum(re_cos * lr - re_sin * li - ims_sin * lr - ims_cos * li, axis=0)  14.1 us
    ppermute x5, waiting for transfers between devices, butterfly_max(): values = jnp.maximum(values, lax.ppermute(values, axes, pairs))  13.9 us
    ppermute x4, starting transfers between devices, gather_by_permutes(): blocks.append(lax.ppermute(values, axis_name, pairs))  8.53 us
    convert_element_type x1, other arithmetic, split_bf16(): lower = (table - upper.astype(jnp.float32)).astype(jnp.bfloat16)  7.25 us
    concatenate x2, local copies, waits for them, and re-layouts, plane_tables(): joined = jnp.concatenate([cos_t, pad, sin_t, pad], axis=-1)  5.99 us
    gather x1, local copies, waits for them, and re-layouts, ligand_spectra(): rows = jnp.take(box_table, yz_index, axis=0)  5.76 us
    dot_general x1, matrix products, ligand_spectra(): plane = jnp.einsum('ntxa,naq->tnxq', weights, rows, precision=HIGH)  5.59 us
  transfers between devices with their start and end apart: 10, of which 5 were waited for; matrix products, arithmetic and copies ran while one was open for 39% of the time, Pallas kernels for 0%

profile of v4, /device:TPU:0, one launch (start us, length us, event | category | flops | bytes accessed | tf_op | source)
XLA Modules:
  0.0 117.6 jit_solution(9019247138318227859)
XLA Ops:
  7.2 3.1 %collective-permute-start = (s32[3,2,256]{2,1,0:T(2,128)}, s32[3,2,256]{2,1,0:T(2,128)S(1)}, u32[]{:S(2)}, u32[]{:S(2)}) collective-permute-start(s32[3,2,256]{2,1,0:T(2,128)} %param.19), channel_id=1, source_target_pairs={{0,8},{8,16},{16,24},{24,0},{1,9},{9,17},{17,25},{25,1},{2,10},{10... | collective-permute-start | bytes 18440 | tf_op jit(solution)/shard_map/ppermute | solution.py:105
  10.3 2.6 %collective-permute-start.1 = (s32[3,2,256]{2,1,0:T(2,128)}, s32[3,2,256]{2,1,0:T(2,128)S(1)}, u32[]{:S(2)}, u32[]{:S(2)}) collective-permute-start(s32[3,2,256]{2,1,0:T(2,128)} %param.19), channel_id=1, source_target_pairs={{0,16},{8,24},{16,0},{24,8},{1,17},{9,25},{17,1},{25,9},{2,18},{10... | collective-permute-start | bytes 18440 | tf_op jit(solution)/shard_map/ppermute | solution.py:105
  12.9 1.3 %collective-permute-start.2 = (s32[3,2,256]{2,1,0:T(2,128)}, s32[3,2,256]{2,1,0:T(2,128)S(1)}, u32[]{:S(2)}, u32[]{:S(2)}) collective-permute-start(s32[3,2,256]{2,1,0:T(2,128)} %param.19), channel_id=1, source_target_pairs={{0,24},{8,0},{16,8},{24,16},{1,25},{9,1},{17,9},{25,17},{2,26},{10... | collective-permute-start | bytes 18440 | tf_op jit(solution)/shard_map/ppermute | solution.py:105
  14.2 0.8 broadcast_multiply_fusion
  15.0 1.5 %collective-permute-start.3 = (f32[11,256]{1,0:T(8,128)S(1)}, f32[11,256]{1,0:T(8,128)S(1)}, u32[]{:S(2)}, u32[]{:S(2)}) collective-permute-start(f32[11,256]{1,0:T(8,128)S(1)} %broadcast_multiply_fusion), channel_id=1, source_target_pairs={{0,1},{1,0},{2,3},{3,2},{4,5},{5,4},{6,7},{7,6},{8,9},{9,8},{10,11... | collective-permute-start | bytes 33800 | tf_op jit(solution)/shard_map/ppermute | solution.py:105
  16.6 0.8 fusion.53
  17.4 3.3 %multiply_add_fusion = (f32[32,32,544]{2,1,0:T(8,128)S(1)}, f32[32,32,544]{2,1,0:T(8,128)}) fusion(f32[32,544]{1,0:T(8,128)} %constant.125.clone, f32[32,544]{1,0:T(8,128)} %constant.123.clone, f32[32,544]{1,0:T(8,128)} %constant.124.clone, f32[32,544]{1,0:T(8,128)} %constant.122.clone), kind=kLoop, calls=%fused_computation.18 | loop fusion | flops 3342336 | bytes 4734976 | tf_op jit(solution)/shard_map/twiddle_tables/add | solution.py:36
  20.7 5.6 %concatenate.14 = f32[1024,1280]{1,0:T(8,128)} concatenate(f32[1024,544]{1,0:T(8,128)} %bitcast.96, f32[1024,96]{1,0:T(8,128)S(1)} %broadcast_in_dim.84, f32[1024,544]{1,0:T(8,128)S(1)} %bitcast.95, f32[1024,96]{1,0:T(8,128)S(1)} %broadcast_in_dim.84), dimensions={1} | concatenate | bytes 10485760 | tf_op jit(solution)/shard_map/twiddle_tables/concatenate | solution.py:38
  26.3 7.3 %subtract_convert_fusion = (bf16[1024,1280]{1,0:T(8,128)(2,1)}, bf16[1024,1280]{1,0:T(8,128)(2,1)}) fusion(f32[1024,1280]{1,0:T(8,128)} %concatenate.14), kind=kLoop, calls=%fused_computation.14 | loop fusion | flops 5242880 | bytes 10485760 | tf_op jit(solution)/shard_map/twiddle_tables/convert_element_type | solution.py:44
  34.5 5.8 %gather_fusion = f32[1024,1280]{1,0:T(8,128)} fusion(f32[256,1280]{1,0:T(8,128)S(1)} %concatenate.15, s32[1024]{0:T(1024)S(1)} %broadcast_clamp_fusion), kind=kCustom, calls=%fused_computation | custom fusion | bytes 10489856 | tf_op jit(solution)/shard_map/ligand_spectra/jit(_take)/gather | solution.py:65
  40.3 0.6 gather_fusion.1
  41.0 5.6 %fusion.3 = f32[4,1280,22,16]{1,3,0,2:T(8,128)S(1)} fusion(f32[4,256,1280]{2,1,0:T(8,128)} %bitcast.97, pred[4,256]{1,0:T(4,128)(4,1)S(1)} %compare_and_fusion, f32[4,16,256]{2,1,0:T(8,128)S(1)} %fusion.24, f32[22,256]{1,0:T(8,128)S(1)} %broadcast_select_fusion), kind=kOutput, calls=%fused_computation.11 | convolution fusion | flops 2769911808 | bytes 12540928 | tf_op jit(solution)/shard_map/ligand_spectra/ntxa,naq->tnxq/dot_general | solution.py:69
  46.6 15.2 %convolution_bitcast_fusion = f32[22,4,64,1280]{3,2,1,0:T(8,128)} fusion(f32[64,16,1,1]{0,1,3,2:T(8,128)S(1)} %copy-done.8, f32[4,1280,22,16]{1,3,0,2:T(8,128)S(1)} %fusion.3), kind=kOutput, calls=%fused_computation.2 | convolution fusion | flops 692060160 | bytes 36048896 | tf_op jit(solution)/shard_map/ligand_spectra/px,tnxq->tnpq/dot_general | solution.py:70
  61.8 1.5 %copy.25 = bf16[2,11,4,8,1024]{4,3,2,1,0:T(8,128)(2,1)S(1)} copy(bf16[2,11,4,8,1024]{4,3,1,2,0:T(8,128)(2,1)} %bitcast.103) | data formatting | bytes 2883584 | tf_op jit(solution)/shard_map/transpose | solution.py:130
  63.3 2.0 %fusion.43 = f32[1280,704]{0,1:T(8,128)S(1)} fusion(bf16[704,1024]{1,0:T(8,128)(2,1)S(1)} %bitcast.104, bf16[1024,1280]{1,0:T(8,128)(2,1)S(1)} %copy-done.1), kind=kOutput, calls=%fused_computation.102 | convolution fusion | flops 1845493760 | bytes 7667712 | tf_op jit(solution)/shard_map/receptor_spectra/dot_general | solution.py:57
  65.4 2.1 %convolution_add_fusion = f32[1280,704]{0,1:T(8,128)S(1)} fusion(f32[1280,704]{0,1:T(8,128)S(1)} %fusion.43, bf16[704,1024]{1,0:T(8,128)(2,1)S(1)} %bitcast.105, bf16[1024,1280]{1,0:T(8,128)(2,1)S(1)} %copy-done), kind=kOutput, calls=%fused_computation.16 | convolution fusion | flops 1846394880 | bytes 11272192 | tf_op jit(solution)/shard_map/receptor_spectra/dot_general | solution.py:58
  67.5 3.1 %convolution_bitcast_fusion.1 = f32[22,1,64,1280]{3,2,0,1:T(8,128)S(1)} fusion(f32[22,32,1280]{2,1,0:T(8,128)S(1)} %bitcast.100, f32[64,32,1]{0,1,2:T(8,128)S(1)} %copy-done.7), kind=kOutput, calls=%fused_computation.15 | convolution fusion | flops 346030080 | bytes 10821632 | tf_op jit(solution)/shard_map/receptor_spectra/px,trxq->trpq/dot_general | solution.py:60
  70.5 2.5 %slice_bitcast_fusion.3 = (f32[22,32,640]{2,1,0:T(8,128)S(1)}, f32[22,32,640]{2,1,0:T(8,128)S(1)}, f32[22,32,640]{2,1,0:T(8,128)}, f32[22,32,640]{2,1,0:T(8,128)}) fusion(f32[22,1,64,1280]{3,2,0,1:T(8,128)S(1)} %convolution_bitcast_fusion.1), kind=kLoop, calls=%fused_computation.24 | loop fusion | bytes 14417920 | tf_op jit(solution)/shard_map/correlate/mul | solution.py:83
  73.0 1.4 %fusion.41 = f32[22,32,640]{2,1,0:T(8,128)} fusion(f32[22,1,64,1280]{3,2,0,1:T(8,128)S(1)} %convolution_bitcast_fusion.1), kind=kLoop, calls=%fused_computation.100 | loop fusion | flops 450560 | bytes 3604480 | tf_op jit(solution)/shard_map/correlate/neg | solution.py:84
  74.4 14.1 %subtract_reduce_fusion = (f32[4,32,640]{2,1,0:T(8,128)S(1)}, f32[4,32,640]{2,1,0:T(8,128)S(1)}) fusion(f32[22,32,640]{2,1,0:T(8,128)S(1)} %get-tuple-element.17, f32[22,32,640]{2,1,0:T(8,128)} %get-tuple-element.18, f32[22,32,640]{2,1,0:T(8,128)} %get-tuple-element.19, f32[22,32,640]{2,1,0:T(8,128)S(1)} %get-tuple-element.16, ...), kind=kLoop, calls=%fused_computation.8 | loop fusion | flops 34078720 | bytes 38502400 | tf_op jit(solution)/shard_map/correlate/reduce_sum | solution.py:83
  88.5 0.7 fusion.14
  89.4 2.9 %fusion.9 = f32[4]{0:T(128)S(1)} fusion(f32[1024,1280]{1,0:T(8,128)S(1)} %bitcast.94, f32[1,4,32,640]{3,2,1,0:T(8,128)S(1)} %get-tuple-element.25, f32[1,4,32,640]{3,2,1,0:T(8,128)S(1)} %get-tuple-element.24), kind=kOutput, calls=%fused_computation.26 | convolution fusion | flops 1006927872 | bytes 5898256 | tf_op jit(solution)/shard_map/inverse_scores/rnxq,cq->rnxc/dot_general | solution.py:98
  92.5 0.6 collective-permute-start.4
  93.0 3.2 %collective-permute-done.4 = f32[4,32]{0,1:T(8,128)S(1)} collective-permute-done((f32[4,32]{0,1:T(8,128)S(1)}, f32[4,32]{0,1:T(8,128)S(1)}, u32[]{:S(2)}, u32[]{:S(2)}) %collective-permute-start.4) | collective-permute-done | bytes 544 | tf_op jit(solution)/shard_map/ppermute | solution.py:113
  96.3 1.2 collective-permute-done.5
  97.5 1.5 %collective-permute-start.6 = (f32[4,32]{0,1:T(8,128)S(1)}, f32[4,32]{0,1:T(8,128)S(1)}, u32[]{:S(2)}, u32[]{:S(2)}) collective-permute-start(f32[4,32]{0,1:T(8,128)S(1)} %fusion.52), channel_id=1, source_target_pairs={{0,4},{1,5},{2,6},{3,7},{4,0},{5,1},{6,2},{7,3},{8,12},{9,13},{10,... | collective-permute-start | bytes 1544 | tf_op jit(solution)/shard_map/ppermute | solution.py:113
  99.1 2.2 %collective-permute-done.6 = f32[4,32]{0,1:T(8,128)S(1)} collective-permute-done((f32[4,32]{0,1:T(8,128)S(1)}, f32[4,32]{0,1:T(8,128)S(1)}, u32[]{:S(2)}, u32[]{:S(2)}) %collective-permute-start.6) | collective-permute-done | bytes 544 | tf_op jit(solution)/shard_map/ppermute | solution.py:113
  101.3 0.7 collective-permute-start.7
  102.0 3.0 %collective-permute-done.7 = f32[4,32]{0,1:T(8,128)S(1)} collective-permute-done((f32[4,32]{0,1:T(8,128)S(1)}, f32[4,32]{0,1:T(8,128)S(1)}, u32[]{:S(2)}, u32[]{:S(2)}) %collective-permute-start.7) | collective-permute-done | bytes 544 | tf_op jit(solution)/shard_map/ppermute | solution.py:113
  105.4 4.3 %collective-permute-done.8 = f32[4,32]{0,1:T(8,128)S(1)} collective-permute-done((f32[4,32]{0,1:T(8,128)S(1)}, f32[4,32]{0,1:T(8,128)S(1)}, u32[]{:S(2)}, u32[]{:S(2)}) %collective-permute-start.8) | collective-permute-done | bytes 544 | tf_op jit(solution)/shard_map/ppermute | solution.py:113
  109.7 0.5 fusion.42
  110.2 0.6 constant_dynamic-slice_fusion
  (64 shorter events, 1.9 us)
Async XLA Ops:
  7.2 54.6 %all-gather.3.cloned.1.call-start = ((), (), s32[]{:S(2)}) async-start(), calls=%async_computation | async-start | bytes 1622016 | tf_op jit(solution)/shard_map/all_gather | solution.py:128
  7.2 27.2 %collective-permute-start = (s32[3,2,256]{2,1,0:T(2,128)}, s32[3,2,256]{2,1,0:T(2,128)S(1)}, u32[]{:S(2)}, u32[]{:S(2)}) collective-permute-start(s32[3,2,256]{2,1,0:T(2,128)} %param.19), channel_id=1, source_target_pairs={{0,8},{8,16},{16,24},{24,0},{1,9},{9,17},{17,25},{25,1},{2,10},{10... | collective-permute-start | bytes 18440 | tf_op jit(solution)/shard_map/ppermute | solution.py:105
  10.3 24.1 %collective-permute-start.1 = (s32[3,2,256]{2,1,0:T(2,128)}, s32[3,2,256]{2,1,0:T(2,128)S(1)}, u32[]{:S(2)}, u32[]{:S(2)}) collective-permute-start(s32[3,2,256]{2,1,0:T(2,128)} %param.19), channel_id=1, source_target_pairs={{0,16},{8,24},{16,0},{24,8},{1,17},{9,25},{17,1},{25,9},{2,18},{10... | collective-permute-start | bytes 18440 | tf_op jit(solution)/shard_map/ppermute | solution.py:105
  12.9 21.5 %collective-permute-start.2 = (s32[3,2,256]{2,1,0:T(2,128)}, s32[3,2,256]{2,1,0:T(2,128)S(1)}, u32[]{:S(2)}, u32[]{:S(2)}) collective-permute-start(s32[3,2,256]{2,1,0:T(2,128)} %param.19), channel_id=1, source_target_pairs={{0,24},{8,0},{16,8},{24,16},{1,25},{9,1},{17,9},{25,17},{2,26},{10... | collective-permute-start | bytes 18440 | tf_op jit(solution)/shard_map/ppermute | solution.py:105
  15.0 25.3 %collective-permute-start.3 = (f32[11,256]{1,0:T(8,128)S(1)}, f32[11,256]{1,0:T(8,128)S(1)}, u32[]{:S(2)}, u32[]{:S(2)}) collective-permute-start(f32[11,256]{1,0:T(8,128)S(1)} %broadcast_multiply_fusion), channel_id=1, source_target_pairs={{0,1},{1,0},{2,3},{3,2},{4,5},{5,4},{6,7},{7,6},{8,9},{9,8},{10,11... | collective-permute-start | bytes 33800 | tf_op jit(solution)/shard_map/ppermute | solution.py:105
  26.3 7.3 %copy-start.2 = (f32[16,544]{1,0:T(8,128)S(1)}, f32[16,544]{1,0:T(8,128)}, u32[]{:S(2)}) copy-start(f32[16,544]{1,0:T(8,128)} %constant.126.clone) | copy-start | bytes 104452
  26.3 7.3 %copy-start.3 = (f32[16,544]{1,0:T(8,128)S(1)}, f32[16,544]{1,0:T(8,128)}, u32[]{:S(2)}) copy-start(f32[16,544]{1,0:T(8,128)} %constant.127.clone) | copy-start | bytes 104452
  26.3 7.3 %copy-start.4 = (f32[16,544]{1,0:T(8,128)S(1)}, f32[16,544]{1,0:T(8,128)}, u32[]{:S(2)}) copy-start(f32[16,544]{1,0:T(8,128)} %constant.128.clone) | copy-start | bytes 104452
  26.3 7.3 %copy-start.5 = (f32[16,544]{1,0:T(8,128)S(1)}, f32[16,544]{1,0:T(8,128)}, u32[]{:S(2)}) copy-start(f32[16,544]{1,0:T(8,128)} %constant.129.clone) | copy-start | bytes 104452
  33.6 0.8 copy-start.9
  41.0 5.6 %copy-start.8 = (f32[64,16,1,1]{0,1,3,2:T(8,128)S(1)}, f32[64,16,1,1]{0,1,3,2:T(8,128)}, u32[]{:S(2)}) copy-start(f32[64,16,1,1]{0,1,3,2:T(8,128)} %constant.138) | copy-start | bytes 12292
  46.6 16.7 %copy-start.1 = (bf16[1024,1280]{1,0:T(8,128)(2,1)S(1)}, bf16[1024,1280]{1,0:T(8,128)(2,1)}, u32[]{:S(2)}) copy-start(bf16[1024,1280]{1,0:T(8,128)(2,1)} %get-tuple-element.6) | copy-start | bytes 7864324
  63.3 2.0 %copy-start = (bf16[1024,1280]{1,0:T(8,128)(2,1)S(1)}, bf16[1024,1280]{1,0:T(8,128)(2,1)}, u32[]{:S(2)}) copy-start(bf16[1024,1280]{1,0:T(8,128)(2,1)} %get-tuple-element.7) | copy-start | bytes 7864324
  65.4 2.1 %copy-start.7 = (f32[64,32,1]{0,1,2:T(8,128)S(1)}, f32[64,32,1]{0,1,2:T(8,128)}, u32[]{:S(2)}) copy-start(f32[64,32,1]{0,1,2:T(8,128)} %constant.137) | copy-start | bytes 24580
  74.4 14.9 %slice-start = ((s8[5242880]{0:T(1024)(128)(4,1)}), s8[4194304]{0:T(1024)(128)(4,1)S(1)}, s32[]{:S(2)}) async-start(s8[5242880]{0:T(1024)(128)(4,1)} %bitcast.93), calls=%async_computation.1 | async-start | bytes 8388608
  74.4 14.1 %copy-start.6 = (f32[64,32,1,1]{0,1,3,2:T(8,128)S(1)}, f32[64,32,1,1]{0,1,3,2:T(8,128)}, u32[]{:S(2)}) copy-start(f32[64,32,1,1]{0,1,3,2:T(8,128)} %constant.139) | copy-start | bytes 24580
  74.4 14.8 %copy-start.10 = (f32[640]{0:T(1024)S(1)}, f32[640]{0:T(1024)}, u32[]{:S(2)}) copy-start(f32[640]{0:T(1024)} %constant.132.clone) | copy-start | bytes 7684
  74.4 14.9 %slice-start.1 = ((s8[5242880]{0:T(1024)(128)(4,1)}), s8[1048576]{0:T(1024)(128)(4,1)S(1)}, s32[]{:S(2)}) async-start(s8[5242880]{0:T(1024)(128)(4,1)} %bitcast.93), calls=%async_computation.2 | async-start | bytes 2097152
  92.5 3.7 %collective-permute-start.4 = (f32[4,32]{0,1:T(8,128)S(1)}, f32[4,32]{0,1:T(8,128)S(1)}, u32[]{:S(2)}, u32[]{:S(2)}) collective-permute-start(f32[4,32]{0,1:T(8,128)S(1)} %broadcast_select_fusion.1), channel_id=1, source_target_pairs={{0,1},{1,0},{2,3},{3,2},{4,5},{5,4},{6,7},{7,6},{8,9},{9,8},{10,11... | collective-permute-start | bytes 1544 | tf_op jit(solution)/shard_map/ppermute | solution.py:113
  96.3 1.2 %collective-permute-start.5 = (f32[4,32]{0,1:T(8,128)S(1)}, f32[4,32]{0,1:T(8,128)S(1)}, u32[]{:S(2)}, u32[]{:S(2)}) collective-permute-start(f32[4,32]{0,1:T(8,128)S(1)} %fusion.28), channel_id=1, source_target_pairs={{0,2},{1,3},{2,0},{3,1},{4,6},{5,7},{6,4},{7,5},{8,10},{9,11},{10,... | collective-permute-start | bytes 1544 | tf_op jit(solution)/shard_map/ppermute | solution.py:113
  97.5 3.7 %collective-permute-start.6 = (f32[4,32]{0,1:T(8,128)S(1)}, f32[4,32]{0,1:T(8,128)S(1)}, u32[]{:S(2)}, u32[]{:S(2)}) collective-permute-start(f32[4,32]{0,1:T(8,128)S(1)} %fusion.52), channel_id=1, source_target_pairs={{0,4},{1,5},{2,6},{3,7},{4,0},{5,1},{6,2},{7,3},{8,12},{9,13},{10,... | collective-permute-start | bytes 1544 | tf_op jit(solution)/shard_map/ppermute | solution.py:113
  101.3 3.7 %collective-permute-start.7 = (f32[4,32]{0,1:T(8,128)S(1)}, f32[4,32]{0,1:T(8,128)S(1)}, u32[]{:S(2)}, u32[]{:S(2)}) collective-permute-start(f32[4,32]{0,1:T(8,128)S(1)} %max.17), channel_id=1, source_target_pairs={{0,8},{1,9},{2,10},{3,11},{4,12},{5,13},{6,14},{7,15},{8,0},{9,1},... | collective-permute-start | bytes 1544 | tf_op jit(solution)/shard_map/ppermute | solution.py:113
  105.0 4.6 %collective-permute-start.8 = (f32[4,32]{0,1:T(8,128)S(1)}, f32[4,32]{0,1:T(8,128)S(1)}, u32[]{:S(2)}, u32[]{:S(2)}) collective-permute-start(f32[4,32]{0,1:T(8,128)S(1)} %max.18), channel_id=1, source_target_pairs={{0,16},{1,17},{2,18},{3,19},{4,20},{5,21},{6,22},{7,23},{8,24},{9,... | collective-permute-start | bytes 1544 | tf_op jit(solution)/shard_map/ppermute | solution.py:113
Sparse Core Ops, SparseCore 0:
  16.7 22.5 all-gather.2

commit v5 on v4

--- a/solution.py
+++ b/solution.py
@@ -23,31 +23,49 @@
     return np.cos(phase).astype(np.float32), np.sin(phase).astype(np.float32)
 
 
-def plane_tables(side):
-    column = np.arange(G * HZ)
-    cell = np.arange(side)[:, None]
-    phase_y = (cell * (column // HZ)[None, :] % G) * (2.0 * math.pi / G)
-    phase_z = (cell * (column % HZ)[None, :] % G) * (2.0 * math.pi / G)
-    cy = jnp.asarray(np.cos(phase_y).astype(np.float32))[:, None, :]
-    sy = jnp.asarray(np.sin(phase_y).astype(np.float32))[:, None, :]
-    cz = jnp.asarray(np.cos(phase_z).astype(np.float32))[None, :, :]
-    sz = jnp.asarray(np.sin(phase_z).astype(np.float32))[None, :, :]
-    cos_t = cy * cz - sy * sz
-    sin_t = sy * cz + cy * sz
-    pad = jnp.zeros((side, side, WIDTH - G * HZ), jnp.float32)
-    joined = jnp.concatenate([cos_t, pad, sin_t, pad], axis=-1)
-    return joined.reshape(side * side, 2 * WIDTH)
+def plane_factors():
+    column = np.arange(2 * WIDTH)
+    half = column // WIDTH
+    freq = column % WIDTH
+    valid = freq < G * HZ
+    cell = np.arange(G)[:, None]
+    phase_y = (cell * (freq // HZ)[None, :] % G) * (2.0 * math.pi / G)
+    phase_z = (cell * (freq % HZ)[None, :] % G) * (2.0 * math.pi / G)
+    cy, sy = np.cos(phase_y), np.sin(phase_y)
+    cz, sz = np.cos(phase_z), np.sin(phase_z)
+    first = np.where(half == 0, cy, sy) * valid
+    third = np.where(half == 0, -sy, cy) * valid
+    return [jnp.asarray(f.astype(np.float32)) for f in (first, cz, third, sz)]
+
+
+def plane_table(factors, side):
+    first, second, third, fourth = [f[:side] for f in factors]
+    table = first[:, None, :] * second[None, :, :] + third[:, None, :] * fourth[None, :, :]
+    return table.reshape(side * side, 2 * WIDTH)
 
 
 def split_bf16(table):
-    upper = table.astype(jnp.bfloat16)
-    lower = (table - upper.astype(jnp.float32)).astype(jnp.bfloat16)
-    return upper, lower
+    upper = lax.reduce_precision(table, exponent_bits=8, mantissa_bits=7)
+    lower = table - upper
+    return upper.astype(jnp.bfloat16), lower.astype(jnp.bfloat16)
+
+
+def mix_tables(cell_count):
+    cos_x, sin_x = line_table(G, cell_count)
+    from_cos = np.concatenate([cos_x, -sin_x], axis=0)
+    from_sin = np.concatenate([-sin_x, -cos_x], axis=0)
+    return jnp.asarray(from_cos), jnp.asarray(from_sin)
 
 
 def mix_table(cell_count):
     cos_x, sin_x = line_table(G, cell_count)
     return jnp.asarray(np.concatenate([cos_x, sin_x], axis=0))
+
+
+def x_transform(plane, cell_count, form):
+    from_cos, from_sin = mix_tables(cell_count)
+    first = jnp.einsum(form, from_cos, plane[..., :WIDTH], precision=HIGH)
+    return first + jnp.einsum(form, from_sin, plane[..., WIDTH:], precision=HIGH)
 
 
 def receptor_mixed(grids, table_hi, table_lo):
@@ -57,7 +75,7 @@
     plane = jnp.dot(flat, table_hi, preferred_element_type=jnp.float32)
     plane = plane + jnp.dot(flat, table_lo, preferred_element_type=jnp.float32)
     plane = plane.reshape(terms, receptors, G, 2 * WIDTH)
-    return jnp.einsum("px,trxq->trpq", mix_table(G), plane, precision=HIGH)
+    return x_transform(plane, G, "px,trxq->trpq")
 
 
 def ligand_spectra(voxels, coefficients, box_table):
@@ -67,25 +85,20 @@
     in_x = (voxels[0][:, None, :] == x_cells[None, :, None]).astype(jnp.float32)
     weights = coefficients[None, :, None, :] * in_x[:, None, :, :]
     plane = jnp.einsum("ntxa,naq->tnxq", weights, rows, precision=HIGH)
-    mixed = jnp.einsum("px,tnxq->tnpq", mix_table(LB), plane, precision=HIGH)
-    lig_re = mixed[:, :, :G, :WIDTH] - mixed[:, :, G:, WIDTH:]
-    lig_im = -mixed[:, :, :G, WIDTH:] - mixed[:, :, G:, :WIDTH]
-    return lig_re, lig_im
-
-
-def correlate(mixed, lig_re, lig_im):
-    re_cos = mixed[:, :, None, :G, :WIDTH]
-    re_sin = mixed[:, :, None, G:, :WIDTH]
-    ims_cos = mixed[:, :, None, :G, WIDTH:]
-    ims_sin = mixed[:, :, None, G:, WIDTH:]
-    lr = lig_re[:, None]
-    li = lig_im[:, None]
-    prod_re = jnp.sum(re_cos * lr - re_sin * li - ims_sin * lr - ims_cos * li, axis=0)
-    prod_im = jnp.sum(-ims_cos * lr - re_sin * lr - re_cos * li + ims_sin * li, axis=0)
+    return x_transform(plane, LB, "px,tnxq->tnpq")
+
+
+def correlate(rec_spec, lig_spec):
+    rr = rec_spec[:, :, None, :G]
+    ri = rec_spec[:, :, None, G:]
+    lr = lig_spec[:, None, :, :G]
+    li = lig_spec[:, None, :, G:]
+    prod_re = jnp.sum(lr * rr + li * ri, axis=0)
+    prod_im = jnp.sum(lr * ri - li * rr, axis=0)
     return jnp.stack([prod_re, prod_im], axis=0)
 
 
-def inverse_scores(products, full_table):
+def inverse_scores(products, table_hi, table_lo):
     mixed = jnp.einsum("xp,srnpq->srnxq", mix_table(G), products, precision=HIGH)
     inv_re = mixed[0, :, :, :G] - mixed[1, :, :, G:]
     inv_im = mixed[1, :, :, :G] + mixed[0, :, :, G:]
@@ -95,7 +108,11 @@
     fold = np.where(column < G * HZ, fold, 0.0)
     fold = jnp.asarray(fold.astype(np.float32))
     joined = jnp.concatenate([inv_re * fold, -inv_im * fold], axis=-1)
-    return jnp.einsum("rnxq,cq->rnxc", joined, full_table, precision=HIGH)
+    upper, lower = lax.optimization_barrier(split_bf16(joined))
+    form = "rnxq,cq->rnxc"
+    scores = jnp.einsum(form, upper, table_hi, preferred_element_type=jnp.float32)
+    scores = scores + jnp.einsum(form, lower, table_hi, preferred_element_type=jnp.float32)
+    return scores + jnp.einsum(form, upper, table_lo, preferred_element_type=jnp.float32)
 
 
 def gather_by_permutes(values, axis_name, count, here):
@@ -107,11 +124,16 @@
 
 
 def butterfly_max(values, axes, device_count):
-    shift = 1
-    while shift < device_count:
-        pairs = [(k, k ^ shift) for k in range(device_count)]
-        values = jnp.maximum(values, lax.ppermute(values, axes, pairs))
-        shift *= 2
+    stride = 1
+    while stride < device_count:
+        radix = 4 if stride * 4 <= device_count else 2
+        received = []
+        for digit in range(1, radix):
+            pairs = [(k, k ^ (digit * stride)) for k in range(device_count)]
+            received.append(lax.ppermute(values, axes, pairs))
+        for block in received:
+            values = jnp.maximum(values, block)
+        stride *= radix
     return values
 
 
@@ -141,19 +163,19 @@
         order = (term - jnp.arange(term_count, dtype=jnp.int32)) % term_count
         coefficients = jnp.take(term_blocks, order, axis=0).reshape(-1, coefficients.shape[1])
         with jax.named_scope("twiddle_tables"):
-            full_table = plane_tables(G)
-            box_table = plane_tables(LB)
-            table_hi, table_lo = split_bf16(full_table)
-            tables = lax.optimization_barrier((full_table, box_table, table_hi, table_lo))
-            full_table, box_table, table_hi, table_lo = tables
+            factors = plane_factors()
+            table_hi, table_lo = split_bf16(plane_table(factors, G))
+            box_table = plane_table(factors, LB)
+            tables = lax.optimization_barrier((box_table, table_hi, table_lo))
+            box_table, table_hi, table_lo = tables
         with jax.named_scope("ligand_spectra"):
-            lig_re, lig_im = ligand_spectra(voxels, coefficients, box_table)
+            lig_spec = ligand_spectra(voxels, coefficients, box_table)
         with jax.named_scope("receptor_spectra"):
-            mixed = receptor_mixed(gathered, table_hi, table_lo)
+            rec_spec = receptor_mixed(gathered, table_hi, table_lo)
         with jax.named_scope("correlate"):
-            products = correlate(mixed, lig_re, lig_im)
+            products = correlate(rec_spec, lig_spec)
         with jax.named_scope("inverse_scores"):
-            scores = inverse_scores(products, full_table)
+            scores = inverse_scores(products, table_hi, table_lo)
             best_here = jnp.max(scores, axis=(2, 3))[0]
         receptors = plane_count
         columns = jnp.arange(rot_total, dtype=jnp.int32)

time: 118 us -> 91.5 us (0.78)
  other arithmetic: 28.9 us -> 10.8 us
  local copies, waits for them, and re-layouts: 17.1 us -> 9.78 us
  waiting for transfers between devices: 13.9 us -> 9.37 us
  starting transfers between devices: 11.8 us -> 14.5 us
    reduce_sum x1, other arithmetic: 14.1 us -> 2.81 us  [correlate(): prod_re = jnp.sum(lr * rr + li * ri, axis=0)]
    concatenate x2 -> x0, local copies, waits for them, and re-layouts: 5.99 us -> none  [plane_tables(): joined = jnp.concatenate([cos_t, pad, sin_t, pad], axis=-1)]
    ppermute x5 -> x7, waiting for transfers between devices: 13.9 us -> 9.34 us  [butterfly_max(): received.append(lax.ppermute(values, axes, pairs))]
    convert_element_type x1 -> x2, other arithmetic: 7.25 us -> 3.22 us  [split_bf16(): return (upper.astype(jnp.bfloat16), lower.astype(jnp.bfloat16))]
    ppermute x5 -> x7, starting transfers between devices: 3.19 us -> 5.95 us  [butterfly_max(): received.append(lax.ppermute(values, axes, pairs))]
    mul x1, local copies, waits for them, and re-layouts: 2.51 us -> 0.28 us  [correlate(): prod_re = jnp.sum(lr * rr + li * ri, axis=0)]
    neg x1 -> x0, other arithmetic: 1.38 us -> none  [correlate(): -ims_cos * lr - re_sin * lr - re_cos * li + ims_sin * li]
    add x2, other arithmetic: 3.41 us -> 2.07 us  [plane_table(): first[:, None, :] * second[None, :, :]]
  transfers between devices with their start and end apart: 10 -> 12, of which waited for: 5 -> 5; matrix products, arithmetic and copies ran while one was open for 39% -> 39% of each run, Pallas kernels for 0% -> 0%
where the time goes in v5:
time: 91.5 us; the launch traced here: 91.1 us
  matrix products  32.2 us (35%)
  starting transfers between devices  14.5 us (16%)
  between operations  14.5 us (16%)
  other arithmetic  10.8 us (12%)
  local copies, waits for them, and re-layouts  9.78 us (11%)
  waiting for transfers between devices  9.37 us (10%)
    dot_general x2, matrix products, x_transform(): jnp.einsum(form, from_sin, plane[..., WIDTH:], precision=HIGH)  10.9 us
    ppermute x7, waiting for transfers between devices, butterfly_max(): received.append(lax.ppermute(values, axes, pairs))  9.34 us
    ppermute x4, starting transfers between devices, gather_by_permutes(): blocks.append(lax.ppermute(values, axis_name, pairs))  8.53 us
    dot_general x2, matrix products, x_transform(): first = jnp.einsum(form, from_cos, plane[..., :WIDTH], precision=HIGH)  7.52 us
    gather x1, local copies, waits for them, and re-layouts, ligand_spectra(): rows = jnp.take(box_table, yz_index, axis=0)  5.97 us
    ppermute x7, starting transfers between devices, butterfly_max(): received.append(lax.ppermute(values, axes, pairs))  5.95 us
    dot_general x1, matrix products, ligand_spectra(): plane = jnp.einsum('ntxa,naq->tnxq', weights, rows, precision=HIGH)  5.87 us
    convert_element_type x2, other arithmetic, split_bf16(): return (upper.astype(jnp.bfloat16), lower.astype(jnp.bfloat16))  3.22 us
  transfers between devices with their start and end apart: 12, of which 5 were waited for; matrix products, arithmetic and copies ran while one was open for 39% of the time, Pallas kernels for 0%

profile of v5, /device:TPU:0, one launch (start us, length us, event | category | flops | bytes accessed | tf_op | source)
XLA Modules:
  0.0 91.1 jit_solution(10011132686651971705)
XLA Ops:
  7.2 3.1 %collective-permute-start = (s32[3,2,256]{2,1,0:T(2,128)}, s32[3,2,256]{2,1,0:T(2,128)S(1)}, u32[]{:S(2)}, u32[]{:S(2)}) collective-permute-start(s32[3,2,256]{2,1,0:T(2,128)} %param.17), channel_id=1, source_target_pairs={{0,8},{8,16},{16,24},{24,0},{1,9},{9,17},{17,25},{25,1},{2,10},{10... | collective-permute-start | bytes 18440 | tf_op jit(solution)/shard_map/ppermute | solution.py:122
  10.3 2.6 %collective-permute-start.1 = (s32[3,2,256]{2,1,0:T(2,128)}, s32[3,2,256]{2,1,0:T(2,128)S(1)}, u32[]{:S(2)}, u32[]{:S(2)}) collective-permute-start(s32[3,2,256]{2,1,0:T(2,128)} %param.17), channel_id=1, source_target_pairs={{0,16},{8,24},{16,0},{24,8},{1,17},{9,25},{17,1},{25,9},{2,18},{10... | collective-permute-start | bytes 18440 | tf_op jit(solution)/shard_map/ppermute | solution.py:122
  12.9 1.3 %collective-permute-start.2 = (s32[3,2,256]{2,1,0:T(2,128)}, s32[3,2,256]{2,1,0:T(2,128)S(1)}, u32[]{:S(2)}, u32[]{:S(2)}) collective-permute-start(s32[3,2,256]{2,1,0:T(2,128)} %param.17), channel_id=1, source_target_pairs={{0,24},{8,0},{16,8},{24,16},{1,25},{9,1},{17,9},{25,17},{2,26},{10... | collective-permute-start | bytes 18440 | tf_op jit(solution)/shard_map/ppermute | solution.py:122
  14.2 0.8 broadcast_multiply_fusion
  15.0 1.5 %collective-permute-start.3 = (f32[11,256]{1,0:T(8,128)S(1)}, f32[11,256]{1,0:T(8,128)S(1)}, u32[]{:S(2)}, u32[]{:S(2)}) collective-permute-start(f32[11,256]{1,0:T(8,128)S(1)} %broadcast_multiply_fusion), channel_id=1, source_target_pairs={{0,1},{1,0},{2,3},{3,2},{4,5},{5,4},{6,7},{7,6},{8,9},{9,8},{10,11... | collective-permute-start | bytes 33800 | tf_op jit(solution)/shard_map/ppermute | solution.py:122
  16.6 0.8 fusion.68
  17.4 1.9 %multiply_add_fusion = f32[32,32,1280]{2,1,0:T(8,128)S(1)} fusion(f32[32,1280]{1,0:T(8,128)} %constant.121.clone, f32[32,1280]{1,0:T(8,128)} %constant.120.clone, f32[32,1280]{1,0:T(8,128)} %constant.119.clone, f32[32,1280]{1,0:T(8,128)} %constant.118.clone), kind=kLoop, calls=%fused_computation.11 | loop fusion | flops 3932160 | bytes 5898240 | tf_op jit(solution)/shard_map/twiddle_tables/add | solution.py:43
  19.4 3.1 %fusion = (bf16[1024,1280]{1,0:T(8,128)(2,1)}, bf16[1024,1280]{1,0:T(8,128)(2,1)}) fusion(f32[32,32,1280]{2,1,0:T(8,128)S(1)} %multiply_add_fusion), kind=kLoop, calls=%fused_computation.8 | loop fusion | flops 5242880 | bytes 10485760 | tf_op jit(solution)/shard_map/twiddle_tables/convert_element_type | solution.py:50
  23.1 6.0 %gather_fusion = f32[1024,1280]{1,0:T(8,128)} fusion(f32[256,1280]{1,0:T(8,128)S(1)} %bitcast.121, s32[1024]{0:T(1024)S(1)} %broadcast_clamp_fusion), kind=kCustom, calls=%fused_computation | custom fusion | bytes 10489856 | tf_op jit(solution)/shard_map/ligand_spectra/jit(_take)/gather | solution.py:83
  29.7 5.9 %convolution_bitcast_fusion = f32[22,4,16,1280]{3,0,2,1:T(8,128)S(1)} fusion(f32[4,256,1280]{2,1,0:T(8,128)} %bitcast.124, pred[4,256]{1,0:T(4,128)(4,1)S(1)} %compare_and_fusion, f32[4,16,256]{2,1,0:T(8,128)S(1)} %fusion.41, f32[22,256]{1,0:T(8,128)S(1)} %broadcast_select_fusion), kind=kOutput, calls=%fused_computation.7 | convolution fusion | flops 2769911808 | bytes 12540928 | tf_op jit(solution)/shard_map/ligand_spectra/ntxa,naq->tnxq/dot_general | solution.py:87
  35.6 0.6 fusion.57
  36.3 5.9 %fusion.4 = f32[22,4,640,64]{2,3,1,0:T(8,128)S(1)} fusion(f32[64,16,1,1]{0,1,3,2:T(8,128)S(1)} %copy-done.10, f32[22,4,16,640]{3,0,2,1:T(8,128)S(1)} %get-tuple-element.17), kind=kOutput, calls=%fused_computation.14 | convolution fusion | flops 346030080 | bytes 18026496 | tf_op jit(solution)/shard_map/ligand_spectra/px,tnxq->tnpq/dot_general | solution.py:67
  42.2 9.3 %add_bitcast_fusion = f32[22,4,64,640]{3,2,1,0:T(8,128)} fusion(f32[22,4,640,64]{2,3,1,0:T(8,128)S(1)} %fusion.4, f32[64,16,1,1]{0,1,3,2:T(8,128)S(1)} %copy-done.9, f32[22,4,16,640]{3,0,2,1:T(8,128)S(1)} %get-tuple-element.16), kind=kOutput, calls=%fused_computation.2 | convolution fusion | flops 349634560 | bytes 32444416 | tf_op jit(solution)/shard_map/ligand_spectra/px,tnxq->tnpq/dot_general | solution.py:68
  51.5 1.5 %copy.31 = bf16[2,11,4,8,1024]{4,3,2,1,0:T(8,128)(2,1)S(1)} copy(bf16[2,11,4,8,1024]{4,3,1,2,0:T(8,128)(2,1)} %bitcast.129) | data formatting | bytes 2883584 | tf_op jit(solution)/shard_map/transpose | solution.py:152
  53.0 2.0 %fusion.58 = f32[1280,704]{0,1:T(8,128)S(1)} fusion(bf16[704,1024]{1,0:T(8,128)(2,1)S(1)} %bitcast.130, bf16[1024,1280]{1,0:T(8,128)(2,1)S(1)} %copy-done), kind=kOutput, calls=%fused_computation.114 | convolution fusion | flops 1845493760 | bytes 7667712 | tf_op jit(solution)/shard_map/receptor_spectra/dot_general | solution.py:75
  55.1 2.0 %convolution_add_fusion = f32[1280,704]{0,1:T(8,128)S(1)} fusion(f32[1280,704]{0,1:T(8,128)S(1)} %fusion.58, bf16[704,1024]{1,0:T(8,128)(2,1)S(1)} %bitcast.131, bf16[1024,1280]{1,0:T(8,128)(2,1)S(1)} %copy-done.1), kind=kOutput, calls=%fused_computation.12 | convolution fusion | flops 1846394880 | bytes 11272192 | tf_op jit(solution)/shard_map/receptor_spectra/dot_general | solution.py:76
  57.1 1.6 %fusion.14 = f32[22,640,64]{1,2,0:T(8,128)S(1)} fusion(f32[64,32,1]{0,1,2:T(8,128)S(1)} %copy-done.8, f32[22,1,32,1280]{3,2,0,1:T(8,128)S(1)} %bitcast.127), kind=kOutput, calls=%fused_computation.29 | convolution fusion | flops 173015040 | bytes 5423104 | tf_op jit(solution)/shard_map/receptor_spectra/px,trxq->trpq/dot_general | solution.py:67
  58.8 1.7 %add_bitcast_fusion.1 = f32[22,1,64,640]{3,2,0,1:T(8,128)S(1)} fusion(f32[22,640,64]{1,2,0:T(8,128)S(1)} %fusion.14, f32[64,32,1]{0,1,2:T(8,128)S(1)} %copy-done.7, f32[22,1,32,1280]{3,2,0,1:T(8,128)S(1)} %bitcast.128), kind=kOutput, calls=%fused_computation.16 | convolution fusion | flops 173916160 | bytes 9027584 | tf_op jit(solution)/shard_map/receptor_spectra/px,trxq->trpq/dot_general | solution.py:68
  60.8 2.8 %add_reduce_fusion = (f32[4,32,640]{2,1,0:T(8,128)S(1)}, f32[4,32,640]{2,1,0:T(8,128)S(1)}) fusion(f32[22,4,64,640]{3,2,1,0:T(8,128)S(1)} %bitcast.123, f32[22,32,640]{2,1,0:T(8,128)S(1)} %get-tuple-element.21, f32[22,32,640]{2,1,0:T(8,128)S(1)} %get-tuple-element.20), kind=kLoop, calls=%fused_computation.6 | loop fusion | flops 14254080 | bytes 18677760 | tf_op jit(solution)/shard_map/correlate/reduce_sum | solution.py:96
  63.7 0.7 fusion.28
  64.6 1.0 %fusion.8 = f32[4,32,1024]{2,1,0:T(8,128)S(1)} fusion(bf16[1024,1280]{1,0:T(8,128)(2,1)S(1)} %copy-done, bf16[1,4,32,1280]{3,2,1,0:T(8,128)(2,1)S(1)} %get-tuple-element.11), kind=kOutput, calls=%fused_computation.19 | convolution fusion | flops 335544320 | bytes 3473408 | tf_op jit(solution)/shard_map/inverse_scores/rnxq,cq->rnxc/dot_general | solution.py:114
  65.6 1.0 %fusion.6 = f32[4,32,1024]{2,1,0:T(8,128)S(1)} fusion(bf16[1024,1280]{1,0:T(8,128)(2,1)S(1)} %copy-done.1, bf16[1,4,32,1280]{3,2,1,0:T(8,128)(2,1)S(1)} %get-tuple-element.10), kind=kOutput, calls=%fused_computation.17 | convolution fusion | flops 335544320 | bytes 3473408 | tf_op jit(solution)/shard_map/inverse_scores/rnxq,cq->rnxc/dot_general | solution.py:115
  66.5 1.1 %fusion.22 = f32[4]{0:T(128)S(1)} fusion(f32[4,32,1024]{2,1,0:T(8,128)S(1)} %fusion.6, f32[4,32,1024]{2,1,0:T(8,128)S(1)} %fusion.8, bf16[1024,1280]{1,0:T(8,128)(2,1)S(1)} %copy-done, bf16[1,4,32,1280]{3,2,1,0:T(8,128)(2,1)S(1)} %get-tuple-element.10), kind=kOutput, calls=%fused_computation.34 | convolution fusion | flops 335937536 | bytes 3997712 | tf_op jit(solution)/shard_map/inverse_scores/rnxq,cq->rnxc/dot_general | solution.py:113
  68.3 1.6 %collective-permute-start.6 = (f32[4,32]{0,1:T(8,128)S(1)}, f32[4,32]{0,1:T(8,128)S(1)}, u32[]{:S(2)}, u32[]{:S(2)}) collective-permute-start(f32[4,32]{0,1:T(8,128)S(1)} %broadcast_select_fusion.1), channel_id=1, source_target_pairs={{0,3},{1,2},{2,1},{3,0},{4,7},{5,6},{6,5},{7,4},{8,11},{9,10},{10,... | collective-permute-start | bytes 1544 | tf_op jit(solution)/shard_map/ppermute | solution.py:133
  70.0 1.7 %collective-permute-done.4 = f32[4,32]{0,1:T(8,128)S(1)} collective-permute-done((f32[4,32]{0,1:T(8,128)S(1)}, f32[4,32]{0,1:T(8,128)S(1)}, u32[]{:S(2)}, u32[]{:S(2)}) %collective-permute-start.4) | collective-permute-done | bytes 544 | tf_op jit(solution)/shard_map/ppermute | solution.py:133
  71.8 1.5 %collective-permute-start.7 = (f32[4,32]{0,1:T(8,128)S(1)}, f32[4,32]{0,1:T(8,128)S(1)}, u32[]{:S(2)}, u32[]{:S(2)}) collective-permute-start(f32[4,32]{0,1:T(8,128)S(1)} %maximum_maximum_fusion.1), channel_id=1, source_target_pairs={{0,4},{1,5},{2,6},{3,7},{4,0},{5,1},{6,2},{7,3},{8,12},{9,13},{10,... | collective-permute-start | bytes 1544 | tf_op jit(solution)/shard_map/ppermute | solution.py:133
  73.2 0.7 collective-permute-start.8
  73.9 1.3 %collective-permute-start.9 = (f32[4,32]{0,1:T(8,128)S(1)}, f32[4,32]{0,1:T(8,128)S(1)}, u32[]{:S(2)}, u32[]{:S(2)}) collective-permute-start(f32[4,32]{0,1:T(8,128)S(1)} %maximum_maximum_fusion.1), channel_id=1, source_target_pairs={{0,12},{1,13},{2,14},{3,15},{4,8},{5,9},{6,10},{7,11},{8,4},{9,5},... | collective-permute-start | bytes 1544 | tf_op jit(solution)/shard_map/ppermute | solution.py:133
  75.5 1.5 %collective-permute-done.8 = f32[4,32]{0,1:T(8,128)S(1)} collective-permute-done((f32[4,32]{0,1:T(8,128)S(1)}, f32[4,32]{0,1:T(8,128)S(1)}, u32[]{:S(2)}, u32[]{:S(2)}) %collective-permute-start.8) | collective-permute-done | bytes 544 | tf_op jit(solution)/shard_map/ppermute | solution.py:133
  77.0 1.6 %collective-permute-done.9 = f32[4,32]{0,1:T(8,128)S(1)} collective-permute-done((f32[4,32]{0,1:T(8,128)S(1)}, f32[4,32]{0,1:T(8,128)S(1)}, u32[]{:S(2)}, u32[]{:S(2)}) %collective-permute-start.9) | collective-permute-done | bytes 544 | tf_op jit(solution)/shard_map/ppermute | solution.py:133
  78.9 4.3 %collective-permute-done.10 = f32[4,32]{0,1:T(8,128)S(1)} collective-permute-done((f32[4,32]{0,1:T(8,128)S(1)}, f32[4,32]{0,1:T(8,128)S(1)}, u32[]{:S(2)}, u32[]{:S(2)}) %collective-permute-start.10) | collective-permute-done | bytes 544 | tf_op jit(solution)/shard_map/ppermute | solution.py:133
  83.7 0.6 constant_dynamic-slice_fusion
  (75 shorter events, 3.7 us)
Async XLA Ops:
  7.2 44.3 %all-gather.3.cloned.1.call-start = ((), (), s32[]{:S(2)}) async-start(), calls=%async_computation | async-start | bytes 1622016 | tf_op jit(solution)/shard_map/all_gather | solution.py:150
  7.2 15.7 %collective-permute-start = (s32[3,2,256]{2,1,0:T(2,128)}, s32[3,2,256]{2,1,0:T(2,128)S(1)}, u32[]{:S(2)}, u32[]{:S(2)}) collective-permute-start(s32[3,2,256]{2,1,0:T(2,128)} %param.17), channel_id=1, source_target_pairs={{0,8},{8,16},{16,24},{24,0},{1,9},{9,17},{17,25},{25,1},{2,10},{10... | collective-permute-start | bytes 18440 | tf_op jit(solution)/shard_map/ppermute | solution.py:122
  10.3 12.6 %collective-permute-start.1 = (s32[3,2,256]{2,1,0:T(2,128)}, s32[3,2,256]{2,1,0:T(2,128)S(1)}, u32[]{:S(2)}, u32[]{:S(2)}) collective-permute-start(s32[3,2,256]{2,1,0:T(2,128)} %param.17), channel_id=1, source_target_pairs={{0,16},{8,24},{16,0},{24,8},{1,17},{9,25},{17,1},{25,9},{2,18},{10... | collective-permute-start | bytes 18440 | tf_op jit(solution)/shard_map/ppermute | solution.py:122
  12.9 10.1 %collective-permute-start.2 = (s32[3,2,256]{2,1,0:T(2,128)}, s32[3,2,256]{2,1,0:T(2,128)S(1)}, u32[]{:S(2)}, u32[]{:S(2)}) collective-permute-start(s32[3,2,256]{2,1,0:T(2,128)} %param.17), channel_id=1, source_target_pairs={{0,24},{8,0},{16,8},{24,16},{1,25},{9,1},{17,9},{25,17},{2,26},{10... | collective-permute-start | bytes 18440 | tf_op jit(solution)/shard_map/ppermute | solution.py:122
  15.0 14.0 %collective-permute-start.3 = (f32[11,256]{1,0:T(8,128)S(1)}, f32[11,256]{1,0:T(8,128)S(1)}, u32[]{:S(2)}, u32[]{:S(2)}) collective-permute-start(f32[11,256]{1,0:T(8,128)S(1)} %broadcast_multiply_fusion), channel_id=1, source_target_pairs={{0,1},{1,0},{2,3},{3,2},{4,5},{5,4},{6,7},{7,6},{8,9},{9,8},{10,11... | collective-permute-start | bytes 33800 | tf_op jit(solution)/shard_map/ppermute | solution.py:122
  19.3 3.2 %copy-start.2 = (f32[16,1280]{1,0:T(8,128)S(1)}, f32[16,1280]{1,0:T(8,128)}, u32[]{:S(2)}) copy-start(f32[16,1280]{1,0:T(8,128)} %constant.132) | copy-start | bytes 245764
  19.3 3.2 %copy-start.3 = (f32[16,1280]{1,0:T(8,128)S(1)}, f32[16,1280]{1,0:T(8,128)}, u32[]{:S(2)}) copy-start(f32[16,1280]{1,0:T(8,128)} %constant.133) | copy-start | bytes 245764
  19.3 3.2 %copy-start.4 = (f32[16,1280]{1,0:T(8,128)S(1)}, f32[16,1280]{1,0:T(8,128)}, u32[]{:S(2)}) copy-start(f32[16,1280]{1,0:T(8,128)} %constant.134) | copy-start | bytes 245764
  19.3 3.2 %copy-start.5 = (f32[16,1280]{1,0:T(8,128)S(1)}, f32[16,1280]{1,0:T(8,128)}, u32[]{:S(2)}) copy-start(f32[16,1280]{1,0:T(8,128)} %constant.135) | copy-start | bytes 245764
  19.3 3.6 %copy-start.11 = (s32[3,2,256]{2,1,0:T(2,128)S(1)}, s32[3,2,256]{2,1,0:T(2,128)}, u32[]{:S(2)}) copy-start(s32[3,2,256]{2,1,0:T(2,128)} %param.17) | copy-start | bytes 18436
  35.6 0.7 copy-start.10
  36.3 5.9 %copy-start.9 = (f32[64,16,1,1]{0,1,3,2:T(8,128)S(1)}, f32[64,16,1,1]{0,1,3,2:T(8,128)}, u32[]{:S(2)}) copy-start(f32[64,16,1,1]{0,1,3,2:T(8,128)} %constant.137) | copy-start | bytes 12292
  42.2 10.8 %copy-start = (bf16[1024,1280]{1,0:T(8,128)(2,1)S(1)}, bf16[1024,1280]{1,0:T(8,128)(2,1)}, u32[]{:S(2)}) copy-start(bf16[1024,1280]{1,0:T(8,128)(2,1)} %get-tuple-element.8) | copy-start | bytes 7864324
  53.0 2.1 %copy-start.1 = (bf16[1024,1280]{1,0:T(8,128)(2,1)S(1)}, bf16[1024,1280]{1,0:T(8,128)(2,1)}, u32[]{:S(2)}) copy-start(bf16[1024,1280]{1,0:T(8,128)(2,1)} %get-tuple-element.9) | copy-start | bytes 7864324
  55.0 2.1 %copy-start.8 = (f32[64,32,1]{0,1,2:T(8,128)S(1)}, f32[64,32,1]{0,1,2:T(8,128)}, u32[]{:S(2)}) copy-start(f32[64,32,1]{0,1,2:T(8,128)} %constant.138) | copy-start | bytes 24580
  55.0 5.7 %slice-start = ((s8[14417920]{0:T(1024)(128)(4,1)}), s8[4194304]{0:T(1024)(128)(4,1)S(1)}, s32[]{:S(2)}) async-start(s8[14417920]{0:T(1024)(128)(4,1)} %bitcast.122), calls=%async_computation.1 | async-start | bytes 8388608
  55.1 5.7 %slice-start.1 = ((s8[14417920]{0:T(1024)(128)(4,1)}), s8[4194304]{0:T(1024)(128)(4,1)S(1)}, s32[]{:S(2)}) async-start(s8[14417920]{0:T(1024)(128)(4,1)} %bitcast.122), calls=%async_computation.2 | async-start | bytes 8388608
  57.1 1.7 %copy-start.7 = (f32[64,32,1]{0,1,2:T(8,128)S(1)}, f32[64,32,1]{0,1,2:T(8,128)}, u32[]{:S(2)}) copy-start(f32[64,32,1]{0,1,2:T(8,128)} %constant.139) | copy-start | bytes 24580
  57.1 3.7 %slice-start.2 = ((s8[14417920]{0:T(1024)(128)(4,1)}), s8[4194304]{0:T(1024)(128)(4,1)S(1)}, s32[]{:S(2)}) async-start(s8[14417920]{0:T(1024)(128)(4,1)} %bitcast.122), calls=%async_computation.3 | async-start | bytes 8388608
  58.8 2.0 %slice-start.3 = ((s8[14417920]{0:T(1024)(128)(4,1)}), s8[1835008]{0:T(1024)(128)(4,1)S(1)}, s32[]{:S(2)}) async-start(s8[14417920]{0:T(1024)(128)(4,1)} %bitcast.122), calls=%async_computation.4 | async-start | bytes 3670016
  60.8 2.8 %copy-start.6 = (f32[64,32,1,1]{0,1,3,2:T(8,128)S(1)}, f32[64,32,1,1]{0,1,3,2:T(8,128)}, u32[]{:S(2)}) copy-start(f32[64,32,1,1]{0,1,3,2:T(8,128)} %constant.140) | copy-start | bytes 24580
  60.8 3.6 %copy-start.12 = (f32[640]{0:T(1024)S(1)}, f32[640]{0:T(1024)}, u32[]{:S(2)}) copy-start(f32[640]{0:T(1024)} %constant.127.clone) | copy-start | bytes 7684
  67.8 3.9 %collective-permute-start.4 = (f32[4,32]{0,1:T(8,128)S(1)}, f32[4,32]{0,1:T(8,128)S(1)}, u32[]{:S(2)}, u32[]{:S(2)}) collective-permute-start(f32[4,32]{0,1:T(8,128)S(1)} %broadcast_select_fusion.1), channel_id=1, source_target_pairs={{0,1},{1,0},{2,3},{3,2},{4,5},{5,4},{6,7},{7,6},{8,9},{9,8},{10,11... | collective-permute-start | bytes 1544 | tf_op jit(solution)/shard_map/ppermute | solution.py:133
  68.3 3.3 %collective-permute-start.5 = (f32[4,32]{0,1:T(8,128)S(1)}, f32[4,32]{0,1:T(8,128)S(1)}, u32[]{:S(2)}, u32[]{:S(2)}) collective-permute-start(f32[4,32]{0,1:T(8,128)S(1)} %broadcast_select_fusion.1), channel_id=1, source_target_pairs={{0,2},{1,3},{2,0},{3,1},{4,6},{5,7},{6,4},{7,5},{8,10},{9,11},{10,... | collective-permute-start | bytes 1544 | tf_op jit(solution)/shard_map/ppermute | solution.py:133
  68.3 3.3 %collective-permute-start.6 = (f32[4,32]{0,1:T(8,128)S(1)}, f32[4,32]{0,1:T(8,128)S(1)}, u32[]{:S(2)}, u32[]{:S(2)}) collective-permute-start(f32[4,32]{0,1:T(8,128)S(1)} %broadcast_select_fusion.1), channel_id=1, source_target_pairs={{0,3},{1,2},{2,1},{3,0},{4,7},{5,6},{6,5},{7,4},{8,11},{9,10},{10,... | collective-permute-start | bytes 1544 | tf_op jit(solution)/shard_map/ppermute | solution.py:133
  71.8 3.7 %collective-permute-start.7 = (f32[4,32]{0,1:T(8,128)S(1)}, f32[4,32]{0,1:T(8,128)S(1)}, u32[]{:S(2)}, u32[]{:S(2)}) collective-permute-start(f32[4,32]{0,1:T(8,128)S(1)} %maximum_maximum_fusion.1), channel_id=1, source_target_pairs={{0,4},{1,5},{2,6},{3,7},{4,0},{5,1},{6,2},{7,3},{8,12},{9,13},{10,... | collective-permute-start | bytes 1544 | tf_op jit(solution)/shard_map/ppermute | solution.py:133
  73.2 3.7 %collective-permute-start.8 = (f32[4,32]{0,1:T(8,128)S(1)}, f32[4,32]{0,1:T(8,128)S(1)}, u32[]{:S(2)}, u32[]{:S(2)}) collective-permute-start(f32[4,32]{0,1:T(8,128)S(1)} %maximum_maximum_fusion.1), channel_id=1, source_target_pairs={{0,8},{1,9},{2,10},{3,11},{4,12},{5,13},{6,14},{7,15},{8,0},{9,1},... | collective-permute-start | bytes 1544 | tf_op jit(solution)/shard_map/ppermute | solution.py:133
  73.9 4.6 %collective-permute-start.9 = (f32[4,32]{0,1:T(8,128)S(1)}, f32[4,32]{0,1:T(8,128)S(1)}, u32[]{:S(2)}, u32[]{:S(2)}) collective-permute-start(f32[4,32]{0,1:T(8,128)S(1)} %maximum_maximum_fusion.1), channel_id=1, source_target_pairs={{0,12},{1,13},{2,14},{3,15},{4,8},{5,9},{6,10},{7,11},{8,4},{9,5},... | collective-permute-start | bytes 1544 | tf_op jit(solution)/shard_map/ppermute | solution.py:133
  78.6 4.6 %collective-permute-start.10 = (f32[4,32]{0,1:T(8,128)S(1)}, f32[4,32]{0,1:T(8,128)S(1)}, u32[]{:S(2)}, u32[]{:S(2)}) collective-permute-start(f32[4,32]{0,1:T(8,128)S(1)} %maximum_maximum_fusion), channel_id=1, source_target_pairs={{0,16},{1,17},{2,18},{3,19},{4,20},{5,21},{6,22},{7,23},{8,24},{9,... | collective-permute-start | bytes 1544 | tf_op jit(solution)/shard_map/ppermute | solution.py:133
Sparse Core Ops, SparseCore 0:
  16.7 22.5 all-gather.2

commit v6 on v5

--- a/solution.py
+++ b/solution.py
@@ -39,9 +39,11 @@
 
 
 def plane_table(factors, side):
-    first, second, third, fourth = [f[:side] for f in factors]
-    table = first[:, None, :] * second[None, :, :] + third[:, None, :] * fourth[None, :, :]
-    return table.reshape(side * side, 2 * WIDTH)
+    first, second, third, fourth = [
+        jnp.transpose(f[:side].reshape(side, 2, WIDTH), (1, 0, 2)) for f in factors
+    ]
+    table = first[:, :, None, :] * second[:, None, :, :] + third[:, :, None, :] * fourth[:, None, :, :]
+    return table.reshape(2, side * side, WIDTH)
 
 
 def split_bf16(table):
@@ -54,7 +56,7 @@
     cos_x, sin_x = line_table(G, cell_count)
     from_cos = np.concatenate([cos_x, -sin_x], axis=0)
     from_sin = np.concatenate([-sin_x, -cos_x], axis=0)
-    return jnp.asarray(from_cos), jnp.asarray(from_sin)
+    return jnp.asarray(np.concatenate([from_cos, from_sin], axis=1))
 
 
 def mix_table(cell_count):
@@ -62,30 +64,32 @@
     return jnp.asarray(np.concatenate([cos_x, sin_x], axis=0))
 
 
-def x_transform(plane, cell_count, form):
-    from_cos, from_sin = mix_tables(cell_count)
-    first = jnp.einsum(form, from_cos, plane[..., :WIDTH], precision=HIGH)
-    return first + jnp.einsum(form, from_sin, plane[..., WIDTH:], precision=HIGH)
-
-
 def receptor_mixed(grids, table_hi, table_lo):
     terms, rows, cells = grids.shape
     receptors = rows // G
-    flat = grids.reshape(terms * rows, cells)
-    plane = jnp.dot(flat, table_hi, preferred_element_type=jnp.float32)
-    plane = plane + jnp.dot(flat, table_lo, preferred_element_type=jnp.float32)
-    plane = plane.reshape(terms, receptors, G, 2 * WIDTH)
-    return x_transform(plane, G, "px,trxq->trpq")
+    grids = grids.reshape(terms, receptors, G, cells)
+    form = "trxc,hcq->trhxq"
+    plane = jnp.einsum(form, grids, table_hi, preferred_element_type=jnp.float32)
+    plane = plane + jnp.einsum(form, grids, table_lo, preferred_element_type=jnp.float32)
+    plane = plane.reshape(terms, receptors, 2 * G, WIDTH)
+    return jnp.einsum("pk,trkq->trpq", mix_tables(G), plane, precision=HIGH)
 
 
 def ligand_spectra(voxels, coefficients, box_table):
     yz_index = voxels[1] * LB + voxels[2]
-    rows = jnp.take(box_table, yz_index, axis=0)
+    cells = jnp.arange(LB * LB, dtype=jnp.int32)
+    onehot = (yz_index[:, :, None] == cells[None, None, :]).astype(jnp.bfloat16)
     x_cells = jnp.arange(LB, dtype=jnp.int32)
     in_x = (voxels[0][:, None, :] == x_cells[None, :, None]).astype(jnp.float32)
     weights = coefficients[None, :, None, :] * in_x[:, None, :, :]
-    plane = jnp.einsum("ntxa,naq->tnxq", weights, rows, precision=HIGH)
-    return x_transform(plane, LB, "px,tnxq->tnpq")
+    upper, lower = split_bf16(weights)
+    form = "ntxa,nac->ntxc"
+    grid = jnp.einsum(form, upper, onehot, preferred_element_type=jnp.float32)
+    grid = grid + jnp.einsum(form, lower, onehot, preferred_element_type=jnp.float32)
+    plane = jnp.einsum("ntxc,hcq->nthxq", grid, box_table, precision=HIGH)
+    rot_count, terms = plane.shape[0], plane.shape[1]
+    plane = plane.reshape(rot_count, terms, 2 * LB, WIDTH)
+    return jnp.einsum("pk,ntkq->tnpq", mix_tables(LB), plane, precision=HIGH)
 
 
 def correlate(rec_spec, lig_spec):
@@ -107,9 +111,9 @@
     fold = np.where((freq_z == 0) | (freq_z == G // 2), 1.0, 2.0) / float(G**3)
     fold = np.where(column < G * HZ, fold, 0.0)
     fold = jnp.asarray(fold.astype(np.float32))
-    joined = jnp.concatenate([inv_re * fold, -inv_im * fold], axis=-1)
+    joined = jnp.stack([inv_re * fold, -inv_im * fold], axis=3)
     upper, lower = lax.optimization_barrier(split_bf16(joined))
-    form = "rnxq,cq->rnxc"
+    form = "rnxhq,hcq->rnxc"
     scores = jnp.einsum(form, upper, table_hi, preferred_element_type=jnp.float32)
     scores = scores + jnp.einsum(form, lower, table_hi, preferred_element_type=jnp.float32)
     return scores + jnp.einsum(form, upper, table_lo, preferred_element_type=jnp.float32)

time: 91.5 us -> 80.8 us (0.88)
  matrix products: 32.2 us -> 23.4 us
  local copies, waits for them, and re-layouts: 9.78 us -> 6.67 us
  starting transfers between devices: 14.5 us -> 16.6 us
    dot_general x7, matrix products: 28.4 us -> 19.6 us  [the longest x1 9.21 us: ligand_spectra(): return jnp.einsum('pk,ntkq->tnpq', mix_tables(LB), plane, precision=HIGH)]
    gather x1 -> x0, local copies, waits for them, and re-layouts: 5.97 us -> none  [ligand_spectra(): rows = jnp.take(box_table, yz_index, axis=0)]
    ppermute x7, starting transfers between devices: 5.95 us -> 8.04 us  [butterfly_max(): received.append(lax.ppermute(values, axes, pairs))]
    unnamed x35 -> x30, local copies, waits for them, and re-layouts: 0.23 us -> 1.88 us
    reshape x0 -> x1, local copies, waits for them, and re-layouts: none -> 1.65 us  [body(): gathered.reshape(term_count, inner_count, terms_here, rows_here, cells)]
    add x2 -> x3, other arithmetic: 2.07 us -> 3.25 us  [the longest x2 3.24 us: plane_table(): first[:, :, None, :] * second[:, None, :, :]]
    ppermute x7, waiting for transfers between devices: 9.34 us -> 8.25 us  [butterfly_max(): received.append(lax.ppermute(values, axes, pairs))]
  transfers between devices with their start and end apart: 12 -> 12, of which waited for: 5 -> 7; matrix products, arithmetic and copies ran while one was open for 39% -> 29% of each run, Pallas kernels for 0% -> 0%
where the time goes in v6:
time: 80.8 us; the launch traced here: 80.5 us
  matrix products  23.4 us (29%)
  starting transfers between devices  16.6 us (21%)
  between operations  14.4 us (18%)
  other arithmetic  10.9 us (13%)
  waiting for transfers between devices  8.46 us (10%)
  local copies, waits for them, and re-layouts  6.67 us (8%)
    dot_general x1, matrix products, ligand_spectra(): return jnp.einsum('pk,ntkq->tnpq', mix_tables(LB), plane, precision=HIGH)  9.21 us
    ppermute x4, starting transfers between devices, gather_by_permutes(): blocks.append(lax.ppermute(values, axis_name, pairs))  8.53 us
    ppermute x7, waiting for transfers between devices, butterfly_max(): received.append(lax.ppermute(values, axes, pairs))  8.25 us
    ppermute x7, starting transfers between devices, butterfly_max(): received.append(lax.ppermute(values, axes, pairs))  8.04 us
    dot_general x1, matrix products, ligand_spectra(): plane = jnp.einsum('ntxc,hcq->nthxq', grid, box_table, precision=HIGH)  3.28 us
    add x2, other arithmetic, plane_table(): first[:, :, None, :] * second[:, None, :, :]  3.24 us
    reduce_sum x1, other arithmetic, correlate(): prod_re = jnp.sum(lr * rr + li * ri, axis=0)  2.61 us
    convert_element_type x2, other arithmetic, split_bf16(): return (upper.astype(jnp.bfloat16), lower.astype(jnp.bfloat16))  2.4 us
  transfers between devices with their start and end apart: 12, of which 7 were waited for; matrix products, arithmetic and copies ran while one was open for 29% of the time, Pallas kernels for 0%

profile of v6, /device:TPU:0, one launch (start us, length us, event | category | flops | bytes accessed | tf_op | source)
XLA Modules:
  0.0 80.5 jit_solution(3642133828509884229)
XLA Ops:
  7.2 3.1 %collective-permute-start.1 = (s32[3,2,256]{2,1,0:T(2,128)}, s32[3,2,256]{2,1,0:T(2,128)S(1)}, u32[]{:S(2)}, u32[]{:S(2)}) collective-permute-start(s32[3,2,256]{2,1,0:T(2,128)} %param.15), channel_id=1, source_target_pairs={{0,8},{8,16},{16,24},{24,0},{1,9},{9,17},{17,25},{25,1},{2,10},{10... | collective-permute-start | bytes 18440 | tf_op jit(solution)/shard_map/ppermute | solution.py:126
  10.3 2.6 %collective-permute-start.2 = (s32[3,2,256]{2,1,0:T(2,128)}, s32[3,2,256]{2,1,0:T(2,128)S(1)}, u32[]{:S(2)}, u32[]{:S(2)}) collective-permute-start(s32[3,2,256]{2,1,0:T(2,128)} %param.15), channel_id=1, source_target_pairs={{0,16},{8,24},{16,0},{24,8},{1,17},{9,25},{17,1},{25,9},{2,18},{10... | collective-permute-start | bytes 18440 | tf_op jit(solution)/shard_map/ppermute | solution.py:126
  12.9 1.3 %collective-permute-start.3 = (s32[3,2,256]{2,1,0:T(2,128)}, s32[3,2,256]{2,1,0:T(2,128)S(1)}, u32[]{:S(2)}, u32[]{:S(2)}) collective-permute-start(s32[3,2,256]{2,1,0:T(2,128)} %param.15), channel_id=1, source_target_pairs={{0,24},{8,0},{16,8},{24,16},{1,25},{9,1},{17,9},{25,17},{2,26},{10... | collective-permute-start | bytes 18440 | tf_op jit(solution)/shard_map/ppermute | solution.py:126
  14.2 0.8 broadcast_multiply_fusion
  15.0 1.5 %collective-permute-start = (f32[11,256]{1,0:T(8,128)S(1)}, f32[11,256]{1,0:T(8,128)S(1)}, u32[]{:S(2)}, u32[]{:S(2)}) collective-permute-start(f32[11,256]{1,0:T(8,128)S(1)} %broadcast_multiply_fusion), channel_id=1, source_target_pairs={{0,1},{1,0},{2,3},{3,2},{4,5},{5,4},{6,7},{7,6},{8,9},{9,8},{10,11... | collective-permute-start | bytes 33800 | tf_op jit(solution)/shard_map/ppermute | solution.py:126
  16.6 0.8 fusion.83
  17.4 2.0 %multiply_add_fusion = f32[2,32,32,640]{3,2,1,0:T(8,128)S(1)} fusion(f32[2,32,640]{2,1,0:T(8,128)} %constant.131, f32[2,32,640]{2,1,0:T(8,128)} %constant.129, f32[2,32,640]{2,1,0:T(8,128)} %constant.127, f32[2,32,640]{2,1,0:T(8,128)} %constant.125), kind=kLoop, calls=%fused_computation.7 | loop fusion | flops 3932160 | bytes 5898240 | tf_op jit(solution)/shard_map/twiddle_tables/add | solution.py:45
  19.5 2.3 %fusion = (bf16[2,1024,640]{2,1,0:T(8,128)(2,1)}, bf16[2,1024,640]{2,1,0:T(8,128)(2,1)S(1)}) fusion(f32[2,32,32,640]{3,2,1,0:T(8,128)S(1)} %multiply_add_fusion), kind=kLoop, calls=%fused_computation.6 | loop fusion | flops 5242880 | bytes 10485760 | tf_op jit(solution)/shard_map/twiddle_tables/convert_element_type | solution.py:52
  21.8 1.2 %multiply_add_fusion.1 = f32[2,16,16,640]{3,2,1,0:T(8,128)} fusion(f32[2,16,640]{2,1,0:T(8,128)S(1)} %copy-done.5, f32[2,16,640]{2,1,0:T(8,128)S(1)} %copy-done.4, f32[2,16,640]{2,1,0:T(8,128)S(1)} %copy-done.3, f32[2,16,640]{2,1,0:T(8,128)S(1)} %copy-done.2), kind=kLoop, calls=%fused_computation.29 | loop fusion | flops 983040 | bytes 1638400 | tf_op jit(solution)/shard_map/twiddle_tables/add | solution.py:45
  25.3 3.3 %convolution_bitcast_fusion.1 = f32[4,22,2,16,640]{4,1,3,0,2:T(8,128)S(1)} fusion(f32[4,22,16,256]{3,1,2,0:T(8,128)S(1)} %fusion.38, f32[4,22,16,256]{3,1,2,0:T(8,128)S(1)} %fusion.36, f32[2,256,640]{2,1,0:T(8,128)S(1)} %bitcast.151), kind=kOutput, calls=%fused_computation.9 | convolution fusion | flops 2768601088 | bytes 11403264 | tf_op jit(solution)/shard_map/ligand_spectra/ntxc,hcq->nthxq/dot_general | solution.py:89
  28.6 1.3 %copy.28 = f32[4,22,2,16,640]{4,3,2,1,0:T(8,128)S(1)} copy(f32[4,22,2,16,640]{4,1,3,0,2:T(8,128)S(1)} %convolution_bitcast_fusion.1) | data formatting | bytes 14417920 | tf_op jit(solution)/shard_map/ligand_spectra/ntxc,hcq->nthxq/transpose | solution.py:89
  29.9 9.2 %convolution_bitcast_fusion = f32[22,4,64,640]{3,2,0,1:T(8,128)} fusion(f32[4,22,32,640]{3,2,1,0:T(8,128)S(1)} %bitcast.144, f32[64,32,1,1]{0,1,3,2:T(8,128)S(1)} %copy-done.8), kind=kOutput, calls=%fused_computation.1 | convolution fusion | flops 692060160 | bytes 21635072 | tf_op jit(solution)/shard_map/ligand_spectra/pk,ntkq->tnpq/dot_general | solution.py:92
  39.2 1.6 %copy.29 = bf16[2,4,11,8,1024]{4,3,1,2,0:T(8,128)(2,1)S(1)} copy(bf16[2,4,11,8,1024]{4,3,2,1,0:T(8,128)(2,1)} %bitcast.148) | data formatting | bytes 2883584 | tf_op jit(solution)/shard_map/reshape | solution.py:155
  41.4 2.2 %fusion.3 = f32[2,640,22,32]{1,3,2,0:T(8,128)S(1)} fusion(bf16[22,32,1024,1]{2,1,0,3:T(8,128)(2,1)S(1)} %bitcast.149, bf16[2,1024,640]{2,1,0:T(8,128)(2,1)S(1)} %copy-done), kind=kOutput, calls=%fused_computation.12 | convolution fusion | flops 1845493760 | bytes 7667712 | tf_op jit(solution)/shard_map/receptor_spectra/trxc,hcq->trhxq/dot_general | solution.py:73
  43.6 2.2 %add_bitcast_fusion = f32[22,1,2,32,640]{4,3,0,2,1:T(8,128)S(1)} fusion(f32[2,640,22,32]{1,3,2,0:T(8,128)S(1)} %fusion.3, bf16[22,32,1024,1]{2,1,0,3:T(8,128)(2,1)S(1)} %bitcast.150, bf16[2,1024,640]{2,1,0:T(8,128)(2,1)S(1)} %get-tuple-element.8), kind=kOutput, calls=%fused_computation.8 | convolution fusion | flops 1846394880 | bytes 11272192 | tf_op jit(solution)/shard_map/receptor_spectra/trxc,hcq->trhxq/dot_general | solution.py:72
  46.2 1.2 %copy-done.6 = f32[64,64,1]{1,0,2:T(8,128)S(1)} copy-done((f32[64,64,1]{1,0,2:T(8,128)S(1)}, f32[64,64,1]{1,0,2:T(8,128)}, u32[]{:S(2)}) %copy-start.6) | copy-done | bytes 16408
  47.4 1.6 %convolution_bitcast_fusion.2 = f32[22,1,64,640]{3,2,0,1:T(8,128)S(1)} fusion(f32[22,64,640]{2,1,0:T(8,128)S(1)} %bitcast.145, f32[64,64,1]{1,0,2:T(8,128)S(1)} %copy-done.6), kind=kOutput, calls=%fused_computation.22 | convolution fusion | flops 346030080 | bytes 7225344 | tf_op jit(solution)/shard_map/receptor_spectra/pk,trkq->trpq/dot_general | solution.py:75
  49.4 2.6 %add_reduce_fusion = (f32[4,32,640]{2,1,0:T(8,128)S(1)}, f32[4,32,640]{2,1,0:T(8,128)S(1)}) fusion(f32[22,4,64,640]{3,2,0,1:T(8,128)S(1)} %bitcast.143, f32[22,32,640]{2,1,0:T(8,128)S(1)} %get-tuple-element.19, f32[22,32,640]{2,1,0:T(8,128)S(1)} %get-tuple-element.18), kind=kLoop, calls=%fused_computation.5 | loop fusion | flops 14254080 | bytes 18677760 | tf_op jit(solution)/shard_map/correlate/reduce_sum | solution.py:100
  52.0 0.7 fusion.46
  52.9 1.0 %fusion.17 = f32[4,32,1024]{2,1,0:T(8,128)S(1)} fusion(bf16[2,1024,640]{2,1,0:T(8,128)(2,1)S(1)} %get-tuple-element.8, bf16[1,4,32,2,640]{4,2,1,3,0:T(8,128)(2,1)S(1)} %get-tuple-element.10), kind=kOutput, calls=%fused_computation.30 | convolution fusion | flops 335544320 | bytes 3473408 | tf_op jit(solution)/shard_map/inverse_scores/rnxhq,hcq->rnxc/dot_general | solution.py:117
  53.9 1.0 %fusion.29 = f32[4,32,1024]{2,1,0:T(8,128)S(1)} fusion(f32[4,32,1024]{2,1,0:T(8,128)S(1)} %fusion.17, bf16[2,1024,640]{2,1,0:T(8,128)(2,1)S(1)} %get-tuple-element.8, bf16[1,4,32,2,640]{4,2,1,3,0:T(8,128)(2,1)S(1)} %get-tuple-element.11), kind=kOutput, calls=%fused_computation.34 | convolution fusion | flops 335675392 | bytes 3997696 | tf_op jit(solution)/shard_map/inverse_scores/rnxhq,hcq->rnxc/dot_general | solution.py:118
  54.9 1.1 %fusion.32 = f32[4]{0:T(128)S(1)} fusion(f32[4,32,1024]{2,1,0:T(8,128)S(1)} %fusion.29, bf16[2,1024,640]{2,1,0:T(8,128)(2,1)S(1)} %copy-done, bf16[1,4,32,2,640]{4,2,1,3,0:T(8,128)(2,1)S(1)} %get-tuple-element.10), kind=kOutput, calls=%fused_computation.35 | convolution fusion | flops 335806464 | bytes 3473424 | tf_op jit(solution)/shard_map/inverse_scores/rnxhq,hcq->rnxc/dot_general | solution.py:119
  56.2 1.4 %collective-permute-start.4 = (f32[4,32]{0,1:T(8,128)S(1)}, f32[4,32]{0,1:T(8,128)S(1)}, u32[]{:S(2)}, u32[]{:S(2)}) collective-permute-start(f32[4,32]{0,1:T(8,128)S(1)} %broadcast_select_fusion.1), channel_id=1, source_target_pairs={{0,1},{1,0},{2,3},{3,2},{4,5},{5,4},{6,7},{7,6},{8,9},{9,8},{10,11... | collective-permute-start | bytes 1544 | tf_op jit(solution)/shard_map/ppermute | solution.py:137
  58.3 1.6 %collective-permute-done.4 = f32[4,32]{0,1:T(8,128)S(1)} collective-permute-done((f32[4,32]{0,1:T(8,128)S(1)}, f32[4,32]{0,1:T(8,128)S(1)}, u32[]{:S(2)}, u32[]{:S(2)}) %collective-permute-start.4) | collective-permute-done | bytes 544 | tf_op jit(solution)/shard_map/ppermute | solution.py:137
  59.9 0.9 %collective-permute-done.6 = f32[4,32]{0,1:T(8,128)S(1)} collective-permute-done((f32[4,32]{0,1:T(8,128)S(1)}, f32[4,32]{0,1:T(8,128)S(1)}, u32[]{:S(2)}, u32[]{:S(2)}) %collective-permute-start.6) | collective-permute-done | bytes 544 | tf_op jit(solution)/shard_map/ppermute | solution.py:137
  60.8 0.8 collective-permute-start.7
  61.6 1.5 %collective-permute-start.8 = (f32[4,32]{0,1:T(8,128)S(1)}, f32[4,32]{0,1:T(8,128)S(1)}, u32[]{:S(2)}, u32[]{:S(2)}) collective-permute-start(f32[4,32]{0,1:T(8,128)S(1)} %maximum_maximum_fusion.1), channel_id=1, source_target_pairs={{0,8},{1,9},{2,10},{3,11},{4,12},{5,13},{6,14},{7,15},{8,0},{9,1},... | collective-permute-start | bytes 1544 | tf_op jit(solution)/shard_map/ppermute | solution.py:137
  63.1 1.2 %collective-permute-start.9 = (f32[4,32]{0,1:T(8,128)S(1)}, f32[4,32]{0,1:T(8,128)S(1)}, u32[]{:S(2)}, u32[]{:S(2)}) collective-permute-start(f32[4,32]{0,1:T(8,128)S(1)} %maximum_maximum_fusion.1), channel_id=1, source_target_pairs={{0,12},{1,13},{2,14},{3,15},{4,8},{5,9},{6,10},{7,11},{8,4},{9,5},... | collective-permute-start | bytes 1544 | tf_op jit(solution)/shard_map/ppermute | solution.py:137
  64.6 0.8 collective-permute-done.8
  65.3 2.4 %collective-permute-done.9 = f32[4,32]{0,1:T(8,128)S(1)} collective-permute-done((f32[4,32]{0,1:T(8,128)S(1)}, f32[4,32]{0,1:T(8,128)S(1)}, u32[]{:S(2)}, u32[]{:S(2)}) %collective-permute-start.9) | collective-permute-done | bytes 544 | tf_op jit(solution)/shard_map/ppermute | solution.py:137
  67.8 2.4 %collective-permute-start.10 = (f32[4,32]{0,1:T(8,128)S(1)}, f32[4,32]{0,1:T(8,128)S(1)}, u32[]{:S(2)}, u32[]{:S(2)}) collective-permute-start(f32[4,32]{0,1:T(8,128)S(1)} %maximum_maximum_fusion), channel_id=1, source_target_pairs={{0,16},{1,17},{2,18},{3,19},{4,20},{5,21},{6,22},{7,23},{8,24},{9,... | collective-permute-start | bytes 1544 | tf_op jit(solution)/shard_map/ppermute | solution.py:137
  70.2 2.4 %collective-permute-done.10 = f32[4,32]{0,1:T(8,128)S(1)} collective-permute-done((f32[4,32]{0,1:T(8,128)S(1)}, f32[4,32]{0,1:T(8,128)S(1)}, u32[]{:S(2)}, u32[]{:S(2)}) %collective-permute-start.10) | collective-permute-done | bytes 544 | tf_op jit(solution)/shard_map/ppermute | solution.py:137
  (67 shorter events, 6.1 us)
Async XLA Ops:
  7.2 32.1 %all-gather.3.cloned.1.call-start = ((), (), s32[]{:S(2)}) async-start(), calls=%async_computation | async-start | bytes 1622016 | tf_op jit(solution)/shard_map/all_gather | solution.py:154
  7.2 16.0 %collective-permute-start.1 = (s32[3,2,256]{2,1,0:T(2,128)}, s32[3,2,256]{2,1,0:T(2,128)S(1)}, u32[]{:S(2)}, u32[]{:S(2)}) collective-permute-start(s32[3,2,256]{2,1,0:T(2,128)} %param.15), channel_id=1, source_target_pairs={{0,8},{8,16},{16,24},{24,0},{1,9},{9,17},{17,25},{25,1},{2,10},{10... | collective-permute-start | bytes 18440 | tf_op jit(solution)/shard_map/ppermute | solution.py:126
  10.3 13.0 %collective-permute-start.2 = (s32[3,2,256]{2,1,0:T(2,128)}, s32[3,2,256]{2,1,0:T(2,128)S(1)}, u32[]{:S(2)}, u32[]{:S(2)}) collective-permute-start(s32[3,2,256]{2,1,0:T(2,128)} %param.15), channel_id=1, source_target_pairs={{0,16},{8,24},{16,0},{24,8},{1,17},{9,25},{17,1},{25,9},{2,18},{10... | collective-permute-start | bytes 18440 | tf_op jit(solution)/shard_map/ppermute | solution.py:126
  12.9 10.4 %collective-permute-start.3 = (s32[3,2,256]{2,1,0:T(2,128)}, s32[3,2,256]{2,1,0:T(2,128)S(1)}, u32[]{:S(2)}, u32[]{:S(2)}) collective-permute-start(s32[3,2,256]{2,1,0:T(2,128)} %param.15), channel_id=1, source_target_pairs={{0,24},{8,0},{16,8},{24,16},{1,25},{9,1},{17,9},{25,17},{2,26},{10... | collective-permute-start | bytes 18440 | tf_op jit(solution)/shard_map/ppermute | solution.py:126
  15.0 8.3 %collective-permute-start = (f32[11,256]{1,0:T(8,128)S(1)}, f32[11,256]{1,0:T(8,128)S(1)}, u32[]{:S(2)}, u32[]{:S(2)}) collective-permute-start(f32[11,256]{1,0:T(8,128)S(1)} %broadcast_multiply_fusion), channel_id=1, source_target_pairs={{0,1},{1,0},{2,3},{3,2},{4,5},{5,4},{6,7},{7,6},{8,9},{9,8},{10,11... | collective-permute-start | bytes 33800 | tf_op jit(solution)/shard_map/ppermute | solution.py:126
  19.4 2.4 %copy-start.2 = (f32[2,16,640]{2,1,0:T(8,128)S(1)}, f32[2,16,640]{2,1,0:T(8,128)}, u32[]{:S(2)}) copy-start(f32[2,16,640]{2,1,0:T(8,128)} %constant.114) | copy-start | bytes 245764
  19.4 2.4 %copy-start.3 = (f32[2,16,640]{2,1,0:T(8,128)S(1)}, f32[2,16,640]{2,1,0:T(8,128)}, u32[]{:S(2)}) copy-start(f32[2,16,640]{2,1,0:T(8,128)} %constant.117) | copy-start | bytes 245764
  19.5 2.4 %copy-start.4 = (f32[2,16,640]{2,1,0:T(8,128)S(1)}, f32[2,16,640]{2,1,0:T(8,128)}, u32[]{:S(2)}) copy-start(f32[2,16,640]{2,1,0:T(8,128)} %constant.120) | copy-start | bytes 245764
  19.5 2.4 %copy-start.5 = (f32[2,16,640]{2,1,0:T(8,128)S(1)}, f32[2,16,640]{2,1,0:T(8,128)}, u32[]{:S(2)}) copy-start(f32[2,16,640]{2,1,0:T(8,128)} %constant.123) | copy-start | bytes 245764
  19.5 3.8 %copy-start.9 = (s32[3,2,256]{2,1,0:T(2,128)S(1)}, s32[3,2,256]{2,1,0:T(2,128)}, u32[]{:S(2)}) copy-start(s32[3,2,256]{2,1,0:T(2,128)} %param.15) | copy-start | bytes 18436
  24.0 1.3 %copy-start.1 = (f32[2,16,16,640]{3,2,1,0:T(8,128)S(1)}, f32[2,16,16,640]{3,2,1,0:T(8,128)}, u32[]{:S(2)}) copy-start(f32[2,16,16,640]{3,2,1,0:T(8,128)} %multiply_add_fusion.1) | copy-start | bytes 3932164
  28.6 1.3 %copy-start.8 = (f32[64,32,1,1]{0,1,3,2:T(8,128)S(1)}, f32[64,32,1,1]{0,1,3,2:T(8,128)}, u32[]{:S(2)}) copy-start(f32[64,32,1,1]{0,1,3,2:T(8,128)} %constant.132) | copy-start | bytes 24580
  39.2 2.2 %copy-start = (bf16[2,1024,640]{2,1,0:T(8,128)(2,1)S(1)}, bf16[2,1024,640]{2,1,0:T(8,128)(2,1)}, u32[]{:S(2)}) copy-start(bf16[2,1024,640]{2,1,0:T(8,128)(2,1)} %get-tuple-element.9) | copy-start | bytes 7864324
  43.6 5.7 %slice-start = ((s8[14417920]{0:T(1024)(128)(4,1)}), s8[4194304]{0:T(1024)(128)(4,1)S(1)}, s32[]{:S(2)}) async-start(s8[14417920]{0:T(1024)(128)(4,1)} %bitcast.142), calls=%async_computation.1 | async-start | bytes 8388608
  43.6 5.7 %slice-start.1 = ((s8[14417920]{0:T(1024)(128)(4,1)}), s8[4194304]{0:T(1024)(128)(4,1)S(1)}, s32[]{:S(2)}) async-start(s8[14417920]{0:T(1024)(128)(4,1)} %bitcast.142), calls=%async_computation.2 | async-start | bytes 8388608
  43.6 5.7 %slice-start.2 = ((s8[14417920]{0:T(1024)(128)(4,1)}), s8[4194304]{0:T(1024)(128)(4,1)S(1)}, s32[]{:S(2)}) async-start(s8[14417920]{0:T(1024)(128)(4,1)} %bitcast.142), calls=%async_computation.3 | async-start | bytes 8388608
  45.8 1.5 %copy-start.6 = (f32[64,64,1]{1,0,2:T(8,128)S(1)}, f32[64,64,1]{1,0,2:T(8,128)}, u32[]{:S(2)}) copy-start(f32[64,64,1]{1,0,2:T(8,128)} %constant.133) | copy-start | bytes 49156
  47.4 1.9 %slice-start.3 = ((s8[14417920]{0:T(1024)(128)(4,1)}), s8[1835008]{0:T(1024)(128)(4,1)S(1)}, s32[]{:S(2)}) async-start(s8[14417920]{0:T(1024)(128)(4,1)} %bitcast.142), calls=%async_computation.4 | async-start | bytes 3670016
  49.3 2.6 %copy-start.7 = (f32[64,32,1,1]{0,1,3,2:T(8,128)S(1)}, f32[64,32,1,1]{0,1,3,2:T(8,128)}, u32[]{:S(2)}) copy-start(f32[64,32,1,1]{0,1,3,2:T(8,128)} %constant.134) | copy-start | bytes 24580
  49.4 3.4 %copy-start.10 = (f32[640]{0:T(1024)S(1)}, f32[640]{0:T(1024)}, u32[]{:S(2)}) copy-start(f32[640]{0:T(1024)} %constant.107.clone) | copy-start | bytes 7684
  56.2 3.7 %collective-permute-start.4 = (f32[4,32]{0,1:T(8,128)S(1)}, f32[4,32]{0,1:T(8,128)S(1)}, u32[]{:S(2)}, u32[]{:S(2)}) collective-permute-start(f32[4,32]{0,1:T(8,128)S(1)} %broadcast_select_fusion.1), channel_id=1, source_target_pairs={{0,1},{1,0},{2,3},{3,2},{4,5},{5,4},{6,7},{7,6},{8,9},{9,8},{10,11... | collective-permute-start | bytes 1544 | tf_op jit(solution)/shard_map/ppermute | solution.py:137
  57.6 2.3 %collective-permute-start.5 = (f32[4,32]{0,1:T(8,128)S(1)}, f32[4,32]{0,1:T(8,128)S(1)}, u32[]{:S(2)}, u32[]{:S(2)}) collective-permute-start(f32[4,32]{0,1:T(8,128)S(1)} %broadcast_select_fusion.1), channel_id=1, source_target_pairs={{0,2},{1,3},{2,0},{3,1},{4,6},{5,7},{6,4},{7,5},{8,10},{9,11},{10,... | collective-permute-start | bytes 1544 | tf_op jit(solution)/shard_map/ppermute | solution.py:137
  57.6 3.2 %collective-permute-start.6 = (f32[4,32]{0,1:T(8,128)S(1)}, f32[4,32]{0,1:T(8,128)S(1)}, u32[]{:S(2)}, u32[]{:S(2)}) collective-permute-start(f32[4,32]{0,1:T(8,128)S(1)} %broadcast_select_fusion.1), channel_id=1, source_target_pairs={{0,3},{1,2},{2,1},{3,0},{4,7},{5,6},{6,5},{7,4},{8,11},{9,10},{10,... | collective-permute-start | bytes 1544 | tf_op jit(solution)/shard_map/ppermute | solution.py:137
  60.8 3.7 %collective-permute-start.7 = (f32[4,32]{0,1:T(8,128)S(1)}, f32[4,32]{0,1:T(8,128)S(1)}, u32[]{:S(2)}, u32[]{:S(2)}) collective-permute-start(f32[4,32]{0,1:T(8,128)S(1)} %maximum_maximum_fusion.1), channel_id=1, source_target_pairs={{0,4},{1,5},{2,6},{3,7},{4,0},{5,1},{6,2},{7,3},{8,12},{9,13},{10,... | collective-permute-start | bytes 1544 | tf_op jit(solution)/shard_map/ppermute | solution.py:137
  61.6 3.7 %collective-permute-start.8 = (f32[4,32]{0,1:T(8,128)S(1)}, f32[4,32]{0,1:T(8,128)S(1)}, u32[]{:S(2)}, u32[]{:S(2)}) collective-permute-start(f32[4,32]{0,1:T(8,128)S(1)} %maximum_maximum_fusion.1), channel_id=1, source_target_pairs={{0,8},{1,9},{2,10},{3,11},{4,12},{5,13},{6,14},{7,15},{8,0},{9,1},... | collective-permute-start | bytes 1544 | tf_op jit(solution)/shard_map/ppermute | solution.py:137
  63.1 4.6 %collective-permute-start.9 = (f32[4,32]{0,1:T(8,128)S(1)}, f32[4,32]{0,1:T(8,128)S(1)}, u32[]{:S(2)}, u32[]{:S(2)}) collective-permute-start(f32[4,32]{0,1:T(8,128)S(1)} %maximum_maximum_fusion.1), channel_id=1, source_target_pairs={{0,12},{1,13},{2,14},{3,15},{4,8},{5,9},{6,10},{7,11},{8,4},{9,5},... | collective-permute-start | bytes 1544 | tf_op jit(solution)/shard_map/ppermute | solution.py:137
  67.8 4.8 %collective-permute-start.10 = (f32[4,32]{0,1:T(8,128)S(1)}, f32[4,32]{0,1:T(8,128)S(1)}, u32[]{:S(2)}, u32[]{:S(2)}) collective-permute-start(f32[4,32]{0,1:T(8,128)S(1)} %maximum_maximum_fusion), channel_id=1, source_target_pairs={{0,16},{1,17},{2,18},{3,19},{4,20},{5,21},{6,22},{7,23},{8,24},{9,... | collective-permute-start | bytes 1544 | tf_op jit(solution)/shard_map/ppermute | solution.py:137
Sparse Core Ops, SparseCore 0:
  16.7 22.5 all-gather.2

commit v7 on v6

--- a/solution.py
+++ b/solution.py
@@ -151,9 +151,18 @@
         plane = lax.axis_index("plane")
         inner = lax.axis_index("inner")
         term = lax.axis_index("term")
-        gathered = lax.all_gather(receptor_grids, ("term", "inner"), axis=0, tiled=False)
-        gathered = gathered.reshape(term_count, inner_count, terms_here, rows_here, cells)
-        gathered = jnp.transpose(gathered, (0, 2, 1, 3, 4))
+        group = inner_count * term_count
+        if group <= 8:
+            here = inner * term_count + term
+            blocks = jnp.stack(gather_by_permutes(receptor_grids, ("inner", "term"), group, here))
+            order = (here - jnp.arange(group, dtype=jnp.int32)) % group
+            gathered = jnp.take(blocks, order, axis=0)
+            gathered = gathered.reshape(inner_count, term_count, terms_here, rows_here, cells)
+            gathered = jnp.transpose(gathered, (1, 2, 0, 3, 4))
+        else:
+            gathered = lax.all_gather(receptor_grids, ("term", "inner"), axis=0, tiled=False)
+            gathered = gathered.reshape(term_count, inner_count, terms_here, rows_here, cells)
+            gathered = jnp.transpose(gathered, (0, 2, 1, 3, 4))
         gathered = gathered.reshape(term_count * terms_here, inner_count * rows_here, cells)
         cell_blocks = gather_by_permutes(ligand_cells, "plane", plane_count, plane)
         cells_here = jnp.concatenate(cell_blocks, axis=1)

time: 80.8 us -> 95.5 us (1.18)
  between operations: 14.4 us -> 1.04 us
  local copies, waits for them, and re-layouts: 6.67 us -> 18.9 us
  waiting for transfers between devices: 8.46 us -> 14.4 us
  other arithmetic: 10.9 us -> 15.8 us
  starting transfers between devices: 16.6 us -> 20.9 us
    unnamed x30 -> x45, local copies, waits for them, and re-layouts: 1.88 us -> 10.9 us
    ppermute x4 -> x11, starting transfers between devices: 8.53 us -> 15 us  [gather_by_permutes(): blocks.append(lax.ppermute(values, axis_name, pairs))]
    ppermute x4 -> x11, waiting for transfers between devices: 0.01 us -> 4.84 us  [gather_by_permutes(): blocks.append(lax.ppermute(values, axis_name, pairs))]
    gather x0 -> x1, local copies, waits for them, and re-layouts: none -> 3.25 us  [body(): gathered = jnp.take(blocks, order, axis=0)]
    ppermute x7, starting transfers between devices: 8.04 us -> 5.99 us  [butterfly_max(): received.append(lax.ppermute(values, axes, pairs))]
    reshape x1 -> x0, local copies, waits for them, and re-layouts: 1.65 us -> none  [body(): gathered.reshape(term_count, inner_count, terms_here, rows_here, cells)]
    transpose x0 -> x1, other arithmetic: none -> 1.56 us  [body(): gathered = jnp.transpose(gathered, (1, 2, 0, 3, 4))]
    ppermute x7, waiting for transfers between devices: 8.25 us -> 9.57 us  [butterfly_max(): received.append(lax.ppermute(values, axes, pairs))]
  transfers between devices with their start and end apart: 12 -> 18, of which waited for: 7 -> 7; matrix products, arithmetic and copies ran while one was open for 29% -> 37% of each run, Pallas kernels for 0% -> 0%
where the time goes in v7:
time: 95.5 us; the launch traced here: 95 us
  matrix products  23.9 us (25%)
  starting transfers between devices  20.9 us (22%)
  local copies, waits for them, and re-layouts  18.9 us (20%)
  other arithmetic  15.8 us (17%)
  waiting for transfers between devices  14.4 us (15%)
  between operations  1.04 us (1%)
    ppermute x11, starting transfers between devices, gather_by_permutes(): blocks.append(lax.ppermute(values, axis_name, pairs))  15 us
    unnamed x45, local copies, waits for them, and re-layouts  10.9 us
    ppermute x7, waiting for transfers between devices, butterfly_max(): received.append(lax.ppermute(values, axes, pairs))  9.57 us
    dot_general x1, matrix products, ligand_spectra(): return jnp.einsum('pk,ntkq->tnpq', mix_tables(LB), plane, precision=HIGH)  9.04 us
    ppermute x7, starting transfers between devices, butterfly_max(): received.append(lax.ppermute(values, axes, pairs))  5.99 us
    ppermute x11, waiting for transfers between devices, gather_by_permutes(): blocks.append(lax.ppermute(values, axis_name, pairs))  4.84 us
    dot_general x1, matrix products, ligand_spectra(): plane = jnp.einsum('ntxc,hcq->nthxq', grid, box_table, precision=HIGH)  3.3 us
    add x2, other arithmetic, plane_table(): first[:, :, None, :] * second[:, None, :, :]  3.25 us
  transfers between devices with their start and end apart: 18, of which 7 were waited for; matrix products, arithmetic and copies ran while one was open for 37% of the time, Pallas kernels for 0%

profile of v7, /device:TPU:0, one launch (start us, length us, event | category | flops | bytes accessed | tf_op | source)
XLA Modules:
  0.0 95.0 jit_solution(13200101477656414830)
XLA Ops:
  0.6 3.1 %collective-permute-start.1 = (s32[3,2,256]{2,1,0:T(2,128)}, s32[3,2,256]{2,1,0:T(2,128)S(1)}, u32[]{:S(2)}, u32[]{:S(2)}) collective-permute-start(s32[3,2,256]{2,1,0:T(2,128)} %param.15), channel_id=1, source_target_pairs={{0,8},{8,16},{16,24},{24,0},{1,9},{9,17},{17,25},{25,1},{2,10},{10... | collective-permute-start | bytes 18440 | tf_op jit(solution)/shard_map/ppermute | solution.py:126
  3.7 2.6 %collective-permute-start.2 = (s32[3,2,256]{2,1,0:T(2,128)}, s32[3,2,256]{2,1,0:T(2,128)S(1)}, u32[]{:S(2)}, u32[]{:S(2)}) collective-permute-start(s32[3,2,256]{2,1,0:T(2,128)} %param.15), channel_id=1, source_target_pairs={{0,16},{8,24},{16,0},{24,8},{1,17},{9,25},{17,1},{25,9},{2,18},{10... | collective-permute-start | bytes 18440 | tf_op jit(solution)/shard_map/ppermute | solution.py:126
  6.3 1.3 %collective-permute-start.3 = (s32[3,2,256]{2,1,0:T(2,128)}, s32[3,2,256]{2,1,0:T(2,128)S(1)}, u32[]{:S(2)}, u32[]{:S(2)}) collective-permute-start(s32[3,2,256]{2,1,0:T(2,128)} %param.15), channel_id=1, source_target_pairs={{0,24},{8,0},{16,8},{24,16},{1,25},{9,1},{17,9},{25,17},{2,26},{10... | collective-permute-start | bytes 18440 | tf_op jit(solution)/shard_map/ppermute | solution.py:126
  7.6 1.5 %collective-permute-start.4 = (bf16[11,8,1024]{2,1,0:T(8,128)(2,1)}, bf16[11,8,1024]{2,1,0:T(8,128)(2,1)S(1)}, u32[]{:S(2)}, u32[]{:S(2)}) collective-permute-start(bf16[11,8,1024]{2,1,0:T(8,128)(2,1)} %param.12), channel_id=1, source_target_pairs={{0,1},{1,2},{2,3},{3,4},{4,5},{5,6},{6,7},{7,0},{8,9},{9,10},{10,1... | collective-permute-start | bytes 540680 | tf_op jit(solution)/shard_map/ppermute | solution.py:126
  11.3 1.6 %bitcast_dynamic-update-slice_fusion.7 = bf16[8,11,8,1024]{3,2,1,0:T(8,128)(2,1)} fusion(bf16[11,8,1024]{2,1,0:T(8,128)(2,1)} %param.12), kind=kLoop, calls=%fused_computation.73 | loop fusion | bytes 360448
  14.6 2.0 %multiply_add_fusion = f32[2,32,32,640]{3,2,1,0:T(8,128)S(1)} fusion(f32[2,32,640]{2,1,0:T(8,128)} %constant.159, f32[2,32,640]{2,1,0:T(8,128)} %constant.157, f32[2,32,640]{2,1,0:T(8,128)} %constant.155, f32[2,32,640]{2,1,0:T(8,128)} %constant.153), kind=kLoop, calls=%fused_computation.8 | loop fusion | flops 3932160 | bytes 5898240 | tf_op jit(solution)/shard_map/twiddle_tables/add | solution.py:45
  16.7 2.3 %fusion = (bf16[2,1024,640]{2,1,0:T(8,128)(2,1)}, bf16[2,1024,640]{2,1,0:T(8,128)(2,1)S(1)}) fusion(f32[2,32,32,640]{3,2,1,0:T(8,128)S(1)} %multiply_add_fusion), kind=kLoop, calls=%fused_computation.7 | loop fusion | flops 5242880 | bytes 10485760 | tf_op jit(solution)/shard_map/twiddle_tables/convert_element_type | solution.py:52
  20.2 1.2 %multiply_add_fusion.1 = f32[2,16,16,640]{3,2,1,0:T(8,128)} fusion(f32[2,16,640]{2,1,0:T(8,128)S(1)} %copy-done.6, f32[2,16,640]{2,1,0:T(8,128)S(1)} %copy-done.5, f32[2,16,640]{2,1,0:T(8,128)S(1)} %copy-done.4, f32[2,16,640]{2,1,0:T(8,128)S(1)} %copy-done.3), kind=kLoop, calls=%fused_computation.31 | loop fusion | flops 983040 | bytes 1638400 | tf_op jit(solution)/shard_map/twiddle_tables/add | solution.py:45
  22.2 1.2 %collective-permute-start.6 = (bf16[11,8,1024]{2,1,0:T(8,128)(2,1)S(1)}, bf16[11,8,1024]{2,1,0:T(8,128)(2,1)S(1)}, u32[]{:S(2)}, u32[]{:S(2)}) collective-permute-start(bf16[11,8,1024]{2,1,0:T(8,128)(2,1)S(1)} %copy-done.2), channel_id=1, source_target_pairs={{0,3},{1,4},{2,5},{3,6},{4,7},{5,0},{6,1},{7,2},{8,11},{9,12},{10,... | collective-permute-start | bytes 540680 | tf_op jit(solution)/shard_map/ppermute | solution.py:126
  24.0 1.7 %collective-permute-start = (f32[11,256]{1,0:T(8,128)S(1)}, f32[11,256]{1,0:T(8,128)S(1)}, u32[]{:S(2)}, u32[]{:S(2)}) collective-permute-start(f32[11,256]{1,0:T(8,128)S(1)} %broadcast_multiply_fusion), channel_id=1, source_target_pairs={{0,1},{1,0},{2,3},{3,2},{4,5},{5,4},{6,7},{7,6},{8,9},{9,8},{10,11... | collective-permute-start | bytes 33800 | tf_op jit(solution)/shard_map/ppermute | solution.py:126
  25.8 4.8 %collective-permute-done = f32[11,256]{1,0:T(8,128)S(1)} collective-permute-done((f32[11,256]{1,0:T(8,128)S(1)}, f32[11,256]{1,0:T(8,128)S(1)}, u32[]{:S(2)}, u32[]{:S(2)}) %collective-permute-start) | collective-permute-done | bytes 11296 | tf_op jit(solution)/shard_map/ppermute | solution.py:126
  34.4 3.3 %convolution_bitcast_fusion.1 = f32[4,22,2,16,640]{4,1,3,0,2:T(8,128)S(1)} fusion(f32[4,22,16,256]{3,1,2,0:T(8,128)S(1)} %fusion.38, f32[4,22,16,256]{3,1,2,0:T(8,128)S(1)} %fusion.36, f32[2,256,640]{2,1,0:T(8,128)S(1)} %bitcast.169), kind=kOutput, calls=%fused_computation.10 | convolution fusion | flops 2768601088 | bytes 11403264 | tf_op jit(solution)/shard_map/ligand_spectra/ntxc,hcq->nthxq/dot_general | solution.py:89
  37.7 1.3 %copy.20 = f32[4,22,2,16,640]{4,3,2,1,0:T(8,128)S(1)} copy(f32[4,22,2,16,640]{4,1,3,0,2:T(8,128)S(1)} %convolution_bitcast_fusion.1) | data formatting | bytes 14417920 | tf_op jit(solution)/shard_map/ligand_spectra/ntxc,hcq->nthxq/transpose | solution.py:89
  39.0 9.0 %convolution_bitcast_fusion = f32[22,4,64,640]{3,2,0,1:T(8,128)} fusion(f32[4,22,32,640]{3,2,1,0:T(8,128)S(1)} %bitcast.162, f32[64,32,1,1]{0,1,3,2:T(8,128)S(1)} %copy-done.9), kind=kOutput, calls=%fused_computation.2 | convolution fusion | flops 692060160 | bytes 21635072 | tf_op jit(solution)/shard_map/ligand_spectra/pk,ntkq->tnpq/dot_general | solution.py:92
  49.2 1.9 %collective-permute-start.10 = (bf16[11,8,1024]{2,1,0:T(8,128)(2,1)S(1)}, bf16[11,8,1024]{2,1,0:T(8,128)(2,1)S(1)}, u32[]{:S(2)}, u32[]{:S(2)}) collective-permute-start(bf16[11,8,1024]{2,1,0:T(8,128)(2,1)S(1)} %copy-done.2), channel_id=1, source_target_pairs={{0,7},{1,0},{2,1},{3,2},{4,3},{5,4},{6,5},{7,6},{8,15},{9,8},{10,9... | collective-permute-start | bytes 540680 | tf_op jit(solution)/shard_map/ppermute | solution.py:126
  52.5 1.6 %bitcast_dynamic-update-slice_fusion.3 = bf16[8,11,8,1024]{3,2,1,0:T(8,128)(2,1)} fusion(bf16[8,11,8,1024]{3,2,1,0:T(8,128)(2,1)} %bitcast_dynamic-update-slice_fusion.4, bf16[11,8,1024]{2,1,0:T(8,128)(2,1)} %collective-permute-done.7), kind=kLoop, calls=%fused_computation.69 | loop fusion | bytes 360448
  54.1 1.6 %bitcast_dynamic-update-slice_fusion.2 = bf16[8,11,8,1024]{3,2,1,0:T(8,128)(2,1)} fusion(bf16[8,11,8,1024]{3,2,1,0:T(8,128)(2,1)} %bitcast_dynamic-update-slice_fusion.3, bf16[11,8,1024]{2,1,0:T(8,128)(2,1)} %collective-permute-done.8), kind=kLoop, calls=%fused_computation.68 | loop fusion | bytes 360448
  57.1 3.2 %gather_fusion.1 = bf16[8,11,8,1024]{3,2,1,0:T(8,128)(2,1)} fusion(bf16[8,11,8,1024]{3,2,1,0:T(8,128)(2,1)} %bitcast_dynamic-update-slice_fusion, s32[1024]{0:T(1024)} %pad_clamp_fusion), kind=kCustom, calls=%fused_computation.1 | custom fusion | bytes 2883616 | tf_op jit(solution)/shard_map/jit(_take)/gather | solution.py:159
  60.3 1.6 %select_bitcast_fusion = bf16[2,11,4,8,1024]{4,3,1,0,2:T(8,128)(2,1)S(1)} fusion(bf16[4,2,11,8,1024]{4,3,2,1,0:T(8,128)(2,1)} %bitcast.164, pred[4,2]{1,0:T(4,128)(4,1)S(1)} %copy-done.13), kind=kLoop, calls=%fused_computation.29 | loop fusion | flops 720896 | bytes 2883592 | tf_op jit(solution)/shard_map/transpose | solution.py:161
  62.0 1.6 %copy-done = bf16[2,1024,640]{2,1,0:T(8,128)(2,1)S(1)} copy-done((bf16[2,1024,640]{2,1,0:T(8,128)(2,1)S(1)}, bf16[2,1024,640]{2,1,0:T(8,128)(2,1)}, u32[]{:S(2)}) %copy-start) | copy-done | bytes 2621464
  63.6 2.2 %fusion.3 = f32[2,640,22,32]{1,3,2,0:T(8,128)S(1)} fusion(bf16[22,32,1024,1]{2,1,0,3:T(8,128)(2,1)S(1)} %bitcast.167, bf16[2,1024,640]{2,1,0:T(8,128)(2,1)S(1)} %copy-done), kind=kOutput, calls=%fused_computation.13 | convolution fusion | flops 1845493760 | bytes 7667712 | tf_op jit(solution)/shard_map/receptor_spectra/trxc,hcq->trhxq/dot_general | solution.py:73
  65.8 2.3 %add_bitcast_fusion = f32[22,1,2,32,640]{4,3,0,2,1:T(8,128)S(1)} fusion(f32[2,640,22,32]{1,3,2,0:T(8,128)S(1)} %fusion.3, bf16[22,32,1024,1]{2,1,0,3:T(8,128)(2,1)S(1)} %bitcast.168, bf16[2,1024,640]{2,1,0:T(8,128)(2,1)S(1)} %get-tuple-element.8), kind=kOutput, calls=%fused_computation.9 | convolution fusion | flops 1846394880 | bytes 11272192 | tf_op jit(solution)/shard_map/receptor_spectra/trxc,hcq->trhxq/dot_general | solution.py:72
  68.5 1.2 %copy-done.7 = f32[64,64,1]{1,0,2:T(8,128)S(1)} copy-done((f32[64,64,1]{1,0,2:T(8,128)S(1)}, f32[64,64,1]{1,0,2:T(8,128)}, u32[]{:S(2)}) %copy-start.7) | copy-done | bytes 16408
  69.7 1.6 %convolution_bitcast_fusion.2 = f32[22,1,64,640]{3,2,0,1:T(8,128)S(1)} fusion(f32[22,64,640]{2,1,0:T(8,128)S(1)} %bitcast.163, f32[64,64,1]{1,0,2:T(8,128)S(1)} %copy-done.7), kind=kOutput, calls=%fused_computation.23 | convolution fusion | flops 346030080 | bytes 7225344 | tf_op jit(solution)/shard_map/receptor_spectra/pk,trkq->trpq/dot_general | solution.py:75
  71.7 2.4 %add_reduce_fusion = (f32[4,32,640]{2,1,0:T(8,128)S(1)}, f32[4,32,640]{2,1,0:T(8,128)S(1)}) fusion(f32[22,4,64,640]{3,2,0,1:T(8,128)S(1)} %bitcast.161, f32[22,32,640]{2,1,0:T(8,128)S(1)} %get-tuple-element.19, f32[22,32,640]{2,1,0:T(8,128)S(1)} %get-tuple-element.18), kind=kLoop, calls=%fused_computation.6 | loop fusion | flops 14254080 | bytes 18677760 | tf_op jit(solution)/shard_map/correlate/reduce_sum | solution.py:100
  77.0 1.1 %fusion.32 = f32[4]{0:T(128)S(1)} fusion(f32[4,32,1024]{2,1,0:T(8,128)S(1)} %fusion.29, bf16[2,1024,640]{2,1,0:T(8,128)(2,1)S(1)} %copy-done, bf16[1,4,32,2,640]{4,2,1,3,0:T(8,128)(2,1)S(1)} %get-tuple-element.10), kind=kOutput, calls=%fused_computation.37 | convolution fusion | flops 335806464 | bytes 3473424 | tf_op jit(solution)/shard_map/inverse_scores/rnxhq,hcq->rnxc/dot_general | solution.py:119
  78.3 1.9 %collective-permute-start.11 = (f32[4,32]{0,1:T(8,128)S(1)}, f32[4,32]{0,1:T(8,128)S(1)}, u32[]{:S(2)}, u32[]{:S(2)}) collective-permute-start(f32[4,32]{0,1:T(8,128)S(1)} %broadcast_select_fusion.1), channel_id=1, source_target_pairs={{0,1},{1,0},{2,3},{3,2},{4,5},{5,4},{6,7},{7,6},{8,9},{9,8},{10,11... | collective-permute-start | bytes 1544 | tf_op jit(solution)/shard_map/ppermute | solution.py:137
  80.4 1.6 %collective-permute-done.11 = f32[4,32]{0,1:T(8,128)S(1)} collective-permute-done((f32[4,32]{0,1:T(8,128)S(1)}, f32[4,32]{0,1:T(8,128)S(1)}, u32[]{:S(2)}, u32[]{:S(2)}) %collective-permute-start.11) | collective-permute-done | bytes 544 | tf_op jit(solution)/shard_map/ppermute | solution.py:137
  82.0 1.3 %collective-permute-done.13 = f32[4,32]{0,1:T(8,128)S(1)} collective-permute-done((f32[4,32]{0,1:T(8,128)S(1)}, f32[4,32]{0,1:T(8,128)S(1)}, u32[]{:S(2)}, u32[]{:S(2)}) %collective-permute-start.13) | collective-permute-done | bytes 544 | tf_op jit(solution)/shard_map/ppermute | solution.py:137
  84.6 2.2 %collective-permute-start.16 = (f32[4,32]{0,1:T(8,128)S(1)}, f32[4,32]{0,1:T(8,128)S(1)}, u32[]{:S(2)}, u32[]{:S(2)}) collective-permute-start(f32[4,32]{0,1:T(8,128)S(1)} %maximum_maximum_fusion.1), channel_id=1, source_target_pairs={{0,12},{1,13},{2,14},{3,15},{4,8},{5,9},{6,10},{7,11},{8,4},{9,5},... | collective-permute-start | bytes 1544 | tf_op jit(solution)/shard_map/ppermute | solution.py:137
  87.7 1.6 %collective-permute-done.16 = f32[4,32]{0,1:T(8,128)S(1)} collective-permute-done((f32[4,32]{0,1:T(8,128)S(1)}, f32[4,32]{0,1:T(8,128)S(1)}, u32[]{:S(2)}, u32[]{:S(2)}) %collective-permute-start.16) | collective-permute-done | bytes 544 | tf_op jit(solution)/shard_map/ppermute | solution.py:137
  89.6 4.3 %collective-permute-done.17 = f32[4,32]{0,1:T(8,128)S(1)} collective-permute-done((f32[4,32]{0,1:T(8,128)S(1)}, f32[4,32]{0,1:T(8,128)S(1)}, u32[]{:S(2)}, u32[]{:S(2)}) %collective-permute-start.17) | collective-permute-done | bytes 544 | tf_op jit(solution)/shard_map/ppermute | solution.py:137
  (100 shorter events, 21.8 us)
Async XLA Ops:
  0.6 21.6 %collective-permute-start.1 = (s32[3,2,256]{2,1,0:T(2,128)}, s32[3,2,256]{2,1,0:T(2,128)S(1)}, u32[]{:S(2)}, u32[]{:S(2)}) collective-permute-start(s32[3,2,256]{2,1,0:T(2,128)} %param.15), channel_id=1, source_target_pairs={{0,8},{8,16},{16,24},{24,0},{1,9},{9,17},{17,25},{25,1},{2,10},{10... | collective-permute-start | bytes 18440 | tf_op jit(solution)/shard_map/ppermute | solution.py:126
  3.7 19.8 %collective-permute-start.2 = (s32[3,2,256]{2,1,0:T(2,128)}, s32[3,2,256]{2,1,0:T(2,128)S(1)}, u32[]{:S(2)}, u32[]{:S(2)}) collective-permute-start(s32[3,2,256]{2,1,0:T(2,128)} %param.15), channel_id=1, source_target_pairs={{0,16},{8,24},{16,0},{24,8},{1,17},{9,25},{17,1},{25,9},{2,18},{10... | collective-permute-start | bytes 18440 | tf_op jit(solution)/shard_map/ppermute | solution.py:126
  6.3 17.7 %collective-permute-start.3 = (s32[3,2,256]{2,1,0:T(2,128)}, s32[3,2,256]{2,1,0:T(2,128)S(1)}, u32[]{:S(2)}, u32[]{:S(2)}) collective-permute-start(s32[3,2,256]{2,1,0:T(2,128)} %param.15), channel_id=1, source_target_pairs={{0,24},{8,0},{16,8},{24,16},{1,25},{9,1},{17,9},{25,17},{2,26},{10... | collective-permute-start | bytes 18440 | tf_op jit(solution)/shard_map/ppermute | solution.py:126
  7.6 40.4 %collective-permute-start.4 = (bf16[11,8,1024]{2,1,0:T(8,128)(2,1)}, bf16[11,8,1024]{2,1,0:T(8,128)(2,1)S(1)}, u32[]{:S(2)}, u32[]{:S(2)}) collective-permute-start(bf16[11,8,1024]{2,1,0:T(8,128)(2,1)} %param.12), channel_id=1, source_target_pairs={{0,1},{1,2},{2,3},{3,4},{4,5},{5,6},{6,7},{7,0},{8,9},{9,10},{10,1... | collective-permute-start | bytes 540680 | tf_op jit(solution)/shard_map/ppermute | solution.py:126
  9.2 40.1 %collective-permute-start.5 = (bf16[11,8,1024]{2,1,0:T(8,128)(2,1)}, bf16[11,8,1024]{2,1,0:T(8,128)(2,1)S(1)}, u32[]{:S(2)}, u32[]{:S(2)}) collective-permute-start(bf16[11,8,1024]{2,1,0:T(8,128)(2,1)} %param.12), channel_id=1, source_target_pairs={{0,2},{1,3},{2,4},{3,5},{4,6},{5,7},{6,0},{7,1},{8,10},{9,11},{10,... | collective-permute-start | bytes 540680 | tf_op jit(solution)/shard_map/ppermute | solution.py:126
  16.7 2.4 %copy-start.14 = (s32[8]{0:T(128)S(1)}, s32[8]{0:T(128)}, u32[]{:S(2)}) copy-start(s32[8]{0:T(128)} %fusion.73) | copy-start | bytes 100
  16.7 3.5 %copy-start.3 = (f32[2,16,640]{2,1,0:T(8,128)S(1)}, f32[2,16,640]{2,1,0:T(8,128)}, u32[]{:S(2)}) copy-start(f32[2,16,640]{2,1,0:T(8,128)} %constant.142) | copy-start | bytes 245764
  16.7 3.5 %copy-start.4 = (f32[2,16,640]{2,1,0:T(8,128)S(1)}, f32[2,16,640]{2,1,0:T(8,128)}, u32[]{:S(2)}) copy-start(f32[2,16,640]{2,1,0:T(8,128)} %constant.145) | copy-start | bytes 245764
  16.7 3.5 %copy-start.5 = (f32[2,16,640]{2,1,0:T(8,128)S(1)}, f32[2,16,640]{2,1,0:T(8,128)}, u32[]{:S(2)}) copy-start(f32[2,16,640]{2,1,0:T(8,128)} %constant.148) | copy-start | bytes 245764
  16.7 3.5 %copy-start.6 = (f32[2,16,640]{2,1,0:T(8,128)S(1)}, f32[2,16,640]{2,1,0:T(8,128)}, u32[]{:S(2)}) copy-start(f32[2,16,640]{2,1,0:T(8,128)} %constant.151) | copy-start | bytes 245764
  19.0 3.2 %copy-start.2 = (bf16[11,8,1024]{2,1,0:T(8,128)(2,1)S(1)}, bf16[11,8,1024]{2,1,0:T(8,128)(2,1)}, u32[]{:S(2)}) copy-start(bf16[11,8,1024]{2,1,0:T(8,128)(2,1)} %param.12) | copy-start | bytes 540676
  19.0 6.7 %copy-start.10 = (s32[3,2,256]{2,1,0:T(2,128)S(1)}, s32[3,2,256]{2,1,0:T(2,128)}, u32[]{:S(2)}) copy-start(s32[3,2,256]{2,1,0:T(2,128)} %param.15) | copy-start | bytes 18436
  22.2 29.5 %collective-permute-start.6 = (bf16[11,8,1024]{2,1,0:T(8,128)(2,1)S(1)}, bf16[11,8,1024]{2,1,0:T(8,128)(2,1)S(1)}, u32[]{:S(2)}, u32[]{:S(2)}) collective-permute-start(bf16[11,8,1024]{2,1,0:T(8,128)(2,1)S(1)} %copy-done.2), channel_id=1, source_target_pairs={{0,3},{1,4},{2,5},{3,6},{4,7},{5,0},{6,1},{7,2},{8,11},{9,12},{10,... | collective-permute-start | bytes 540680 | tf_op jit(solution)/shard_map/ppermute | solution.py:126
  23.5 29.0 %collective-permute-start.7 = (bf16[11,8,1024]{2,1,0:T(8,128)(2,1)S(1)}, bf16[11,8,1024]{2,1,0:T(8,128)(2,1)}, u32[]{:S(2)}, u32[]{:S(2)}) collective-permute-start(bf16[11,8,1024]{2,1,0:T(8,128)(2,1)S(1)} %copy-done.2), channel_id=1, source_target_pairs={{0,4},{1,5},{2,6},{3,7},{4,0},{5,1},{6,2},{7,3},{8,12},{9,13},{10,... | collective-permute-start | bytes 540680 | tf_op jit(solution)/shard_map/ppermute | solution.py:126
  24.0 6.6 %collective-permute-start = (f32[11,256]{1,0:T(8,128)S(1)}, f32[11,256]{1,0:T(8,128)S(1)}, u32[]{:S(2)}, u32[]{:S(2)}) collective-permute-start(f32[11,256]{1,0:T(8,128)S(1)} %broadcast_multiply_fusion), channel_id=1, source_target_pairs={{0,1},{1,0},{2,3},{3,2},{4,5},{5,4},{6,7},{7,6},{8,9},{9,8},{10,11... | collective-permute-start | bytes 33800 | tf_op jit(solution)/shard_map/ppermute | solution.py:126
  30.7 23.4 %collective-permute-start.8 = (bf16[11,8,1024]{2,1,0:T(8,128)(2,1)S(1)}, bf16[11,8,1024]{2,1,0:T(8,128)(2,1)}, u32[]{:S(2)}, u32[]{:S(2)}) collective-permute-start(bf16[11,8,1024]{2,1,0:T(8,128)(2,1)S(1)} %copy-done.2), channel_id=1, source_target_pairs={{0,5},{1,6},{2,7},{3,0},{4,1},{5,2},{6,3},{7,4},{8,13},{9,14},{10,... | collective-permute-start | bytes 540680 | tf_op jit(solution)/shard_map/ppermute | solution.py:126
  48.1 7.6 %collective-permute-start.9 = (bf16[11,8,1024]{2,1,0:T(8,128)(2,1)S(1)}, bf16[11,8,1024]{2,1,0:T(8,128)(2,1)S(1)}, u32[]{:S(2)}, u32[]{:S(2)}) collective-permute-start(bf16[11,8,1024]{2,1,0:T(8,128)(2,1)S(1)} %copy-done.2), channel_id=1, source_target_pairs={{0,6},{1,7},{2,0},{3,1},{4,2},{5,3},{6,4},{7,5},{8,14},{9,15},{10,... | collective-permute-start | bytes 540680 | tf_op jit(solution)/shard_map/ppermute | solution.py:126
  49.2 7.1 %collective-permute-start.10 = (bf16[11,8,1024]{2,1,0:T(8,128)(2,1)S(1)}, bf16[11,8,1024]{2,1,0:T(8,128)(2,1)S(1)}, u32[]{:S(2)}, u32[]{:S(2)}) collective-permute-start(bf16[11,8,1024]{2,1,0:T(8,128)(2,1)S(1)} %copy-done.2), channel_id=1, source_target_pairs={{0,7},{1,0},{2,1},{3,2},{4,3},{5,4},{6,5},{7,6},{8,15},{9,8},{10,9... | collective-permute-start | bytes 540680 | tf_op jit(solution)/shard_map/ppermute | solution.py:126
  56.4 3.9 %copy-start.13 = (pred[4,2]{1,0:T(4,128)(4,1)S(1)}, pred[4,2]{1,0:T(4,128)(4,1)}, u32[]{:S(2)}) copy-start(pred[4,2]{1,0:T(4,128)(4,1)} %compare_and_fusion) | copy-start | bytes 28
  61.9 1.7 %copy-start = (bf16[2,1024,640]{2,1,0:T(8,128)(2,1)S(1)}, bf16[2,1024,640]{2,1,0:T(8,128)(2,1)}, u32[]{:S(2)}) copy-start(bf16[2,1024,640]{2,1,0:T(8,128)(2,1)} %get-tuple-element.9) | copy-start | bytes 7864324
  65.8 5.8 %slice-start = ((s8[14417920]{0:T(1024)(128)(4,1)}), s8[4194304]{0:T(1024)(128)(4,1)S(1)}, s32[]{:S(2)}) async-start(s8[14417920]{0:T(1024)(128)(4,1)} %bitcast.160), calls=%async_computation | async-start | bytes 8388608
  65.8 5.8 %slice-start.1 = ((s8[14417920]{0:T(1024)(128)(4,1)}), s8[4194304]{0:T(1024)(128)(4,1)S(1)}, s32[]{:S(2)}) async-start(s8[14417920]{0:T(1024)(128)(4,1)} %bitcast.160), calls=%async_computation.1 | async-start | bytes 8388608
  65.8 5.8 %slice-start.2 = ((s8[14417920]{0:T(1024)(128)(4,1)}), s8[4194304]{0:T(1024)(128)(4,1)S(1)}, s32[]{:S(2)}) async-start(s8[14417920]{0:T(1024)(128)(4,1)} %bitcast.160), calls=%async_computation.2 | async-start | bytes 8388608
  69.7 2.0 %slice-start.3 = ((s8[14417920]{0:T(1024)(128)(4,1)}), s8[1835008]{0:T(1024)(128)(4,1)S(1)}, s32[]{:S(2)}) async-start(s8[14417920]{0:T(1024)(128)(4,1)} %bitcast.160), calls=%async_computation.3 | async-start | bytes 3670016
  71.6 2.4 %copy-start.8 = (f32[64,32,1,1]{0,1,3,2:T(8,128)S(1)}, f32[64,32,1,1]{0,1,3,2:T(8,128)}, u32[]{:S(2)}) copy-start(f32[64,32,1,1]{0,1,3,2:T(8,128)} %constant.162) | copy-start | bytes 24580
  78.3 3.7 %collective-permute-start.11 = (f32[4,32]{0,1:T(8,128)S(1)}, f32[4,32]{0,1:T(8,128)S(1)}, u32[]{:S(2)}, u32[]{:S(2)}) collective-permute-start(f32[4,32]{0,1:T(8,128)S(1)} %broadcast_select_fusion.1), channel_id=1, source_target_pairs={{0,1},{1,0},{2,3},{3,2},{4,5},{5,4},{6,7},{7,6},{8,9},{9,8},{10,11... | collective-permute-start | bytes 1544 | tf_op jit(solution)/shard_map/ppermute | solution.py:137
  80.1 1.9 %collective-permute-start.12 = (f32[4,32]{0,1:T(8,128)S(1)}, f32[4,32]{0,1:T(8,128)S(1)}, u32[]{:S(2)}, u32[]{:S(2)}) collective-permute-start(f32[4,32]{0,1:T(8,128)S(1)} %broadcast_select_fusion.1), channel_id=1, source_target_pairs={{0,2},{1,3},{2,0},{3,1},{4,6},{5,7},{6,4},{7,5},{8,10},{9,11},{10,... | collective-permute-start | bytes 1544 | tf_op jit(solution)/shard_map/ppermute | solution.py:137
  80.1 3.2 %collective-permute-start.13 = (f32[4,32]{0,1:T(8,128)S(1)}, f32[4,32]{0,1:T(8,128)S(1)}, u32[]{:S(2)}, u32[]{:S(2)}) collective-permute-start(f32[4,32]{0,1:T(8,128)S(1)} %broadcast_select_fusion.1), channel_id=1, source_target_pairs={{0,3},{1,2},{2,1},{3,0},{4,7},{5,6},{6,5},{7,4},{8,11},{9,10},{10,... | collective-permute-start | bytes 1544 | tf_op jit(solution)/shard_map/ppermute | solution.py:137
  83.4 3.7 %collective-permute-start.14 = (f32[4,32]{0,1:T(8,128)S(1)}, f32[4,32]{0,1:T(8,128)S(1)}, u32[]{:S(2)}, u32[]{:S(2)}) collective-permute-start(f32[4,32]{0,1:T(8,128)S(1)} %maximum_maximum_fusion.1), channel_id=1, source_target_pairs={{0,4},{1,5},{2,6},{3,7},{4,0},{5,1},{6,2},{7,3},{8,12},{9,13},{10,... | collective-permute-start | bytes 1544 | tf_op jit(solution)/shard_map/ppermute | solution.py:137
  84.0 3.7 %collective-permute-start.15 = (f32[4,32]{0,1:T(8,128)S(1)}, f32[4,32]{0,1:T(8,128)S(1)}, u32[]{:S(2)}, u32[]{:S(2)}) collective-permute-start(f32[4,32]{0,1:T(8,128)S(1)} %maximum_maximum_fusion.1), channel_id=1, source_target_pairs={{0,8},{1,9},{2,10},{3,11},{4,12},{5,13},{6,14},{7,15},{8,0},{9,1},... | collective-permute-start | bytes 1544 | tf_op jit(solution)/shard_map/ppermute | solution.py:137
  84.6 4.6 %collective-permute-start.16 = (f32[4,32]{0,1:T(8,128)S(1)}, f32[4,32]{0,1:T(8,128)S(1)}, u32[]{:S(2)}, u32[]{:S(2)}) collective-permute-start(f32[4,32]{0,1:T(8,128)S(1)} %maximum_maximum_fusion.1), channel_id=1, source_target_pairs={{0,12},{1,13},{2,14},{3,15},{4,8},{5,9},{6,10},{7,11},{8,4},{9,5},... | collective-permute-start | bytes 1544 | tf_op jit(solution)/shard_map/ppermute | solution.py:137
  89.3 4.6 %collective-permute-start.17 = (f32[4,32]{0,1:T(8,128)S(1)}, f32[4,32]{0,1:T(8,128)S(1)}, u32[]{:S(2)}, u32[]{:S(2)}) collective-permute-start(f32[4,32]{0,1:T(8,128)S(1)} %maximum_maximum_fusion), channel_id=1, source_target_pairs={{0,16},{1,17},{2,18},{3,19},{4,20},{5,21},{6,22},{7,23},{8,24},{9,... | collective-permute-start | bytes 1544 | tf_op jit(solution)/shard_map/ppermute | solution.py:137
  (5 other events, 6.1 us)

commit v8 on v6

--- a/solution.py
+++ b/solution.py
@@ -151,10 +151,11 @@
         plane = lax.axis_index("plane")
         inner = lax.axis_index("inner")
         term = lax.axis_index("term")
-        gathered = lax.all_gather(receptor_grids, ("term", "inner"), axis=0, tiled=False)
-        gathered = gathered.reshape(term_count, inner_count, terms_here, rows_here, cells)
-        gathered = jnp.transpose(gathered, (0, 2, 1, 3, 4))
-        gathered = gathered.reshape(term_count * terms_here, inner_count * rows_here, cells)
+        groups = [lax.all_gather(receptor_grids, "inner", axis=1, tiled=True)]
+        for shift in range(1, term_count):
+            pairs = [(k, (k + shift) % term_count) for k in range(term_count)]
+            moved = lax.ppermute(receptor_grids, "term", pairs)
+            groups.append(lax.all_gather(moved, "inner", axis=1, tiled=True))
         cell_blocks = gather_by_permutes(ligand_cells, "plane", plane_count, plane)
         cells_here = jnp.concatenate(cell_blocks, axis=1)
         share = cells_here.shape[1] // term_count
@@ -163,9 +164,7 @@
         source_plane = (plane - local // rot_here) % plane_count
         rot_ids = (source_plane * inner_count + inner) * rot_here + local % rot_here
         coefficients = atom_weights * term_weights[:, None]
-        term_blocks = jnp.stack(gather_by_permutes(coefficients, "term", term_count, term))
-        order = (term - jnp.arange(term_count, dtype=jnp.int32)) % term_count
-        coefficients = jnp.take(term_blocks, order, axis=0).reshape(-1, coefficients.shape[1])
+        coefficients = jnp.concatenate(gather_by_permutes(coefficients, "term", term_count, term))
         with jax.named_scope("twiddle_tables"):
             factors = plane_factors()
             table_hi, table_lo = split_bf16(plane_table(factors, G))
@@ -174,10 +173,13 @@
             box_table, table_hi, table_lo = tables
         with jax.named_scope("ligand_spectra"):
             lig_spec = ligand_spectra(voxels, coefficients, box_table)
-        with jax.named_scope("receptor_spectra"):
-            rec_spec = receptor_mixed(gathered, table_hi, table_lo)
-        with jax.named_scope("correlate"):
-            products = correlate(rec_spec, lig_spec)
+        products = 0.0
+        for index, grids in enumerate(groups):
+            lo = index * terms_here
+            with jax.named_scope("receptor_spectra"):
+                rec_spec = receptor_mixed(grids, table_hi, table_lo)
+            with jax.named_scope("correlate"):
+                products = products + correlate(rec_spec, lig_spec[lo : lo + terms_here])
         with jax.named_scope("inverse_scores"):
             scores = inverse_scores(products, table_hi, table_lo)
             best_here = jnp.max(scores, axis=(2, 3))[0]

time: 80.8 us -> 80.6 us (level)
  blocking collectives: 0 us -> 17 us
  between operations: 14.4 us -> 1.01 us
  local copies, waits for them, and re-layouts: 6.67 us -> 4.39 us
  starting transfers between devices: 16.6 us -> 15 us
  other arithmetic: 10.9 us -> 9.59 us
  waiting for transfers between devices: 8.46 us -> 9.31 us
    all_gather x0 -> x2, blocking collectives: none -> 17 us  [the longest x1 8.59 us: body(): groups.append(lax.all_gather(moved, 'inner', axis=1, tiled=True))]
    dot_general x1, matrix products: 9.21 us -> 6 us  [ligand_spectra(): return jnp.einsum('pk,ntkq->tnpq', mix_tables(LB), plane, precision=HIGH)]
    dot_general x1 -> x2, matrix products: 1.63 us -> 4.41 us  [receptor_mixed(): return jnp.einsum('pk,trkq->trpq', mix_tables(G), plane, precision=HIGH)]
    ppermute x7, starting transfers between devices: 8.04 us -> 5.98 us  [butterfly_max(): received.append(lax.ppermute(values, axes, pairs))]
    reshape x1 -> x0, local copies, waits for them, and re-layouts: 1.65 us -> none  [body(): gathered.reshape(term_count, inner_count, terms_here, rows_here, cells)]
    convert_element_type x2 -> x3, other arithmetic: 2.4 us -> 1.18 us  [split_bf16(): return (upper.astype(jnp.bfloat16), lower.astype(jnp.bfloat16))]
    add x1 -> x2, local copies, waits for them, and re-layouts: 0.32 us -> 1.52 us  [receptor_mixed(): plane + jnp.einsum(form, grids, table_lo, preferred_element_type=jnp.floa...]
    unnamed x30 -> x26, local copies, waits for them, and re-layouts: 1.88 us -> 0.77 us
  transfers between devices with their start and end apart: 12 -> 12, of which waited for: 7 -> 5; matrix products, arithmetic and copies ran while one was open for 29% -> 32% of each run, Pallas kernels for 0% -> 0%
where the time goes in v8:
time: 80.6 us; the launch traced here: 80.2 us
  matrix products  23.9 us (30%)
  blocking collectives  17 us (21%)
  starting transfers between devices  15 us (19%)
  other arithmetic  9.59 us (12%)
  waiting for transfers between devices  9.31 us (12%)
  local copies, waits for them, and re-layouts  4.39 us (5%)
  between operations  1.01 us (1%)
    ppermute x7, waiting for transfers between devices, butterfly_max(): received.append(lax.ppermute(values, axes, pairs))  9.3 us
    all_gather x1, blocking collectives, body(): groups.append(lax.all_gather(moved, 'inner', axis=1, tiled=True))  8.59 us
    ppermute x4, starting transfers between devices, gather_by_permutes(): blocks.append(lax.ppermute(values, axis_name, pairs))  8.53 us
    all_gather x1, blocking collectives, body(): groups = [lax.all_gather(receptor_grids, 'inner', axis=1, tiled=True)]  8.44 us
    dot_general x1, matrix products, ligand_spectra(): return jnp.einsum('pk,ntkq->tnpq', mix_tables(LB), plane, precision=HIGH)  6 us
    ppermute x7, starting transfers between devices, butterfly_max(): received.append(lax.ppermute(values, axes, pairs))  5.98 us
    dot_general x2, matrix products, receptor_mixed(): return jnp.einsum('pk,trkq->trpq', mix_tables(G), plane, precision=HIGH)  4.41 us
    add x2, other arithmetic, plane_table(): first[:, :, None, :] * second[:, None, :, :]  3.4 us
  transfers between devices with their start and end apart: 12, of which 5 were waited for; matrix products, arithmetic and copies ran while one was open for 32% of the time, Pallas kernels for 0%

profile of v8, /device:TPU:0, one launch (start us, length us, event | category | flops | bytes accessed | tf_op | source)
XLA Modules:
  0.0 80.2 jit_solution(1907639900725771461)
XLA Ops:
  0.6 3.1 %collective-permute-start.1 = (s32[3,2,256]{2,1,0:T(2,128)}, s32[3,2,256]{2,1,0:T(2,128)}, u32[]{:S(2)}, u32[]{:S(2)}) collective-permute-start(s32[3,2,256]{2,1,0:T(2,128)} %param.16), channel_id=1, source_target_pairs={{0,8},{8,16},{16,24},{24,0},{1,9},{9,17},{17,25},{25,1},{2,10},{10... | collective-permute-start | bytes 18440 | tf_op jit(solution)/shard_map/ppermute | solution.py:126
  3.7 2.6 %collective-permute-start.2 = (s32[3,2,256]{2,1,0:T(2,128)}, s32[3,2,256]{2,1,0:T(2,128)}, u32[]{:S(2)}, u32[]{:S(2)}) collective-permute-start(s32[3,2,256]{2,1,0:T(2,128)} %param.16), channel_id=1, source_target_pairs={{0,16},{8,24},{16,0},{24,8},{1,17},{9,25},{17,1},{25,9},{2,18},{10... | collective-permute-start | bytes 18440 | tf_op jit(solution)/shard_map/ppermute | solution.py:126
  6.3 1.3 %collective-permute-start.3 = (s32[3,2,256]{2,1,0:T(2,128)}, s32[3,2,256]{2,1,0:T(2,128)}, u32[]{:S(2)}, u32[]{:S(2)}) collective-permute-start(s32[3,2,256]{2,1,0:T(2,128)} %param.16), channel_id=1, source_target_pairs={{0,24},{8,0},{16,8},{24,16},{1,25},{9,1},{17,9},{25,17},{2,26},{10... | collective-permute-start | bytes 18440 | tf_op jit(solution)/shard_map/ppermute | solution.py:126
  8.4 1.5 %collective-permute-start = (f32[11,256]{1,0:T(8,128)S(1)}, f32[11,256]{1,0:T(8,128)S(1)}, u32[]{:S(2)}, u32[]{:S(2)}) collective-permute-start(f32[11,256]{1,0:T(8,128)S(1)} %broadcast_multiply_fusion), channel_id=1, source_target_pairs={{0,1},{1,0},{2,3},{3,2},{4,5},{5,4},{6,7},{7,6},{8,9},{9,8},{10,11... | collective-permute-start | bytes 33800 | tf_op jit(solution)/shard_map/ppermute | solution.py:126
  10.5 8.4 %all_gather.6 = bf16[11,32,1024]{2,1,0:T(8,128)(2,1)S(1)} all-gather(bf16[11,8,1024]{2,1,0:T(8,128)(2,1)} %param.13), channel_id=1, replica_groups=mesh['plane'=4,'inner'=4,'term'=2] {'inner'}, dimensions={1}, use_global_device_ids=true | all-gather | bytes 901120 | tf_op jit(solution)/shard_map/all_gather | solution.py:154
  18.9 2.0 %multiply_add_fusion = f32[2,32,32,640]{3,2,1,0:T(8,128)S(1)} fusion(f32[2,32,640]{2,1,0:T(8,128)} %constant.108, f32[2,32,640]{2,1,0:T(8,128)} %constant.106, f32[2,32,640]{2,1,0:T(8,128)} %constant.104, f32[2,32,640]{2,1,0:T(8,128)} %constant.102), kind=kLoop, calls=%fused_computation.4 | loop fusion | flops 3932160 | bytes 5898240 | tf_op jit(solution)/shard_map/twiddle_tables/add | solution.py:45
  21.0 0.9 %fusion = (bf16[2,1024,640]{2,1,0:T(8,128)(2,1)S(1)}, bf16[2,1024,640]{2,1,0:T(8,128)(2,1)S(1)}) fusion(f32[2,32,32,640]{3,2,1,0:T(8,128)S(1)} %multiply_add_fusion), kind=kLoop, calls=%fused_computation.3 | loop fusion | flops 5242880 | bytes 10485760 | tf_op jit(solution)/shard_map/twiddle_tables/convert_element_type | solution.py:52
  21.9 1.4 %multiply_add_fusion.1 = f32[2,16,16,640]{3,2,1,0:T(8,128)} fusion(f32[2,16,640]{2,1,0:T(8,128)S(1)} %copy-done.5, f32[2,16,640]{2,1,0:T(8,128)S(1)} %copy-done.8, f32[2,16,640]{2,1,0:T(8,128)S(1)} %copy-done.7, f32[2,16,640]{2,1,0:T(8,128)S(1)} %copy-done.6), kind=kLoop, calls=%fused_computation.34 | loop fusion | flops 983040 | bytes 1638400 | tf_op jit(solution)/shard_map/twiddle_tables/add | solution.py:45
  23.3 1.1 %fusion.5 = f32[2,640,11,32]{1,3,2,0:T(8,128)S(1)} fusion(bf16[2,1024,640]{2,1,0:T(8,128)(2,1)S(1)} %get-tuple-element.9, bf16[11,32,1024]{2,1,0:T(8,128)(2,1)S(1)} %all_gather.6), kind=kOutput, calls=%fused_computation.14 | convolution fusion | flops 922746880 | bytes 5144576 | tf_op jit(solution)/shard_map/receptor_spectra/trxc,hcq->trhxq/dot_general | solution.py:73
  24.5 1.1 %add_bitcast_fusion.1 = f32[11,1,2,32,640]{4,3,0,2,1:T(8,128)S(1)} fusion(f32[2,640,11,32]{1,3,2,0:T(8,128)S(1)} %fusion.5, bf16[2,1024,640]{2,1,0:T(8,128)(2,1)S(1)} %get-tuple-element.8, bf16[11,32,1024]{2,1,0:T(8,128)(2,1)S(1)} %all_gather.6), kind=kOutput, calls=%fused_computation.27 | convolution fusion | flops 923197440 | bytes 6946816 | tf_op jit(solution)/shard_map/receptor_spectra/trxc,hcq->trhxq/dot_general | solution.py:72
  25.6 1.4 %copy.21 = f32[11,1,2,32,640]{4,3,2,0,1:T(8,128)} copy(f32[11,1,2,32,640]{4,3,0,2,1:T(8,128)S(1)} %add_bitcast_fusion.1) | data formatting | bytes 3604480 | tf_op jit(solution)/shard_map/receptor_spectra/add | solution.py:73
  27.0 3.5 %convolution_bitcast_fusion.3 = f32[11,1,64,640]{3,2,0,1:T(8,128)} fusion(f32[11,64,640]{2,1,0:T(8,128)} %bitcast.160, f32[64,64,1]{1,0,2:T(8,128)S(1)} %copy-done.4), kind=kOutput, calls=%fused_computation.31 | convolution fusion | flops 173015040 | bytes 3620864 | tf_op jit(solution)/shard_map/receptor_spectra/pk,trkq->trpq/dot_general | solution.py:75
  31.7 1.0 %fusion.42 = f32[4,22,16,256]{3,1,2,0:T(8,128)S(1)} fusion(bf16[4,22,16,256]{3,2,1,0:T(8,128)(2,1)S(1)} %get-tuple-element.28, s32[4,256]{1,0:T(4,128)S(1)} %get-tuple-element.30), kind=kOutput, calls=%fused_computation.43 | convolution fusion | flops 184811520 | bytes 2166784 | tf_op jit(solution)/shard_map/ligand_spectra/ntxa,nac->ntxc/dot_general | solution.py:88
  33.6 3.3 %convolution_bitcast_fusion.1 = f32[4,22,2,16,640]{4,1,3,0,2:T(8,128)S(1)} fusion(f32[4,22,16,256]{3,1,2,0:T(8,128)S(1)} %fusion.44, f32[4,22,16,256]{3,1,2,0:T(8,128)S(1)} %fusion.42, f32[2,256,640]{2,1,0:T(8,128)S(1)} %bitcast.164), kind=kOutput, calls=%fused_computation.9 | convolution fusion | flops 2768601088 | bytes 11403264 | tf_op jit(solution)/shard_map/ligand_spectra/ntxc,hcq->nthxq/dot_general | solution.py:89
  36.9 1.3 %copy.20 = f32[4,22,2,16,640]{4,3,2,1,0:T(8,128)S(1)} copy(f32[4,22,2,16,640]{4,1,3,0,2:T(8,128)S(1)} %convolution_bitcast_fusion.1) | data formatting | bytes 14417920 | tf_op jit(solution)/shard_map/ligand_spectra/ntxc,hcq->nthxq/transpose | solution.py:89
  38.2 6.0 %convolution_bitcast_fusion = f32[22,4,64,640]{3,2,0,1:T(8,128)S(1)} fusion(f32[4,22,32,640]{3,2,1,0:T(8,128)S(1)} %bitcast.159, f32[64,32,1,1]{0,1,3,2:T(8,128)S(1)} %copy-done.10), kind=kOutput, calls=%fused_computation | convolution fusion | flops 692060160 | bytes 21635072 | tf_op jit(solution)/shard_map/ligand_spectra/pk,ntkq->tnpq/dot_general | solution.py:92
  44.2 8.6 %all_gather.7 = bf16[11,32,1024]{2,1,0:T(8,128)(2,1)S(1)} all-gather(bf16[11,8,1024]{2,1,0:T(8,128)(2,1)S(1)} %collective-permute-done.4), channel_id=1, replica_groups=mesh['plane'=4,'inner'=4,'term'=2] {'inner'}, dimensions={1}, use_global_device_ids=true | all-gather | bytes 901120 | tf_op jit(solution)/shard_map/all_gather | solution.py:158
  52.8 1.1 %fusion.3 = f32[2,640,11,32]{1,3,2,0:T(8,128)S(1)} fusion(bf16[2,1024,640]{2,1,0:T(8,128)(2,1)S(1)} %copy-done.1, bf16[11,32,1024]{2,1,0:T(8,128)(2,1)S(1)} %all_gather.7), kind=kOutput, calls=%fused_computation.12 | convolution fusion | flops 922746880 | bytes 5144576 | tf_op jit(solution)/shard_map/receptor_spectra/trxc,hcq->trhxq/dot_general | solution.py:73
  54.0 1.1 %add_bitcast_fusion = f32[11,1,2,32,640]{4,3,0,2,1:T(8,128)S(1)} fusion(f32[2,640,11,32]{1,3,2,0:T(8,128)S(1)} %fusion.3, bf16[2,1024,640]{2,1,0:T(8,128)(2,1)S(1)} %get-tuple-element.8, bf16[11,32,1024]{2,1,0:T(8,128)(2,1)S(1)} %all_gather.7), kind=kOutput, calls=%fused_computation.26 | convolution fusion | flops 923197440 | bytes 6946816 | tf_op jit(solution)/shard_map/receptor_spectra/trxc,hcq->trhxq/dot_general | solution.py:72
  55.3 0.9 %convolution_bitcast_fusion.2 = f32[11,1,64,640]{3,2,0,1:T(8,128)S(1)} fusion(f32[11,64,640]{2,1,0:T(8,128)S(1)} %bitcast.161, f32[64,64,1]{1,0,2:T(8,128)S(1)} %copy-done.4), kind=kOutput, calls=%fused_computation.30 | convolution fusion | flops 173015040 | bytes 3620864 | tf_op jit(solution)/shard_map/receptor_spectra/pk,trkq->trpq/dot_general | solution.py:75
  57.0 2.5 %add_reduce_fusion = (f32[4,32,640]{2,1,0:T(8,128)S(1)}, f32[4,32,640]{2,1,0:T(8,128)S(1)}, f32[4,32,640]{2,1,0:T(8,128)S(1)}, f32[4,32,640]{2,1,0:T(8,128)S(1)}) fusion(f32[22,4,64,640]{3,2,0,1:T(8,128)S(1)} %convolution_bitcast_fusion, f32[11,32,640]{2,1,0:T(8,128)S(1)} %get-tuple-element.25, f32[11,32,640]{2,1,0:T(8,128)S(1)} %get-tuple-element.24, ...), kind=kLoop, calls=%fused_computation.6 | loop fusion | flops 14090240 | bytes 19333120 | tf_op jit(solution)/shard_map/correlate/reduce_sum | solution.py:100
  60.5 1.0 %fusion.23 = f32[4,32,1024]{2,1,0:T(8,128)S(1)} fusion(bf16[2,1024,640]{2,1,0:T(8,128)(2,1)S(1)} %get-tuple-element.8, bf16[1,4,32,2,640]{4,2,1,3,0:T(8,128)(2,1)S(1)} %get-tuple-element.10), kind=kOutput, calls=%fused_computation.35 | convolution fusion | flops 335544320 | bytes 3473408 | tf_op jit(solution)/shard_map/inverse_scores/rnxhq,hcq->rnxc/dot_general | solution.py:117
  61.5 1.0 %fusion.35 = f32[4,32,1024]{2,1,0:T(8,128)S(1)} fusion(f32[4,32,1024]{2,1,0:T(8,128)S(1)} %fusion.23, bf16[2,1024,640]{2,1,0:T(8,128)(2,1)S(1)} %get-tuple-element.8, bf16[1,4,32,2,640]{4,2,1,3,0:T(8,128)(2,1)S(1)} %get-tuple-element.11), kind=kOutput, calls=%fused_computation.39 | convolution fusion | flops 335675392 | bytes 3997696 | tf_op jit(solution)/shard_map/inverse_scores/rnxhq,hcq->rnxc/dot_general | solution.py:118
  62.5 1.1 %fusion.38 = f32[4]{0:T(128)S(1)} fusion(f32[4,32,1024]{2,1,0:T(8,128)S(1)} %fusion.35, bf16[2,1024,640]{2,1,0:T(8,128)(2,1)S(1)} %copy-done.1, bf16[1,4,32,2,640]{4,2,1,3,0:T(8,128)(2,1)S(1)} %get-tuple-element.10), kind=kOutput, calls=%fused_computation.40 | convolution fusion | flops 335806464 | bytes 3473424 | tf_op jit(solution)/shard_map/inverse_scores/rnxhq,hcq->rnxc/dot_general | solution.py:119
  63.7 1.5 %collective-permute-start.5 = (f32[4,32]{0,1:T(8,128)S(1)}, f32[4,32]{0,1:T(8,128)S(1)}, u32[]{:S(2)}, u32[]{:S(2)}) collective-permute-start(f32[4,32]{0,1:T(8,128)S(1)} %broadcast_select_fusion), channel_id=1, source_target_pairs={{0,1},{1,0},{2,3},{3,2},{4,5},{5,4},{6,7},{7,6},{8,9},{9,8},{10,11... | collective-permute-start | bytes 1544 | tf_op jit(solution)/shard_map/ppermute | solution.py:137
  65.9 1.6 %collective-permute-done.5 = f32[4,32]{0,1:T(8,128)S(1)} collective-permute-done((f32[4,32]{0,1:T(8,128)S(1)}, f32[4,32]{0,1:T(8,128)S(1)}, u32[]{:S(2)}, u32[]{:S(2)}) %collective-permute-start.5) | collective-permute-done | bytes 544 | tf_op jit(solution)/shard_map/ppermute | solution.py:137
  67.5 1.0 %collective-permute-done.7 = f32[4,32]{0,1:T(8,128)S(1)} collective-permute-done((f32[4,32]{0,1:T(8,128)S(1)}, f32[4,32]{0,1:T(8,128)S(1)}, u32[]{:S(2)}, u32[]{:S(2)}) %collective-permute-start.7) | collective-permute-done | bytes 544 | tf_op jit(solution)/shard_map/ppermute | solution.py:137
  69.2 1.5 %collective-permute-start.8 = (f32[4,32]{0,1:T(8,128)S(1)}, f32[4,32]{0,1:T(8,128)S(1)}, u32[]{:S(2)}, u32[]{:S(2)}) collective-permute-start(f32[4,32]{0,1:T(8,128)S(1)} %maximum_maximum_fusion.1), channel_id=1, source_target_pairs={{0,4},{1,5},{2,6},{3,7},{4,0},{5,1},{6,2},{7,3},{8,12},{9,13},{10,... | collective-permute-start | bytes 1544 | tf_op jit(solution)/shard_map/ppermute | solution.py:137
  70.7 1.3 %collective-permute-start.9 = (f32[4,32]{0,1:T(8,128)S(1)}, f32[4,32]{0,1:T(8,128)S(1)}, u32[]{:S(2)}, u32[]{:S(2)}) collective-permute-start(f32[4,32]{0,1:T(8,128)S(1)} %maximum_maximum_fusion.1), channel_id=1, source_target_pairs={{0,8},{1,9},{2,10},{3,11},{4,12},{5,13},{6,14},{7,15},{8,0},{9,1},... | collective-permute-start | bytes 1544 | tf_op jit(solution)/shard_map/ppermute | solution.py:137
  72.1 1.2 %collective-permute-done.10 = f32[4,32]{0,1:T(8,128)S(1)} collective-permute-done((f32[4,32]{0,1:T(8,128)S(1)}, f32[4,32]{0,1:T(8,128)S(1)}, u32[]{:S(2)}, u32[]{:S(2)}) %collective-permute-start.10) | collective-permute-done | bytes 544 | tf_op jit(solution)/shard_map/ppermute | solution.py:137
  73.3 1.2 %collective-permute-done.9 = f32[4,32]{0,1:T(8,128)S(1)} collective-permute-done((f32[4,32]{0,1:T(8,128)S(1)}, f32[4,32]{0,1:T(8,128)S(1)}, u32[]{:S(2)}, u32[]{:S(2)}) %collective-permute-start.9) | collective-permute-done | bytes 544 | tf_op jit(solution)/shard_map/ppermute | solution.py:137
  74.8 4.3 %collective-permute-done.11 = f32[4,32]{0,1:T(8,128)S(1)} collective-permute-done((f32[4,32]{0,1:T(8,128)S(1)}, f32[4,32]{0,1:T(8,128)S(1)}, u32[]{:S(2)}, u32[]{:S(2)}) %collective-permute-start.11) | collective-permute-done | bytes 544 | tf_op jit(solution)/shard_map/ppermute | solution.py:137
  (58 shorter events, 8.2 us)
Async XLA Ops:
  0.6 30.0 %collective-permute-start.1 = (s32[3,2,256]{2,1,0:T(2,128)}, s32[3,2,256]{2,1,0:T(2,128)}, u32[]{:S(2)}, u32[]{:S(2)}) collective-permute-start(s32[3,2,256]{2,1,0:T(2,128)} %param.16), channel_id=1, source_target_pairs={{0,8},{8,16},{16,24},{24,0},{1,9},{9,17},{17,25},{25,1},{2,10},{10... | collective-permute-start | bytes 18440 | tf_op jit(solution)/shard_map/ppermute | solution.py:126
  3.7 26.9 %collective-permute-start.2 = (s32[3,2,256]{2,1,0:T(2,128)}, s32[3,2,256]{2,1,0:T(2,128)}, u32[]{:S(2)}, u32[]{:S(2)}) collective-permute-start(s32[3,2,256]{2,1,0:T(2,128)} %param.16), channel_id=1, source_target_pairs={{0,16},{8,24},{16,0},{24,8},{1,17},{9,25},{17,1},{25,9},{2,18},{10... | collective-permute-start | bytes 18440 | tf_op jit(solution)/shard_map/ppermute | solution.py:126
  6.3 24.3 %collective-permute-start.3 = (s32[3,2,256]{2,1,0:T(2,128)}, s32[3,2,256]{2,1,0:T(2,128)}, u32[]{:S(2)}, u32[]{:S(2)}) collective-permute-start(s32[3,2,256]{2,1,0:T(2,128)} %param.16), channel_id=1, source_target_pairs={{0,24},{8,0},{16,8},{24,16},{1,25},{9,1},{17,9},{25,17},{2,26},{10... | collective-permute-start | bytes 18440 | tf_op jit(solution)/shard_map/ppermute | solution.py:126
  8.4 23.0 %collective-permute-start = (f32[11,256]{1,0:T(8,128)S(1)}, f32[11,256]{1,0:T(8,128)S(1)}, u32[]{:S(2)}, u32[]{:S(2)}) collective-permute-start(f32[11,256]{1,0:T(8,128)S(1)} %broadcast_multiply_fusion), channel_id=1, source_target_pairs={{0,1},{1,0},{2,3},{3,2},{4,5},{5,4},{6,7},{7,6},{8,9},{9,8},{10,11... | collective-permute-start | bytes 33800 | tf_op jit(solution)/shard_map/ppermute | solution.py:126
  10.0 34.3 %collective-permute-start.4 = (bf16[11,8,1024]{2,1,0:T(8,128)(2,1)}, bf16[11,8,1024]{2,1,0:T(8,128)(2,1)S(1)}, u32[]{:S(2)}, u32[]{:S(2)}) collective-permute-start(bf16[11,8,1024]{2,1,0:T(8,128)(2,1)} %param.13), channel_id=1, source_target_pairs={{0,1},{1,0},{2,3},{3,2},{4,5},{5,4},{6,7},{7,6},{8,9},{9,8},{10,11... | collective-permute-start | bytes 540680 | tf_op jit(solution)/shard_map/ppermute | solution.py:157
  20.9 0.9 %copy-start.5 = (f32[2,16,640]{2,1,0:T(8,128)S(1)}, f32[2,16,640]{2,1,0:T(8,128)}, u32[]{:S(2)}) copy-start(f32[2,16,640]{2,1,0:T(8,128)} %constant.100) | copy-start | bytes 245764
  20.9 0.9 %copy-start.6 = (f32[2,16,640]{2,1,0:T(8,128)S(1)}, f32[2,16,640]{2,1,0:T(8,128)}, u32[]{:S(2)}) copy-start(f32[2,16,640]{2,1,0:T(8,128)} %constant.91) | copy-start | bytes 245764
  21.0 0.9 %copy-start.7 = (f32[2,16,640]{2,1,0:T(8,128)S(1)}, f32[2,16,640]{2,1,0:T(8,128)}, u32[]{:S(2)}) copy-start(f32[2,16,640]{2,1,0:T(8,128)} %constant.94) | copy-start | bytes 245764
  21.0 1.0 %copy-start.8 = (f32[2,16,640]{2,1,0:T(8,128)S(1)}, f32[2,16,640]{2,1,0:T(8,128)}, u32[]{:S(2)}) copy-start(f32[2,16,640]{2,1,0:T(8,128)} %constant.97) | copy-start | bytes 245764
  21.9 2.5 %copy-start = (bf16[2,1024,640]{2,1,0:T(8,128)(2,1)}, bf16[2,1024,640]{2,1,0:T(8,128)(2,1)S(1)}, u32[]{:S(2)}) copy-start(bf16[2,1024,640]{2,1,0:T(8,128)(2,1)S(1)} %get-tuple-element.9) | copy-start | bytes 7864324
  25.6 1.4 %copy-start.4 = (f32[64,64,1]{1,0,2:T(8,128)S(1)}, f32[64,64,1]{1,0,2:T(8,128)}, u32[]{:S(2)}) copy-start(f32[64,64,1]{1,0,2:T(8,128)} %constant.110) | copy-start | bytes 49156
  27.0 3.6 %copy-start.11 = (s32[3,2,256]{2,1,0:T(2,128)S(1)}, s32[3,2,256]{2,1,0:T(2,128)}, u32[]{:S(2)}) copy-start(s32[3,2,256]{2,1,0:T(2,128)} %param.16) | copy-start | bytes 18436
  31.7 1.9 %copy-start.3 = (f32[2,16,16,640]{3,2,1,0:T(8,128)S(1)}, f32[2,16,16,640]{3,2,1,0:T(8,128)}, u32[]{:S(2)}) copy-start(f32[2,16,16,640]{3,2,1,0:T(8,128)} %multiply_add_fusion.1) | copy-start | bytes 3932164
  36.9 1.3 %copy-start.10 = (f32[64,32,1,1]{0,1,3,2:T(8,128)S(1)}, f32[64,32,1,1]{0,1,3,2:T(8,128)}, u32[]{:S(2)}) copy-start(f32[64,32,1,1]{0,1,3,2:T(8,128)} %constant.109) | copy-start | bytes 24580
  38.2 14.6 %copy-start.1 = (bf16[2,1024,640]{2,1,0:T(8,128)(2,1)S(1)}, bf16[2,1024,640]{2,1,0:T(8,128)(2,1)}, u32[]{:S(2)}) copy-start(bf16[2,1024,640]{2,1,0:T(8,128)(2,1)} %copy-done) | copy-start | bytes 7864324
  55.3 1.5 %copy-start.2 = (f32[11,1,64,640]{3,2,0,1:T(8,128)S(1)}, f32[11,1,64,640]{3,2,0,1:T(8,128)}, u32[]{:S(2)}) copy-start(f32[11,1,64,640]{3,2,0,1:T(8,128)} %convolution_bitcast_fusion.3) | copy-start | bytes 5406724
  57.0 2.6 %copy-start.9 = (f32[64,32,1,1]{0,1,3,2:T(8,128)S(1)}, f32[64,32,1,1]{0,1,3,2:T(8,128)}, u32[]{:S(2)}) copy-start(f32[64,32,1,1]{0,1,3,2:T(8,128)} %constant.111) | copy-start | bytes 24580
  59.5 0.8 copy-start.12
  63.7 3.7 %collective-permute-start.5 = (f32[4,32]{0,1:T(8,128)S(1)}, f32[4,32]{0,1:T(8,128)S(1)}, u32[]{:S(2)}, u32[]{:S(2)}) collective-permute-start(f32[4,32]{0,1:T(8,128)S(1)} %broadcast_select_fusion), channel_id=1, source_target_pairs={{0,1},{1,0},{2,3},{3,2},{4,5},{5,4},{6,7},{7,6},{8,9},{9,8},{10,11... | collective-permute-start | bytes 1544 | tf_op jit(solution)/shard_map/ppermute | solution.py:137
  65.3 2.2 %collective-permute-start.6 = (f32[4,32]{0,1:T(8,128)S(1)}, f32[4,32]{0,1:T(8,128)S(1)}, u32[]{:S(2)}, u32[]{:S(2)}) collective-permute-start(f32[4,32]{0,1:T(8,128)S(1)} %broadcast_select_fusion), channel_id=1, source_target_pairs={{0,2},{1,3},{2,0},{3,1},{4,6},{5,7},{6,4},{7,5},{8,10},{9,11},{10,... | collective-permute-start | bytes 1544 | tf_op jit(solution)/shard_map/ppermute | solution.py:137
  65.3 3.2 %collective-permute-start.7 = (f32[4,32]{0,1:T(8,128)S(1)}, f32[4,32]{0,1:T(8,128)S(1)}, u32[]{:S(2)}, u32[]{:S(2)}) collective-permute-start(f32[4,32]{0,1:T(8,128)S(1)} %broadcast_select_fusion), channel_id=1, source_target_pairs={{0,3},{1,2},{2,1},{3,0},{4,7},{5,6},{6,5},{7,4},{8,11},{9,10},{10,... | collective-permute-start | bytes 1544 | tf_op jit(solution)/shard_map/ppermute | solution.py:137
  68.6 4.7 %collective-permute-start.10 = (f32[4,32]{0,1:T(8,128)S(1)}, f32[4,32]{0,1:T(8,128)S(1)}, u32[]{:S(2)}, u32[]{:S(2)}) collective-permute-start(f32[4,32]{0,1:T(8,128)S(1)} %maximum_maximum_fusion.1), channel_id=1, source_target_pairs={{0,12},{1,13},{2,14},{3,15},{4,8},{5,9},{6,10},{7,11},{8,4},{9,5},... | collective-permute-start | bytes 1544 | tf_op jit(solution)/shard_map/ppermute | solution.py:137
  69.2 4.0 %collective-permute-start.8 = (f32[4,32]{0,1:T(8,128)S(1)}, f32[4,32]{0,1:T(8,128)S(1)}, u32[]{:S(2)}, u32[]{:S(2)}) collective-permute-start(f32[4,32]{0,1:T(8,128)S(1)} %maximum_maximum_fusion.1), channel_id=1, source_target_pairs={{0,4},{1,5},{2,6},{3,7},{4,0},{5,1},{6,2},{7,3},{8,12},{9,13},{10,... | collective-permute-start | bytes 1544 | tf_op jit(solution)/shard_map/ppermute | solution.py:137
  70.7 3.7 %collective-permute-start.9 = (f32[4,32]{0,1:T(8,128)S(1)}, f32[4,32]{0,1:T(8,128)S(1)}, u32[]{:S(2)}, u32[]{:S(2)}) collective-permute-start(f32[4,32]{0,1:T(8,128)S(1)} %maximum_maximum_fusion.1), channel_id=1, source_target_pairs={{0,8},{1,9},{2,10},{3,11},{4,12},{5,13},{6,14},{7,15},{8,0},{9,1},... | collective-permute-start | bytes 1544 | tf_op jit(solution)/shard_map/ppermute | solution.py:137
  74.5 4.6 %collective-permute-start.11 = (f32[4,32]{0,1:T(8,128)S(1)}, f32[4,32]{0,1:T(8,128)S(1)}, u32[]{:S(2)}, u32[]{:S(2)}) collective-permute-start(f32[4,32]{0,1:T(8,128)S(1)} %maximum_maximum_fusion), channel_id=1, source_target_pairs={{0,16},{1,17},{2,18},{3,19},{4,20},{5,21},{6,22},{7,23},{8,24},{9,... | collective-permute-start | bytes 1544 | tf_op jit(solution)/shard_map/ppermute | solution.py:137

commit v9 on v8

--- a/solution.py
+++ b/solution.py
@@ -151,11 +151,8 @@
         plane = lax.axis_index("plane")
         inner = lax.axis_index("inner")
         term = lax.axis_index("term")
-        groups = [lax.all_gather(receptor_grids, "inner", axis=1, tiled=True)]
-        for shift in range(1, term_count):
-            pairs = [(k, (k + shift) % term_count) for k in range(term_count)]
-            moved = lax.ppermute(receptor_grids, "term", pairs)
-            groups.append(lax.all_gather(moved, "inner", axis=1, tiled=True))
+        own_rows = lax.all_gather(receptor_grids, "inner", axis=1, tiled=True)
+        groups = gather_by_permutes(own_rows, "term", term_count, term)
         cell_blocks = gather_by_permutes(ligand_cells, "plane", plane_count, plane)
         cells_here = jnp.concatenate(cell_blocks, axis=1)
         share = cells_here.shape[1] // term_count

time: 80.6 us -> 73.6 us (0.913)
  blocking collectives: 17 us -> 8.44 us
  matrix products: 23.9 us -> 26.3 us
    all_gather x2 -> x1, blocking collectives: 17 us -> 8.44 us  [body(): own_rows = lax.all_gather(receptor_grids, 'inner', axis=1, tiled=True)]
    dot_general x2, matrix products: 2.27 us -> 3.61 us  [receptor_mixed(): jnp.einsum(form, grids, table_hi, preferred_element_type=jnp.float32)]
    dot_general x2, matrix products: 2.27 us -> 3.36 us  [receptor_mixed(): jnp.einsum(form, grids, table_lo, preferred_element_type=jnp.float32)]
    ppermute x4 -> x5, starting transfers between devices: 8.53 us -> 9.04 us  [gather_by_permutes(): blocks.append(lax.ppermute(values, axis_name, pairs))]
  transfers between devices with their start and end apart: 12 -> 12, of which waited for: 5 -> 5; matrix products, arithmetic and copies ran while one was open for 32% -> 34% of each run, Pallas kernels for 0% -> 0%
where the time goes in v9:
time: 73.6 us; the launch traced here: 73.3 us
  matrix products  26.3 us (36%)
  starting transfers between devices  15 us (20%)
  waiting for transfers between devices  9.22 us (13%)
  other arithmetic  8.86 us (12%)
  blocking collectives  8.44 us (11%)
  local copies, waits for them, and re-layouts  4.39 us (6%)
  between operations  1.02 us (1%)
    ppermute x7, waiting for transfers between devices, butterfly_max(): received.append(lax.ppermute(values, axes, pairs))  9.21 us
    ppermute x5, starting transfers between devices, gather_by_permutes(): blocks.append(lax.ppermute(values, axis_name, pairs))  9.04 us
    all_gather x1, blocking collectives, body(): own_rows = lax.all_gather(receptor_grids, 'inner', axis=1, tiled=True)  8.44 us
    dot_general x1, matrix products, ligand_spectra(): return jnp.einsum('pk,ntkq->tnpq', mix_tables(LB), plane, precision=HIGH)  5.99 us
    ppermute x7, starting transfers between devices, butterfly_max(): received.append(lax.ppermute(values, axes, pairs))  5.99 us
    dot_general x2, matrix products, receptor_mixed(): return jnp.einsum('pk,trkq->trpq', mix_tables(G), plane, precision=HIGH)  4.41 us
    dot_general x2, matrix products, receptor_mixed(): jnp.einsum(form, grids, table_hi, preferred_element_type=jnp.float32)  3.61 us
    add x2, other arithmetic, plane_table(): first[:, :, None, :] * second[:, None, :, :]  3.4 us
  transfers between devices with their start and end apart: 12, of which 5 were waited for; matrix products, arithmetic and copies ran while one was open for 34% of the time, Pallas kernels for 0%

profile of v9, /device:TPU:0, one launch (start us, length us, event | category | flops | bytes accessed | tf_op | source)
XLA Modules:
  0.0 73.3 jit_solution(18436507847303667763)
XLA Ops:
  0.6 3.1 %collective-permute-start.1 = (s32[3,2,256]{2,1,0:T(2,128)}, s32[3,2,256]{2,1,0:T(2,128)S(1)}, u32[]{:S(2)}, u32[]{:S(2)}) collective-permute-start(s32[3,2,256]{2,1,0:T(2,128)} %param.16), channel_id=1, source_target_pairs={{0,8},{8,16},{16,24},{24,0},{1,9},{9,17},{17,25},{25,1},{2,10},{10... | collective-permute-start | bytes 18440 | tf_op jit(solution)/shard_map/ppermute | solution.py:126
  3.7 2.6 %collective-permute-start.2 = (s32[3,2,256]{2,1,0:T(2,128)}, s32[3,2,256]{2,1,0:T(2,128)S(1)}, u32[]{:S(2)}, u32[]{:S(2)}) collective-permute-start(s32[3,2,256]{2,1,0:T(2,128)} %param.16), channel_id=1, source_target_pairs={{0,16},{8,24},{16,0},{24,8},{1,17},{9,25},{17,1},{25,9},{2,18},{10... | collective-permute-start | bytes 18440 | tf_op jit(solution)/shard_map/ppermute | solution.py:126
  6.3 1.3 %collective-permute-start.3 = (s32[3,2,256]{2,1,0:T(2,128)}, s32[3,2,256]{2,1,0:T(2,128)S(1)}, u32[]{:S(2)}, u32[]{:S(2)}) collective-permute-start(s32[3,2,256]{2,1,0:T(2,128)} %param.16), channel_id=1, source_target_pairs={{0,24},{8,0},{16,8},{24,16},{1,25},{9,1},{17,9},{25,17},{2,26},{10... | collective-permute-start | bytes 18440 | tf_op jit(solution)/shard_map/ppermute | solution.py:126
  8.4 1.5 %collective-permute-start = (f32[11,256]{1,0:T(8,128)S(1)}, f32[11,256]{1,0:T(8,128)S(1)}, u32[]{:S(2)}, u32[]{:S(2)}) collective-permute-start(f32[11,256]{1,0:T(8,128)S(1)} %broadcast_multiply_fusion), channel_id=1, source_target_pairs={{0,1},{1,0},{2,3},{3,2},{4,5},{5,4},{6,7},{7,6},{8,9},{9,8},{10,11... | collective-permute-start | bytes 33800 | tf_op jit(solution)/shard_map/ppermute | solution.py:126
  10.0 8.4 %all_gather.3 = bf16[11,32,1024]{2,1,0:T(8,128)(2,1)S(1)} all-gather(bf16[11,8,1024]{2,1,0:T(8,128)(2,1)} %param.13), channel_id=1, replica_groups=mesh['plane'=4,'inner'=4,'term'=2] {'inner'}, dimensions={1}, use_global_device_ids=true | all-gather | bytes 901120 | tf_op jit(solution)/shard_map/all_gather | solution.py:154
  18.9 2.0 %multiply_add_fusion = f32[2,32,32,640]{3,2,1,0:T(8,128)S(1)} fusion(f32[2,32,640]{2,1,0:T(8,128)} %constant.108, f32[2,32,640]{2,1,0:T(8,128)} %constant.106, f32[2,32,640]{2,1,0:T(8,128)} %constant.104, f32[2,32,640]{2,1,0:T(8,128)} %constant.102), kind=kLoop, calls=%fused_computation.4 | loop fusion | flops 3932160 | bytes 5898240 | tf_op jit(solution)/shard_map/twiddle_tables/add | solution.py:45
  21.0 0.9 %fusion = (bf16[2,1024,640]{2,1,0:T(8,128)(2,1)S(1)}, bf16[2,1024,640]{2,1,0:T(8,128)(2,1)S(1)}) fusion(f32[2,32,32,640]{3,2,1,0:T(8,128)S(1)} %multiply_add_fusion), kind=kLoop, calls=%fused_computation.3 | loop fusion | flops 5242880 | bytes 10485760 | tf_op jit(solution)/shard_map/twiddle_tables/convert_element_type | solution.py:52
  21.9 1.4 %multiply_add_fusion.1 = f32[2,16,16,640]{3,2,1,0:T(8,128)} fusion(f32[2,16,640]{2,1,0:T(8,128)S(1)} %copy-done.5, f32[2,16,640]{2,1,0:T(8,128)S(1)} %copy-done.8, f32[2,16,640]{2,1,0:T(8,128)S(1)} %copy-done.7, f32[2,16,640]{2,1,0:T(8,128)S(1)} %copy-done.6), kind=kLoop, calls=%fused_computation.34 | loop fusion | flops 983040 | bytes 1638400 | tf_op jit(solution)/shard_map/twiddle_tables/add | solution.py:45
  23.3 1.1 %fusion.5 = f32[2,640,11,32]{1,3,2,0:T(8,128)S(1)} fusion(bf16[2,1024,640]{2,1,0:T(8,128)(2,1)S(1)} %get-tuple-element.9, bf16[11,32,1024]{2,1,0:T(8,128)(2,1)S(1)} %all_gather.3), kind=kOutput, calls=%fused_computation.14 | convolution fusion | flops 922746880 | bytes 5144576 | tf_op jit(solution)/shard_map/receptor_spectra/trxc,hcq->trhxq/dot_general | solution.py:73
  24.5 1.1 %add_bitcast_fusion.1 = f32[11,1,2,32,640]{4,3,0,2,1:T(8,128)S(1)} fusion(f32[2,640,11,32]{1,3,2,0:T(8,128)S(1)} %fusion.5, bf16[2,1024,640]{2,1,0:T(8,128)(2,1)S(1)} %get-tuple-element.8, bf16[11,32,1024]{2,1,0:T(8,128)(2,1)S(1)} %all_gather.3), kind=kOutput, calls=%fused_computation.27 | convolution fusion | flops 923197440 | bytes 6946816 | tf_op jit(solution)/shard_map/receptor_spectra/trxc,hcq->trhxq/dot_general | solution.py:72
  25.6 1.4 %copy.21 = f32[11,1,2,32,640]{4,3,2,0,1:T(8,128)} copy(f32[11,1,2,32,640]{4,3,0,2,1:T(8,128)S(1)} %add_bitcast_fusion.1) | data formatting | bytes 3604480 | tf_op jit(solution)/shard_map/receptor_spectra/add | solution.py:73
  27.0 3.5 %convolution_bitcast_fusion.3 = f32[11,1,64,640]{3,2,0,1:T(8,128)} fusion(f32[11,64,640]{2,1,0:T(8,128)} %bitcast.160, f32[64,64,1]{1,0,2:T(8,128)S(1)} %copy-done.4), kind=kOutput, calls=%fused_computation.31 | convolution fusion | flops 173015040 | bytes 3620864 | tf_op jit(solution)/shard_map/receptor_spectra/pk,trkq->trpq/dot_general | solution.py:75
  31.0 0.8 %fusion.42 = f32[4,22,16,256]{3,1,2,0:T(8,128)S(1)} fusion(bf16[4,22,16,256]{3,2,1,0:T(8,128)(2,1)S(1)} %get-tuple-element.28, s32[4,256]{1,0:T(4,128)S(1)} %get-tuple-element.30), kind=kOutput, calls=%fused_computation.43 | convolution fusion | flops 184811520 | bytes 2166784 | tf_op jit(solution)/shard_map/ligand_spectra/ntxa,nac->ntxc/dot_general | solution.py:88
  31.9 1.0 %fusion.44 = f32[4,22,16,256]{3,1,2,0:T(8,128)S(1)} fusion(bf16[4,22,16,256]{3,2,1,0:T(8,128)(2,1)S(1)} %get-tuple-element.29, s32[4,256]{1,0:T(4,128)S(1)} %get-tuple-element.30), kind=kOutput, calls=%fused_computation.44 | convolution fusion | flops 184811520 | bytes 2166784 | tf_op jit(solution)/shard_map/ligand_spectra/ntxa,nac->ntxc/dot_general | solution.py:87
  32.9 3.3 %convolution_bitcast_fusion.1 = f32[4,22,2,16,640]{4,1,3,0,2:T(8,128)S(1)} fusion(f32[4,22,16,256]{3,1,2,0:T(8,128)S(1)} %fusion.44, f32[4,22,16,256]{3,1,2,0:T(8,128)S(1)} %fusion.42, f32[2,256,640]{2,1,0:T(8,128)S(1)} %bitcast.164), kind=kOutput, calls=%fused_computation.9 | convolution fusion | flops 2768601088 | bytes 11403264 | tf_op jit(solution)/shard_map/ligand_spectra/ntxc,hcq->nthxq/dot_general | solution.py:89
  36.2 1.3 %copy.20 = f32[4,22,2,16,640]{4,3,2,1,0:T(8,128)S(1)} copy(f32[4,22,2,16,640]{4,1,3,0,2:T(8,128)S(1)} %convolution_bitcast_fusion.1) | data formatting | bytes 14417920 | tf_op jit(solution)/shard_map/ligand_spectra/ntxc,hcq->nthxq/transpose | solution.py:89
  37.5 6.0 %convolution_bitcast_fusion = f32[22,4,64,640]{3,2,0,1:T(8,128)S(1)} fusion(f32[4,22,32,640]{3,2,1,0:T(8,128)S(1)} %bitcast.159, f32[64,32,1,1]{0,1,3,2:T(8,128)S(1)} %copy-done.10), kind=kOutput, calls=%fused_computation | convolution fusion | flops 692060160 | bytes 21635072 | tf_op jit(solution)/shard_map/ligand_spectra/pk,ntkq->tnpq/dot_general | solution.py:92
  43.5 2.2 %fusion.3 = f32[2,640,11,32]{1,3,2,0:T(8,128)S(1)} fusion(bf16[2,1024,640]{2,1,0:T(8,128)(2,1)S(1)} %copy-done.1, bf16[11,32,1024]{2,1,0:T(8,128)(2,1)} %collective-permute-done.4), kind=kOutput, calls=%fused_computation.12 | convolution fusion | flops 922746880 | bytes 5144576 | tf_op jit(solution)/shard_map/receptor_spectra/trxc,hcq->trhxq/dot_general | solution.py:73
  45.8 2.5 %add_bitcast_fusion = f32[11,1,2,32,640]{4,3,0,2,1:T(8,128)S(1)} fusion(f32[2,640,11,32]{1,3,2,0:T(8,128)S(1)} %fusion.3, bf16[2,1024,640]{2,1,0:T(8,128)(2,1)S(1)} %get-tuple-element.8, bf16[11,32,1024]{2,1,0:T(8,128)(2,1)} %collective-permute-done.4), kind=kOutput, calls=%fused_computation.26 | convolution fusion | flops 923197440 | bytes 6946816 | tf_op jit(solution)/shard_map/receptor_spectra/trxc,hcq->trhxq/dot_general | solution.py:72
  48.4 0.9 %convolution_bitcast_fusion.2 = f32[11,1,64,640]{3,2,0,1:T(8,128)S(1)} fusion(f32[11,64,640]{2,1,0:T(8,128)S(1)} %bitcast.161, f32[64,64,1]{1,0,2:T(8,128)S(1)} %copy-done.4), kind=kOutput, calls=%fused_computation.30 | convolution fusion | flops 173015040 | bytes 3620864 | tf_op jit(solution)/shard_map/receptor_spectra/pk,trkq->trpq/dot_general | solution.py:75
  50.2 2.5 %add_reduce_fusion = (f32[4,32,640]{2,1,0:T(8,128)S(1)}, f32[4,32,640]{2,1,0:T(8,128)S(1)}, f32[4,32,640]{2,1,0:T(8,128)S(1)}, f32[4,32,640]{2,1,0:T(8,128)S(1)}) fusion(f32[22,4,64,640]{3,2,0,1:T(8,128)S(1)} %convolution_bitcast_fusion, f32[11,32,640]{2,1,0:T(8,128)S(1)} %get-tuple-element.25, f32[11,32,640]{2,1,0:T(8,128)S(1)} %get-tuple-element.24, ...), kind=kLoop, calls=%fused_computation.6 | loop fusion | flops 14090240 | bytes 19333120 | tf_op jit(solution)/shard_map/correlate/reduce_sum | solution.py:100
  53.6 1.0 %fusion.23 = f32[4,32,1024]{2,1,0:T(8,128)S(1)} fusion(bf16[2,1024,640]{2,1,0:T(8,128)(2,1)S(1)} %get-tuple-element.8, bf16[1,4,32,2,640]{4,2,1,3,0:T(8,128)(2,1)S(1)} %get-tuple-element.10), kind=kOutput, calls=%fused_computation.35 | convolution fusion | flops 335544320 | bytes 3473408 | tf_op jit(solution)/shard_map/inverse_scores/rnxhq,hcq->rnxc/dot_general | solution.py:117
  54.6 1.0 %fusion.35 = f32[4,32,1024]{2,1,0:T(8,128)S(1)} fusion(f32[4,32,1024]{2,1,0:T(8,128)S(1)} %fusion.23, bf16[2,1024,640]{2,1,0:T(8,128)(2,1)S(1)} %get-tuple-element.8, bf16[1,4,32,2,640]{4,2,1,3,0:T(8,128)(2,1)S(1)} %get-tuple-element.11), kind=kOutput, calls=%fused_computation.39 | convolution fusion | flops 335675392 | bytes 3997696 | tf_op jit(solution)/shard_map/inverse_scores/rnxhq,hcq->rnxc/dot_general | solution.py:118
  55.6 1.1 %fusion.38 = f32[4]{0:T(128)S(1)} fusion(f32[4,32,1024]{2,1,0:T(8,128)S(1)} %fusion.35, bf16[2,1024,640]{2,1,0:T(8,128)(2,1)S(1)} %copy-done.1, bf16[1,4,32,2,640]{4,2,1,3,0:T(8,128)(2,1)S(1)} %get-tuple-element.10), kind=kOutput, calls=%fused_computation.40 | convolution fusion | flops 335806464 | bytes 3473424 | tf_op jit(solution)/shard_map/inverse_scores/rnxhq,hcq->rnxc/dot_general | solution.py:119
  56.9 1.5 %collective-permute-start.5 = (f32[4,32]{0,1:T(8,128)S(1)}, f32[4,32]{0,1:T(8,128)S(1)}, u32[]{:S(2)}, u32[]{:S(2)}) collective-permute-start(f32[4,32]{0,1:T(8,128)S(1)} %broadcast_select_fusion), channel_id=1, source_target_pairs={{0,1},{1,0},{2,3},{3,2},{4,5},{5,4},{6,7},{7,6},{8,9},{9,8},{10,11... | collective-permute-start | bytes 1544 | tf_op jit(solution)/shard_map/ppermute | solution.py:137
  59.0 1.6 %collective-permute-done.5 = f32[4,32]{0,1:T(8,128)S(1)} collective-permute-done((f32[4,32]{0,1:T(8,128)S(1)}, f32[4,32]{0,1:T(8,128)S(1)}, u32[]{:S(2)}, u32[]{:S(2)}) %collective-permute-start.5) | collective-permute-done | bytes 544 | tf_op jit(solution)/shard_map/ppermute | solution.py:137
  60.6 0.9 %collective-permute-done.7 = f32[4,32]{0,1:T(8,128)S(1)} collective-permute-done((f32[4,32]{0,1:T(8,128)S(1)}, f32[4,32]{0,1:T(8,128)S(1)}, u32[]{:S(2)}, u32[]{:S(2)}) %collective-permute-start.7) | collective-permute-done | bytes 544 | tf_op jit(solution)/shard_map/ppermute | solution.py:137
  62.3 1.5 %collective-permute-start.8 = (f32[4,32]{0,1:T(8,128)S(1)}, f32[4,32]{0,1:T(8,128)S(1)}, u32[]{:S(2)}, u32[]{:S(2)}) collective-permute-start(f32[4,32]{0,1:T(8,128)S(1)} %maximum_maximum_fusion.1), channel_id=1, source_target_pairs={{0,4},{1,5},{2,6},{3,7},{4,0},{5,1},{6,2},{7,3},{8,12},{9,13},{10,... | collective-permute-start | bytes 1544 | tf_op jit(solution)/shard_map/ppermute | solution.py:137
  63.8 1.4 %collective-permute-start.9 = (f32[4,32]{0,1:T(8,128)S(1)}, f32[4,32]{0,1:T(8,128)S(1)}, u32[]{:S(2)}, u32[]{:S(2)}) collective-permute-start(f32[4,32]{0,1:T(8,128)S(1)} %maximum_maximum_fusion.1), channel_id=1, source_target_pairs={{0,8},{1,9},{2,10},{3,11},{4,12},{5,13},{6,14},{7,15},{8,0},{9,1},... | collective-permute-start | bytes 1544 | tf_op jit(solution)/shard_map/ppermute | solution.py:137
  65.1 1.1 %collective-permute-done.10 = f32[4,32]{0,1:T(8,128)S(1)} collective-permute-done((f32[4,32]{0,1:T(8,128)S(1)}, f32[4,32]{0,1:T(8,128)S(1)}, u32[]{:S(2)}, u32[]{:S(2)}) %collective-permute-start.10) | collective-permute-done | bytes 544 | tf_op jit(solution)/shard_map/ppermute | solution.py:137
  66.3 1.2 %collective-permute-done.9 = f32[4,32]{0,1:T(8,128)S(1)} collective-permute-done((f32[4,32]{0,1:T(8,128)S(1)}, f32[4,32]{0,1:T(8,128)S(1)}, u32[]{:S(2)}, u32[]{:S(2)}) %collective-permute-start.9) | collective-permute-done | bytes 544 | tf_op jit(solution)/shard_map/ppermute | solution.py:137
  67.9 4.3 %collective-permute-done.11 = f32[4,32]{0,1:T(8,128)S(1)} collective-permute-done((f32[4,32]{0,1:T(8,128)S(1)}, f32[4,32]{0,1:T(8,128)S(1)}, u32[]{:S(2)}, u32[]{:S(2)}) %collective-permute-start.11) | collective-permute-done | bytes 544 | tf_op jit(solution)/shard_map/ppermute | solution.py:137
  (57 shorter events, 6.7 us)
Async XLA Ops:
  0.6 30.0 %collective-permute-start.1 = (s32[3,2,256]{2,1,0:T(2,128)}, s32[3,2,256]{2,1,0:T(2,128)S(1)}, u32[]{:S(2)}, u32[]{:S(2)}) collective-permute-start(s32[3,2,256]{2,1,0:T(2,128)} %param.16), channel_id=1, source_target_pairs={{0,8},{8,16},{16,24},{24,0},{1,9},{9,17},{17,25},{25,1},{2,10},{10... | collective-permute-start | bytes 18440 | tf_op jit(solution)/shard_map/ppermute | solution.py:126
  3.7 26.9 %collective-permute-start.2 = (s32[3,2,256]{2,1,0:T(2,128)}, s32[3,2,256]{2,1,0:T(2,128)S(1)}, u32[]{:S(2)}, u32[]{:S(2)}) collective-permute-start(s32[3,2,256]{2,1,0:T(2,128)} %param.16), channel_id=1, source_target_pairs={{0,16},{8,24},{16,0},{24,8},{1,17},{9,25},{17,1},{25,9},{2,18},{10... | collective-permute-start | bytes 18440 | tf_op jit(solution)/shard_map/ppermute | solution.py:126
  6.3 24.3 %collective-permute-start.3 = (s32[3,2,256]{2,1,0:T(2,128)}, s32[3,2,256]{2,1,0:T(2,128)S(1)}, u32[]{:S(2)}, u32[]{:S(2)}) collective-permute-start(s32[3,2,256]{2,1,0:T(2,128)} %param.16), channel_id=1, source_target_pairs={{0,24},{8,0},{16,8},{24,16},{1,25},{9,1},{17,9},{25,17},{2,26},{10... | collective-permute-start | bytes 18440 | tf_op jit(solution)/shard_map/ppermute | solution.py:126
  8.4 22.3 %collective-permute-start = (f32[11,256]{1,0:T(8,128)S(1)}, f32[11,256]{1,0:T(8,128)S(1)}, u32[]{:S(2)}, u32[]{:S(2)}) collective-permute-start(f32[11,256]{1,0:T(8,128)S(1)} %broadcast_multiply_fusion), channel_id=1, source_target_pairs={{0,1},{1,0},{2,3},{3,2},{4,5},{5,4},{6,7},{7,6},{8,9},{9,8},{10,11... | collective-permute-start | bytes 33800 | tf_op jit(solution)/shard_map/ppermute | solution.py:126
  18.4 25.1 %collective-permute-start.4 = (bf16[11,32,1024]{2,1,0:T(8,128)(2,1)S(1)}, bf16[11,32,1024]{2,1,0:T(8,128)(2,1)}, u32[]{:S(2)}, u32[]{:S(2)}) collective-permute-start(bf16[11,32,1024]{2,1,0:T(8,128)(2,1)S(1)} %all_gather.3), channel_id=1, source_target_pairs={{0,1},{1,0},{2,3},{3,2},{4,5},{5,4},{6,7},{7,6},{8,9},{9,8},{10,11... | collective-permute-start | bytes 2162696 | tf_op jit(solution)/shard_map/ppermute | solution.py:126
  20.9 0.9 %copy-start.5 = (f32[2,16,640]{2,1,0:T(8,128)S(1)}, f32[2,16,640]{2,1,0:T(8,128)}, u32[]{:S(2)}) copy-start(f32[2,16,640]{2,1,0:T(8,128)} %constant.100) | copy-start | bytes 245764
  20.9 0.9 %copy-start.6 = (f32[2,16,640]{2,1,0:T(8,128)S(1)}, f32[2,16,640]{2,1,0:T(8,128)}, u32[]{:S(2)}) copy-start(f32[2,16,640]{2,1,0:T(8,128)} %constant.91) | copy-start | bytes 245764
  20.9 0.9 %copy-start.7 = (f32[2,16,640]{2,1,0:T(8,128)S(1)}, f32[2,16,640]{2,1,0:T(8,128)}, u32[]{:S(2)}) copy-start(f32[2,16,640]{2,1,0:T(8,128)} %constant.94) | copy-start | bytes 245764
  21.0 1.0 %copy-start.8 = (f32[2,16,640]{2,1,0:T(8,128)S(1)}, f32[2,16,640]{2,1,0:T(8,128)}, u32[]{:S(2)}) copy-start(f32[2,16,640]{2,1,0:T(8,128)} %constant.97) | copy-start | bytes 245764
  21.9 2.5 %copy-start = (bf16[2,1024,640]{2,1,0:T(8,128)(2,1)}, bf16[2,1024,640]{2,1,0:T(8,128)(2,1)S(1)}, u32[]{:S(2)}) copy-start(bf16[2,1024,640]{2,1,0:T(8,128)(2,1)S(1)} %get-tuple-element.9) | copy-start | bytes 7864324
  25.6 1.4 %copy-start.4 = (f32[64,64,1]{1,0,2:T(8,128)S(1)}, f32[64,64,1]{1,0,2:T(8,128)}, u32[]{:S(2)}) copy-start(f32[64,64,1]{1,0,2:T(8,128)} %constant.110) | copy-start | bytes 49156
  27.0 3.6 %copy-start.11 = (s32[3,2,256]{2,1,0:T(2,128)S(1)}, s32[3,2,256]{2,1,0:T(2,128)}, u32[]{:S(2)}) copy-start(s32[3,2,256]{2,1,0:T(2,128)} %param.16) | copy-start | bytes 18436
  31.0 1.9 %copy-start.3 = (f32[2,16,16,640]{3,2,1,0:T(8,128)S(1)}, f32[2,16,16,640]{3,2,1,0:T(8,128)}, u32[]{:S(2)}) copy-start(f32[2,16,16,640]{3,2,1,0:T(8,128)} %multiply_add_fusion.1) | copy-start | bytes 3932164
  36.2 1.3 %copy-start.10 = (f32[64,32,1,1]{0,1,3,2:T(8,128)S(1)}, f32[64,32,1,1]{0,1,3,2:T(8,128)}, u32[]{:S(2)}) copy-start(f32[64,32,1,1]{0,1,3,2:T(8,128)} %constant.109) | copy-start | bytes 24580
  37.5 6.0 %copy-start.1 = (bf16[2,1024,640]{2,1,0:T(8,128)(2,1)S(1)}, bf16[2,1024,640]{2,1,0:T(8,128)(2,1)}, u32[]{:S(2)}) copy-start(bf16[2,1024,640]{2,1,0:T(8,128)(2,1)} %copy-done) | copy-start | bytes 7864324
  48.4 1.5 %copy-start.2 = (f32[11,1,64,640]{3,2,0,1:T(8,128)S(1)}, f32[11,1,64,640]{3,2,0,1:T(8,128)}, u32[]{:S(2)}) copy-start(f32[11,1,64,640]{3,2,0,1:T(8,128)} %convolution_bitcast_fusion.3) | copy-start | bytes 5406724
  50.1 2.6 %copy-start.9 = (f32[64,32,1,1]{0,1,3,2:T(8,128)S(1)}, f32[64,32,1,1]{0,1,3,2:T(8,128)}, u32[]{:S(2)}) copy-start(f32[64,32,1,1]{0,1,3,2:T(8,128)} %constant.111) | copy-start | bytes 24580
  52.7 0.8 %copy-start.12 = (f32[640]{0:T(1024)S(1)}, f32[640]{0:T(1024)}, u32[]{:S(2)}) copy-start(f32[640]{0:T(1024)} %constant.84.clone) | copy-start | bytes 7684
  56.9 3.7 %collective-permute-start.5 = (f32[4,32]{0,1:T(8,128)S(1)}, f32[4,32]{0,1:T(8,128)S(1)}, u32[]{:S(2)}, u32[]{:S(2)}) collective-permute-start(f32[4,32]{0,1:T(8,128)S(1)} %broadcast_select_fusion), channel_id=1, source_target_pairs={{0,1},{1,0},{2,3},{3,2},{4,5},{5,4},{6,7},{7,6},{8,9},{9,8},{10,11... | collective-permute-start | bytes 1544 | tf_op jit(solution)/shard_map/ppermute | solution.py:137
  58.4 2.2 %collective-permute-start.6 = (f32[4,32]{0,1:T(8,128)S(1)}, f32[4,32]{0,1:T(8,128)S(1)}, u32[]{:S(2)}, u32[]{:S(2)}) collective-permute-start(f32[4,32]{0,1:T(8,128)S(1)} %broadcast_select_fusion), channel_id=1, source_target_pairs={{0,2},{1,3},{2,0},{3,1},{4,6},{5,7},{6,4},{7,5},{8,10},{9,11},{10,... | collective-permute-start | bytes 1544 | tf_op jit(solution)/shard_map/ppermute | solution.py:137
  58.4 3.2 %collective-permute-start.7 = (f32[4,32]{0,1:T(8,128)S(1)}, f32[4,32]{0,1:T(8,128)S(1)}, u32[]{:S(2)}, u32[]{:S(2)}) collective-permute-start(f32[4,32]{0,1:T(8,128)S(1)} %broadcast_select_fusion), channel_id=1, source_target_pairs={{0,3},{1,2},{2,1},{3,0},{4,7},{5,6},{6,5},{7,4},{8,11},{9,10},{10,... | collective-permute-start | bytes 1544 | tf_op jit(solution)/shard_map/ppermute | solution.py:137
  61.6 4.6 %collective-permute-start.10 = (f32[4,32]{0,1:T(8,128)S(1)}, f32[4,32]{0,1:T(8,128)S(1)}, u32[]{:S(2)}, u32[]{:S(2)}) collective-permute-start(f32[4,32]{0,1:T(8,128)S(1)} %maximum_maximum_fusion.1), channel_id=1, source_target_pairs={{0,12},{1,13},{2,14},{3,15},{4,8},{5,9},{6,10},{7,11},{8,4},{9,5},... | collective-permute-start | bytes 1544 | tf_op jit(solution)/shard_map/ppermute | solution.py:137
  62.3 4.0 %collective-permute-start.8 = (f32[4,32]{0,1:T(8,128)S(1)}, f32[4,32]{0,1:T(8,128)S(1)}, u32[]{:S(2)}, u32[]{:S(2)}) collective-permute-start(f32[4,32]{0,1:T(8,128)S(1)} %maximum_maximum_fusion.1), channel_id=1, source_target_pairs={{0,4},{1,5},{2,6},{3,7},{4,0},{5,1},{6,2},{7,3},{8,12},{9,13},{10,... | collective-permute-start | bytes 1544 | tf_op jit(solution)/shard_map/ppermute | solution.py:137
  63.8 3.7 %collective-permute-start.9 = (f32[4,32]{0,1:T(8,128)S(1)}, f32[4,32]{0,1:T(8,128)S(1)}, u32[]{:S(2)}, u32[]{:S(2)}) collective-permute-start(f32[4,32]{0,1:T(8,128)S(1)} %maximum_maximum_fusion.1), channel_id=1, source_target_pairs={{0,8},{1,9},{2,10},{3,11},{4,12},{5,13},{6,14},{7,15},{8,0},{9,1},... | collective-permute-start | bytes 1544 | tf_op jit(solution)/shard_map/ppermute | solution.py:137
  67.5 4.6 %collective-permute-start.11 = (f32[4,32]{0,1:T(8,128)S(1)}, f32[4,32]{0,1:T(8,128)S(1)}, u32[]{:S(2)}, u32[]{:S(2)}) collective-permute-start(f32[4,32]{0,1:T(8,128)S(1)} %maximum_maximum_fusion), channel_id=1, source_target_pairs={{0,16},{1,17},{2,18},{3,19},{4,20},{5,21},{6,22},{7,23},{8,24},{9,... | collective-permute-start | bytes 1544 | tf_op jit(solution)/shard_map/ppermute | solution.py:137

commit v10 on v9

--- a/solution.py
+++ b/solution.py
@@ -64,7 +64,7 @@
     return jnp.asarray(np.concatenate([cos_x, sin_x], axis=0))
 
 
-def receptor_mixed(grids, table_hi, table_lo):
+def receptor_mixed(grids, table_hi, table_lo, mix):
     terms, rows, cells = grids.shape
     receptors = rows // G
     grids = grids.reshape(terms, receptors, G, cells)
@@ -72,7 +72,7 @@
     plane = jnp.einsum(form, grids, table_hi, preferred_element_type=jnp.float32)
     plane = plane + jnp.einsum(form, grids, table_lo, preferred_element_type=jnp.float32)
     plane = plane.reshape(terms, receptors, 2 * G, WIDTH)
-    return jnp.einsum("pk,trkq->trpq", mix_tables(G), plane, precision=HIGH)
+    return jnp.einsum("pk,trkq->trpq", mix, plane, precision=HIGH)
 
 
 def ligand_spectra(voxels, coefficients, box_table):
@@ -151,8 +151,18 @@
         plane = lax.axis_index("plane")
         inner = lax.axis_index("inner")
         term = lax.axis_index("term")
-        own_rows = lax.all_gather(receptor_grids, "inner", axis=1, tiled=True)
+        if inner_count <= 4:
+            row_blocks = gather_by_permutes(receptor_grids, "inner", inner_count, inner)
+            own_rows = jnp.concatenate(row_blocks, axis=1)
+            slot_inner = (inner - jnp.arange(inner_count, dtype=jnp.int32)) % inner_count
+        else:
+            own_rows = lax.all_gather(receptor_grids, "inner", axis=1, tiled=True)
+            slot_inner = jnp.arange(inner_count, dtype=jnp.int32)
         groups = gather_by_permutes(own_rows, "term", term_count, term)
+        row_order = slot_inner[:, None] * rows_here + jnp.arange(rows_here, dtype=jnp.int32)
+        row_order = row_order.reshape(-1)
+        rec_mix = mix_tables(G)
+        rec_mix = jnp.take(rec_mix, jnp.concatenate([row_order, row_order + G]), axis=1)
         cell_blocks = gather_by_permutes(ligand_cells, "plane", plane_count, plane)
         cells_here = jnp.concatenate(cell_blocks, axis=1)
         share = cells_here.shape[1] // term_count
@@ -174,7 +184,7 @@
         for index, grids in enumerate(groups):
             lo = index * terms_here
             with jax.named_scope("receptor_spectra"):
-                rec_spec = receptor_mixed(grids, table_hi, table_lo)
+                rec_spec = receptor_mixed(grids, table_hi, table_lo, rec_mix)
             with jax.named_scope("correlate"):
                 products = products + correlate(rec_spec, lig_spec[lo : lo + terms_here])
         with jax.named_scope("inverse_scores"):

time: 73.6 us -> 82.4 us (1.12)
  waiting for transfers between devices: 9.22 us -> 21.5 us
  blocking collectives: 8.44 us -> 0 us
  starting transfers between devices: 15 us -> 19 us
  local copies, waits for them, and re-layouts: 4.39 us -> 7 us
  matrix products: 26.3 us -> 23.9 us
  other arithmetic: 8.86 us -> 9.72 us
    ppermute x5 -> x8, waiting for transfers between devices: 0.01 us -> 10.8 us  [gather_by_permutes(): blocks.append(lax.ppermute(values, axis_name, pairs))]
    all_gather x1 -> x0, blocking collectives: 8.44 us -> none  [body(): own_rows = lax.all_gather(receptor_grids, 'inner', axis=1, tiled=True)]
    ppermute x5 -> x8, starting transfers between devices: 9.04 us -> 13.1 us  [gather_by_permutes(): blocks.append(lax.ppermute(values, axis_name, pairs))]
    dot_general x2, matrix products: 4.41 us -> 1.98 us  [receptor_mixed(): return jnp.einsum('pk,trkq->trpq', mix, plane, precision=HIGH)]
    unnamed x26 -> x31, local copies, waits for them, and re-layouts: 0.77 us -> 3.14 us
    convert_element_type x3, other arithmetic: 1.18 us -> 2.68 us  [split_bf16(): return (upper.astype(jnp.bfloat16), lower.astype(jnp.bfloat16))]
    ppermute x7, waiting for transfers between devices: 9.21 us -> 10.7 us  [butterfly_max(): received.append(lax.ppermute(values, axes, pairs))]
    add x2, local copies, waits for them, and re-layouts: 1.52 us -> 0.29 us  [receptor_mixed(): plane + jnp.einsum(form, grids, table_lo, preferred_element_type=jnp.floa...]
  transfers between devices with their start and end apart: 12 -> 15, of which waited for: 5 -> 8; matrix products, arithmetic and copies ran while one was open for 34% -> 35% of each run, Pallas kernels for 0% -> 0%
where the time goes in v10:
time: 82.4 us; the launch traced here: 82.1 us
  matrix products  23.9 us (29%)
  waiting for transfers between devices  21.5 us (26%)
  starting transfers between devices  19 us (23%)
  other arithmetic  9.72 us (12%)
  local copies, waits for them, and re-layouts  7 us (8%)
  between operations  1.04 us (1%)
    ppermute x8, starting transfers between devices, gather_by_permutes(): blocks.append(lax.ppermute(values, axis_name, pairs))  13.1 us
    ppermute x8, waiting for transfers between devices, gather_by_permutes(): blocks.append(lax.ppermute(values, axis_name, pairs))  10.8 us
    ppermute x7, waiting for transfers between devices, butterfly_max(): received.append(lax.ppermute(values, axes, pairs))  10.7 us
    dot_general x1, matrix products, ligand_spectra(): return jnp.einsum('pk,ntkq->tnpq', mix_tables(LB), plane, precision=HIGH)  6 us
    ppermute x7, starting transfers between devices, butterfly_max(): received.append(lax.ppermute(values, axes, pairs))  5.94 us
    dot_general x2, matrix products, receptor_mixed(): jnp.einsum(form, grids, table_hi, preferred_element_type=jnp.float32)  3.59 us
    dot_general x2, matrix products, receptor_mixed(): jnp.einsum(form, grids, table_lo, preferred_element_type=jnp.float32)  3.39 us
    dot_general x1, matrix products, ligand_spectra(): plane = jnp.einsum('ntxc,hcq->nthxq', grid, box_table, precision=HIGH)  3.28 us
  transfers between devices with their start and end apart: 15, of which 8 were waited for; matrix products, arithmetic and copies ran while one was open for 35% of the time, Pallas kernels for 0%

profile of v10, /device:TPU:0, one launch (start us, length us, event | category | flops | bytes accessed | tf_op | source)
XLA Modules:
  0.0 82.1 jit_solution(18064149566874359848)
XLA Ops:
  0.6 3.1 %collective-permute-start.1 = (s32[3,2,256]{2,1,0:T(2,128)}, s32[3,2,256]{2,1,0:T(2,128)S(1)}, u32[]{:S(2)}, u32[]{:S(2)}) collective-permute-start(s32[3,2,256]{2,1,0:T(2,128)} %param.15), channel_id=1, source_target_pairs={{0,8},{8,16},{16,24},{24,0},{1,9},{9,17},{17,25},{25,1},{2,10},{10... | collective-permute-start | bytes 18440 | tf_op jit(solution)/shard_map/ppermute | solution.py:126
  3.7 2.6 %collective-permute-start.2 = (s32[3,2,256]{2,1,0:T(2,128)}, s32[3,2,256]{2,1,0:T(2,128)S(1)}, u32[]{:S(2)}, u32[]{:S(2)}) collective-permute-start(s32[3,2,256]{2,1,0:T(2,128)} %param.15), channel_id=1, source_target_pairs={{0,16},{8,24},{16,0},{24,8},{1,17},{9,25},{17,1},{25,9},{2,18},{10... | collective-permute-start | bytes 18440 | tf_op jit(solution)/shard_map/ppermute | solution.py:126
  6.3 1.3 %collective-permute-start.3 = (s32[3,2,256]{2,1,0:T(2,128)}, s32[3,2,256]{2,1,0:T(2,128)S(1)}, u32[]{:S(2)}, u32[]{:S(2)}) collective-permute-start(s32[3,2,256]{2,1,0:T(2,128)} %param.15), channel_id=1, source_target_pairs={{0,24},{8,0},{16,8},{24,16},{1,25},{9,1},{17,9},{25,17},{2,26},{10... | collective-permute-start | bytes 18440 | tf_op jit(solution)/shard_map/ppermute | solution.py:126
  7.6 1.5 %collective-permute-start.5 = (bf16[11,8,1024]{2,1,0:T(8,128)(2,1)}, bf16[11,8,1024]{2,1,0:T(8,128)(2,1)S(1)}, u32[]{:S(2)}, u32[]{:S(2)}) collective-permute-start(bf16[11,8,1024]{2,1,0:T(8,128)(2,1)} %param.12), channel_id=1, source_target_pairs={{0,4},{2,6},{4,0},{6,2},{1,5},{3,7},{5,1},{7,3},{8,12},{10,14},{12... | collective-permute-start | bytes 540680 | tf_op jit(solution)/shard_map/ppermute | solution.py:126
  9.2 1.6 %constant_dynamic-update-slice_fusion.3 = bf16[11,32,1024]{2,1,0:T(8,128)(2,1)} fusion(bf16[11,8,1024]{2,1,0:T(8,128)(2,1)} %param.12), kind=kLoop, calls=%fused_computation.106 | loop fusion | bytes 360448
  11.1 2.0 %multiply_add_fusion = f32[2,32,32,640]{3,2,1,0:T(8,128)S(1)} fusion(f32[2,32,640]{2,1,0:T(8,128)} %constant.130, f32[2,32,640]{2,1,0:T(8,128)} %constant.128, f32[2,32,640]{2,1,0:T(8,128)} %constant.126, f32[2,32,640]{2,1,0:T(8,128)} %constant.124), kind=kLoop, calls=%fused_computation.5 | loop fusion | flops 3932160 | bytes 5898240 | tf_op jit(solution)/shard_map/twiddle_tables/add | solution.py:45
  13.2 2.4 %fusion = (bf16[2,1024,640]{2,1,0:T(8,128)(2,1)}, bf16[2,1024,640]{2,1,0:T(8,128)(2,1)S(1)}) fusion(f32[2,32,32,640]{3,2,1,0:T(8,128)S(1)} %multiply_add_fusion), kind=kLoop, calls=%fused_computation.4 | loop fusion | flops 5242880 | bytes 10485760 | tf_op jit(solution)/shard_map/twiddle_tables/convert_element_type | solution.py:52
  15.8 1.2 %multiply_add_fusion.1 = f32[2,16,16,640]{3,2,1,0:T(8,128)} fusion(f32[2,16,640]{2,1,0:T(8,128)S(1)} %copy-done.4, f32[2,16,640]{2,1,0:T(8,128)S(1)} %copy-done.5, f32[2,16,640]{2,1,0:T(8,128)S(1)} %copy-done.6, f32[2,16,640]{2,1,0:T(8,128)S(1)} %copy-done.7), kind=kLoop, calls=%fused_computation.35 | loop fusion | flops 983040 | bytes 1638400 | tf_op jit(solution)/shard_map/twiddle_tables/add | solution.py:45
  17.7 1.5 %collective-permute-start.6 = (bf16[11,8,1024]{2,1,0:T(8,128)(2,1)S(1)}, bf16[11,8,1024]{2,1,0:T(8,128)(2,1)S(1)}, u32[]{:S(2)}, u32[]{:S(2)}) collective-permute-start(bf16[11,8,1024]{2,1,0:T(8,128)(2,1)S(1)} %copy-done.3), channel_id=1, source_target_pairs={{0,6},{2,0},{4,2},{6,4},{1,7},{3,1},{5,3},{7,5},{8,14},{10,8},{12,... | collective-permute-start | bytes 540680 | tf_op jit(solution)/shard_map/ppermute | solution.py:126
  19.2 1.5 %collective-permute-start = (f32[11,256]{1,0:T(8,128)S(1)}, f32[11,256]{1,0:T(8,128)S(1)}, u32[]{:S(2)}, u32[]{:S(2)}) collective-permute-start(f32[11,256]{1,0:T(8,128)S(1)} %broadcast_multiply_fusion), channel_id=1, source_target_pairs={{0,1},{1,0},{2,3},{3,2},{4,5},{5,4},{6,7},{7,6},{8,9},{9,8},{10,11... | collective-permute-start | bytes 33800 | tf_op jit(solution)/shard_map/ppermute | solution.py:126
  20.8 2.1 %collective-permute-done = f32[11,256]{1,0:T(8,128)S(1)} collective-permute-done((f32[11,256]{1,0:T(8,128)S(1)}, f32[11,256]{1,0:T(8,128)S(1)}, u32[]{:S(2)}, u32[]{:S(2)}) %collective-permute-start) | collective-permute-done | bytes 11296 | tf_op jit(solution)/shard_map/ppermute | solution.py:126
  24.0 1.0 %fusion.42 = f32[4,22,16,256]{3,1,2,0:T(8,128)S(1)} fusion(bf16[4,22,16,256]{3,2,1,0:T(8,128)(2,1)S(1)} %get-tuple-element.28, s32[4,256]{1,0:T(4,128)S(1)} %get-tuple-element.30), kind=kOutput, calls=%fused_computation.44 | convolution fusion | flops 184811520 | bytes 2166784 | tf_op jit(solution)/shard_map/ligand_spectra/ntxa,nac->ntxc/dot_general | solution.py:88
  25.1 3.3 %convolution_bitcast_fusion.1 = f32[4,22,2,16,640]{4,1,3,0,2:T(8,128)S(1)} fusion(f32[4,22,16,256]{3,1,2,0:T(8,128)S(1)} %fusion.44, f32[4,22,16,256]{3,1,2,0:T(8,128)S(1)} %fusion.42, f32[2,256,640]{2,1,0:T(8,128)S(1)} %bitcast.171), kind=kOutput, calls=%fused_computation.10 | convolution fusion | flops 2768601088 | bytes 11403264 | tf_op jit(solution)/shard_map/ligand_spectra/ntxc,hcq->nthxq/dot_general | solution.py:89
  28.4 1.3 %copy.21 = f32[4,22,2,16,640]{4,3,2,1,0:T(8,128)S(1)} copy(f32[4,22,2,16,640]{4,1,3,0,2:T(8,128)S(1)} %convolution_bitcast_fusion.1) | data formatting | bytes 14417920 | tf_op jit(solution)/shard_map/ligand_spectra/ntxc,hcq->nthxq/transpose | solution.py:89
  29.7 6.0 %convolution_bitcast_fusion = f32[22,4,64,640]{3,2,0,1:T(8,128)S(1)} fusion(f32[4,22,32,640]{3,2,1,0:T(8,128)S(1)} %bitcast.166, f32[64,32,1,1]{0,1,3,2:T(8,128)S(1)} %copy-done.9), kind=kOutput, calls=%fused_computation.1 | convolution fusion | flops 692060160 | bytes 21635072 | tf_op jit(solution)/shard_map/ligand_spectra/pk,ntkq->tnpq/dot_general | solution.py:92
  37.8 1.5 %collective-permute-start.7 = (bf16[11,32,1024]{2,1,0:T(8,128)(2,1)}, bf16[11,32,1024]{2,1,0:T(8,128)(2,1)S(1)}, u32[]{:S(2)}, u32[]{:S(2)}) collective-permute-start(bf16[11,32,1024]{2,1,0:T(8,128)(2,1)} %constant_dynamic-update-slice_fusion), channel_id=1, source_target_pairs={{0,1},{1,0},{2,3},{3,2},{4,5},{5,4},{6,7},{7,6},{8,9},{9,8},{10,11... | collective-permute-start | bytes 2162696 | tf_op jit(solution)/shard_map/ppermute | solution.py:126
  39.4 2.3 %fusion.5 = f32[2,640,11,32]{1,3,2,0:T(8,128)S(1)} fusion(bf16[2,1024,640]{2,1,0:T(8,128)(2,1)S(1)} %copy-done, bf16[11,32,1024]{2,1,0:T(8,128)(2,1)} %constant_dynamic-update-slice_fusion), kind=kOutput, calls=%fused_computation.15 | convolution fusion | flops 922746880 | bytes 5144576 | tf_op jit(solution)/shard_map/receptor_spectra/trxc,hcq->trhxq/dot_general | solution.py:73
  41.6 2.5 %add_bitcast_fusion.1 = f32[11,1,2,32,640]{4,3,0,2,1:T(8,128)S(1)} fusion(f32[2,640,11,32]{1,3,2,0:T(8,128)S(1)} %fusion.5, bf16[2,1024,640]{2,1,0:T(8,128)(2,1)S(1)} %get-tuple-element.8, bf16[11,32,1024]{2,1,0:T(8,128)(2,1)} %constant_dynamic-update-slice_fusion), kind=kOutput, calls=%fused_computation.28 | convolution fusion | flops 923197440 | bytes 6946816 | tf_op jit(solution)/shard_map/receptor_spectra/trxc,hcq->trhxq/dot_general | solution.py:72
  45.4 8.6 %collective-permute-done.7 = bf16[11,32,1024]{2,1,0:T(8,128)(2,1)S(1)} collective-permute-done((bf16[11,32,1024]{2,1,0:T(8,128)(2,1)}, bf16[11,32,1024]{2,1,0:T(8,128)(2,1)S(1)}, u32[]{:S(2)}, u32[]{:S(2)}) %collective-permute-start.7) | collective-permute-done | bytes 720928 | tf_op jit(solution)/shard_map/ppermute | solution.py:126
  54.0 1.1 %fusion.3 = f32[2,640,11,32]{1,3,2,0:T(8,128)S(1)} fusion(bf16[2,1024,640]{2,1,0:T(8,128)(2,1)S(1)} %copy-done, bf16[11,32,1024]{2,1,0:T(8,128)(2,1)S(1)} %collective-permute-done.7), kind=kOutput, calls=%fused_computation.13 | convolution fusion | flops 922746880 | bytes 5144576 | tf_op jit(solution)/shard_map/receptor_spectra/trxc,hcq->trhxq/dot_general | solution.py:73
  55.1 1.1 %add_bitcast_fusion = f32[11,1,2,32,640]{4,3,0,2,1:T(8,128)S(1)} fusion(f32[2,640,11,32]{1,3,2,0:T(8,128)S(1)} %fusion.3, bf16[2,1024,640]{2,1,0:T(8,128)(2,1)S(1)} %get-tuple-element.8, bf16[11,32,1024]{2,1,0:T(8,128)(2,1)S(1)} %collective-permute-done.7), kind=kOutput, calls=%fused_computation.27 | convolution fusion | flops 923197440 | bytes 6946816 | tf_op jit(solution)/shard_map/receptor_spectra/trxc,hcq->trhxq/dot_general | solution.py:72
  57.6 2.5 %add_reduce_fusion = (f32[4,32,640]{2,1,0:T(8,128)S(1)}, f32[4,32,640]{2,1,0:T(8,128)S(1)}, f32[4,32,640]{2,1,0:T(8,128)S(1)}, f32[4,32,640]{2,1,0:T(8,128)S(1)}) fusion(f32[22,4,64,640]{3,2,0,1:T(8,128)S(1)} %convolution_bitcast_fusion, f32[11,32,640]{2,1,0:T(8,128)S(1)} %get-tuple-element.25, f32[11,32,640]{2,1,0:T(8,128)S(1)} %get-tuple-element.24, ...), kind=kLoop, calls=%fused_computation.7 | loop fusion | flops 14090240 | bytes 19333120 | tf_op jit(solution)/shard_map/correlate/reduce_sum | solution.py:100
  62.0 1.0 %fusion.35 = f32[4,32,1024]{2,1,0:T(8,128)S(1)} fusion(f32[4,32,1024]{2,1,0:T(8,128)S(1)} %fusion.23, bf16[2,1024,640]{2,1,0:T(8,128)(2,1)S(1)} %get-tuple-element.8, bf16[1,4,32,2,640]{4,2,1,3,0:T(8,128)(2,1)S(1)} %get-tuple-element.11), kind=kOutput, calls=%fused_computation.40 | convolution fusion | flops 335675392 | bytes 3997696 | tf_op jit(solution)/shard_map/inverse_scores/rnxhq,hcq->rnxc/dot_general | solution.py:118
  63.0 1.1 %fusion.38 = f32[4]{0:T(128)S(1)} fusion(f32[4,32,1024]{2,1,0:T(8,128)S(1)} %fusion.35, bf16[2,1024,640]{2,1,0:T(8,128)(2,1)S(1)} %copy-done, bf16[1,4,32,2,640]{4,2,1,3,0:T(8,128)(2,1)S(1)} %get-tuple-element.10), kind=kOutput, calls=%fused_computation.41 | convolution fusion | flops 335806464 | bytes 3473424 | tf_op jit(solution)/shard_map/inverse_scores/rnxhq,hcq->rnxc/dot_general | solution.py:119
  64.3 1.6 %collective-permute-start.9 = (f32[4,32]{0,1:T(8,128)S(1)}, f32[4,32]{0,1:T(8,128)S(1)}, u32[]{:S(2)}, u32[]{:S(2)}) collective-permute-start(f32[4,32]{0,1:T(8,128)S(1)} %broadcast_select_fusion), channel_id=1, source_target_pairs={{0,2},{1,3},{2,0},{3,1},{4,6},{5,7},{6,4},{7,5},{8,10},{9,11},{10,... | collective-permute-start | bytes 1544 | tf_op jit(solution)/shard_map/ppermute | solution.py:137
  66.4 1.1 %collective-permute-done.10 = f32[4,32]{0,1:T(8,128)S(1)} collective-permute-done((f32[4,32]{0,1:T(8,128)S(1)}, f32[4,32]{0,1:T(8,128)S(1)}, u32[]{:S(2)}, u32[]{:S(2)}) %collective-permute-start.10) | collective-permute-done | bytes 544 | tf_op jit(solution)/shard_map/ppermute | solution.py:137
  67.6 2.1 %collective-permute-done.8 = f32[4,32]{0,1:T(8,128)S(1)} collective-permute-done((f32[4,32]{0,1:T(8,128)S(1)}, f32[4,32]{0,1:T(8,128)S(1)}, u32[]{:S(2)}, u32[]{:S(2)}) %collective-permute-start.8) | collective-permute-done | bytes 544 | tf_op jit(solution)/shard_map/ppermute | solution.py:137
  69.7 1.5 %collective-permute-start.13 = (f32[4,32]{0,1:T(8,128)S(1)}, f32[4,32]{0,1:T(8,128)S(1)}, u32[]{:S(2)}, u32[]{:S(2)}) collective-permute-start(f32[4,32]{0,1:T(8,128)S(1)} %maximum_maximum_fusion.1), channel_id=1, source_target_pairs={{0,12},{1,13},{2,14},{3,15},{4,8},{5,9},{6,10},{7,11},{8,4},{9,5},... | collective-permute-start | bytes 1544 | tf_op jit(solution)/shard_map/ppermute | solution.py:137
  71.2 1.4 %collective-permute-start.12 = (f32[4,32]{0,1:T(8,128)S(1)}, f32[4,32]{0,1:T(8,128)S(1)}, u32[]{:S(2)}, u32[]{:S(2)}) collective-permute-start(f32[4,32]{0,1:T(8,128)S(1)} %maximum_maximum_fusion.1), channel_id=1, source_target_pairs={{0,8},{1,9},{2,10},{3,11},{4,12},{5,13},{6,14},{7,15},{8,0},{9,1},... | collective-permute-start | bytes 1544 | tf_op jit(solution)/shard_map/ppermute | solution.py:137
  73.2 1.1 %collective-permute-done.13 = f32[4,32]{0,1:T(8,128)S(1)} collective-permute-done((f32[4,32]{0,1:T(8,128)S(1)}, f32[4,32]{0,1:T(8,128)S(1)}, u32[]{:S(2)}, u32[]{:S(2)}) %collective-permute-start.13) | collective-permute-done | bytes 544 | tf_op jit(solution)/shard_map/ppermute | solution.py:137
  75.0 1.4 %collective-permute-done.11 = f32[4,32]{0,1:T(8,128)S(1)} collective-permute-done((f32[4,32]{0,1:T(8,128)S(1)}, f32[4,32]{0,1:T(8,128)S(1)}, u32[]{:S(2)}, u32[]{:S(2)}) %collective-permute-start.11) | collective-permute-done | bytes 544 | tf_op jit(solution)/shard_map/ppermute | solution.py:137
  76.7 4.3 %collective-permute-done.14 = f32[4,32]{0,1:T(8,128)S(1)} collective-permute-done((f32[4,32]{0,1:T(8,128)S(1)}, f32[4,32]{0,1:T(8,128)S(1)}, u32[]{:S(2)}, u32[]{:S(2)}) %collective-permute-start.14) | collective-permute-done | bytes 544 | tf_op jit(solution)/shard_map/ppermute | solution.py:137
  (77 shorter events, 12.3 us)
Async XLA Ops:
  0.6 17.1 %collective-permute-start.1 = (s32[3,2,256]{2,1,0:T(2,128)}, s32[3,2,256]{2,1,0:T(2,128)S(1)}, u32[]{:S(2)}, u32[]{:S(2)}) collective-permute-start(s32[3,2,256]{2,1,0:T(2,128)} %param.15), channel_id=1, source_target_pairs={{0,8},{8,16},{16,24},{24,0},{1,9},{9,17},{17,25},{25,1},{2,10},{10... | collective-permute-start | bytes 18440 | tf_op jit(solution)/shard_map/ppermute | solution.py:126
  3.7 15.5 %collective-permute-start.2 = (s32[3,2,256]{2,1,0:T(2,128)}, s32[3,2,256]{2,1,0:T(2,128)S(1)}, u32[]{:S(2)}, u32[]{:S(2)}) collective-permute-start(s32[3,2,256]{2,1,0:T(2,128)} %param.15), channel_id=1, source_target_pairs={{0,16},{8,24},{16,0},{24,8},{1,17},{9,25},{17,1},{25,9},{2,18},{10... | collective-permute-start | bytes 18440 | tf_op jit(solution)/shard_map/ppermute | solution.py:126
  6.3 14.4 %collective-permute-start.3 = (s32[3,2,256]{2,1,0:T(2,128)}, s32[3,2,256]{2,1,0:T(2,128)S(1)}, u32[]{:S(2)}, u32[]{:S(2)}) collective-permute-start(s32[3,2,256]{2,1,0:T(2,128)} %param.15), channel_id=1, source_target_pairs={{0,24},{8,0},{16,8},{24,16},{1,25},{9,1},{17,9},{25,17},{2,26},{10... | collective-permute-start | bytes 18440 | tf_op jit(solution)/shard_map/ppermute | solution.py:126
  7.6 28.0 %collective-permute-start.4 = (bf16[11,8,1024]{2,1,0:T(8,128)(2,1)}, bf16[11,8,1024]{2,1,0:T(8,128)(2,1)S(1)}, u32[]{:S(2)}, u32[]{:S(2)}) collective-permute-start(bf16[11,8,1024]{2,1,0:T(8,128)(2,1)} %param.12), channel_id=1, source_target_pairs={{0,2},{2,4},{4,6},{6,0},{1,3},{3,5},{5,7},{7,1},{8,10},{10,12},{12... | collective-permute-start | bytes 540680 | tf_op jit(solution)/shard_map/ppermute | solution.py:126
  7.6 28.7 %collective-permute-start.5 = (bf16[11,8,1024]{2,1,0:T(8,128)(2,1)}, bf16[11,8,1024]{2,1,0:T(8,128)(2,1)S(1)}, u32[]{:S(2)}, u32[]{:S(2)}) collective-permute-start(bf16[11,8,1024]{2,1,0:T(8,128)(2,1)} %param.12), channel_id=1, source_target_pairs={{0,4},{2,6},{4,0},{6,2},{1,5},{3,7},{5,1},{7,3},{8,12},{10,14},{12... | collective-permute-start | bytes 540680 | tf_op jit(solution)/shard_map/ppermute | solution.py:126
  13.1 2.6 %copy-start.10 = (f32[11,256]{1,0:T(8,128)S(1)}, f32[11,256]{1,0:T(8,128)}, u32[]{:S(2)}) copy-start(f32[11,256]{1,0:T(8,128)} %param.14) | copy-start | bytes 33796
  13.1 2.5 %copy-start.13 = (f32[11]{0:T(128)S(1)}, f32[11]{0:T(128)}, u32[]{:S(2)}) copy-start(f32[11]{0:T(128)} %param.13) | copy-start | bytes 136
  13.1 2.6 %copy-start.4 = (f32[2,16,640]{2,1,0:T(8,128)S(1)}, f32[2,16,640]{2,1,0:T(8,128)}, u32[]{:S(2)}) copy-start(f32[2,16,640]{2,1,0:T(8,128)} %constant.122) | copy-start | bytes 245764
  13.1 2.6 %copy-start.5 = (f32[2,16,640]{2,1,0:T(8,128)S(1)}, f32[2,16,640]{2,1,0:T(8,128)}, u32[]{:S(2)}) copy-start(f32[2,16,640]{2,1,0:T(8,128)} %constant.119) | copy-start | bytes 245764
  13.2 2.6 %copy-start.6 = (f32[2,16,640]{2,1,0:T(8,128)S(1)}, f32[2,16,640]{2,1,0:T(8,128)}, u32[]{:S(2)}) copy-start(f32[2,16,640]{2,1,0:T(8,128)} %constant.116) | copy-start | bytes 245764
  13.2 2.6 %copy-start.7 = (f32[2,16,640]{2,1,0:T(8,128)S(1)}, f32[2,16,640]{2,1,0:T(8,128)}, u32[]{:S(2)}) copy-start(f32[2,16,640]{2,1,0:T(8,128)} %constant.113) | copy-start | bytes 245764
  13.2 3.9 %copy-start.1 = (f32[64,64]{0,1:T(8,128)S(1)}, f32[64,64]{0,1:T(8,128)}, u32[]{:S(2)}) copy-start(f32[64,64]{0,1:T(8,128)} %constant.99.clone) | copy-start | bytes 49156
  13.2 4.5 %copy-start.3 = (bf16[11,8,1024]{2,1,0:T(8,128)(2,1)S(1)}, bf16[11,8,1024]{2,1,0:T(8,128)(2,1)}, u32[]{:S(2)}) copy-start(bf16[11,8,1024]{2,1,0:T(8,128)(2,1)} %param.12) | copy-start | bytes 540676
  13.2 7.5 %copy-start.11 = (s32[3,2,256]{2,1,0:T(2,128)S(1)}, s32[3,2,256]{2,1,0:T(2,128)}, u32[]{:S(2)}) copy-start(s32[3,2,256]{2,1,0:T(2,128)} %param.15) | copy-start | bytes 18436
  17.7 19.4 %collective-permute-start.6 = (bf16[11,8,1024]{2,1,0:T(8,128)(2,1)S(1)}, bf16[11,8,1024]{2,1,0:T(8,128)(2,1)S(1)}, u32[]{:S(2)}, u32[]{:S(2)}) collective-permute-start(bf16[11,8,1024]{2,1,0:T(8,128)(2,1)S(1)} %copy-done.3), channel_id=1, source_target_pairs={{0,6},{2,0},{4,2},{6,4},{1,7},{3,1},{5,3},{7,5},{8,14},{10,8},{12,... | collective-permute-start | bytes 540680 | tf_op jit(solution)/shard_map/ppermute | solution.py:126
  19.2 3.7 %collective-permute-start = (f32[11,256]{1,0:T(8,128)S(1)}, f32[11,256]{1,0:T(8,128)S(1)}, u32[]{:S(2)}, u32[]{:S(2)}) collective-permute-start(f32[11,256]{1,0:T(8,128)S(1)} %broadcast_multiply_fusion), channel_id=1, source_target_pairs={{0,1},{1,0},{2,3},{3,2},{4,5},{5,4},{6,7},{7,6},{8,9},{9,8},{10,11... | collective-permute-start | bytes 33800 | tf_op jit(solution)/shard_map/ppermute | solution.py:126
  23.2 1.9 %copy-start.2 = (f32[2,16,16,640]{3,2,1,0:T(8,128)S(1)}, f32[2,16,16,640]{3,2,1,0:T(8,128)}, u32[]{:S(2)}) copy-start(f32[2,16,16,640]{3,2,1,0:T(8,128)} %multiply_add_fusion.1) | copy-start | bytes 3932164
  28.4 1.3 %copy-start.9 = (f32[64,32,1,1]{0,1,3,2:T(8,128)S(1)}, f32[64,32,1,1]{0,1,3,2:T(8,128)}, u32[]{:S(2)}) copy-start(f32[64,32,1,1]{0,1,3,2:T(8,128)} %constant.131) | copy-start | bytes 24580
  29.7 9.7 %copy-start = (bf16[2,1024,640]{2,1,0:T(8,128)(2,1)S(1)}, bf16[2,1024,640]{2,1,0:T(8,128)(2,1)}, u32[]{:S(2)}) copy-start(bf16[2,1024,640]{2,1,0:T(8,128)(2,1)} %get-tuple-element.9) | copy-start | bytes 7864324
  37.8 16.2 %collective-permute-start.7 = (bf16[11,32,1024]{2,1,0:T(8,128)(2,1)}, bf16[11,32,1024]{2,1,0:T(8,128)(2,1)S(1)}, u32[]{:S(2)}, u32[]{:S(2)}) collective-permute-start(bf16[11,32,1024]{2,1,0:T(8,128)(2,1)} %constant_dynamic-update-slice_fusion), channel_id=1, source_target_pairs={{0,1},{1,0},{2,3},{3,2},{4,5},{5,4},{6,7},{7,6},{8,9},{9,8},{10,11... | collective-permute-start | bytes 2162696 | tf_op jit(solution)/shard_map/ppermute | solution.py:126
  57.6 2.6 %copy-start.8 = (f32[64,32,1,1]{0,1,3,2:T(8,128)S(1)}, f32[64,32,1,1]{0,1,3,2:T(8,128)}, u32[]{:S(2)}) copy-start(f32[64,32,1,1]{0,1,3,2:T(8,128)} %constant.132) | copy-start | bytes 24580
  60.1 0.8 copy-start.12
  64.3 3.3 %collective-permute-start.10 = (f32[4,32]{0,1:T(8,128)S(1)}, f32[4,32]{0,1:T(8,128)S(1)}, u32[]{:S(2)}, u32[]{:S(2)}) collective-permute-start(f32[4,32]{0,1:T(8,128)S(1)} %broadcast_select_fusion), channel_id=1, source_target_pairs={{0,3},{1,2},{2,1},{3,0},{4,7},{5,6},{6,5},{7,4},{8,11},{9,10},{10,... | collective-permute-start | bytes 1544 | tf_op jit(solution)/shard_map/ppermute | solution.py:137
  64.3 3.3 %collective-permute-start.9 = (f32[4,32]{0,1:T(8,128)S(1)}, f32[4,32]{0,1:T(8,128)S(1)}, u32[]{:S(2)}, u32[]{:S(2)}) collective-permute-start(f32[4,32]{0,1:T(8,128)S(1)} %broadcast_select_fusion), channel_id=1, source_target_pairs={{0,2},{1,3},{2,0},{3,1},{4,6},{5,7},{6,4},{7,5},{8,10},{9,11},{10,... | collective-permute-start | bytes 1544 | tf_op jit(solution)/shard_map/ppermute | solution.py:137
  65.9 3.7 %collective-permute-start.8 = (f32[4,32]{0,1:T(8,128)S(1)}, f32[4,32]{0,1:T(8,128)S(1)}, u32[]{:S(2)}, u32[]{:S(2)}) collective-permute-start(f32[4,32]{0,1:T(8,128)S(1)} %broadcast_select_fusion), channel_id=1, source_target_pairs={{0,1},{1,0},{2,3},{3,2},{4,5},{5,4},{6,7},{7,6},{8,9},{9,8},{10,11... | collective-permute-start | bytes 1544 | tf_op jit(solution)/shard_map/ppermute | solution.py:137
  69.7 4.6 %collective-permute-start.13 = (f32[4,32]{0,1:T(8,128)S(1)}, f32[4,32]{0,1:T(8,128)S(1)}, u32[]{:S(2)}, u32[]{:S(2)}) collective-permute-start(f32[4,32]{0,1:T(8,128)S(1)} %maximum_maximum_fusion.1), channel_id=1, source_target_pairs={{0,12},{1,13},{2,14},{3,15},{4,8},{5,9},{6,10},{7,11},{8,4},{9,5},... | collective-permute-start | bytes 1544 | tf_op jit(solution)/shard_map/ppermute | solution.py:137
  71.2 3.7 %collective-permute-start.12 = (f32[4,32]{0,1:T(8,128)S(1)}, f32[4,32]{0,1:T(8,128)S(1)}, u32[]{:S(2)}, u32[]{:S(2)}) collective-permute-start(f32[4,32]{0,1:T(8,128)S(1)} %maximum_maximum_fusion.1), channel_id=1, source_target_pairs={{0,8},{1,9},{2,10},{3,11},{4,12},{5,13},{6,14},{7,15},{8,0},{9,1},... | collective-permute-start | bytes 1544 | tf_op jit(solution)/shard_map/ppermute | solution.py:137
  72.6 3.7 %collective-permute-start.11 = (f32[4,32]{0,1:T(8,128)S(1)}, f32[4,32]{0,1:T(8,128)S(1)}, u32[]{:S(2)}, u32[]{:S(2)}) collective-permute-start(f32[4,32]{0,1:T(8,128)S(1)} %maximum_maximum_fusion.1), channel_id=1, source_target_pairs={{0,4},{1,5},{2,6},{3,7},{4,0},{5,1},{6,2},{7,3},{8,12},{9,13},{10,... | collective-permute-start | bytes 1544 | tf_op jit(solution)/shard_map/ppermute | solution.py:137
  76.4 4.6 %collective-permute-start.14 = (f32[4,32]{0,1:T(8,128)S(1)}, f32[4,32]{0,1:T(8,128)S(1)}, u32[]{:S(2)}, u32[]{:S(2)}) collective-permute-start(f32[4,32]{0,1:T(8,128)S(1)} %maximum_maximum_fusion), channel_id=1, source_target_pairs={{0,16},{1,17},{2,18},{3,19},{4,20},{5,21},{6,22},{7,23},{8,24},{9,... | collective-permute-start | bytes 1544 | tf_op jit(solution)/shard_map/ppermute | solution.py:137

commit v11 on v9

--- a/solution.py
+++ b/solution.py
@@ -64,13 +64,11 @@
     return jnp.asarray(np.concatenate([cos_x, sin_x], axis=0))
 
 
-def receptor_mixed(grids, table_hi, table_lo):
+def receptor_mixed(grids, table_hi):
     terms, rows, cells = grids.shape
     receptors = rows // G
     grids = grids.reshape(terms, receptors, G, cells)
-    form = "trxc,hcq->trhxq"
-    plane = jnp.einsum(form, grids, table_hi, preferred_element_type=jnp.float32)
-    plane = plane + jnp.einsum(form, grids, table_lo, preferred_element_type=jnp.float32)
+    plane = jnp.einsum("trxc,hcq->trhxq", grids, table_hi, preferred_element_type=jnp.float32)
     plane = plane.reshape(terms, receptors, 2 * G, WIDTH)
     return jnp.einsum("pk,trkq->trpq", mix_tables(G), plane, precision=HIGH)
 
@@ -174,7 +172,7 @@
         for index, grids in enumerate(groups):
             lo = index * terms_here
             with jax.named_scope("receptor_spectra"):
-                rec_spec = receptor_mixed(grids, table_hi, table_lo)
+                rec_spec = receptor_mixed(grids, table_hi)
             with jax.named_scope("correlate"):
                 products = products + correlate(rec_spec, lig_spec[lo : lo + terms_here])
         with jax.named_scope("inverse_scores"):

time: 73.6 us -> 71.9 us (0.977)
  matrix products: 26.3 us -> 22.9 us
  other arithmetic: 8.86 us -> 10.2 us
    dot_general x4 -> x2, matrix products: 6.97 us -> 3.33 us  [receptor_mixed(): jnp.einsum('trxc,hcq->trhxq', grids, table_hi, preferred_element_type=jnp...]
    add x2 -> x0, local copies, waits for them, and re-layouts: 1.52 us -> none  [receptor_mixed(): plane + jnp.einsum(form, grids, table_lo, preferred_element_type=jnp.floa...]
    transpose x0 -> x2, local copies, waits for them, and re-layouts: none -> 1.52 us  [receptor_mixed(): jnp.einsum('trxc,hcq->trhxq', grids, table_hi, preferred_element_type=jnp...]
    convert_element_type x3, other arithmetic: 1.18 us -> 2.7 us  [split_bf16(): return (upper.astype(jnp.bfloat16), lower.astype(jnp.bfloat16))]
  transfers between devices with their start and end apart: 12 -> 12, of which waited for: 5 -> 5; matrix products, arithmetic and copies ran while one was open for 34% -> 35% of each run, Pallas kernels for 0% -> 0%
where the time goes in v11:
time: 71.9 us; the launch traced here: 71.6 us
  matrix products  22.9 us (32%)
  starting transfers between devices  15 us (21%)
  other arithmetic  10.2 us (14%)
  waiting for transfers between devices  9.26 us (13%)
  blocking collectives  8.44 us (12%)
  local copies, waits for them, and re-layouts  4.78 us (7%)
  between operations  0.98 us (1%)
    ppermute x7, waiting for transfers between devices, butterfly_max(): received.append(lax.ppermute(values, axes, pairs))  9.25 us
    ppermute x5, starting transfers between devices, gather_by_permutes(): blocks.append(lax.ppermute(values, axis_name, pairs))  9.04 us
    all_gather x1, blocking collectives, body(): own_rows = lax.all_gather(receptor_grids, 'inner', axis=1, tiled=True)  8.44 us
    dot_general x1, matrix products, ligand_spectra(): return jnp.einsum('pk,ntkq->tnpq', mix_tables(LB), plane, precision=HIGH)  6 us
    ppermute x7, starting transfers between devices, butterfly_max(): received.append(lax.ppermute(values, axes, pairs))  5.98 us
    dot_general x2, matrix products, receptor_mixed(): return jnp.einsum('pk,trkq->trpq', mix_tables(G), plane, precision=HIGH)  4.66 us
    dot_general x2, matrix products, receptor_mixed(): jnp.einsum('trxc,hcq->trhxq', grids, table_hi, preferred_element_type=jnp...  3.33 us
    dot_general x1, matrix products, ligand_spectra(): plane = jnp.einsum('ntxc,hcq->nthxq', grid, box_table, precision=HIGH)  3.28 us
  transfers between devices with their start and end apart: 12, of which 5 were waited for; matrix products, arithmetic and copies ran while one was open for 35% of the time, Pallas kernels for 0%

profile of v11, /device:TPU:0, one launch (start us, length us, event | category | flops | bytes accessed | tf_op | source)
XLA Modules:
  0.0 71.6 jit_solution(6601497767526081060)
XLA Ops:
  0.6 3.1 %collective-permute-start.1 = (s32[3,2,256]{2,1,0:T(2,128)}, s32[3,2,256]{2,1,0:T(2,128)S(1)}, u32[]{:S(2)}, u32[]{:S(2)}) collective-permute-start(s32[3,2,256]{2,1,0:T(2,128)} %param.16), channel_id=1, source_target_pairs={{0,8},{8,16},{16,24},{24,0},{1,9},{9,17},{17,25},{25,1},{2,10},{10... | collective-permute-start | bytes 18440 | tf_op jit(solution)/shard_map/ppermute | solution.py:124
  3.7 2.6 %collective-permute-start.2 = (s32[3,2,256]{2,1,0:T(2,128)}, s32[3,2,256]{2,1,0:T(2,128)S(1)}, u32[]{:S(2)}, u32[]{:S(2)}) collective-permute-start(s32[3,2,256]{2,1,0:T(2,128)} %param.16), channel_id=1, source_target_pairs={{0,16},{8,24},{16,0},{24,8},{1,17},{9,25},{17,1},{25,9},{2,18},{10... | collective-permute-start | bytes 18440 | tf_op jit(solution)/shard_map/ppermute | solution.py:124
  6.3 1.3 %collective-permute-start.3 = (s32[3,2,256]{2,1,0:T(2,128)}, s32[3,2,256]{2,1,0:T(2,128)S(1)}, u32[]{:S(2)}, u32[]{:S(2)}) collective-permute-start(s32[3,2,256]{2,1,0:T(2,128)} %param.16), channel_id=1, source_target_pairs={{0,24},{8,0},{16,8},{24,16},{1,25},{9,1},{17,9},{25,17},{2,26},{10... | collective-permute-start | bytes 18440 | tf_op jit(solution)/shard_map/ppermute | solution.py:124
  7.6 0.8 %broadcast_multiply_fusion = f32[11,256]{1,0:T(8,128)S(1)} fusion(f32[11,256]{1,0:T(8,128)} %param.15, f32[11]{0:T(128)} %param.14), kind=kLoop, calls=%fused_computation.89 | loop fusion | flops 2816 | bytes 22572 | tf_op jit(solution)/shard_map/mul | solution.py:161
  8.4 1.5 %collective-permute-start = (f32[11,256]{1,0:T(8,128)S(1)}, f32[11,256]{1,0:T(8,128)S(1)}, u32[]{:S(2)}, u32[]{:S(2)}) collective-permute-start(f32[11,256]{1,0:T(8,128)S(1)} %broadcast_multiply_fusion), channel_id=1, source_target_pairs={{0,1},{1,0},{2,3},{3,2},{4,5},{5,4},{6,7},{7,6},{8,9},{9,8},{10,11... | collective-permute-start | bytes 33800 | tf_op jit(solution)/shard_map/ppermute | solution.py:124
  10.0 8.4 %all_gather.3 = bf16[11,32,1024]{2,1,0:T(8,128)(2,1)S(1)} all-gather(bf16[11,8,1024]{2,1,0:T(8,128)(2,1)} %param.13), channel_id=1, replica_groups=mesh['plane'=4,'inner'=4,'term'=2] {'inner'}, dimensions={1}, use_global_device_ids=true | all-gather | bytes 901120 | tf_op jit(solution)/shard_map/all_gather | solution.py:152
  18.9 2.0 %multiply_add_fusion = f32[2,32,32,640]{3,2,1,0:T(8,128)S(1)} fusion(f32[2,32,640]{2,1,0:T(8,128)} %constant.108, f32[2,32,640]{2,1,0:T(8,128)} %constant.106, f32[2,32,640]{2,1,0:T(8,128)} %constant.104, f32[2,32,640]{2,1,0:T(8,128)} %constant.102), kind=kLoop, calls=%fused_computation.4 | loop fusion | flops 3932160 | bytes 5898240 | tf_op jit(solution)/shard_map/twiddle_tables/add | solution.py:45
  21.0 2.4 %fusion = (bf16[2,1024,640]{2,1,0:T(8,128)(2,1)}, bf16[2,1024,640]{2,1,0:T(8,128)(2,1)S(1)}) fusion(f32[2,32,32,640]{3,2,1,0:T(8,128)S(1)} %multiply_add_fusion), kind=kLoop, calls=%fused_computation.3 | loop fusion | flops 5242880 | bytes 10485760 | tf_op jit(solution)/shard_map/twiddle_tables/convert_element_type | solution.py:52
  23.4 1.2 %multiply_add_fusion.1 = f32[2,16,16,640]{3,2,1,0:T(8,128)} fusion(f32[2,16,640]{2,1,0:T(8,128)S(1)} %copy-done.4, f32[2,16,640]{2,1,0:T(8,128)S(1)} %copy-done.7, f32[2,16,640]{2,1,0:T(8,128)S(1)} %copy-done.6, f32[2,16,640]{2,1,0:T(8,128)S(1)} %copy-done.5), kind=kLoop, calls=%fused_computation.30 | loop fusion | flops 983040 | bytes 1638400 | tf_op jit(solution)/shard_map/twiddle_tables/add | solution.py:45
  24.6 1.1 %fusion.13 = f32[11,1,2,32,640]{4,3,0,2,1:T(8,128)S(1)} fusion(bf16[2,1024,640]{2,1,0:T(8,128)(2,1)S(1)} %get-tuple-element.8, bf16[11,32,1024]{2,1,0:T(8,128)(2,1)S(1)} %all_gather.3), kind=kOutput, calls=%fused_computation.24 | convolution fusion | flops 922746880 | bytes 5144576 | tf_op jit(solution)/shard_map/receptor_spectra/trxc,hcq->trhxq/dot_general | solution.py:71
  25.7 1.4 %copy.21 = f32[11,1,2,32,640]{4,3,2,0,1:T(8,128)} copy(f32[11,1,2,32,640]{4,3,0,2,1:T(8,128)S(1)} %fusion.13) | data formatting | bytes 3604480 | tf_op jit(solution)/shard_map/receptor_spectra/trxc,hcq->trhxq/transpose | solution.py:71
  27.1 3.6 %convolution_bitcast_fusion.3 = f32[11,1,64,640]{3,2,0,1:T(8,128)} fusion(f32[11,64,640]{2,1,0:T(8,128)} %bitcast.152, f32[64,64,1]{1,0,2:T(8,128)S(1)} %copy-done.3), kind=kOutput, calls=%fused_computation.27 | convolution fusion | flops 173015040 | bytes 3620864 | tf_op jit(solution)/shard_map/receptor_spectra/pk,trkq->trpq/dot_general | solution.py:73
  31.1 0.8 %fusion.40 = f32[4,22,16,256]{3,1,2,0:T(8,128)S(1)} fusion(bf16[4,22,16,256]{3,2,1,0:T(8,128)(2,1)S(1)} %get-tuple-element.28, s32[4,256]{1,0:T(4,128)S(1)} %get-tuple-element.30), kind=kOutput, calls=%fused_computation.39 | convolution fusion | flops 184811520 | bytes 2166784 | tf_op jit(solution)/shard_map/ligand_spectra/ntxa,nac->ntxc/dot_general | solution.py:86
  31.9 1.0 %fusion.42 = f32[4,22,16,256]{3,1,2,0:T(8,128)S(1)} fusion(bf16[4,22,16,256]{3,2,1,0:T(8,128)(2,1)S(1)} %get-tuple-element.29, s32[4,256]{1,0:T(4,128)S(1)} %get-tuple-element.30), kind=kOutput, calls=%fused_computation.40 | convolution fusion | flops 184811520 | bytes 2166784 | tf_op jit(solution)/shard_map/ligand_spectra/ntxa,nac->ntxc/dot_general | solution.py:85
  33.0 3.3 %convolution_bitcast_fusion.1 = f32[4,22,2,16,640]{4,1,3,0,2:T(8,128)S(1)} fusion(f32[4,22,16,256]{3,1,2,0:T(8,128)S(1)} %fusion.42, f32[4,22,16,256]{3,1,2,0:T(8,128)S(1)} %fusion.40, f32[2,256,640]{2,1,0:T(8,128)S(1)} %bitcast.156), kind=kOutput, calls=%fused_computation.9 | convolution fusion | flops 2768601088 | bytes 11403264 | tf_op jit(solution)/shard_map/ligand_spectra/ntxc,hcq->nthxq/dot_general | solution.py:87
  36.3 1.3 %copy.20 = f32[4,22,2,16,640]{4,3,2,1,0:T(8,128)S(1)} copy(f32[4,22,2,16,640]{4,1,3,0,2:T(8,128)S(1)} %convolution_bitcast_fusion.1) | data formatting | bytes 14417920 | tf_op jit(solution)/shard_map/ligand_spectra/ntxc,hcq->nthxq/transpose | solution.py:87
  37.6 6.0 %convolution_bitcast_fusion = f32[22,4,64,640]{3,2,0,1:T(8,128)S(1)} fusion(f32[4,22,32,640]{3,2,1,0:T(8,128)S(1)} %bitcast.151, f32[64,32,1,1]{0,1,3,2:T(8,128)S(1)} %copy-done.9), kind=kOutput, calls=%fused_computation | convolution fusion | flops 692060160 | bytes 21635072 | tf_op jit(solution)/shard_map/ligand_spectra/pk,ntkq->tnpq/dot_general | solution.py:90
  43.6 2.2 %fusion.16 = f32[11,1,2,32,640]{4,3,0,2,1:T(8,128)S(1)} fusion(bf16[2,1024,640]{2,1,0:T(8,128)(2,1)S(1)} %get-tuple-element.8, bf16[11,32,1024]{2,1,0:T(8,128)(2,1)} %collective-permute-done.4), kind=kOutput, calls=%fused_computation.25 | convolution fusion | flops 922746880 | bytes 5144576 | tf_op jit(solution)/shard_map/receptor_spectra/trxc,hcq->trhxq/dot_general | solution.py:71
  46.0 1.1 %convolution_bitcast_fusion.2 = f32[11,1,64,640]{3,2,0,1:T(8,128)S(1)} fusion(f32[11,64,640]{2,1,0:T(8,128)S(1)} %bitcast.153, f32[64,64,1]{1,0,2:T(8,128)S(1)} %copy-done.3), kind=kOutput, calls=%fused_computation.26 | convolution fusion | flops 173015040 | bytes 3620864 | tf_op jit(solution)/shard_map/receptor_spectra/pk,trkq->trpq/dot_general | solution.py:73
  47.7 2.5 %add_reduce_fusion = (f32[4,32,640]{2,1,0:T(8,128)S(1)}, f32[4,32,640]{2,1,0:T(8,128)S(1)}, f32[4,32,640]{2,1,0:T(8,128)S(1)}, f32[4,32,640]{2,1,0:T(8,128)S(1)}) fusion(f32[22,4,64,640]{3,2,0,1:T(8,128)S(1)} %convolution_bitcast_fusion, f32[11,32,640]{2,1,0:T(8,128)S(1)} %get-tuple-element.25, f32[11,32,640]{2,1,0:T(8,128)S(1)} %get-tuple-element.24, ...), kind=kLoop, calls=%fused_computation.6 | loop fusion | flops 14090240 | bytes 19333120 | tf_op jit(solution)/shard_map/correlate/reduce_sum | solution.py:98
  51.2 1.0 %fusion.21 = f32[4,32,1024]{2,1,0:T(8,128)S(1)} fusion(bf16[2,1024,640]{2,1,0:T(8,128)(2,1)S(1)} %get-tuple-element.8, bf16[1,4,32,2,640]{4,2,1,3,0:T(8,128)(2,1)S(1)} %get-tuple-element.9), kind=kOutput, calls=%fused_computation.31 | convolution fusion | flops 335544320 | bytes 3473408 | tf_op jit(solution)/shard_map/inverse_scores/rnxhq,hcq->rnxc/dot_general | solution.py:115
  52.2 1.0 %fusion.33 = f32[4,32,1024]{2,1,0:T(8,128)S(1)} fusion(f32[4,32,1024]{2,1,0:T(8,128)S(1)} %fusion.21, bf16[2,1024,640]{2,1,0:T(8,128)(2,1)S(1)} %get-tuple-element.8, bf16[1,4,32,2,640]{4,2,1,3,0:T(8,128)(2,1)S(1)} %get-tuple-element.10), kind=kOutput, calls=%fused_computation.35 | convolution fusion | flops 335675392 | bytes 3997696 | tf_op jit(solution)/shard_map/inverse_scores/rnxhq,hcq->rnxc/dot_general | solution.py:116
  53.2 0.7 %copy-done = bf16[2,1024,640]{2,1,0:T(8,128)(2,1)S(1)} copy-done((bf16[2,1024,640]{2,1,0:T(8,128)(2,1)S(1)}, bf16[2,1024,640]{2,1,0:T(8,128)(2,1)}, u32[]{:S(2)}) %copy-start) | copy-done | bytes 2621464
  53.9 1.1 %fusion.36 = f32[4]{0:T(128)S(1)} fusion(f32[4,32,1024]{2,1,0:T(8,128)S(1)} %fusion.33, bf16[2,1024,640]{2,1,0:T(8,128)(2,1)S(1)} %copy-done, bf16[1,4,32,2,640]{4,2,1,3,0:T(8,128)(2,1)S(1)} %get-tuple-element.9), kind=kOutput, calls=%fused_computation.36 | convolution fusion | flops 335806464 | bytes 3473424 | tf_op jit(solution)/shard_map/inverse_scores/rnxhq,hcq->rnxc/dot_general | solution.py:117
  55.2 1.5 %collective-permute-start.5 = (f32[4,32]{0,1:T(8,128)S(1)}, f32[4,32]{0,1:T(8,128)S(1)}, u32[]{:S(2)}, u32[]{:S(2)}) collective-permute-start(f32[4,32]{0,1:T(8,128)S(1)} %broadcast_select_fusion), channel_id=1, source_target_pairs={{0,1},{1,0},{2,3},{3,2},{4,5},{5,4},{6,7},{7,6},{8,9},{9,8},{10,11... | collective-permute-start | bytes 1544 | tf_op jit(solution)/shard_map/ppermute | solution.py:135
  57.3 1.6 %collective-permute-done.5 = f32[4,32]{0,1:T(8,128)S(1)} collective-permute-done((f32[4,32]{0,1:T(8,128)S(1)}, f32[4,32]{0,1:T(8,128)S(1)}, u32[]{:S(2)}, u32[]{:S(2)}) %collective-permute-start.5) | collective-permute-done | bytes 544 | tf_op jit(solution)/shard_map/ppermute | solution.py:135
  58.9 1.0 %collective-permute-done.7 = f32[4,32]{0,1:T(8,128)S(1)} collective-permute-done((f32[4,32]{0,1:T(8,128)S(1)}, f32[4,32]{0,1:T(8,128)S(1)}, u32[]{:S(2)}, u32[]{:S(2)}) %collective-permute-start.7) | collective-permute-done | bytes 544 | tf_op jit(solution)/shard_map/ppermute | solution.py:135
  60.6 1.5 %collective-permute-start.8 = (f32[4,32]{0,1:T(8,128)S(1)}, f32[4,32]{0,1:T(8,128)S(1)}, u32[]{:S(2)}, u32[]{:S(2)}) collective-permute-start(f32[4,32]{0,1:T(8,128)S(1)} %maximum_maximum_fusion.1), channel_id=1, source_target_pairs={{0,4},{1,5},{2,6},{3,7},{4,0},{5,1},{6,2},{7,3},{8,12},{9,13},{10,... | collective-permute-start | bytes 1544 | tf_op jit(solution)/shard_map/ppermute | solution.py:135
  62.1 1.3 %collective-permute-start.9 = (f32[4,32]{0,1:T(8,128)S(1)}, f32[4,32]{0,1:T(8,128)S(1)}, u32[]{:S(2)}, u32[]{:S(2)}) collective-permute-start(f32[4,32]{0,1:T(8,128)S(1)} %maximum_maximum_fusion.1), channel_id=1, source_target_pairs={{0,8},{1,9},{2,10},{3,11},{4,12},{5,13},{6,14},{7,15},{8,0},{9,1},... | collective-permute-start | bytes 1544 | tf_op jit(solution)/shard_map/ppermute | solution.py:135
  63.4 1.1 %collective-permute-done.10 = f32[4,32]{0,1:T(8,128)S(1)} collective-permute-done((f32[4,32]{0,1:T(8,128)S(1)}, f32[4,32]{0,1:T(8,128)S(1)}, u32[]{:S(2)}, u32[]{:S(2)}) %collective-permute-start.10) | collective-permute-done | bytes 544 | tf_op jit(solution)/shard_map/ppermute | solution.py:135
  64.6 1.2 %collective-permute-done.9 = f32[4,32]{0,1:T(8,128)S(1)} collective-permute-done((f32[4,32]{0,1:T(8,128)S(1)}, f32[4,32]{0,1:T(8,128)S(1)}, u32[]{:S(2)}, u32[]{:S(2)}) %collective-permute-start.9) | collective-permute-done | bytes 544 | tf_op jit(solution)/shard_map/ppermute | solution.py:135
  66.2 4.3 %collective-permute-done.11 = f32[4,32]{0,1:T(8,128)S(1)} collective-permute-done((f32[4,32]{0,1:T(8,128)S(1)}, f32[4,32]{0,1:T(8,128)S(1)}, u32[]{:S(2)}, u32[]{:S(2)}) %collective-permute-start.11) | collective-permute-done | bytes 544 | tf_op jit(solution)/shard_map/ppermute | solution.py:135
  (53 shorter events, 5.5 us)
Async XLA Ops:
  0.6 30.1 %collective-permute-start.1 = (s32[3,2,256]{2,1,0:T(2,128)}, s32[3,2,256]{2,1,0:T(2,128)S(1)}, u32[]{:S(2)}, u32[]{:S(2)}) collective-permute-start(s32[3,2,256]{2,1,0:T(2,128)} %param.16), channel_id=1, source_target_pairs={{0,8},{8,16},{16,24},{24,0},{1,9},{9,17},{17,25},{25,1},{2,10},{10... | collective-permute-start | bytes 18440 | tf_op jit(solution)/shard_map/ppermute | solution.py:124
  3.7 27.0 %collective-permute-start.2 = (s32[3,2,256]{2,1,0:T(2,128)}, s32[3,2,256]{2,1,0:T(2,128)S(1)}, u32[]{:S(2)}, u32[]{:S(2)}) collective-permute-start(s32[3,2,256]{2,1,0:T(2,128)} %param.16), channel_id=1, source_target_pairs={{0,16},{8,24},{16,0},{24,8},{1,17},{9,25},{17,1},{25,9},{2,18},{10... | collective-permute-start | bytes 18440 | tf_op jit(solution)/shard_map/ppermute | solution.py:124
  6.3 24.4 %collective-permute-start.3 = (s32[3,2,256]{2,1,0:T(2,128)}, s32[3,2,256]{2,1,0:T(2,128)S(1)}, u32[]{:S(2)}, u32[]{:S(2)}) collective-permute-start(s32[3,2,256]{2,1,0:T(2,128)} %param.16), channel_id=1, source_target_pairs={{0,24},{8,0},{16,8},{24,16},{1,25},{9,1},{17,9},{25,17},{2,26},{10... | collective-permute-start | bytes 18440 | tf_op jit(solution)/shard_map/ppermute | solution.py:124
  8.4 22.4 %collective-permute-start = (f32[11,256]{1,0:T(8,128)S(1)}, f32[11,256]{1,0:T(8,128)S(1)}, u32[]{:S(2)}, u32[]{:S(2)}) collective-permute-start(f32[11,256]{1,0:T(8,128)S(1)} %broadcast_multiply_fusion), channel_id=1, source_target_pairs={{0,1},{1,0},{2,3},{3,2},{4,5},{5,4},{6,7},{7,6},{8,9},{9,8},{10,11... | collective-permute-start | bytes 33800 | tf_op jit(solution)/shard_map/ppermute | solution.py:124
  18.4 25.2 %collective-permute-start.4 = (bf16[11,32,1024]{2,1,0:T(8,128)(2,1)S(1)}, bf16[11,32,1024]{2,1,0:T(8,128)(2,1)}, u32[]{:S(2)}, u32[]{:S(2)}) collective-permute-start(bf16[11,32,1024]{2,1,0:T(8,128)(2,1)S(1)} %all_gather.3), channel_id=1, source_target_pairs={{0,1},{1,0},{2,3},{3,2},{4,5},{5,4},{6,7},{7,6},{8,9},{9,8},{10,11... | collective-permute-start | bytes 2162696 | tf_op jit(solution)/shard_map/ppermute | solution.py:124
  20.9 2.4 %copy-start.4 = (f32[2,16,640]{2,1,0:T(8,128)S(1)}, f32[2,16,640]{2,1,0:T(8,128)}, u32[]{:S(2)}) copy-start(f32[2,16,640]{2,1,0:T(8,128)} %constant.100) | copy-start | bytes 245764
  20.9 2.4 %copy-start.5 = (f32[2,16,640]{2,1,0:T(8,128)S(1)}, f32[2,16,640]{2,1,0:T(8,128)}, u32[]{:S(2)}) copy-start(f32[2,16,640]{2,1,0:T(8,128)} %constant.91) | copy-start | bytes 245764
  20.9 2.4 %copy-start.6 = (f32[2,16,640]{2,1,0:T(8,128)S(1)}, f32[2,16,640]{2,1,0:T(8,128)}, u32[]{:S(2)}) copy-start(f32[2,16,640]{2,1,0:T(8,128)} %constant.94) | copy-start | bytes 245764
  21.0 2.4 %copy-start.7 = (f32[2,16,640]{2,1,0:T(8,128)S(1)}, f32[2,16,640]{2,1,0:T(8,128)}, u32[]{:S(2)}) copy-start(f32[2,16,640]{2,1,0:T(8,128)} %constant.97) | copy-start | bytes 245764
  25.7 1.4 %copy-start.3 = (f32[64,64,1]{1,0,2:T(8,128)S(1)}, f32[64,64,1]{1,0,2:T(8,128)}, u32[]{:S(2)}) copy-start(f32[64,64,1]{1,0,2:T(8,128)} %constant.110) | copy-start | bytes 49156
  27.1 3.6 %copy-start.10 = (s32[3,2,256]{2,1,0:T(2,128)S(1)}, s32[3,2,256]{2,1,0:T(2,128)}, u32[]{:S(2)}) copy-start(s32[3,2,256]{2,1,0:T(2,128)} %param.16) | copy-start | bytes 18436
  31.1 1.9 %copy-start.2 = (f32[2,16,16,640]{3,2,1,0:T(8,128)S(1)}, f32[2,16,16,640]{3,2,1,0:T(8,128)}, u32[]{:S(2)}) copy-start(f32[2,16,16,640]{3,2,1,0:T(8,128)} %multiply_add_fusion.1) | copy-start | bytes 3932164
  36.3 1.3 %copy-start.9 = (f32[64,32,1,1]{0,1,3,2:T(8,128)S(1)}, f32[64,32,1,1]{0,1,3,2:T(8,128)}, u32[]{:S(2)}) copy-start(f32[64,32,1,1]{0,1,3,2:T(8,128)} %constant.109) | copy-start | bytes 24580
  46.0 1.5 %copy-start.1 = (f32[11,1,64,640]{3,2,0,1:T(8,128)S(1)}, f32[11,1,64,640]{3,2,0,1:T(8,128)}, u32[]{:S(2)}) copy-start(f32[11,1,64,640]{3,2,0,1:T(8,128)} %convolution_bitcast_fusion.3) | copy-start | bytes 5406724
  47.7 2.6 %copy-start.8 = (f32[64,32,1,1]{0,1,3,2:T(8,128)S(1)}, f32[64,32,1,1]{0,1,3,2:T(8,128)}, u32[]{:S(2)}) copy-start(f32[64,32,1,1]{0,1,3,2:T(8,128)} %constant.111) | copy-start | bytes 24580
  50.3 0.8 %copy-start.11 = (f32[640]{0:T(1024)S(1)}, f32[640]{0:T(1024)}, u32[]{:S(2)}) copy-start(f32[640]{0:T(1024)} %constant.84.clone) | copy-start | bytes 7684
  52.2 1.7 %copy-start = (bf16[2,1024,640]{2,1,0:T(8,128)(2,1)S(1)}, bf16[2,1024,640]{2,1,0:T(8,128)(2,1)}, u32[]{:S(2)}) copy-start(bf16[2,1024,640]{2,1,0:T(8,128)(2,1)} %get-tuple-element.11) | copy-start | bytes 7864324
  55.2 3.7 %collective-permute-start.5 = (f32[4,32]{0,1:T(8,128)S(1)}, f32[4,32]{0,1:T(8,128)S(1)}, u32[]{:S(2)}, u32[]{:S(2)}) collective-permute-start(f32[4,32]{0,1:T(8,128)S(1)} %broadcast_select_fusion), channel_id=1, source_target_pairs={{0,1},{1,0},{2,3},{3,2},{4,5},{5,4},{6,7},{7,6},{8,9},{9,8},{10,11... | collective-permute-start | bytes 1544 | tf_op jit(solution)/shard_map/ppermute | solution.py:135
  56.7 2.2 %collective-permute-start.6 = (f32[4,32]{0,1:T(8,128)S(1)}, f32[4,32]{0,1:T(8,128)S(1)}, u32[]{:S(2)}, u32[]{:S(2)}) collective-permute-start(f32[4,32]{0,1:T(8,128)S(1)} %broadcast_select_fusion), channel_id=1, source_target_pairs={{0,2},{1,3},{2,0},{3,1},{4,6},{5,7},{6,4},{7,5},{8,10},{9,11},{10,... | collective-permute-start | bytes 1544 | tf_op jit(solution)/shard_map/ppermute | solution.py:135
  56.7 3.2 %collective-permute-start.7 = (f32[4,32]{0,1:T(8,128)S(1)}, f32[4,32]{0,1:T(8,128)S(1)}, u32[]{:S(2)}, u32[]{:S(2)}) collective-permute-start(f32[4,32]{0,1:T(8,128)S(1)} %broadcast_select_fusion), channel_id=1, source_target_pairs={{0,3},{1,2},{2,1},{3,0},{4,7},{5,6},{6,5},{7,4},{8,11},{9,10},{10,... | collective-permute-start | bytes 1544 | tf_op jit(solution)/shard_map/ppermute | solution.py:135
  60.0 4.6 %collective-permute-start.10 = (f32[4,32]{0,1:T(8,128)S(1)}, f32[4,32]{0,1:T(8,128)S(1)}, u32[]{:S(2)}, u32[]{:S(2)}) collective-permute-start(f32[4,32]{0,1:T(8,128)S(1)} %maximum_maximum_fusion.1), channel_id=1, source_target_pairs={{0,12},{1,13},{2,14},{3,15},{4,8},{5,9},{6,10},{7,11},{8,4},{9,5},... | collective-permute-start | bytes 1544 | tf_op jit(solution)/shard_map/ppermute | solution.py:135
  60.6 4.0 %collective-permute-start.8 = (f32[4,32]{0,1:T(8,128)S(1)}, f32[4,32]{0,1:T(8,128)S(1)}, u32[]{:S(2)}, u32[]{:S(2)}) collective-permute-start(f32[4,32]{0,1:T(8,128)S(1)} %maximum_maximum_fusion.1), channel_id=1, source_target_pairs={{0,4},{1,5},{2,6},{3,7},{4,0},{5,1},{6,2},{7,3},{8,12},{9,13},{10,... | collective-permute-start | bytes 1544 | tf_op jit(solution)/shard_map/ppermute | solution.py:135
  62.1 3.7 %collective-permute-start.9 = (f32[4,32]{0,1:T(8,128)S(1)}, f32[4,32]{0,1:T(8,128)S(1)}, u32[]{:S(2)}, u32[]{:S(2)}) collective-permute-start(f32[4,32]{0,1:T(8,128)S(1)} %maximum_maximum_fusion.1), channel_id=1, source_target_pairs={{0,8},{1,9},{2,10},{3,11},{4,12},{5,13},{6,14},{7,15},{8,0},{9,1},... | collective-permute-start | bytes 1544 | tf_op jit(solution)/shard_map/ppermute | solution.py:135
  65.8 4.6 %collective-permute-start.11 = (f32[4,32]{0,1:T(8,128)S(1)}, f32[4,32]{0,1:T(8,128)S(1)}, u32[]{:S(2)}, u32[]{:S(2)}) collective-permute-start(f32[4,32]{0,1:T(8,128)S(1)} %maximum_maximum_fusion), channel_id=1, source_target_pairs={{0,16},{1,17},{2,18},{3,19},{4,20},{5,21},{6,22},{7,23},{8,24},{9,... | collective-permute-start | bytes 1544 | tf_op jit(solution)/shard_map/ppermute | solution.py:135

commit v12 on v11

--- a/solution.py
+++ b/solution.py
@@ -151,12 +151,24 @@
         term = lax.axis_index("term")
         own_rows = lax.all_gather(receptor_grids, "inner", axis=1, tiled=True)
         groups = gather_by_permutes(own_rows, "term", term_count, term)
-        cell_blocks = gather_by_permutes(ligand_cells, "plane", plane_count, plane)
-        cells_here = jnp.concatenate(cell_blocks, axis=1)
+        local_slots = jnp.arange(rot_here * plane_count, dtype=jnp.int32) // rot_here
+        if plane_count & (plane_count - 1):
+            cell_blocks = gather_by_permutes(ligand_cells, "plane", plane_count, plane)
+            cells_here = jnp.concatenate(cell_blocks, axis=1)
+            slot_plane = (plane - local_slots) % plane_count
+        else:
+            cells_here = ligand_cells
+            shift = 1
+            while shift < plane_count:
+                pairs = [(k, k ^ shift) for k in range(plane_count)]
+                moved = lax.ppermute(cells_here, "plane", pairs)
+                cells_here = jnp.concatenate([cells_here, moved], axis=1)
+                shift *= 2
+            slot_plane = jnp.bitwise_xor(plane, local_slots)
         share = cells_here.shape[1] // term_count
         voxels = lax.dynamic_slice_in_dim(cells_here, term * share, share, axis=1)
         local = term * share + jnp.arange(share, dtype=jnp.int32)
-        source_plane = (plane - local // rot_here) % plane_count
+        source_plane = lax.dynamic_slice_in_dim(slot_plane, term * share, share)
         rot_ids = (source_plane * inner_count + inner) * rot_here + local % rot_here
         coefficients = atom_weights * term_weights[:, None]
         coefficients = jnp.concatenate(gather_by_permutes(coefficients, "term", term_count, term))

time: 71.9 us -> 70.6 us (0.982)
  matrix products: 22.9 us -> 21.5 us
  starting transfers between devices: 15 us -> 16 us
    ppermute x5 -> x2, starting transfers between devices: 9.04 us -> 2.03 us  [gather_by_permutes(): blocks.append(lax.ppermute(values, axis_name, pairs))]
    ppermute x0 -> x2, starting transfers between devices: none -> 5.76 us  [body(): moved = lax.ppermute(cells_here, 'plane', pairs)]
    ppermute x7, waiting for transfers between devices: 9.25 us -> 6.72 us  [butterfly_max(): received.append(lax.ppermute(values, axes, pairs))]
    ppermute x7, starting transfers between devices: 5.98 us -> 8.23 us  [butterfly_max(): received.append(lax.ppermute(values, axes, pairs))]
    ppermute x0 -> x2, waiting for transfers between devices: none -> 2 us  [body(): moved = lax.ppermute(cells_here, 'plane', pairs)]
    dot_general x2, matrix products: 4.66 us -> 3.43 us  [receptor_mixed(): return jnp.einsum('pk,trkq->trpq', mix_tables(G), plane, precision=HIGH)]
  transfers between devices with their start and end apart: 12 -> 11, of which waited for: 5 -> 7; matrix products, arithmetic and copies ran while one was open for 35% -> 34% of each run, Pallas kernels for 0% -> 0%
where the time goes in v12:
time: 70.6 us; the launch traced here: 70.3 us
  matrix products  21.5 us (30%)
  starting transfers between devices  16 us (23%)
  other arithmetic  10.3 us (15%)
  waiting for transfers between devices  8.73 us (12%)
  blocking collectives  8.44 us (12%)
  local copies, waits for them, and re-layouts  4.39 us (6%)
  between operations  0.95 us (1%)
    all_gather x1, blocking collectives, body(): own_rows = lax.all_gather(receptor_grids, 'inner', axis=1, tiled=True)  8.44 us
    ppermute x7, starting transfers between devices, butterfly_max(): received.append(lax.ppermute(values, axes, pairs))  8.23 us
    ppermute x7, waiting for transfers between devices, butterfly_max(): received.append(lax.ppermute(values, axes, pairs))  6.72 us
    dot_general x1, matrix products, ligand_spectra(): return jnp.einsum('pk,ntkq->tnpq', mix_tables(LB), plane, precision=HIGH)  5.81 us
    ppermute x2, starting transfers between devices, body(): moved = lax.ppermute(cells_here, 'plane', pairs)  5.76 us
    dot_general x2, matrix products, receptor_mixed(): return jnp.einsum('pk,trkq->trpq', mix_tables(G), plane, precision=HIGH)  3.43 us
    dot_general x2, matrix products, receptor_mixed(): jnp.einsum('trxc,hcq->trhxq', grids, table_hi, preferred_element_type=jnp...  3.31 us
    dot_general x1, matrix products, ligand_spectra(): plane = jnp.einsum('ntxc,hcq->nthxq', grid, box_table, precision=HIGH)  3.27 us
  transfers between devices with their start and end apart: 11, of which 7 were waited for; matrix products, arithmetic and copies ran while one was open for 34% of the time, Pallas kernels for 0%

profile of v12, /device:TPU:0, one launch (start us, length us, event | category | flops | bytes accessed | tf_op | source)
XLA Modules:
  0.0 70.3 jit_solution(7312025514103496550)
XLA Ops:
  0.6 3.1 %collective-permute-start.1 = (s32[3,2,256]{2,1,0:T(2,128)}, s32[3,2,256]{2,1,0:T(2,128)S(1)}, u32[]{:S(2)}, u32[]{:S(2)}) collective-permute-start(s32[3,2,256]{2,1,0:T(2,128)} %param.16), channel_id=1, source_target_pairs={{0,8},{8,0},{16,24},{24,16},{1,9},{9,1},{17,25},{25,17},{2,10},{10... | collective-permute-start | bytes 18440 | tf_op jit(solution)/shard_map/ppermute | solution.py:164
  3.7 0.8 %broadcast_multiply_fusion = f32[11,256]{1,0:T(8,128)S(1)} fusion(f32[11,256]{1,0:T(8,128)} %param.15, f32[11]{0:T(128)} %param.14), kind=kLoop, calls=%fused_computation.88 | loop fusion | flops 2816 | bytes 22572 | tf_op jit(solution)/shard_map/mul | solution.py:173
  4.5 1.5 %collective-permute-start = (f32[11,256]{1,0:T(8,128)S(1)}, f32[11,256]{1,0:T(8,128)S(1)}, u32[]{:S(2)}, u32[]{:S(2)}) collective-permute-start(f32[11,256]{1,0:T(8,128)S(1)} %broadcast_multiply_fusion), channel_id=1, source_target_pairs={{0,1},{1,0},{2,3},{3,2},{4,5},{5,4},{6,7},{7,6},{8,9},{9,8},{10,11... | collective-permute-start | bytes 33800 | tf_op jit(solution)/shard_map/ppermute | solution.py:124
  6.0 8.4 %all_gather.3 = bf16[11,32,1024]{2,1,0:T(8,128)(2,1)S(1)} all-gather(bf16[11,8,1024]{2,1,0:T(8,128)(2,1)} %param.13), channel_id=1, replica_groups=mesh['plane'=4,'inner'=4,'term'=2] {'inner'}, dimensions={1}, use_global_device_ids=true | all-gather | bytes 901120 | tf_op jit(solution)/shard_map/all_gather | solution.py:152
  15.0 2.0 %multiply_add_fusion = f32[2,32,32,640]{3,2,1,0:T(8,128)S(1)} fusion(f32[2,32,640]{2,1,0:T(8,128)} %constant.101, f32[2,32,640]{2,1,0:T(8,128)} %constant.99, f32[2,32,640]{2,1,0:T(8,128)} %constant.97, f32[2,32,640]{2,1,0:T(8,128)} %constant.95), kind=kLoop, calls=%fused_computation.4 | loop fusion | flops 3932160 | bytes 5898240 | tf_op jit(solution)/shard_map/twiddle_tables/add | solution.py:45
  17.1 2.4 %fusion = (bf16[2,1024,640]{2,1,0:T(8,128)(2,1)}, bf16[2,1024,640]{2,1,0:T(8,128)(2,1)S(1)}) fusion(f32[2,32,32,640]{3,2,1,0:T(8,128)S(1)} %multiply_add_fusion), kind=kLoop, calls=%fused_computation.3 | loop fusion | flops 5242880 | bytes 10485760 | tf_op jit(solution)/shard_map/twiddle_tables/convert_element_type | solution.py:52
  19.4 1.2 %multiply_add_fusion.1 = f32[2,16,16,640]{3,2,1,0:T(8,128)} fusion(f32[2,16,640]{2,1,0:T(8,128)S(1)} %copy-done.6, f32[2,16,640]{2,1,0:T(8,128)S(1)} %copy-done.5, f32[2,16,640]{2,1,0:T(8,128)S(1)} %copy-done.4, f32[2,16,640]{2,1,0:T(8,128)S(1)} %copy-done.3), kind=kLoop, calls=%fused_computation.30 | loop fusion | flops 983040 | bytes 1638400 | tf_op jit(solution)/shard_map/twiddle_tables/add | solution.py:45
  20.7 1.1 %fusion.13 = f32[11,1,2,32,640]{4,3,0,2,1:T(8,128)S(1)} fusion(bf16[2,1024,640]{2,1,0:T(8,128)(2,1)S(1)} %get-tuple-element.8, bf16[11,32,1024]{2,1,0:T(8,128)(2,1)S(1)} %all_gather.3), kind=kOutput, calls=%fused_computation.24 | convolution fusion | flops 922746880 | bytes 5144576 | tf_op jit(solution)/shard_map/receptor_spectra/trxc,hcq->trhxq/dot_general | solution.py:71
  21.8 1.3 %copy.21 = f32[11,1,2,32,640]{4,3,2,0,1:T(8,128)} copy(f32[11,1,2,32,640]{4,3,0,2,1:T(8,128)S(1)} %fusion.13) | data formatting | bytes 3604480 | tf_op jit(solution)/shard_map/receptor_spectra/trxc,hcq->trhxq/transpose | solution.py:71
  23.2 2.3 %convolution_bitcast_fusion.3 = f32[11,1,64,640]{3,2,0,1:T(8,128)S(1)} fusion(f32[11,64,640]{2,1,0:T(8,128)} %bitcast.152, f32[64,64,1]{1,0,2:T(8,128)S(1)} %copy-done.2), kind=kOutput, calls=%fused_computation.27 | convolution fusion | flops 173015040 | bytes 3620864 | tf_op jit(solution)/shard_map/receptor_spectra/pk,trkq->trpq/dot_general | solution.py:73
  25.6 2.7 %collective-permute-start.2 = (s32[3,4,256]{2,1,0:T(4,128)S(1)}, s32[3,4,256]{2,1,0:T(4,128)S(1)}, u32[]{:S(2)}, u32[]{:S(2)}) collective-permute-start(s32[3,4,256]{2,1,0:T(4,128)S(1)} %pad_add_fusion), channel_id=1, source_target_pairs={{0,16},{8,24},{16,0},{24,8},{1,17},{9,25},{17,1},{25,9},{2,18},{10... | collective-permute-start | bytes 36872 | tf_op jit(solution)/shard_map/ppermute | solution.py:164
  28.3 2.0 %collective-permute-done.2 = s32[3,4,256]{2,1,0:T(4,128)S(1)} collective-permute-done((s32[3,4,256]{2,1,0:T(4,128)S(1)}, s32[3,4,256]{2,1,0:T(4,128)S(1)}, u32[]{:S(2)}, u32[]{:S(2)}) %collective-permute-start.2) | collective-permute-done | bytes 12320 | tf_op jit(solution)/shard_map/ppermute | solution.py:164
  30.6 0.8 %fusion.40 = f32[4,22,16,256]{3,1,2,0:T(8,128)S(1)} fusion(bf16[4,22,16,256]{3,2,1,0:T(8,128)(2,1)S(1)} %get-tuple-element.28, s32[4,256]{1,0:T(4,128)S(1)} %get-tuple-element.30), kind=kOutput, calls=%fused_computation.39 | convolution fusion | flops 184811520 | bytes 2166784 | tf_op jit(solution)/shard_map/ligand_spectra/ntxa,nac->ntxc/dot_general | solution.py:86
  31.5 1.0 %fusion.42 = f32[4,22,16,256]{3,1,2,0:T(8,128)S(1)} fusion(bf16[4,22,16,256]{3,2,1,0:T(8,128)(2,1)S(1)} %get-tuple-element.29, s32[4,256]{1,0:T(4,128)S(1)} %get-tuple-element.30), kind=kOutput, calls=%fused_computation.40 | convolution fusion | flops 184811520 | bytes 2166784 | tf_op jit(solution)/shard_map/ligand_spectra/ntxa,nac->ntxc/dot_general | solution.py:85
  32.5 3.3 %convolution_bitcast_fusion.1 = f32[4,22,2,16,640]{4,1,3,0,2:T(8,128)S(1)} fusion(f32[4,22,16,256]{3,1,2,0:T(8,128)S(1)} %fusion.42, f32[4,22,16,256]{3,1,2,0:T(8,128)S(1)} %fusion.40, f32[2,256,640]{2,1,0:T(8,128)S(1)} %bitcast.156), kind=kOutput, calls=%fused_computation.9 | convolution fusion | flops 2768601088 | bytes 11403264 | tf_op jit(solution)/shard_map/ligand_spectra/ntxc,hcq->nthxq/dot_general | solution.py:87
  35.8 1.3 %copy.20 = f32[4,22,2,16,640]{4,3,2,1,0:T(8,128)S(1)} copy(f32[4,22,2,16,640]{4,1,3,0,2:T(8,128)S(1)} %convolution_bitcast_fusion.1) | data formatting | bytes 14417920 | tf_op jit(solution)/shard_map/ligand_spectra/ntxc,hcq->nthxq/transpose | solution.py:87
  37.1 5.8 %convolution_bitcast_fusion = f32[22,4,64,640]{3,2,0,1:T(8,128)S(1)} fusion(f32[4,22,32,640]{3,2,1,0:T(8,128)S(1)} %bitcast.151, f32[64,32,1,1]{0,1,3,2:T(8,128)S(1)} %copy-done.9), kind=kOutput, calls=%fused_computation | convolution fusion | flops 692060160 | bytes 21635072 | tf_op jit(solution)/shard_map/ligand_spectra/pk,ntkq->tnpq/dot_general | solution.py:90
  42.9 2.2 %fusion.16 = f32[11,1,2,32,640]{4,3,0,2,1:T(8,128)S(1)} fusion(bf16[2,1024,640]{2,1,0:T(8,128)(2,1)S(1)} %get-tuple-element.8, bf16[11,32,1024]{2,1,0:T(8,128)(2,1)} %collective-permute-done.3), kind=kOutput, calls=%fused_computation.25 | convolution fusion | flops 922746880 | bytes 5144576 | tf_op jit(solution)/shard_map/receptor_spectra/trxc,hcq->trhxq/dot_general | solution.py:71
  45.3 1.1 %convolution_bitcast_fusion.2 = f32[11,1,64,640]{3,2,0,1:T(8,128)S(1)} fusion(f32[11,64,640]{2,1,0:T(8,128)S(1)} %bitcast.153, f32[64,64,1]{1,0,2:T(8,128)S(1)} %copy-done.2), kind=kOutput, calls=%fused_computation.26 | convolution fusion | flops 173015040 | bytes 3620864 | tf_op jit(solution)/shard_map/receptor_spectra/pk,trkq->trpq/dot_general | solution.py:73
  46.7 2.5 %add_reduce_fusion = (f32[4,32,640]{2,1,0:T(8,128)S(1)}, f32[4,32,640]{2,1,0:T(8,128)S(1)}, f32[4,32,640]{2,1,0:T(8,128)S(1)}, f32[4,32,640]{2,1,0:T(8,128)S(1)}) fusion(f32[22,4,64,640]{3,2,0,1:T(8,128)S(1)} %convolution_bitcast_fusion, f32[11,32,640]{2,1,0:T(8,128)S(1)} %get-tuple-element.25, f32[11,32,640]{2,1,0:T(8,128)S(1)} %get-tuple-element.24, ...), kind=kLoop, calls=%fused_computation.6 | loop fusion | flops 14090240 | bytes 19333120 | tf_op jit(solution)/shard_map/correlate/reduce_sum | solution.py:98
  49.2 0.7 %fusion.49 = f32[2,4,640,64]{2,3,1,0:T(8,128)S(1)} fusion(f32[64,32,1,1]{0,1,3,2:T(8,128)S(1)} %copy-done.8, f32[1,4,32,640]{3,2,1,0:T(8,128)S(1)} %bitcast.159, f32[1,4,32,640]{3,2,1,0:T(8,128)S(1)} %bitcast.160, f32[1,4,32,640]{3,2,1,0:T(8,128)S(1)} %bitcast.158, f32[1,4,32,640]{3,2,1,0:T(8,128)S(1)} %bitcast.157), kind=kOutput, calls=%fused_computation.53 | convolution fusion | flops 63406080 | bytes 2629632 | tf_op jit(solution)/shard_map/inverse_scores/xp,srnpq->srnxq/dot_general | solution.py:104
  50.1 1.0 %fusion.21 = f32[4,32,1024]{2,1,0:T(8,128)S(1)} fusion(bf16[2,1024,640]{2,1,0:T(8,128)(2,1)S(1)} %get-tuple-element.8, bf16[1,4,32,2,640]{4,2,1,3,0:T(8,128)(2,1)S(1)} %get-tuple-element.9), kind=kOutput, calls=%fused_computation.31 | convolution fusion | flops 335544320 | bytes 3473408 | tf_op jit(solution)/shard_map/inverse_scores/rnxhq,hcq->rnxc/dot_general | solution.py:115
  51.1 1.0 %fusion.33 = f32[4,32,1024]{2,1,0:T(8,128)S(1)} fusion(f32[4,32,1024]{2,1,0:T(8,128)S(1)} %fusion.21, bf16[2,1024,640]{2,1,0:T(8,128)(2,1)S(1)} %get-tuple-element.8, bf16[1,4,32,2,640]{4,2,1,3,0:T(8,128)(2,1)S(1)} %get-tuple-element.10), kind=kOutput, calls=%fused_computation.35 | convolution fusion | flops 335675392 | bytes 3997696 | tf_op jit(solution)/shard_map/inverse_scores/rnxhq,hcq->rnxc/dot_general | solution.py:116
  52.1 0.7 %copy-done = bf16[2,1024,640]{2,1,0:T(8,128)(2,1)S(1)} copy-done((bf16[2,1024,640]{2,1,0:T(8,128)(2,1)S(1)}, bf16[2,1024,640]{2,1,0:T(8,128)(2,1)}, u32[]{:S(2)}) %copy-start) | copy-done | bytes 2621464
  52.9 1.1 %fusion.36 = f32[4]{0:T(128)S(1)} fusion(f32[4,32,1024]{2,1,0:T(8,128)S(1)} %fusion.33, bf16[2,1024,640]{2,1,0:T(8,128)(2,1)S(1)} %copy-done, bf16[1,4,32,2,640]{4,2,1,3,0:T(8,128)(2,1)S(1)} %get-tuple-element.9), kind=kOutput, calls=%fused_computation.36 | convolution fusion | flops 335806464 | bytes 3473424 | tf_op jit(solution)/shard_map/inverse_scores/rnxhq,hcq->rnxc/dot_general | solution.py:117
  54.1 1.5 %collective-permute-start.4 = (f32[4,32]{0,1:T(8,128)S(1)}, f32[4,32]{0,1:T(8,128)S(1)}, u32[]{:S(2)}, u32[]{:S(2)}) collective-permute-start(f32[4,32]{0,1:T(8,128)S(1)} %broadcast_select_fusion), channel_id=1, source_target_pairs={{0,1},{1,0},{2,3},{3,2},{4,5},{5,4},{6,7},{7,6},{8,9},{9,8},{10,11... | collective-permute-start | bytes 1544 | tf_op jit(solution)/shard_map/ppermute | solution.py:135
  56.3 1.6 %collective-permute-done.4 = f32[4,32]{0,1:T(8,128)S(1)} collective-permute-done((f32[4,32]{0,1:T(8,128)S(1)}, f32[4,32]{0,1:T(8,128)S(1)}, u32[]{:S(2)}, u32[]{:S(2)}) %collective-permute-start.4) | collective-permute-done | bytes 544 | tf_op jit(solution)/shard_map/ppermute | solution.py:135
  57.9 1.0 %collective-permute-done.6 = f32[4,32]{0,1:T(8,128)S(1)} collective-permute-done((f32[4,32]{0,1:T(8,128)S(1)}, f32[4,32]{0,1:T(8,128)S(1)}, u32[]{:S(2)}, u32[]{:S(2)}) %collective-permute-start.6) | collective-permute-done | bytes 544 | tf_op jit(solution)/shard_map/ppermute | solution.py:135
  59.9 2.5 %collective-permute-start.9 = (f32[4,32]{0,1:T(8,128)S(1)}, f32[4,32]{0,1:T(8,128)S(1)}, u32[]{:S(2)}, u32[]{:S(2)}) collective-permute-start(f32[4,32]{0,1:T(8,128)S(1)} %maximum_maximum_fusion.1), channel_id=1, source_target_pairs={{0,12},{1,13},{2,14},{3,15},{4,8},{5,9},{6,10},{7,11},{8,4},{9,5},... | collective-permute-start | bytes 1544 | tf_op jit(solution)/shard_map/ppermute | solution.py:135
  63.2 1.3 %collective-permute-done.9 = f32[4,32]{0,1:T(8,128)S(1)} collective-permute-done((f32[4,32]{0,1:T(8,128)S(1)}, f32[4,32]{0,1:T(8,128)S(1)}, u32[]{:S(2)}, u32[]{:S(2)}) %collective-permute-start.9) | collective-permute-done | bytes 544 | tf_op jit(solution)/shard_map/ppermute | solution.py:135
  64.5 2.6 %collective-permute-start.10 = (f32[4,32]{0,1:T(8,128)S(1)}, f32[4,32]{0,1:T(8,128)S(1)}, u32[]{:S(2)}, u32[]{:S(2)}) collective-permute-start(f32[4,32]{0,1:T(8,128)S(1)} %maximum_maximum_fusion), channel_id=1, source_target_pairs={{0,16},{1,17},{2,18},{3,19},{4,20},{5,21},{6,22},{7,23},{8,24},{9,... | collective-permute-start | bytes 1544 | tf_op jit(solution)/shard_map/ppermute | solution.py:135
  67.1 2.0 %collective-permute-done.10 = f32[4,32]{0,1:T(8,128)S(1)} collective-permute-done((f32[4,32]{0,1:T(8,128)S(1)}, f32[4,32]{0,1:T(8,128)S(1)}, u32[]{:S(2)}, u32[]{:S(2)}) %collective-permute-start.10) | collective-permute-done | bytes 544 | tf_op jit(solution)/shard_map/ppermute | solution.py:135
  (51 shorter events, 5.3 us)
Async XLA Ops:
  0.6 25.0 %collective-permute-start.1 = (s32[3,2,256]{2,1,0:T(2,128)}, s32[3,2,256]{2,1,0:T(2,128)S(1)}, u32[]{:S(2)}, u32[]{:S(2)}) collective-permute-start(s32[3,2,256]{2,1,0:T(2,128)} %param.16), channel_id=1, source_target_pairs={{0,8},{8,0},{16,24},{24,16},{1,9},{9,1},{17,25},{25,17},{2,10},{10... | collective-permute-start | bytes 18440 | tf_op jit(solution)/shard_map/ppermute | solution.py:164
  4.5 23.8 %collective-permute-start = (f32[11,256]{1,0:T(8,128)S(1)}, f32[11,256]{1,0:T(8,128)S(1)}, u32[]{:S(2)}, u32[]{:S(2)}) collective-permute-start(f32[11,256]{1,0:T(8,128)S(1)} %broadcast_multiply_fusion), channel_id=1, source_target_pairs={{0,1},{1,0},{2,3},{3,2},{4,5},{5,4},{6,7},{7,6},{8,9},{9,8},{10,11... | collective-permute-start | bytes 33800 | tf_op jit(solution)/shard_map/ppermute | solution.py:124
  14.5 28.5 %collective-permute-start.3 = (bf16[11,32,1024]{2,1,0:T(8,128)(2,1)S(1)}, bf16[11,32,1024]{2,1,0:T(8,128)(2,1)}, u32[]{:S(2)}, u32[]{:S(2)}) collective-permute-start(bf16[11,32,1024]{2,1,0:T(8,128)(2,1)S(1)} %all_gather.3), channel_id=1, source_target_pairs={{0,1},{1,0},{2,3},{3,2},{4,5},{5,4},{6,7},{7,6},{8,9},{9,8},{10,11... | collective-permute-start | bytes 2162696 | tf_op jit(solution)/shard_map/ppermute | solution.py:124
  17.0 2.4 %copy-start.3 = (f32[2,16,640]{2,1,0:T(8,128)S(1)}, f32[2,16,640]{2,1,0:T(8,128)}, u32[]{:S(2)}) copy-start(f32[2,16,640]{2,1,0:T(8,128)} %constant.84) | copy-start | bytes 245764
  17.0 2.4 %copy-start.4 = (f32[2,16,640]{2,1,0:T(8,128)S(1)}, f32[2,16,640]{2,1,0:T(8,128)}, u32[]{:S(2)}) copy-start(f32[2,16,640]{2,1,0:T(8,128)} %constant.87) | copy-start | bytes 245764
  17.0 2.4 %copy-start.5 = (f32[2,16,640]{2,1,0:T(8,128)S(1)}, f32[2,16,640]{2,1,0:T(8,128)}, u32[]{:S(2)}) copy-start(f32[2,16,640]{2,1,0:T(8,128)} %constant.90) | copy-start | bytes 245764
  17.1 2.4 %copy-start.6 = (f32[2,16,640]{2,1,0:T(8,128)S(1)}, f32[2,16,640]{2,1,0:T(8,128)}, u32[]{:S(2)}) copy-start(f32[2,16,640]{2,1,0:T(8,128)} %constant.93) | copy-start | bytes 245764
  21.8 1.4 %copy-start.2 = (f32[64,64,1]{1,0,2:T(8,128)S(1)}, f32[64,64,1]{1,0,2:T(8,128)}, u32[]{:S(2)}) copy-start(f32[64,64,1]{1,0,2:T(8,128)} %constant.103) | copy-start | bytes 49156
  23.2 2.4 %copy-start.7 = (s32[3,2,256]{2,1,0:T(2,128)S(1)}, s32[3,2,256]{2,1,0:T(2,128)}, u32[]{:S(2)}) copy-start(s32[3,2,256]{2,1,0:T(2,128)} %param.16) | copy-start | bytes 18436
  25.6 4.7 %collective-permute-start.2 = (s32[3,4,256]{2,1,0:T(4,128)S(1)}, s32[3,4,256]{2,1,0:T(4,128)S(1)}, u32[]{:S(2)}, u32[]{:S(2)}) collective-permute-start(s32[3,4,256]{2,1,0:T(4,128)S(1)} %pad_add_fusion), channel_id=1, source_target_pairs={{0,16},{8,24},{16,0},{24,8},{1,17},{9,25},{17,1},{25,9},{2,18},{10... | collective-permute-start | bytes 36872 | tf_op jit(solution)/shard_map/ppermute | solution.py:164
  30.6 1.9 %copy-start.1 = (f32[2,16,16,640]{3,2,1,0:T(8,128)S(1)}, f32[2,16,16,640]{3,2,1,0:T(8,128)}, u32[]{:S(2)}) copy-start(f32[2,16,16,640]{3,2,1,0:T(8,128)} %multiply_add_fusion.1) | copy-start | bytes 3932164
  35.8 1.3 %copy-start.9 = (f32[64,32,1,1]{0,1,3,2:T(8,128)S(1)}, f32[64,32,1,1]{0,1,3,2:T(8,128)}, u32[]{:S(2)}) copy-start(f32[64,32,1,1]{0,1,3,2:T(8,128)} %constant.102) | copy-start | bytes 24580
  46.7 2.5 %copy-start.8 = (f32[64,32,1,1]{0,1,3,2:T(8,128)S(1)}, f32[64,32,1,1]{0,1,3,2:T(8,128)}, u32[]{:S(2)}) copy-start(f32[64,32,1,1]{0,1,3,2:T(8,128)} %constant.104) | copy-start | bytes 24580
  49.2 0.8 %copy-start.10 = (f32[640]{0:T(1024)S(1)}, f32[640]{0:T(1024)}, u32[]{:S(2)}) copy-start(f32[640]{0:T(1024)} %constant.77.clone) | copy-start | bytes 7684
  51.1 1.7 %copy-start = (bf16[2,1024,640]{2,1,0:T(8,128)(2,1)S(1)}, bf16[2,1024,640]{2,1,0:T(8,128)(2,1)}, u32[]{:S(2)}) copy-start(bf16[2,1024,640]{2,1,0:T(8,128)(2,1)} %get-tuple-element.11) | copy-start | bytes 7864324
  54.1 3.7 %collective-permute-start.4 = (f32[4,32]{0,1:T(8,128)S(1)}, f32[4,32]{0,1:T(8,128)S(1)}, u32[]{:S(2)}, u32[]{:S(2)}) collective-permute-start(f32[4,32]{0,1:T(8,128)S(1)} %broadcast_select_fusion), channel_id=1, source_target_pairs={{0,1},{1,0},{2,3},{3,2},{4,5},{5,4},{6,7},{7,6},{8,9},{9,8},{10,11... | collective-permute-start | bytes 1544 | tf_op jit(solution)/shard_map/ppermute | solution.py:135
  55.7 2.2 %collective-permute-start.5 = (f32[4,32]{0,1:T(8,128)S(1)}, f32[4,32]{0,1:T(8,128)S(1)}, u32[]{:S(2)}, u32[]{:S(2)}) collective-permute-start(f32[4,32]{0,1:T(8,128)S(1)} %broadcast_select_fusion), channel_id=1, source_target_pairs={{0,2},{1,3},{2,0},{3,1},{4,6},{5,7},{6,4},{7,5},{8,10},{9,11},{10,... | collective-permute-start | bytes 1544 | tf_op jit(solution)/shard_map/ppermute | solution.py:135
  55.7 3.2 %collective-permute-start.6 = (f32[4,32]{0,1:T(8,128)S(1)}, f32[4,32]{0,1:T(8,128)S(1)}, u32[]{:S(2)}, u32[]{:S(2)}) collective-permute-start(f32[4,32]{0,1:T(8,128)S(1)} %broadcast_select_fusion), channel_id=1, source_target_pairs={{0,3},{1,2},{2,1},{3,0},{4,7},{5,6},{6,5},{7,4},{8,11},{9,10},{10,... | collective-permute-start | bytes 1544 | tf_op jit(solution)/shard_map/ppermute | solution.py:135
  58.9 3.7 %collective-permute-start.7 = (f32[4,32]{0,1:T(8,128)S(1)}, f32[4,32]{0,1:T(8,128)S(1)}, u32[]{:S(2)}, u32[]{:S(2)}) collective-permute-start(f32[4,32]{0,1:T(8,128)S(1)} %maximum_maximum_fusion.1), channel_id=1, source_target_pairs={{0,4},{1,5},{2,6},{3,7},{4,0},{5,1},{6,2},{7,3},{8,12},{9,13},{10,... | collective-permute-start | bytes 1544 | tf_op jit(solution)/shard_map/ppermute | solution.py:135
  59.4 3.7 %collective-permute-start.8 = (f32[4,32]{0,1:T(8,128)S(1)}, f32[4,32]{0,1:T(8,128)S(1)}, u32[]{:S(2)}, u32[]{:S(2)}) collective-permute-start(f32[4,32]{0,1:T(8,128)S(1)} %maximum_maximum_fusion.1), channel_id=1, source_target_pairs={{0,8},{1,9},{2,10},{3,11},{4,12},{5,13},{6,14},{7,15},{8,0},{9,1},... | collective-permute-start | bytes 1544 | tf_op jit(solution)/shard_map/ppermute | solution.py:135
  59.9 4.6 %collective-permute-start.9 = (f32[4,32]{0,1:T(8,128)S(1)}, f32[4,32]{0,1:T(8,128)S(1)}, u32[]{:S(2)}, u32[]{:S(2)}) collective-permute-start(f32[4,32]{0,1:T(8,128)S(1)} %maximum_maximum_fusion.1), channel_id=1, source_target_pairs={{0,12},{1,13},{2,14},{3,15},{4,8},{5,9},{6,10},{7,11},{8,4},{9,5},... | collective-permute-start | bytes 1544 | tf_op jit(solution)/shard_map/ppermute | solution.py:135
  64.5 4.6 %collective-permute-start.10 = (f32[4,32]{0,1:T(8,128)S(1)}, f32[4,32]{0,1:T(8,128)S(1)}, u32[]{:S(2)}, u32[]{:S(2)}) collective-permute-start(f32[4,32]{0,1:T(8,128)S(1)} %maximum_maximum_fusion), channel_id=1, source_target_pairs={{0,16},{1,17},{2,18},{3,19},{4,20},{5,21},{6,22},{7,23},{8,24},{9,... | collective-permute-start | bytes 1544 | tf_op jit(solution)/shard_map/ppermute | solution.py:135

commit v13 on v12

--- a/solution.py
+++ b/solution.py
@@ -174,10 +174,13 @@
         coefficients = jnp.concatenate(gather_by_permutes(coefficients, "term", term_count, term))
         with jax.named_scope("twiddle_tables"):
             factors = plane_factors()
-            table_hi, table_lo = split_bf16(plane_table(factors, G))
-            box_table = plane_table(factors, LB)
-            tables = lax.optimization_barrier((box_table, table_hi, table_lo))
-            box_table, table_hi, table_lo = tables
+            full = plane_table(factors, G)
+            table_hi = lax.reduce_precision(full, exponent_bits=8, mantissa_bits=7)
+            table_lo = (plane_table(factors, G) - table_hi).astype(jnp.bfloat16)
+            table_hi = table_hi.astype(jnp.bfloat16)
+            table_hi, table_lo = lax.optimization_barrier((table_hi, table_lo))
+            box_rows = table_hi.astype(jnp.float32) + table_lo.astype(jnp.float32)
+            box_table = box_rows.reshape(2, G, G, WIDTH)[:, :LB, :LB].reshape(2, LB * LB, WIDTH)
         with jax.named_scope("ligand_spectra"):
             lig_spec = ligand_spectra(voxels, coefficients, box_table)
         products = 0.0

time: 70.6 us -> 72.7 us (1.030)
  local copies, waits for them, and re-layouts: 4.39 us -> 6.26 us
    add x0 -> x1, other arithmetic: none -> 2.96 us  [body(): box_rows = table_hi.astype(jnp.float32) + table_lo.astype(jnp.float32)]
    convert_element_type x3 -> x2, other arithmetic: 2.69 us -> 0.33 us  [split_bf16(): return (upper.astype(jnp.bfloat16), lower.astype(jnp.bfloat16))]
    slice x0 -> x1, local copies, waits for them, and re-layouts: none -> 1.41 us  [body(): box_rows.reshape(2, G, G, WIDTH)[:, :LB, :LB].reshape(2, LB * LB, WIDTH)]
    add x2 -> x1, other arithmetic: 3.27 us -> 2.02 us  [plane_table(): first[:, :, None, :] * second[:, None, :, :]]
    convert_element_type x0 -> x1, other arithmetic: none -> 0.86 us  [body(): table_lo = (plane_table(factors, G) - table_hi).astype(jnp.bfloat16)]
  transfers between devices with their start and end apart: 11 -> 11, of which waited for: 7 -> 7; matrix products, arithmetic and copies ran while one was open for 34% -> 35% of each run, Pallas kernels for 0% -> 0%
where the time goes in v13:
time: 72.7 us; the launch traced here: 72.3 us
  matrix products  21.5 us (30%)
  starting transfers between devices  16 us (22%)
  other arithmetic  10.5 us (14%)
  waiting for transfers between devices  8.72 us (12%)
  blocking collectives  8.44 us (12%)
  local copies, waits for them, and re-layouts  6.26 us (9%)
  between operations  0.92 us (1%)
    all_gather x1, blocking collectives, body(): own_rows = lax.all_gather(receptor_grids, 'inner', axis=1, tiled=True)  8.44 us
    ppermute x7, starting transfers between devices, butterfly_max(): received.append(lax.ppermute(values, axes, pairs))  8.24 us
    ppermute x7, waiting for transfers between devices, butterfly_max(): received.append(lax.ppermute(values, axes, pairs))  6.71 us
    dot_general x1, matrix products, ligand_spectra(): return jnp.einsum('pk,ntkq->tnpq', mix_tables(LB), plane, precision=HIGH)  5.81 us
    ppermute x2, starting transfers between devices, body(): moved = lax.ppermute(cells_here, 'plane', pairs)  5.74 us
    dot_general x2, matrix products, receptor_mixed(): return jnp.einsum('pk,trkq->trpq', mix_tables(G), plane, precision=HIGH)  3.45 us
    dot_general x2, matrix products, receptor_mixed(): jnp.einsum('trxc,hcq->trhxq', grids, table_hi, preferred_element_type=jnp...  3.33 us
    dot_general x1, matrix products, ligand_spectra(): plane = jnp.einsum('ntxc,hcq->nthxq', grid, box_table, precision=HIGH)  3.28 us
  transfers between devices with their start and end apart: 11, of which 7 were waited for; matrix products, arithmetic and copies ran while one was open for 35% of the time, Pallas kernels for 0%

profile of v13, /device:TPU:0, one launch (start us, length us, event | category | flops | bytes accessed | tf_op | source)
XLA Modules:
  0.0 72.3 jit_solution(7457963867551330183)
XLA Ops:
  0.6 3.1 %collective-permute-start.1 = (s32[3,2,256]{2,1,0:T(2,128)}, s32[3,2,256]{2,1,0:T(2,128)S(1)}, u32[]{:S(2)}, u32[]{:S(2)}) collective-permute-start(s32[3,2,256]{2,1,0:T(2,128)} %param.16), channel_id=1, source_target_pairs={{0,8},{8,0},{16,24},{24,16},{1,9},{9,1},{17,25},{25,17},{2,10},{10... | collective-permute-start | bytes 18440 | tf_op jit(solution)/shard_map/ppermute | solution.py:164
  3.7 0.8 %broadcast_multiply_fusion = f32[11,256]{1,0:T(8,128)S(1)} fusion(f32[11,256]{1,0:T(8,128)} %param.15, f32[11]{0:T(128)} %param.14), kind=kLoop, calls=%fused_computation.87 | loop fusion | flops 2816 | bytes 22572 | tf_op jit(solution)/shard_map/mul | solution.py:173
  4.5 1.5 %collective-permute-start = (f32[11,256]{1,0:T(8,128)S(1)}, f32[11,256]{1,0:T(8,128)S(1)}, u32[]{:S(2)}, u32[]{:S(2)}) collective-permute-start(f32[11,256]{1,0:T(8,128)S(1)} %broadcast_multiply_fusion), channel_id=1, source_target_pairs={{0,1},{1,0},{2,3},{3,2},{4,5},{5,4},{6,7},{7,6},{8,9},{9,8},{10,11... | collective-permute-start | bytes 33800 | tf_op jit(solution)/shard_map/ppermute | solution.py:124
  6.0 8.4 %all_gather.3 = bf16[11,32,1024]{2,1,0:T(8,128)(2,1)S(1)} all-gather(bf16[11,8,1024]{2,1,0:T(8,128)(2,1)} %param.13), channel_id=1, replica_groups=mesh['plane'=4,'inner'=4,'term'=2] {'inner'}, dimensions={1}, use_global_device_ids=true | all-gather | bytes 901120 | tf_op jit(solution)/shard_map/all_gather | solution.py:152
  15.0 2.0 %multiply_add_fusion = f32[2,32,32,640]{3,2,1,0:T(8,128)S(1)} fusion(f32[2,32,640]{2,1,0:T(8,128)} %constant.89, f32[2,32,640]{2,1,0:T(8,128)} %constant.87, f32[2,32,640]{2,1,0:T(8,128)} %constant.85, f32[2,32,640]{2,1,0:T(8,128)} %constant.83), kind=kLoop, calls=%fused_computation.5 | loop fusion | flops 3932160 | bytes 5898240 | tf_op jit(solution)/shard_map/twiddle_tables/add | solution.py:45
  17.0 0.9 %fusion = (bf16[2,1024,640]{2,1,0:T(8,128)(2,1)S(1)}, bf16[2,1024,640]{2,1,0:T(8,128)(2,1)S(1)}) fusion(f32[2,32,32,640]{3,2,1,0:T(8,128)S(1)} %multiply_add_fusion), kind=kLoop, calls=%fused_computation.3 | loop fusion | flops 5242880 | bytes 10485760 | tf_op jit(solution)/shard_map/twiddle_tables/convert_element_type | solution.py:179
  17.9 1.1 %fusion.13 = f32[11,1,2,32,640]{4,3,0,2,1:T(8,128)S(1)} fusion(bf16[2,1024,640]{2,1,0:T(8,128)(2,1)S(1)} %get-tuple-element.6, bf16[11,32,1024]{2,1,0:T(8,128)(2,1)S(1)} %all_gather.3), kind=kOutput, calls=%fused_computation.25 | convolution fusion | flops 922746880 | bytes 5144576 | tf_op jit(solution)/shard_map/receptor_spectra/trxc,hcq->trhxq/dot_general | solution.py:71
  19.4 3.0 %convert_add_fusion = f32[2,1024,640]{2,1,0:T(8,128)} fusion(bf16[2,1024,640]{2,1,0:T(8,128)(2,1)S(1)} %get-tuple-element.7, bf16[2,1024,640]{2,1,0:T(8,128)(2,1)S(1)} %get-tuple-element.6), kind=kLoop, calls=%fused_computation.4 | loop fusion | flops 3932160 | bytes 10485760 | tf_op jit(solution)/shard_map/twiddle_tables/add | solution.py:182
  22.3 1.4 %copy.21 = f32[11,1,2,32,640]{4,3,2,0,1:T(8,128)} copy(f32[11,1,2,32,640]{4,3,0,2,1:T(8,128)S(1)} %fusion.13) | data formatting | bytes 3604480 | tf_op jit(solution)/shard_map/receptor_spectra/trxc,hcq->trhxq/transpose | solution.py:71
  23.8 2.4 %convolution_bitcast_fusion.3 = f32[11,1,64,640]{3,2,0,1:T(8,128)S(1)} fusion(f32[11,64,640]{2,1,0:T(8,128)} %bitcast.154, f32[64,64,1]{1,0,2:T(8,128)S(1)} %copy-done.2), kind=kOutput, calls=%fused_computation.28 | convolution fusion | flops 173015040 | bytes 3620864 | tf_op jit(solution)/shard_map/receptor_spectra/pk,trkq->trpq/dot_general | solution.py:73
  26.2 1.4 %slice.70 = f32[2,16,16,640]{3,2,1,0:T(8,128)S(1)} slice(f32[2,32,32,640]{3,2,1,0:T(8,128)} %bitcast.153), slice={[0:2], [0:16], [0:16], [0:640]} | slice | bytes 2621440 | tf_op jit(solution)/shard_map/twiddle_tables/slice | solution.py:183
  27.7 2.6 %collective-permute-start.2 = (s32[3,4,256]{2,1,0:T(4,128)S(1)}, s32[3,4,256]{2,1,0:T(4,128)S(1)}, u32[]{:S(2)}, u32[]{:S(2)}) collective-permute-start(s32[3,4,256]{2,1,0:T(4,128)S(1)} %pad_add_fusion), channel_id=1, source_target_pairs={{0,16},{8,24},{16,0},{24,8},{1,17},{9,25},{17,1},{25,9},{2,18},{10... | collective-permute-start | bytes 36872 | tf_op jit(solution)/shard_map/ppermute | solution.py:164
  30.3 2.0 %collective-permute-done.2 = s32[3,4,256]{2,1,0:T(4,128)S(1)} collective-permute-done((s32[3,4,256]{2,1,0:T(4,128)S(1)}, s32[3,4,256]{2,1,0:T(4,128)S(1)}, u32[]{:S(2)}, u32[]{:S(2)}) %collective-permute-start.2) | collective-permute-done | bytes 12320 | tf_op jit(solution)/shard_map/ppermute | solution.py:164
  32.7 0.8 %fusion.39 = f32[4,22,16,256]{3,1,2,0:T(8,128)S(1)} fusion(bf16[4,22,16,256]{3,2,1,0:T(8,128)(2,1)S(1)} %get-tuple-element.26, s32[4,256]{1,0:T(4,128)S(1)} %get-tuple-element.28), kind=kOutput, calls=%fused_computation.38 | convolution fusion | flops 184811520 | bytes 2166784 | tf_op jit(solution)/shard_map/ligand_spectra/ntxa,nac->ntxc/dot_general | solution.py:86
  33.5 1.0 %fusion.41 = f32[4,22,16,256]{3,1,2,0:T(8,128)S(1)} fusion(bf16[4,22,16,256]{3,2,1,0:T(8,128)(2,1)S(1)} %get-tuple-element.27, s32[4,256]{1,0:T(4,128)S(1)} %get-tuple-element.28), kind=kOutput, calls=%fused_computation.39 | convolution fusion | flops 184811520 | bytes 2166784 | tf_op jit(solution)/shard_map/ligand_spectra/ntxa,nac->ntxc/dot_general | solution.py:85
  34.6 3.3 %convolution_bitcast_fusion.1 = f32[4,22,2,16,640]{4,1,3,0,2:T(8,128)S(1)} fusion(f32[2,256,640,1,1]{2,1,4,3,0:T(8,128)S(1)} %bitcast.158, f32[4,22,16,256]{3,1,2,0:T(8,128)S(1)} %fusion.41, f32[4,22,16,256]{3,1,2,0:T(8,128)S(1)} %fusion.39), kind=kOutput, calls=%fused_computation.10 | convolution fusion | flops 2768601088 | bytes 11403264 | tf_op jit(solution)/shard_map/ligand_spectra/ntxc,hcq->nthxq/dot_general | solution.py:87
  37.9 1.3 %copy.20 = f32[4,22,2,16,640]{4,3,2,1,0:T(8,128)S(1)} copy(f32[4,22,2,16,640]{4,1,3,0,2:T(8,128)S(1)} %convolution_bitcast_fusion.1) | data formatting | bytes 14417920 | tf_op jit(solution)/shard_map/ligand_spectra/ntxc,hcq->nthxq/transpose | solution.py:87
  39.1 5.8 %convolution_bitcast_fusion = f32[22,4,64,640]{3,2,0,1:T(8,128)S(1)} fusion(f32[4,22,32,640]{3,2,1,0:T(8,128)S(1)} %bitcast.152, f32[64,32,1,1]{0,1,3,2:T(8,128)S(1)} %copy-done.5), kind=kOutput, calls=%fused_computation | convolution fusion | flops 692060160 | bytes 21635072 | tf_op jit(solution)/shard_map/ligand_spectra/pk,ntkq->tnpq/dot_general | solution.py:90
  45.0 2.2 %fusion.16 = f32[11,1,2,32,640]{4,3,0,2,1:T(8,128)S(1)} fusion(bf16[2,1024,640]{2,1,0:T(8,128)(2,1)S(1)} %get-tuple-element.6, bf16[11,32,1024]{2,1,0:T(8,128)(2,1)} %collective-permute-done.3), kind=kOutput, calls=%fused_computation.26 | convolution fusion | flops 922746880 | bytes 5144576 | tf_op jit(solution)/shard_map/receptor_spectra/trxc,hcq->trhxq/dot_general | solution.py:71
  47.3 1.1 %convolution_bitcast_fusion.2 = f32[11,1,64,640]{3,2,0,1:T(8,128)S(1)} fusion(f32[11,64,640]{2,1,0:T(8,128)S(1)} %bitcast.155, f32[64,64,1]{1,0,2:T(8,128)S(1)} %copy-done.2), kind=kOutput, calls=%fused_computation.27 | convolution fusion | flops 173015040 | bytes 3620864 | tf_op jit(solution)/shard_map/receptor_spectra/pk,trkq->trpq/dot_general | solution.py:73
  48.8 2.5 %add_reduce_fusion = (f32[4,32,640]{2,1,0:T(8,128)S(1)}, f32[4,32,640]{2,1,0:T(8,128)S(1)}, f32[4,32,640]{2,1,0:T(8,128)S(1)}, f32[4,32,640]{2,1,0:T(8,128)S(1)}) fusion(f32[22,4,64,640]{3,2,0,1:T(8,128)S(1)} %convolution_bitcast_fusion, f32[11,32,640]{2,1,0:T(8,128)S(1)} %get-tuple-element.23, f32[11,32,640]{2,1,0:T(8,128)S(1)} %get-tuple-element.22, ...), kind=kLoop, calls=%fused_computation.7 | loop fusion | flops 14090240 | bytes 19333120 | tf_op jit(solution)/shard_map/correlate/reduce_sum | solution.py:98
  52.2 1.0 %fusion.20 = f32[4,32,1024]{2,1,0:T(8,128)S(1)} fusion(bf16[2,1024,640]{2,1,0:T(8,128)(2,1)S(1)} %get-tuple-element.6, bf16[1,4,32,2,640]{4,2,1,3,0:T(8,128)(2,1)S(1)} %get-tuple-element.8), kind=kOutput, calls=%fused_computation.30 | convolution fusion | flops 335544320 | bytes 3473408 | tf_op jit(solution)/shard_map/inverse_scores/rnxhq,hcq->rnxc/dot_general | solution.py:115
  53.2 1.0 %fusion.32 = f32[4,32,1024]{2,1,0:T(8,128)S(1)} fusion(f32[4,32,1024]{2,1,0:T(8,128)S(1)} %fusion.20, bf16[2,1024,640]{2,1,0:T(8,128)(2,1)S(1)} %get-tuple-element.6, bf16[1,4,32,2,640]{4,2,1,3,0:T(8,128)(2,1)S(1)} %get-tuple-element.9), kind=kOutput, calls=%fused_computation.34 | convolution fusion | flops 335675392 | bytes 3997696 | tf_op jit(solution)/shard_map/inverse_scores/rnxhq,hcq->rnxc/dot_general | solution.py:116
  54.2 0.7 %copy-done.1 = bf16[2,1024,640]{2,1,0:T(8,128)(2,1)S(1)} copy-done((bf16[2,1024,640]{2,1,0:T(8,128)(2,1)S(1)}, bf16[2,1024,640]{2,1,0:T(8,128)(2,1)}, u32[]{:S(2)}) %copy-start.1) | copy-done | bytes 2621464
  54.9 1.1 %fusion.35 = f32[4]{0:T(128)S(1)} fusion(f32[4,32,1024]{2,1,0:T(8,128)S(1)} %fusion.32, bf16[2,1024,640]{2,1,0:T(8,128)(2,1)S(1)} %copy-done.1, bf16[1,4,32,2,640]{4,2,1,3,0:T(8,128)(2,1)S(1)} %get-tuple-element.8), kind=kOutput, calls=%fused_computation.35 | convolution fusion | flops 335806464 | bytes 3473424 | tf_op jit(solution)/shard_map/inverse_scores/rnxhq,hcq->rnxc/dot_general | solution.py:117
  56.2 1.5 %collective-permute-start.4 = (f32[4,32]{0,1:T(8,128)S(1)}, f32[4,32]{0,1:T(8,128)S(1)}, u32[]{:S(2)}, u32[]{:S(2)}) collective-permute-start(f32[4,32]{0,1:T(8,128)S(1)} %broadcast_select_fusion), channel_id=1, source_target_pairs={{0,1},{1,0},{2,3},{3,2},{4,5},{5,4},{6,7},{7,6},{8,9},{9,8},{10,11... | collective-permute-start | bytes 1544 | tf_op jit(solution)/shard_map/ppermute | solution.py:135
  58.3 1.6 %collective-permute-done.4 = f32[4,32]{0,1:T(8,128)S(1)} collective-permute-done((f32[4,32]{0,1:T(8,128)S(1)}, f32[4,32]{0,1:T(8,128)S(1)}, u32[]{:S(2)}, u32[]{:S(2)}) %collective-permute-start.4) | collective-permute-done | bytes 544 | tf_op jit(solution)/shard_map/ppermute | solution.py:135
  59.9 0.9 %collective-permute-done.6 = f32[4,32]{0,1:T(8,128)S(1)} collective-permute-done((f32[4,32]{0,1:T(8,128)S(1)}, f32[4,32]{0,1:T(8,128)S(1)}, u32[]{:S(2)}, u32[]{:S(2)}) %collective-permute-start.6) | collective-permute-done | bytes 544 | tf_op jit(solution)/shard_map/ppermute | solution.py:135
  61.9 2.5 %collective-permute-start.9 = (f32[4,32]{0,1:T(8,128)S(1)}, f32[4,32]{0,1:T(8,128)S(1)}, u32[]{:S(2)}, u32[]{:S(2)}) collective-permute-start(f32[4,32]{0,1:T(8,128)S(1)} %maximum_maximum_fusion.1), channel_id=1, source_target_pairs={{0,12},{1,13},{2,14},{3,15},{4,8},{5,9},{6,10},{7,11},{8,4},{9,5},... | collective-permute-start | bytes 1544 | tf_op jit(solution)/shard_map/ppermute | solution.py:135
  65.2 1.3 %collective-permute-done.9 = f32[4,32]{0,1:T(8,128)S(1)} collective-permute-done((f32[4,32]{0,1:T(8,128)S(1)}, f32[4,32]{0,1:T(8,128)S(1)}, u32[]{:S(2)}, u32[]{:S(2)}) %collective-permute-start.9) | collective-permute-done | bytes 544 | tf_op jit(solution)/shard_map/ppermute | solution.py:135
  66.6 2.6 %collective-permute-start.10 = (f32[4,32]{0,1:T(8,128)S(1)}, f32[4,32]{0,1:T(8,128)S(1)}, u32[]{:S(2)}, u32[]{:S(2)}) collective-permute-start(f32[4,32]{0,1:T(8,128)S(1)} %maximum_maximum_fusion), channel_id=1, source_target_pairs={{0,16},{1,17},{2,18},{3,19},{4,20},{5,21},{6,22},{7,23},{8,24},{9,... | collective-permute-start | bytes 1544 | tf_op jit(solution)/shard_map/ppermute | solution.py:135
  69.2 2.0 %collective-permute-done.10 = f32[4,32]{0,1:T(8,128)S(1)} collective-permute-done((f32[4,32]{0,1:T(8,128)S(1)}, f32[4,32]{0,1:T(8,128)S(1)}, u32[]{:S(2)}, u32[]{:S(2)}) %collective-permute-start.10) | collective-permute-done | bytes 544 | tf_op jit(solution)/shard_map/ppermute | solution.py:135
  (44 shorter events, 6.4 us)
Async XLA Ops:
  0.6 27.0 %collective-permute-start.1 = (s32[3,2,256]{2,1,0:T(2,128)}, s32[3,2,256]{2,1,0:T(2,128)S(1)}, u32[]{:S(2)}, u32[]{:S(2)}) collective-permute-start(s32[3,2,256]{2,1,0:T(2,128)} %param.16), channel_id=1, source_target_pairs={{0,8},{8,0},{16,24},{24,16},{1,9},{9,1},{17,25},{25,17},{2,10},{10... | collective-permute-start | bytes 18440 | tf_op jit(solution)/shard_map/ppermute | solution.py:164
  4.5 25.8 %collective-permute-start = (f32[11,256]{1,0:T(8,128)S(1)}, f32[11,256]{1,0:T(8,128)S(1)}, u32[]{:S(2)}, u32[]{:S(2)}) collective-permute-start(f32[11,256]{1,0:T(8,128)S(1)} %broadcast_multiply_fusion), channel_id=1, source_target_pairs={{0,1},{1,0},{2,3},{3,2},{4,5},{5,4},{6,7},{7,6},{8,9},{9,8},{10,11... | collective-permute-start | bytes 33800 | tf_op jit(solution)/shard_map/ppermute | solution.py:124
  14.5 30.5 %collective-permute-start.3 = (bf16[11,32,1024]{2,1,0:T(8,128)(2,1)S(1)}, bf16[11,32,1024]{2,1,0:T(8,128)(2,1)}, u32[]{:S(2)}, u32[]{:S(2)}) collective-permute-start(bf16[11,32,1024]{2,1,0:T(8,128)(2,1)S(1)} %all_gather.3), channel_id=1, source_target_pairs={{0,1},{1,0},{2,3},{3,2},{4,5},{5,4},{6,7},{7,6},{8,9},{9,8},{10,11... | collective-permute-start | bytes 2162696 | tf_op jit(solution)/shard_map/ppermute | solution.py:124
  17.9 1.5 %copy-start = (bf16[2,1024,640]{2,1,0:T(8,128)(2,1)}, bf16[2,1024,640]{2,1,0:T(8,128)(2,1)S(1)}, u32[]{:S(2)}) copy-start(bf16[2,1024,640]{2,1,0:T(8,128)(2,1)S(1)} %get-tuple-element.7) | copy-start | bytes 7864324
  22.3 1.5 %copy-start.2 = (f32[64,64,1]{1,0,2:T(8,128)S(1)}, f32[64,64,1]{1,0,2:T(8,128)}, u32[]{:S(2)}) copy-start(f32[64,64,1]{1,0,2:T(8,128)} %constant.91) | copy-start | bytes 49156
  23.8 3.9 %copy-start.3 = (s32[3,2,256]{2,1,0:T(2,128)S(1)}, s32[3,2,256]{2,1,0:T(2,128)}, u32[]{:S(2)}) copy-start(s32[3,2,256]{2,1,0:T(2,128)} %param.16) | copy-start | bytes 18436
  27.7 4.7 %collective-permute-start.2 = (s32[3,4,256]{2,1,0:T(4,128)S(1)}, s32[3,4,256]{2,1,0:T(4,128)S(1)}, u32[]{:S(2)}, u32[]{:S(2)}) collective-permute-start(s32[3,4,256]{2,1,0:T(4,128)S(1)} %pad_add_fusion), channel_id=1, source_target_pairs={{0,16},{8,24},{16,0},{24,8},{1,17},{9,25},{17,1},{25,9},{2,18},{10... | collective-permute-start | bytes 36872 | tf_op jit(solution)/shard_map/ppermute | solution.py:164
  37.8 1.3 %copy-start.5 = (f32[64,32,1,1]{0,1,3,2:T(8,128)S(1)}, f32[64,32,1,1]{0,1,3,2:T(8,128)}, u32[]{:S(2)}) copy-start(f32[64,32,1,1]{0,1,3,2:T(8,128)} %constant.90) | copy-start | bytes 24580
  48.7 2.5 %copy-start.4 = (f32[64,32,1,1]{0,1,3,2:T(8,128)S(1)}, f32[64,32,1,1]{0,1,3,2:T(8,128)}, u32[]{:S(2)}) copy-start(f32[64,32,1,1]{0,1,3,2:T(8,128)} %constant.92) | copy-start | bytes 24580
  51.3 0.8 %copy-start.6 = (f32[640]{0:T(1024)S(1)}, f32[640]{0:T(1024)}, u32[]{:S(2)}) copy-start(f32[640]{0:T(1024)} %constant.77.clone) | copy-start | bytes 7684
  53.2 1.7 %copy-start.1 = (bf16[2,1024,640]{2,1,0:T(8,128)(2,1)S(1)}, bf16[2,1024,640]{2,1,0:T(8,128)(2,1)}, u32[]{:S(2)}) copy-start(bf16[2,1024,640]{2,1,0:T(8,128)(2,1)} %copy-done) | copy-start | bytes 7864324
  56.2 3.7 %collective-permute-start.4 = (f32[4,32]{0,1:T(8,128)S(1)}, f32[4,32]{0,1:T(8,128)S(1)}, u32[]{:S(2)}, u32[]{:S(2)}) collective-permute-start(f32[4,32]{0,1:T(8,128)S(1)} %broadcast_select_fusion), channel_id=1, source_target_pairs={{0,1},{1,0},{2,3},{3,2},{4,5},{5,4},{6,7},{7,6},{8,9},{9,8},{10,11... | collective-permute-start | bytes 1544 | tf_op jit(solution)/shard_map/ppermute | solution.py:135
  57.7 2.2 %collective-permute-start.5 = (f32[4,32]{0,1:T(8,128)S(1)}, f32[4,32]{0,1:T(8,128)S(1)}, u32[]{:S(2)}, u32[]{:S(2)}) collective-permute-start(f32[4,32]{0,1:T(8,128)S(1)} %broadcast_select_fusion), channel_id=1, source_target_pairs={{0,2},{1,3},{2,0},{3,1},{4,6},{5,7},{6,4},{7,5},{8,10},{9,11},{10,... | collective-permute-start | bytes 1544 | tf_op jit(solution)/shard_map/ppermute | solution.py:135
  57.7 3.2 %collective-permute-start.6 = (f32[4,32]{0,1:T(8,128)S(1)}, f32[4,32]{0,1:T(8,128)S(1)}, u32[]{:S(2)}, u32[]{:S(2)}) collective-permute-start(f32[4,32]{0,1:T(8,128)S(1)} %broadcast_select_fusion), channel_id=1, source_target_pairs={{0,3},{1,2},{2,1},{3,0},{4,7},{5,6},{6,5},{7,4},{8,11},{9,10},{10,... | collective-permute-start | bytes 1544 | tf_op jit(solution)/shard_map/ppermute | solution.py:135
  61.0 3.7 %collective-permute-start.7 = (f32[4,32]{0,1:T(8,128)S(1)}, f32[4,32]{0,1:T(8,128)S(1)}, u32[]{:S(2)}, u32[]{:S(2)}) collective-permute-start(f32[4,32]{0,1:T(8,128)S(1)} %maximum_maximum_fusion.1), channel_id=1, source_target_pairs={{0,4},{1,5},{2,6},{3,7},{4,0},{5,1},{6,2},{7,3},{8,12},{9,13},{10,... | collective-permute-start | bytes 1544 | tf_op jit(solution)/shard_map/ppermute | solution.py:135
  61.5 3.7 %collective-permute-start.8 = (f32[4,32]{0,1:T(8,128)S(1)}, f32[4,32]{0,1:T(8,128)S(1)}, u32[]{:S(2)}, u32[]{:S(2)}) collective-permute-start(f32[4,32]{0,1:T(8,128)S(1)} %maximum_maximum_fusion.1), channel_id=1, source_target_pairs={{0,8},{1,9},{2,10},{3,11},{4,12},{5,13},{6,14},{7,15},{8,0},{9,1},... | collective-permute-start | bytes 1544 | tf_op jit(solution)/shard_map/ppermute | solution.py:135
  61.9 4.6 %collective-permute-start.9 = (f32[4,32]{0,1:T(8,128)S(1)}, f32[4,32]{0,1:T(8,128)S(1)}, u32[]{:S(2)}, u32[]{:S(2)}) collective-permute-start(f32[4,32]{0,1:T(8,128)S(1)} %maximum_maximum_fusion.1), channel_id=1, source_target_pairs={{0,12},{1,13},{2,14},{3,15},{4,8},{5,9},{6,10},{7,11},{8,4},{9,5},... | collective-permute-start | bytes 1544 | tf_op jit(solution)/shard_map/ppermute | solution.py:135
  66.6 4.6 %collective-permute-start.10 = (f32[4,32]{0,1:T(8,128)S(1)}, f32[4,32]{0,1:T(8,128)S(1)}, u32[]{:S(2)}, u32[]{:S(2)}) collective-permute-start(f32[4,32]{0,1:T(8,128)S(1)} %maximum_maximum_fusion), channel_id=1, source_target_pairs={{0,16},{1,17},{2,18},{3,19},{4,20},{5,21},{6,22},{7,23},{8,24},{9,... | collective-permute-start | bytes 1544 | tf_op jit(solution)/shard_map/ppermute | solution.py:135

commit v14 on v12

--- a/solution.py
+++ b/solution.py
@@ -81,9 +81,10 @@
     in_x = (voxels[0][:, None, :] == x_cells[None, :, None]).astype(jnp.float32)
     weights = coefficients[None, :, None, :] * in_x[:, None, :, :]
     upper, lower = split_bf16(weights)
-    form = "ntxa,nac->ntxc"
-    grid = jnp.einsum(form, upper, onehot, preferred_element_type=jnp.float32)
-    grid = grid + jnp.einsum(form, lower, onehot, preferred_element_type=jnp.float32)
+    terms = upper.shape[1]
+    both = jnp.concatenate([upper, lower], axis=1)
+    both = jnp.einsum("ntxa,nac->ntxc", both, onehot, preferred_element_type=jnp.float32)
+    grid = both[:, :terms] + both[:, terms:]
     plane = jnp.einsum("ntxc,hcq->nthxq", grid, box_table, precision=HIGH)
     rot_count, terms = plane.shape[0], plane.shape[1]
     plane = plane.reshape(rot_count, terms, 2 * LB, WIDTH)
@@ -112,8 +113,10 @@
     joined = jnp.stack([inv_re * fold, -inv_im * fold], axis=3)
     upper, lower = lax.optimization_barrier(split_bf16(joined))
     form = "rnxhq,hcq->rnxc"
-    scores = jnp.einsum(form, upper, table_hi, preferred_element_type=jnp.float32)
-    scores = scores + jnp.einsum(form, lower, table_hi, preferred_element_type=jnp.float32)
+    count = upper.shape[0]
+    both = jnp.concatenate([upper, lower], axis=0)
+    both = jnp.einsum(form, both, table_hi, preferred_element_type=jnp.float32)
+    scores = both[:count] + both[count:]
     return scores + jnp.einsum(form, upper, table_lo, preferred_element_type=jnp.float32)
 
 

time: 70.6 us -> 73.5 us (1.041)
  local copies, waits for them, and re-layouts: 4.39 us -> 5.45 us
  waiting for transfers between devices: 8.73 us -> 9.58 us
    dot_general x2, matrix products: 3.31 us -> 5.32 us  [receptor_mixed(): jnp.einsum('trxc,hcq->trhxq', grids, table_hi, preferred_element_type=jnp...]
    dot_general x4 -> x2, matrix products: 3.83 us -> 2.03 us  [the longest x1 1.16 us: ligand_spectra(): jnp.einsum('ntxa,nac->ntxc', both, onehot, preferred_element_type=jnp.flo...]
    unnamed x22 -> x24, local copies, waits for them, and re-layouts: 0.8 us -> 1.88 us
    ppermute x7, waiting for transfers between devices: 6.72 us -> 7.59 us  [butterfly_max(): received.append(lax.ppermute(values, axes, pairs))]
  transfers between devices with their start and end apart: 11 -> 11, of which waited for: 7 -> 6; matrix products, arithmetic and copies ran while one was open for 34% -> 35% of each run, Pallas kernels for 0% -> 0%
where the time goes in v14:
time: 73.5 us; the launch traced here: 73.2 us
  matrix products  22.2 us (30%)
  starting transfers between devices  16 us (22%)
  other arithmetic  10.6 us (14%)
  waiting for transfers between devices  9.58 us (13%)
  blocking collectives  8.44 us (11%)
  local copies, waits for them, and re-layouts  5.45 us (7%)
  between operations  0.94 us (1%)
    all_gather x1, blocking collectives, body(): own_rows = lax.all_gather(receptor_grids, 'inner', axis=1, tiled=True)  8.44 us
    ppermute x7, starting transfers between devices, butterfly_max(): received.append(lax.ppermute(values, axes, pairs))  8.22 us
    ppermute x7, waiting for transfers between devices, butterfly_max(): received.append(lax.ppermute(values, axes, pairs))  7.59 us
    dot_general x1, matrix products, ligand_spectra(): return jnp.einsum('pk,ntkq->tnpq', mix_tables(LB), plane, precision=HIGH)  5.81 us
    ppermute x2, starting transfers between devices, body(): moved = lax.ppermute(cells_here, 'plane', pairs)  5.76 us
    dot_general x2, matrix products, receptor_mixed(): jnp.einsum('trxc,hcq->trhxq', grids, table_hi, preferred_element_type=jnp...  5.32 us
    dot_general x1, matrix products, ligand_spectra(): plane = jnp.einsum('ntxc,hcq->nthxq', grid, box_table, precision=HIGH)  3.99 us
    add x2, other arithmetic, plane_table(): first[:, :, None, :] * second[:, None, :, :]  3.27 us
  transfers between devices with their start and end apart: 11, of which 6 were waited for; matrix products, arithmetic and copies ran while one was open for 35% of the time, Pallas kernels for 0%

profile of v14, /device:TPU:0, one launch (start us, length us, event | category | flops | bytes accessed | tf_op | source)
XLA Modules:
  0.0 73.2 jit_solution(9171947030485842047)
XLA Ops:
  0.6 3.1 %collective-permute-start.1 = (s32[3,2,256]{2,1,0:T(2,128)}, s32[3,2,256]{2,1,0:T(2,128)S(1)}, u32[]{:S(2)}, u32[]{:S(2)}) collective-permute-start(s32[3,2,256]{2,1,0:T(2,128)} %param.16), channel_id=1, source_target_pairs={{0,8},{8,0},{16,24},{24,16},{1,9},{9,1},{17,25},{25,17},{2,10},{10... | collective-permute-start | bytes 18440 | tf_op jit(solution)/shard_map/ppermute | solution.py:167
  3.7 0.8 %broadcast_multiply_fusion = f32[11,256]{1,0:T(8,128)S(1)} fusion(f32[11,256]{1,0:T(8,128)} %param.15, f32[11]{0:T(128)} %param.14), kind=kLoop, calls=%fused_computation.86 | loop fusion | flops 2816 | bytes 22572 | tf_op jit(solution)/shard_map/mul | solution.py:176
  4.5 1.5 %collective-permute-start = (f32[11,256]{1,0:T(8,128)S(1)}, f32[11,256]{1,0:T(8,128)S(1)}, u32[]{:S(2)}, u32[]{:S(2)}) collective-permute-start(f32[11,256]{1,0:T(8,128)S(1)} %broadcast_multiply_fusion), channel_id=1, source_target_pairs={{0,1},{1,0},{2,3},{3,2},{4,5},{5,4},{6,7},{7,6},{8,9},{9,8},{10,11... | collective-permute-start | bytes 33800 | tf_op jit(solution)/shard_map/ppermute | solution.py:127
  6.0 8.4 %all_gather.3 = bf16[11,32,1024]{2,1,0:T(8,128)(2,1)S(1)} all-gather(bf16[11,8,1024]{2,1,0:T(8,128)(2,1)} %param.13), channel_id=1, replica_groups=mesh['plane'=4,'inner'=4,'term'=2] {'inner'}, dimensions={1}, use_global_device_ids=true | all-gather | bytes 901120 | tf_op jit(solution)/shard_map/all_gather | solution.py:155
  15.0 2.0 %multiply_add_fusion = f32[2,32,32,640]{3,2,1,0:T(8,128)S(1)} fusion(f32[2,32,640]{2,1,0:T(8,128)} %constant.101, f32[2,32,640]{2,1,0:T(8,128)} %constant.99, f32[2,32,640]{2,1,0:T(8,128)} %constant.97, f32[2,32,640]{2,1,0:T(8,128)} %constant.95), kind=kLoop, calls=%fused_computation.4 | loop fusion | flops 3932160 | bytes 5898240 | tf_op jit(solution)/shard_map/twiddle_tables/add | solution.py:45
  17.1 2.4 %fusion = (bf16[2,1024,640]{2,1,0:T(8,128)(2,1)S(1)}, bf16[2,1024,640]{2,1,0:T(8,128)(2,1)}) fusion(f32[2,32,32,640]{3,2,1,0:T(8,128)S(1)} %multiply_add_fusion), kind=kLoop, calls=%fused_computation.3 | loop fusion | flops 5242880 | bytes 10485760 | tf_op jit(solution)/shard_map/twiddle_tables/convert_element_type | solution.py:52
  19.5 1.2 %multiply_add_fusion.1 = f32[2,16,16,640]{3,2,1,0:T(8,128)} fusion(f32[2,16,640]{2,1,0:T(8,128)S(1)} %copy-done.4, f32[2,16,640]{2,1,0:T(8,128)S(1)} %copy-done.5, f32[2,16,640]{2,1,0:T(8,128)S(1)} %copy-done.6, f32[2,16,640]{2,1,0:T(8,128)S(1)} %copy-done.7), kind=kLoop, calls=%fused_computation.34 | loop fusion | flops 983040 | bytes 1638400 | tf_op jit(solution)/shard_map/twiddle_tables/add | solution.py:45
  20.7 2.8 %fusion.11 = f32[11,1,2,32,640]{4,3,0,2,1:T(8,128)S(1)} fusion(bf16[2,1024,640]{2,1,0:T(8,128)(2,1)} %get-tuple-element.8, bf16[11,32,1024]{2,1,0:T(8,128)(2,1)S(1)} %all_gather.3), kind=kOutput, calls=%fused_computation.22 | convolution fusion | flops 922746880 | bytes 5144576 | tf_op jit(solution)/shard_map/receptor_spectra/trxc,hcq->trhxq/dot_general | solution.py:71
  23.6 1.4 %copy.22 = f32[11,1,2,32,640]{4,3,2,0,1:T(8,128)} copy(f32[11,1,2,32,640]{4,3,0,2,1:T(8,128)S(1)} %fusion.11) | data formatting | bytes 3604480 | tf_op jit(solution)/shard_map/receptor_spectra/trxc,hcq->trhxq/transpose | solution.py:71
  24.9 2.3 %convolution_bitcast_fusion.3 = f32[11,1,64,640]{3,2,0,1:T(8,128)S(1)} fusion(f32[11,64,640]{2,1,0:T(8,128)} %bitcast.145, f32[64,64,1]{1,0,2:T(8,128)S(1)} %copy-done.3), kind=kOutput, calls=%fused_computation.25 | convolution fusion | flops 173015040 | bytes 3620864 | tf_op jit(solution)/shard_map/receptor_spectra/pk,trkq->trpq/dot_general | solution.py:73
  27.4 2.7 %collective-permute-start.2 = (s32[3,4,256]{2,1,0:T(4,128)S(1)}, s32[3,4,256]{2,1,0:T(4,128)S(1)}, u32[]{:S(2)}, u32[]{:S(2)}) collective-permute-start(s32[3,4,256]{2,1,0:T(4,128)S(1)} %pad_add_fusion), channel_id=1, source_target_pairs={{0,16},{8,24},{16,0},{24,8},{1,17},{9,25},{17,1},{25,9},{2,18},{10... | collective-permute-start | bytes 36872 | tf_op jit(solution)/shard_map/ppermute | solution.py:167
  30.1 2.0 %collective-permute-done.2 = s32[3,4,256]{2,1,0:T(4,128)S(1)} collective-permute-done((s32[3,4,256]{2,1,0:T(4,128)S(1)}, s32[3,4,256]{2,1,0:T(4,128)S(1)}, u32[]{:S(2)}, u32[]{:S(2)}) %collective-permute-start.2) | collective-permute-done | bytes 12320 | tf_op jit(solution)/shard_map/ppermute | solution.py:167
  32.4 1.2 %fusion.18 = f32[4,44,16,256]{3,2,1,0:T(8,128)S(1)} fusion(bf16[4,22,16,256]{3,2,1,0:T(8,128)(2,1)S(1)} %get-tuple-element.29, bf16[4,22,16,256]{3,2,1,0:T(8,128)(2,1)S(1)} %get-tuple-element.28, s32[4,256]{1,0:T(4,128)S(1)} %get-tuple-element.30), kind=kOutput, calls=%fused_computation.28 | convolution fusion | flops 370081792 | bytes 4329472 | tf_op jit(solution)/shard_map/ligand_spectra/ntxa,nac->ntxc/dot_general | solution.py:86
  33.9 1.0 %copy-done.2 = f32[2,16,16,640]{3,2,1,0:T(8,128)S(1)} copy-done((f32[2,16,16,640]{3,2,1,0:T(8,128)S(1)}, f32[2,16,16,640]{3,2,1,0:T(8,128)}, u32[]{:S(2)}) %copy-start.2) | copy-done | bytes 1310744
  34.8 4.0 %convolution_bitcast_fusion.1 = f32[4,22,2,16,640]{4,1,3,0,2:T(8,128)S(1)} fusion(f32[4,22,16,256]{3,2,1,0:T(8,128)S(1)} %slice_add_fusion, f32[2,256,640]{2,1,0:T(8,128)S(1)} %bitcast.149), kind=kOutput, calls=%fused_computation.9 | convolution fusion | flops 2768240640 | bytes 9961472 | tf_op jit(solution)/shard_map/ligand_spectra/ntxc,hcq->nthxq/dot_general | solution.py:88
  38.9 1.3 %copy.21 = f32[4,22,2,16,640]{4,3,2,1,0:T(8,128)S(1)} copy(f32[4,22,2,16,640]{4,1,3,0,2:T(8,128)S(1)} %convolution_bitcast_fusion.1) | data formatting | bytes 14417920 | tf_op jit(solution)/shard_map/ligand_spectra/ntxc,hcq->nthxq/transpose | solution.py:88
  40.2 5.8 %convolution_bitcast_fusion = f32[22,4,64,640]{3,2,0,1:T(8,128)S(1)} fusion(f32[4,22,32,640]{3,2,1,0:T(8,128)S(1)} %bitcast.144, f32[64,32,1,1]{0,1,3,2:T(8,128)S(1)} %copy-done.10), kind=kOutput, calls=%fused_computation | convolution fusion | flops 692060160 | bytes 21635072 | tf_op jit(solution)/shard_map/ligand_spectra/pk,ntkq->tnpq/dot_general | solution.py:91
  46.0 2.5 %fusion.14 = f32[11,1,2,32,640]{4,3,0,2,1:T(8,128)S(1)} fusion(bf16[2,1024,640]{2,1,0:T(8,128)(2,1)S(1)} %copy-done, bf16[11,32,1024]{2,1,0:T(8,128)(2,1)} %collective-permute-done.3), kind=kOutput, calls=%fused_computation.23 | convolution fusion | flops 922746880 | bytes 5144576 | tf_op jit(solution)/shard_map/receptor_spectra/trxc,hcq->trhxq/dot_general | solution.py:71
  48.6 0.9 %convolution_bitcast_fusion.2 = f32[11,1,64,640]{3,2,0,1:T(8,128)S(1)} fusion(f32[11,64,640]{2,1,0:T(8,128)S(1)} %bitcast.146, f32[64,64,1]{1,0,2:T(8,128)S(1)} %copy-done.3), kind=kOutput, calls=%fused_computation.24 | convolution fusion | flops 173015040 | bytes 3620864 | tf_op jit(solution)/shard_map/receptor_spectra/pk,trkq->trpq/dot_general | solution.py:73
  49.7 2.5 %add_reduce_fusion = (f32[4,32,640]{2,1,0:T(8,128)S(1)}, f32[4,32,640]{2,1,0:T(8,128)S(1)}, f32[4,32,640]{2,1,0:T(8,128)S(1)}, f32[4,32,640]{2,1,0:T(8,128)S(1)}) fusion(f32[22,4,64,640]{3,2,0,1:T(8,128)S(1)} %convolution_bitcast_fusion, f32[11,32,640]{2,1,0:T(8,128)S(1)} %get-tuple-element.25, f32[11,32,640]{2,1,0:T(8,128)S(1)} %get-tuple-element.24, ...), kind=kLoop, calls=%fused_computation.6 | loop fusion | flops 14090240 | bytes 19333120 | tf_op jit(solution)/shard_map/correlate/reduce_sum | solution.py:99
  53.2 0.8 %copy-done.1 = bf16[2,1024,640]{2,1,0:T(8,128)(2,1)S(1)} copy-done((bf16[2,1024,640]{2,1,0:T(8,128)(2,1)S(1)}, bf16[2,1024,640]{2,1,0:T(8,128)(2,1)}, u32[]{:S(2)}) %copy-start.1) | copy-done | bytes 2621464
  54.0 0.9 %fusion.22 = f32[2,4,32,1024]{3,2,1,0:T(8,128)S(1)} fusion(bf16[2,1024,640]{2,1,0:T(8,128)(2,1)S(1)} %copy-done.1, bf16[1,4,32,2,640]{4,2,1,3,0:T(8,128)(2,1)S(1)} %get-tuple-element.10, bf16[1,4,32,2,640]{4,2,1,3,0:T(8,128)(2,1)S(1)} %get-tuple-element.9), kind=kOutput, calls=%fused_computation.32 | convolution fusion | flops 671416320 | bytes 4325376 | tf_op jit(solution)/shard_map/inverse_scores/rnxhq,hcq->rnxc/dot_general | solution.py:118
  54.9 1.1 %fusion.32 = f32[4]{0:T(128)S(1)} fusion(bf16[2,1024,640]{2,1,0:T(8,128)(2,1)S(1)} %get-tuple-element.11, f32[2,4,32,1024]{3,2,1,0:T(8,128)S(1)} %fusion.22, bf16[1,4,32,2,640]{4,2,1,3,0:T(8,128)(2,1)S(1)} %get-tuple-element.9), kind=kOutput, calls=%fused_computation.37 | convolution fusion | flops 335937536 | bytes 3997712 | tf_op jit(solution)/shard_map/inverse_scores/rnxhq,hcq->rnxc/dot_general | solution.py:120
  56.3 1.6 %collective-permute-start.5 = (f32[4,32]{0,1:T(8,128)S(1)}, f32[4,32]{0,1:T(8,128)S(1)}, u32[]{:S(2)}, u32[]{:S(2)}) collective-permute-start(f32[4,32]{0,1:T(8,128)S(1)} %broadcast_select_fusion), channel_id=1, source_target_pairs={{0,2},{1,3},{2,0},{3,1},{4,6},{5,7},{6,4},{7,5},{8,10},{9,11},{10,... | collective-permute-start | bytes 1544 | tf_op jit(solution)/shard_map/ppermute | solution.py:138
  58.3 1.1 %collective-permute-done.6 = f32[4,32]{0,1:T(8,128)S(1)} collective-permute-done((f32[4,32]{0,1:T(8,128)S(1)}, f32[4,32]{0,1:T(8,128)S(1)}, u32[]{:S(2)}, u32[]{:S(2)}) %collective-permute-start.6) | collective-permute-done | bytes 544 | tf_op jit(solution)/shard_map/ppermute | solution.py:138
  59.5 2.1 %collective-permute-done.4 = f32[4,32]{0,1:T(8,128)S(1)} collective-permute-done((f32[4,32]{0,1:T(8,128)S(1)}, f32[4,32]{0,1:T(8,128)S(1)}, u32[]{:S(2)}, u32[]{:S(2)}) %collective-permute-start.4) | collective-permute-done | bytes 544 | tf_op jit(solution)/shard_map/ppermute | solution.py:138
  62.0 1.6 %collective-permute-start.8 = (f32[4,32]{0,1:T(8,128)S(1)}, f32[4,32]{0,1:T(8,128)S(1)}, u32[]{:S(2)}, u32[]{:S(2)}) collective-permute-start(f32[4,32]{0,1:T(8,128)S(1)} %maximum_maximum_fusion.1), channel_id=1, source_target_pairs={{0,8},{1,9},{2,10},{3,11},{4,12},{5,13},{6,14},{7,15},{8,0},{9,1},... | collective-permute-start | bytes 1544 | tf_op jit(solution)/shard_map/ppermute | solution.py:138
  63.6 1.5 %collective-permute-start.7 = (f32[4,32]{0,1:T(8,128)S(1)}, f32[4,32]{0,1:T(8,128)S(1)}, u32[]{:S(2)}, u32[]{:S(2)}) collective-permute-start(f32[4,32]{0,1:T(8,128)S(1)} %maximum_maximum_fusion.1), channel_id=1, source_target_pairs={{0,4},{1,5},{2,6},{3,7},{4,0},{5,1},{6,2},{7,3},{8,12},{9,13},{10,... | collective-permute-start | bytes 1544 | tf_op jit(solution)/shard_map/ppermute | solution.py:138
  65.1 1.1 %collective-permute-done.9 = f32[4,32]{0,1:T(8,128)S(1)} collective-permute-done((f32[4,32]{0,1:T(8,128)S(1)}, f32[4,32]{0,1:T(8,128)S(1)}, u32[]{:S(2)}, u32[]{:S(2)}) %collective-permute-start.9) | collective-permute-done | bytes 544 | tf_op jit(solution)/shard_map/ppermute | solution.py:138
  66.3 1.1 %collective-permute-done.7 = f32[4,32]{0,1:T(8,128)S(1)} collective-permute-done((f32[4,32]{0,1:T(8,128)S(1)}, f32[4,32]{0,1:T(8,128)S(1)}, u32[]{:S(2)}, u32[]{:S(2)}) %collective-permute-start.7) | collective-permute-done | bytes 544 | tf_op jit(solution)/shard_map/ppermute | solution.py:138
  67.4 2.6 %collective-permute-start.10 = (f32[4,32]{0,1:T(8,128)S(1)}, f32[4,32]{0,1:T(8,128)S(1)}, u32[]{:S(2)}, u32[]{:S(2)}) collective-permute-start(f32[4,32]{0,1:T(8,128)S(1)} %maximum_maximum_fusion), channel_id=1, source_target_pairs={{0,16},{1,17},{2,18},{3,19},{4,20},{5,21},{6,22},{7,23},{8,24},{9,... | collective-permute-start | bytes 1544 | tf_op jit(solution)/shard_map/ppermute | solution.py:138
  70.0 2.1 %collective-permute-done.10 = f32[4,32]{0,1:T(8,128)S(1)} collective-permute-done((f32[4,32]{0,1:T(8,128)S(1)}, f32[4,32]{0,1:T(8,128)S(1)}, u32[]{:S(2)}, u32[]{:S(2)}) %collective-permute-start.10) | collective-permute-done | bytes 544 | tf_op jit(solution)/shard_map/ppermute | solution.py:138
  (52 shorter events, 4.9 us)
Async XLA Ops:
  0.6 26.7 %collective-permute-start.1 = (s32[3,2,256]{2,1,0:T(2,128)}, s32[3,2,256]{2,1,0:T(2,128)S(1)}, u32[]{:S(2)}, u32[]{:S(2)}) collective-permute-start(s32[3,2,256]{2,1,0:T(2,128)} %param.16), channel_id=1, source_target_pairs={{0,8},{8,0},{16,24},{24,16},{1,9},{9,1},{17,25},{25,17},{2,10},{10... | collective-permute-start | bytes 18440 | tf_op jit(solution)/shard_map/ppermute | solution.py:167
  4.5 25.5 %collective-permute-start = (f32[11,256]{1,0:T(8,128)S(1)}, f32[11,256]{1,0:T(8,128)S(1)}, u32[]{:S(2)}, u32[]{:S(2)}) collective-permute-start(f32[11,256]{1,0:T(8,128)S(1)} %broadcast_multiply_fusion), channel_id=1, source_target_pairs={{0,1},{1,0},{2,3},{3,2},{4,5},{5,4},{6,7},{7,6},{8,9},{9,8},{10,11... | collective-permute-start | bytes 33800 | tf_op jit(solution)/shard_map/ppermute | solution.py:127
  14.5 31.5 %collective-permute-start.3 = (bf16[11,32,1024]{2,1,0:T(8,128)(2,1)S(1)}, bf16[11,32,1024]{2,1,0:T(8,128)(2,1)}, u32[]{:S(2)}, u32[]{:S(2)}) collective-permute-start(bf16[11,32,1024]{2,1,0:T(8,128)(2,1)S(1)} %all_gather.3), channel_id=1, source_target_pairs={{0,1},{1,0},{2,3},{3,2},{4,5},{5,4},{6,7},{7,6},{8,9},{9,8},{10,11... | collective-permute-start | bytes 2162696 | tf_op jit(solution)/shard_map/ppermute | solution.py:127
  17.0 2.4 %copy-start.4 = (f32[2,16,640]{2,1,0:T(8,128)S(1)}, f32[2,16,640]{2,1,0:T(8,128)}, u32[]{:S(2)}) copy-start(f32[2,16,640]{2,1,0:T(8,128)} %constant.93) | copy-start | bytes 245764
  17.0 2.4 %copy-start.5 = (f32[2,16,640]{2,1,0:T(8,128)S(1)}, f32[2,16,640]{2,1,0:T(8,128)}, u32[]{:S(2)}) copy-start(f32[2,16,640]{2,1,0:T(8,128)} %constant.90) | copy-start | bytes 245764
  17.0 2.4 %copy-start.6 = (f32[2,16,640]{2,1,0:T(8,128)S(1)}, f32[2,16,640]{2,1,0:T(8,128)}, u32[]{:S(2)}) copy-start(f32[2,16,640]{2,1,0:T(8,128)} %constant.87) | copy-start | bytes 245764
  17.1 2.4 %copy-start.7 = (f32[2,16,640]{2,1,0:T(8,128)S(1)}, f32[2,16,640]{2,1,0:T(8,128)}, u32[]{:S(2)}) copy-start(f32[2,16,640]{2,1,0:T(8,128)} %constant.84) | copy-start | bytes 245764
  23.5 1.4 %copy-start.3 = (f32[64,64,1]{1,0,2:T(8,128)S(1)}, f32[64,64,1]{1,0,2:T(8,128)}, u32[]{:S(2)}) copy-start(f32[64,64,1]{1,0,2:T(8,128)} %constant.103) | copy-start | bytes 49156
  24.9 2.5 %copy-start.8 = (s32[3,2,256]{2,1,0:T(2,128)S(1)}, s32[3,2,256]{2,1,0:T(2,128)}, u32[]{:S(2)}) copy-start(s32[3,2,256]{2,1,0:T(2,128)} %param.16) | copy-start | bytes 18436
  27.4 4.7 %collective-permute-start.2 = (s32[3,4,256]{2,1,0:T(4,128)S(1)}, s32[3,4,256]{2,1,0:T(4,128)S(1)}, u32[]{:S(2)}, u32[]{:S(2)}) collective-permute-start(s32[3,4,256]{2,1,0:T(4,128)S(1)} %pad_add_fusion), channel_id=1, source_target_pairs={{0,16},{8,24},{16,0},{24,8},{1,17},{9,25},{17,1},{25,9},{2,18},{10... | collective-permute-start | bytes 36872 | tf_op jit(solution)/shard_map/ppermute | solution.py:167
  33.5 1.3 %copy-start.2 = (f32[2,16,16,640]{3,2,1,0:T(8,128)S(1)}, f32[2,16,16,640]{3,2,1,0:T(8,128)}, u32[]{:S(2)}) copy-start(f32[2,16,16,640]{3,2,1,0:T(8,128)} %multiply_add_fusion.1) | copy-start | bytes 3932164
  38.8 1.3 %copy-start.10 = (f32[64,32,1,1]{0,1,3,2:T(8,128)S(1)}, f32[64,32,1,1]{0,1,3,2:T(8,128)}, u32[]{:S(2)}) copy-start(f32[64,32,1,1]{0,1,3,2:T(8,128)} %constant.102) | copy-start | bytes 24580
  40.1 5.8 %copy-start = (bf16[2,1024,640]{2,1,0:T(8,128)(2,1)S(1)}, bf16[2,1024,640]{2,1,0:T(8,128)(2,1)}, u32[]{:S(2)}) copy-start(bf16[2,1024,640]{2,1,0:T(8,128)(2,1)} %get-tuple-element.8) | copy-start | bytes 7864324
  49.7 2.5 %copy-start.9 = (f32[64,32,1,1]{0,1,3,2:T(8,128)S(1)}, f32[64,32,1,1]{0,1,3,2:T(8,128)}, u32[]{:S(2)}) copy-start(f32[64,32,1,1]{0,1,3,2:T(8,128)} %constant.104) | copy-start | bytes 24580
  52.3 0.8 %copy-start.11 = (f32[640]{0:T(1024)S(1)}, f32[640]{0:T(1024)}, u32[]{:S(2)}) copy-start(f32[640]{0:T(1024)} %constant.77.clone) | copy-start | bytes 7684
  52.3 1.7 %copy-start.1 = (bf16[2,1024,640]{2,1,0:T(8,128)(2,1)S(1)}, bf16[2,1024,640]{2,1,0:T(8,128)(2,1)}, u32[]{:S(2)}) copy-start(bf16[2,1024,640]{2,1,0:T(8,128)(2,1)} %get-tuple-element.8) | copy-start | bytes 7864324
  56.2 3.3 %collective-permute-start.6 = (f32[4,32]{0,1:T(8,128)S(1)}, f32[4,32]{0,1:T(8,128)S(1)}, u32[]{:S(2)}, u32[]{:S(2)}) collective-permute-start(f32[4,32]{0,1:T(8,128)S(1)} %broadcast_select_fusion), channel_id=1, source_target_pairs={{0,3},{1,2},{2,1},{3,0},{4,7},{5,6},{6,5},{7,4},{8,11},{9,10},{10,... | collective-permute-start | bytes 1544 | tf_op jit(solution)/shard_map/ppermute | solution.py:138
  56.3 3.2 %collective-permute-start.5 = (f32[4,32]{0,1:T(8,128)S(1)}, f32[4,32]{0,1:T(8,128)S(1)}, u32[]{:S(2)}, u32[]{:S(2)}) collective-permute-start(f32[4,32]{0,1:T(8,128)S(1)} %broadcast_select_fusion), channel_id=1, source_target_pairs={{0,2},{1,3},{2,0},{3,1},{4,6},{5,7},{6,4},{7,5},{8,10},{9,11},{10,... | collective-permute-start | bytes 1544 | tf_op jit(solution)/shard_map/ppermute | solution.py:138
  57.8 3.7 %collective-permute-start.4 = (f32[4,32]{0,1:T(8,128)S(1)}, f32[4,32]{0,1:T(8,128)S(1)}, u32[]{:S(2)}, u32[]{:S(2)}) collective-permute-start(f32[4,32]{0,1:T(8,128)S(1)} %broadcast_select_fusion), channel_id=1, source_target_pairs={{0,1},{1,0},{2,3},{3,2},{4,5},{5,4},{6,7},{7,6},{8,9},{9,8},{10,11... | collective-permute-start | bytes 1544 | tf_op jit(solution)/shard_map/ppermute | solution.py:138
  61.6 4.6 %collective-permute-start.9 = (f32[4,32]{0,1:T(8,128)S(1)}, f32[4,32]{0,1:T(8,128)S(1)}, u32[]{:S(2)}, u32[]{:S(2)}) collective-permute-start(f32[4,32]{0,1:T(8,128)S(1)} %maximum_maximum_fusion.1), channel_id=1, source_target_pairs={{0,12},{1,13},{2,14},{3,15},{4,8},{5,9},{6,10},{7,11},{8,4},{9,5},... | collective-permute-start | bytes 1544 | tf_op jit(solution)/shard_map/ppermute | solution.py:138
  62.0 4.2 %collective-permute-start.8 = (f32[4,32]{0,1:T(8,128)S(1)}, f32[4,32]{0,1:T(8,128)S(1)}, u32[]{:S(2)}, u32[]{:S(2)}) collective-permute-start(f32[4,32]{0,1:T(8,128)S(1)} %maximum_maximum_fusion.1), channel_id=1, source_target_pairs={{0,8},{1,9},{2,10},{3,11},{4,12},{5,13},{6,14},{7,15},{8,0},{9,1},... | collective-permute-start | bytes 1544 | tf_op jit(solution)/shard_map/ppermute | solution.py:138
  63.6 3.7 %collective-permute-start.7 = (f32[4,32]{0,1:T(8,128)S(1)}, f32[4,32]{0,1:T(8,128)S(1)}, u32[]{:S(2)}, u32[]{:S(2)}) collective-permute-start(f32[4,32]{0,1:T(8,128)S(1)} %maximum_maximum_fusion.1), channel_id=1, source_target_pairs={{0,4},{1,5},{2,6},{3,7},{4,0},{5,1},{6,2},{7,3},{8,12},{9,13},{10,... | collective-permute-start | bytes 1544 | tf_op jit(solution)/shard_map/ppermute | solution.py:138
  67.4 4.7 %collective-permute-start.10 = (f32[4,32]{0,1:T(8,128)S(1)}, f32[4,32]{0,1:T(8,128)S(1)}, u32[]{:S(2)}, u32[]{:S(2)}) collective-permute-start(f32[4,32]{0,1:T(8,128)S(1)} %maximum_maximum_fusion), channel_id=1, source_target_pairs={{0,16},{1,17},{2,18},{3,19},{4,20},{5,21},{6,22},{7,23},{8,24},{9,... | collective-permute-start | bytes 1544 | tf_op jit(solution)/shard_map/ppermute | solution.py:138

commit v15 on v12

--- a/solution.py
+++ b/solution.py
@@ -128,7 +128,7 @@
 def butterfly_max(values, axes, device_count):
     stride = 1
     while stride < device_count:
-        radix = 4 if stride * 4 <= device_count else 2
+        radix = 2
         received = []
         for digit in range(1, radix):
             pairs = [(k, k ^ (digit * stride)) for k in range(device_count)]

time: 70.6 us -> 72.8 us (1.031)
  waiting for transfers between devices: 8.73 us -> 14.1 us
  starting transfers between devices: 16 us -> 12.8 us
    ppermute x7 -> x5, waiting for transfers between devices: 6.72 us -> 12 us  [butterfly_max(): received.append(lax.ppermute(values, axes, pairs))]
    ppermute x7 -> x5, starting transfers between devices: 8.23 us -> 5.04 us  [butterfly_max(): received.append(lax.ppermute(values, axes, pairs))]
  transfers between devices with their start and end apart: 11 -> 9, of which waited for: 7 -> 6; matrix products, arithmetic and copies ran while one was open for 34% -> 33% of each run, Pallas kernels for 0% -> 0%
where the time goes in v15:
time: 72.8 us; the launch traced here: 72.5 us
  matrix products  21.5 us (30%)
  waiting for transfers between devices  14.1 us (19%)
  starting transfers between devices  12.8 us (18%)
  other arithmetic  10.4 us (14%)
  blocking collectives  8.44 us (12%)
  local copies, waits for them, and re-layouts  4.4 us (6%)
  between operations  0.95 us (1%)
    ppermute x5, waiting for transfers between devices, butterfly_max(): received.append(lax.ppermute(values, axes, pairs))  12 us
    all_gather x1, blocking collectives, body(): own_rows = lax.all_gather(receptor_grids, 'inner', axis=1, tiled=True)  8.44 us
    dot_general x1, matrix products, ligand_spectra(): return jnp.einsum('pk,ntkq->tnpq', mix_tables(LB), plane, precision=HIGH)  5.81 us
    ppermute x2, starting transfers between devices, body(): moved = lax.ppermute(cells_here, 'plane', pairs)  5.72 us
    ppermute x5, starting transfers between devices, butterfly_max(): received.append(lax.ppermute(values, axes, pairs))  5.04 us
    dot_general x2, matrix products, receptor_mixed(): return jnp.einsum('pk,trkq->trpq', mix_tables(G), plane, precision=HIGH)  3.44 us
    dot_general x2, matrix products, receptor_mixed(): jnp.einsum('trxc,hcq->trhxq', grids, table_hi, preferred_element_type=jnp...  3.32 us
    add x2, other arithmetic, plane_table(): first[:, :, None, :] * second[:, None, :, :]  3.28 us
  transfers between devices with their start and end apart: 9, of which 6 were waited for; matrix products, arithmetic and copies ran while one was open for 33% of the time, Pallas kernels for 0%

profile of v15, /device:TPU:0, one launch (start us, length us, event | category | flops | bytes accessed | tf_op | source)
XLA Modules:
  0.0 72.5 jit_solution(16188685105679369304)
XLA Ops:
  0.6 3.1 %collective-permute-start.1 = (s32[3,2,256]{2,1,0:T(2,128)}, s32[3,2,256]{2,1,0:T(2,128)S(1)}, u32[]{:S(2)}, u32[]{:S(2)}) collective-permute-start(s32[3,2,256]{2,1,0:T(2,128)} %param.16), channel_id=1, source_target_pairs={{0,8},{8,0},{16,24},{24,16},{1,9},{9,1},{17,25},{25,17},{2,10},{10... | collective-permute-start | bytes 18440 | tf_op jit(solution)/shard_map/ppermute | solution.py:164
  3.7 0.8 %broadcast_multiply_fusion = f32[11,256]{1,0:T(8,128)S(1)} fusion(f32[11,256]{1,0:T(8,128)} %param.15, f32[11]{0:T(128)} %param.14), kind=kLoop, calls=%fused_computation.86 | loop fusion | flops 2816 | bytes 22572 | tf_op jit(solution)/shard_map/mul | solution.py:173
  4.5 1.5 %collective-permute-start = (f32[11,256]{1,0:T(8,128)S(1)}, f32[11,256]{1,0:T(8,128)S(1)}, u32[]{:S(2)}, u32[]{:S(2)}) collective-permute-start(f32[11,256]{1,0:T(8,128)S(1)} %broadcast_multiply_fusion), channel_id=1, source_target_pairs={{0,1},{1,0},{2,3},{3,2},{4,5},{5,4},{6,7},{7,6},{8,9},{9,8},{10,11... | collective-permute-start | bytes 33800 | tf_op jit(solution)/shard_map/ppermute | solution.py:124
  6.0 8.4 %all_gather.3 = bf16[11,32,1024]{2,1,0:T(8,128)(2,1)S(1)} all-gather(bf16[11,8,1024]{2,1,0:T(8,128)(2,1)} %param.13), channel_id=1, replica_groups=mesh['plane'=4,'inner'=4,'term'=2] {'inner'}, dimensions={1}, use_global_device_ids=true | all-gather | bytes 901120 | tf_op jit(solution)/shard_map/all_gather | solution.py:152
  15.0 2.0 %multiply_add_fusion = f32[2,32,32,640]{3,2,1,0:T(8,128)S(1)} fusion(f32[2,32,640]{2,1,0:T(8,128)} %constant.101, f32[2,32,640]{2,1,0:T(8,128)} %constant.99, f32[2,32,640]{2,1,0:T(8,128)} %constant.97, f32[2,32,640]{2,1,0:T(8,128)} %constant.95), kind=kLoop, calls=%fused_computation.4 | loop fusion | flops 3932160 | bytes 5898240 | tf_op jit(solution)/shard_map/twiddle_tables/add | solution.py:45
  17.1 2.4 %fusion = (bf16[2,1024,640]{2,1,0:T(8,128)(2,1)}, bf16[2,1024,640]{2,1,0:T(8,128)(2,1)S(1)}) fusion(f32[2,32,32,640]{3,2,1,0:T(8,128)S(1)} %multiply_add_fusion), kind=kLoop, calls=%fused_computation.3 | loop fusion | flops 5242880 | bytes 10485760 | tf_op jit(solution)/shard_map/twiddle_tables/convert_element_type | solution.py:52
  19.5 1.3 %multiply_add_fusion.1 = f32[2,16,16,640]{3,2,1,0:T(8,128)} fusion(f32[2,16,640]{2,1,0:T(8,128)S(1)} %copy-done.6, f32[2,16,640]{2,1,0:T(8,128)S(1)} %copy-done.5, f32[2,16,640]{2,1,0:T(8,128)S(1)} %copy-done.4, f32[2,16,640]{2,1,0:T(8,128)S(1)} %copy-done.3), kind=kLoop, calls=%fused_computation.30 | loop fusion | flops 983040 | bytes 1638400 | tf_op jit(solution)/shard_map/twiddle_tables/add | solution.py:45
  20.7 1.1 %fusion.13 = f32[11,1,2,32,640]{4,3,0,2,1:T(8,128)S(1)} fusion(bf16[2,1024,640]{2,1,0:T(8,128)(2,1)S(1)} %get-tuple-element.8, bf16[11,32,1024]{2,1,0:T(8,128)(2,1)S(1)} %all_gather.3), kind=kOutput, calls=%fused_computation.24 | convolution fusion | flops 922746880 | bytes 5144576 | tf_op jit(solution)/shard_map/receptor_spectra/trxc,hcq->trhxq/dot_general | solution.py:71
  21.8 1.4 %copy.21 = f32[11,1,2,32,640]{4,3,2,0,1:T(8,128)} copy(f32[11,1,2,32,640]{4,3,0,2,1:T(8,128)S(1)} %fusion.13) | data formatting | bytes 3604480 | tf_op jit(solution)/shard_map/receptor_spectra/trxc,hcq->trhxq/transpose | solution.py:71
  23.2 2.4 %convolution_bitcast_fusion.3 = f32[11,1,64,640]{3,2,0,1:T(8,128)S(1)} fusion(f32[11,64,640]{2,1,0:T(8,128)} %bitcast.152, f32[64,64,1]{1,0,2:T(8,128)S(1)} %copy-done.2), kind=kOutput, calls=%fused_computation.27 | convolution fusion | flops 173015040 | bytes 3620864 | tf_op jit(solution)/shard_map/receptor_spectra/pk,trkq->trpq/dot_general | solution.py:73
  25.7 2.6 %collective-permute-start.2 = (s32[3,4,256]{2,1,0:T(4,128)S(1)}, s32[3,4,256]{2,1,0:T(4,128)S(1)}, u32[]{:S(2)}, u32[]{:S(2)}) collective-permute-start(s32[3,4,256]{2,1,0:T(4,128)S(1)} %pad_add_fusion), channel_id=1, source_target_pairs={{0,16},{8,24},{16,0},{24,8},{1,17},{9,25},{17,1},{25,9},{2,18},{10... | collective-permute-start | bytes 36872 | tf_op jit(solution)/shard_map/ppermute | solution.py:164
  28.3 2.0 %collective-permute-done.2 = s32[3,4,256]{2,1,0:T(4,128)S(1)} collective-permute-done((s32[3,4,256]{2,1,0:T(4,128)S(1)}, s32[3,4,256]{2,1,0:T(4,128)S(1)}, u32[]{:S(2)}, u32[]{:S(2)}) %collective-permute-start.2) | collective-permute-done | bytes 12320 | tf_op jit(solution)/shard_map/ppermute | solution.py:164
  30.7 0.8 %fusion.40 = f32[4,22,16,256]{3,1,2,0:T(8,128)S(1)} fusion(bf16[4,22,16,256]{3,2,1,0:T(8,128)(2,1)S(1)} %get-tuple-element.28, s32[4,256]{1,0:T(4,128)S(1)} %get-tuple-element.30), kind=kOutput, calls=%fused_computation.39 | convolution fusion | flops 184811520 | bytes 2166784 | tf_op jit(solution)/shard_map/ligand_spectra/ntxa,nac->ntxc/dot_general | solution.py:86
  31.5 1.0 %fusion.42 = f32[4,22,16,256]{3,1,2,0:T(8,128)S(1)} fusion(bf16[4,22,16,256]{3,2,1,0:T(8,128)(2,1)S(1)} %get-tuple-element.29, s32[4,256]{1,0:T(4,128)S(1)} %get-tuple-element.30), kind=kOutput, calls=%fused_computation.40 | convolution fusion | flops 184811520 | bytes 2166784 | tf_op jit(solution)/shard_map/ligand_spectra/ntxa,nac->ntxc/dot_general | solution.py:85
  32.6 3.3 %convolution_bitcast_fusion.1 = f32[4,22,2,16,640]{4,1,3,0,2:T(8,128)S(1)} fusion(f32[4,22,16,256]{3,1,2,0:T(8,128)S(1)} %fusion.42, f32[4,22,16,256]{3,1,2,0:T(8,128)S(1)} %fusion.40, f32[2,256,640]{2,1,0:T(8,128)S(1)} %bitcast.156), kind=kOutput, calls=%fused_computation.9 | convolution fusion | flops 2768601088 | bytes 11403264 | tf_op jit(solution)/shard_map/ligand_spectra/ntxc,hcq->nthxq/dot_general | solution.py:87
  35.9 1.3 %copy.20 = f32[4,22,2,16,640]{4,3,2,1,0:T(8,128)S(1)} copy(f32[4,22,2,16,640]{4,1,3,0,2:T(8,128)S(1)} %convolution_bitcast_fusion.1) | data formatting | bytes 14417920 | tf_op jit(solution)/shard_map/ligand_spectra/ntxc,hcq->nthxq/transpose | solution.py:87
  37.1 5.8 %convolution_bitcast_fusion = f32[22,4,64,640]{3,2,0,1:T(8,128)S(1)} fusion(f32[4,22,32,640]{3,2,1,0:T(8,128)S(1)} %bitcast.151, f32[64,32,1,1]{0,1,3,2:T(8,128)S(1)} %copy-done.9), kind=kOutput, calls=%fused_computation | convolution fusion | flops 692060160 | bytes 21635072 | tf_op jit(solution)/shard_map/ligand_spectra/pk,ntkq->tnpq/dot_general | solution.py:90
  43.0 2.2 %fusion.16 = f32[11,1,2,32,640]{4,3,0,2,1:T(8,128)S(1)} fusion(bf16[2,1024,640]{2,1,0:T(8,128)(2,1)S(1)} %get-tuple-element.8, bf16[11,32,1024]{2,1,0:T(8,128)(2,1)} %collective-permute-done.3), kind=kOutput, calls=%fused_computation.25 | convolution fusion | flops 922746880 | bytes 5144576 | tf_op jit(solution)/shard_map/receptor_spectra/trxc,hcq->trhxq/dot_general | solution.py:71
  45.3 1.1 %convolution_bitcast_fusion.2 = f32[11,1,64,640]{3,2,0,1:T(8,128)S(1)} fusion(f32[11,64,640]{2,1,0:T(8,128)S(1)} %bitcast.153, f32[64,64,1]{1,0,2:T(8,128)S(1)} %copy-done.2), kind=kOutput, calls=%fused_computation.26 | convolution fusion | flops 173015040 | bytes 3620864 | tf_op jit(solution)/shard_map/receptor_spectra/pk,trkq->trpq/dot_general | solution.py:73
  46.7 2.5 %add_reduce_fusion = (f32[4,32,640]{2,1,0:T(8,128)S(1)}, f32[4,32,640]{2,1,0:T(8,128)S(1)}, f32[4,32,640]{2,1,0:T(8,128)S(1)}, f32[4,32,640]{2,1,0:T(8,128)S(1)}) fusion(f32[22,4,64,640]{3,2,0,1:T(8,128)S(1)} %convolution_bitcast_fusion, f32[11,32,640]{2,1,0:T(8,128)S(1)} %get-tuple-element.25, f32[11,32,640]{2,1,0:T(8,128)S(1)} %get-tuple-element.24, ...), kind=kLoop, calls=%fused_computation.6 | loop fusion | flops 14090240 | bytes 19333120 | tf_op jit(solution)/shard_map/correlate/reduce_sum | solution.py:98
  49.3 0.7 fusion.49
  50.2 1.0 %fusion.21 = f32[4,32,1024]{2,1,0:T(8,128)S(1)} fusion(bf16[2,1024,640]{2,1,0:T(8,128)(2,1)S(1)} %get-tuple-element.8, bf16[1,4,32,2,640]{4,2,1,3,0:T(8,128)(2,1)S(1)} %get-tuple-element.9), kind=kOutput, calls=%fused_computation.31 | convolution fusion | flops 335544320 | bytes 3473408 | tf_op jit(solution)/shard_map/inverse_scores/rnxhq,hcq->rnxc/dot_general | solution.py:115
  51.2 1.0 %fusion.33 = f32[4,32,1024]{2,1,0:T(8,128)S(1)} fusion(f32[4,32,1024]{2,1,0:T(8,128)S(1)} %fusion.21, bf16[2,1024,640]{2,1,0:T(8,128)(2,1)S(1)} %get-tuple-element.8, bf16[1,4,32,2,640]{4,2,1,3,0:T(8,128)(2,1)S(1)} %get-tuple-element.10), kind=kOutput, calls=%fused_computation.35 | convolution fusion | flops 335675392 | bytes 3997696 | tf_op jit(solution)/shard_map/inverse_scores/rnxhq,hcq->rnxc/dot_general | solution.py:116
  52.2 0.7 %copy-done = bf16[2,1024,640]{2,1,0:T(8,128)(2,1)S(1)} copy-done((bf16[2,1024,640]{2,1,0:T(8,128)(2,1)S(1)}, bf16[2,1024,640]{2,1,0:T(8,128)(2,1)}, u32[]{:S(2)}) %copy-start) | copy-done | bytes 2621464
  52.9 1.1 %fusion.36 = f32[4]{0:T(128)S(1)} fusion(f32[4,32,1024]{2,1,0:T(8,128)S(1)} %fusion.33, bf16[2,1024,640]{2,1,0:T(8,128)(2,1)S(1)} %copy-done, bf16[1,4,32,2,640]{4,2,1,3,0:T(8,128)(2,1)S(1)} %get-tuple-element.9), kind=kOutput, calls=%fused_computation.36 | convolution fusion | flops 335806464 | bytes 3473424 | tf_op jit(solution)/shard_map/inverse_scores/rnxhq,hcq->rnxc/dot_general | solution.py:117
  54.2 1.5 %collective-permute-start.4 = (f32[4,32]{0,1:T(8,128)S(1)}, f32[4,32]{0,1:T(8,128)S(1)}, u32[]{:S(2)}, u32[]{:S(2)}) collective-permute-start(f32[4,32]{0,1:T(8,128)S(1)} %broadcast_select_fusion), channel_id=1, source_target_pairs={{0,1},{1,0},{2,3},{3,2},{4,5},{5,4},{6,7},{7,6},{8,9},{9,8},{10,11... | collective-permute-start | bytes 1544 | tf_op jit(solution)/shard_map/ppermute | solution.py:135
  55.7 2.2 %collective-permute-done.4 = f32[4,32]{0,1:T(8,128)S(1)} collective-permute-done((f32[4,32]{0,1:T(8,128)S(1)}, f32[4,32]{0,1:T(8,128)S(1)}, u32[]{:S(2)}, u32[]{:S(2)}) %collective-permute-start.4) | collective-permute-done | bytes 544 | tf_op jit(solution)/shard_map/ppermute | solution.py:135
  58.0 1.2 %collective-permute-done.5 = f32[4,32]{0,1:T(8,128)S(1)} collective-permute-done((f32[4,32]{0,1:T(8,128)S(1)}, f32[4,32]{0,1:T(8,128)S(1)}, u32[]{:S(2)}, u32[]{:S(2)}) %collective-permute-start.5) | collective-permute-done | bytes 544 | tf_op jit(solution)/shard_map/ppermute | solution.py:135
  59.8 3.2 %collective-permute-done.6 = f32[4,32]{0,1:T(8,128)S(1)} collective-permute-done((f32[4,32]{0,1:T(8,128)S(1)}, f32[4,32]{0,1:T(8,128)S(1)}, u32[]{:S(2)}, u32[]{:S(2)}) %collective-permute-start.6) | collective-permute-done | bytes 544 | tf_op jit(solution)/shard_map/ppermute | solution.py:135
  63.4 3.3 %collective-permute-done.7 = f32[4,32]{0,1:T(8,128)S(1)} collective-permute-done((f32[4,32]{0,1:T(8,128)S(1)}, f32[4,32]{0,1:T(8,128)S(1)}, u32[]{:S(2)}, u32[]{:S(2)}) %collective-permute-start.7) | collective-permute-done | bytes 544 | tf_op jit(solution)/shard_map/ppermute | solution.py:135
  66.7 2.5 %collective-permute-start.8 = (f32[4,32]{0,1:T(8,128)S(1)}, f32[4,32]{0,1:T(8,128)S(1)}, u32[]{:S(2)}, u32[]{:S(2)}) collective-permute-start(f32[4,32]{0,1:T(8,128)S(1)} %max.18), channel_id=1, source_target_pairs={{0,16},{1,17},{2,18},{3,19},{4,20},{5,21},{6,22},{7,23},{8,24},{9,... | collective-permute-start | bytes 1544 | tf_op jit(solution)/shard_map/ppermute | solution.py:135
  69.3 2.1 %collective-permute-done.8 = f32[4,32]{0,1:T(8,128)S(1)} collective-permute-done((f32[4,32]{0,1:T(8,128)S(1)}, f32[4,32]{0,1:T(8,128)S(1)}, u32[]{:S(2)}, u32[]{:S(2)}) %collective-permute-start.8) | collective-permute-done | bytes 544 | tf_op jit(solution)/shard_map/ppermute | solution.py:135
  (49 shorter events, 4.0 us)
Async XLA Ops:
  0.6 25.0 %collective-permute-start.1 = (s32[3,2,256]{2,1,0:T(2,128)}, s32[3,2,256]{2,1,0:T(2,128)S(1)}, u32[]{:S(2)}, u32[]{:S(2)}) collective-permute-start(s32[3,2,256]{2,1,0:T(2,128)} %param.16), channel_id=1, source_target_pairs={{0,8},{8,0},{16,24},{24,16},{1,9},{9,1},{17,25},{25,17},{2,10},{10... | collective-permute-start | bytes 18440 | tf_op jit(solution)/shard_map/ppermute | solution.py:164
  4.5 23.8 %collective-permute-start = (f32[11,256]{1,0:T(8,128)S(1)}, f32[11,256]{1,0:T(8,128)S(1)}, u32[]{:S(2)}, u32[]{:S(2)}) collective-permute-start(f32[11,256]{1,0:T(8,128)S(1)} %broadcast_multiply_fusion), channel_id=1, source_target_pairs={{0,1},{1,0},{2,3},{3,2},{4,5},{5,4},{6,7},{7,6},{8,9},{9,8},{10,11... | collective-permute-start | bytes 33800 | tf_op jit(solution)/shard_map/ppermute | solution.py:124
  14.5 28.5 %collective-permute-start.3 = (bf16[11,32,1024]{2,1,0:T(8,128)(2,1)S(1)}, bf16[11,32,1024]{2,1,0:T(8,128)(2,1)}, u32[]{:S(2)}, u32[]{:S(2)}) collective-permute-start(bf16[11,32,1024]{2,1,0:T(8,128)(2,1)S(1)} %all_gather.3), channel_id=1, source_target_pairs={{0,1},{1,0},{2,3},{3,2},{4,5},{5,4},{6,7},{7,6},{8,9},{9,8},{10,11... | collective-permute-start | bytes 2162696 | tf_op jit(solution)/shard_map/ppermute | solution.py:124
  17.0 2.4 %copy-start.3 = (f32[2,16,640]{2,1,0:T(8,128)S(1)}, f32[2,16,640]{2,1,0:T(8,128)}, u32[]{:S(2)}) copy-start(f32[2,16,640]{2,1,0:T(8,128)} %constant.84) | copy-start | bytes 245764
  17.0 2.4 %copy-start.4 = (f32[2,16,640]{2,1,0:T(8,128)S(1)}, f32[2,16,640]{2,1,0:T(8,128)}, u32[]{:S(2)}) copy-start(f32[2,16,640]{2,1,0:T(8,128)} %constant.87) | copy-start | bytes 245764
  17.0 2.4 %copy-start.5 = (f32[2,16,640]{2,1,0:T(8,128)S(1)}, f32[2,16,640]{2,1,0:T(8,128)}, u32[]{:S(2)}) copy-start(f32[2,16,640]{2,1,0:T(8,128)} %constant.90) | copy-start | bytes 245764
  17.1 2.4 %copy-start.6 = (f32[2,16,640]{2,1,0:T(8,128)S(1)}, f32[2,16,640]{2,1,0:T(8,128)}, u32[]{:S(2)}) copy-start(f32[2,16,640]{2,1,0:T(8,128)} %constant.93) | copy-start | bytes 245764
  21.8 1.4 %copy-start.2 = (f32[64,64,1]{1,0,2:T(8,128)S(1)}, f32[64,64,1]{1,0,2:T(8,128)}, u32[]{:S(2)}) copy-start(f32[64,64,1]{1,0,2:T(8,128)} %constant.103) | copy-start | bytes 49156
  23.2 2.5 %copy-start.7 = (s32[3,2,256]{2,1,0:T(2,128)S(1)}, s32[3,2,256]{2,1,0:T(2,128)}, u32[]{:S(2)}) copy-start(s32[3,2,256]{2,1,0:T(2,128)} %param.16) | copy-start | bytes 18436
  25.7 4.7 %collective-permute-start.2 = (s32[3,4,256]{2,1,0:T(4,128)S(1)}, s32[3,4,256]{2,1,0:T(4,128)S(1)}, u32[]{:S(2)}, u32[]{:S(2)}) collective-permute-start(s32[3,4,256]{2,1,0:T(4,128)S(1)} %pad_add_fusion), channel_id=1, source_target_pairs={{0,16},{8,24},{16,0},{24,8},{1,17},{9,25},{17,1},{25,9},{2,18},{10... | collective-permute-start | bytes 36872 | tf_op jit(solution)/shard_map/ppermute | solution.py:164
  30.6 1.9 %copy-start.1 = (f32[2,16,16,640]{3,2,1,0:T(8,128)S(1)}, f32[2,16,16,640]{3,2,1,0:T(8,128)}, u32[]{:S(2)}) copy-start(f32[2,16,16,640]{3,2,1,0:T(8,128)} %multiply_add_fusion.1) | copy-start | bytes 3932164
  35.8 1.3 %copy-start.9 = (f32[64,32,1,1]{0,1,3,2:T(8,128)S(1)}, f32[64,32,1,1]{0,1,3,2:T(8,128)}, u32[]{:S(2)}) copy-start(f32[64,32,1,1]{0,1,3,2:T(8,128)} %constant.102) | copy-start | bytes 24580
  46.7 2.5 %copy-start.8 = (f32[64,32,1,1]{0,1,3,2:T(8,128)S(1)}, f32[64,32,1,1]{0,1,3,2:T(8,128)}, u32[]{:S(2)}) copy-start(f32[64,32,1,1]{0,1,3,2:T(8,128)} %constant.104) | copy-start | bytes 24580
  49.2 0.8 %copy-start.10 = (f32[640]{0:T(1024)S(1)}, f32[640]{0:T(1024)}, u32[]{:S(2)}) copy-start(f32[640]{0:T(1024)} %constant.77.clone) | copy-start | bytes 7684
  51.2 1.7 %copy-start = (bf16[2,1024,640]{2,1,0:T(8,128)(2,1)S(1)}, bf16[2,1024,640]{2,1,0:T(8,128)(2,1)}, u32[]{:S(2)}) copy-start(bf16[2,1024,640]{2,1,0:T(8,128)(2,1)} %get-tuple-element.11) | copy-start | bytes 7864324
  54.2 3.7 %collective-permute-start.4 = (f32[4,32]{0,1:T(8,128)S(1)}, f32[4,32]{0,1:T(8,128)S(1)}, u32[]{:S(2)}, u32[]{:S(2)}) collective-permute-start(f32[4,32]{0,1:T(8,128)S(1)} %broadcast_select_fusion), channel_id=1, source_target_pairs={{0,1},{1,0},{2,3},{3,2},{4,5},{5,4},{6,7},{7,6},{8,9},{9,8},{10,11... | collective-permute-start | bytes 1544 | tf_op jit(solution)/shard_map/ppermute | solution.py:135
  58.0 1.2 %collective-permute-start.5 = (f32[4,32]{0,1:T(8,128)S(1)}, f32[4,32]{0,1:T(8,128)S(1)}, u32[]{:S(2)}, u32[]{:S(2)}) collective-permute-start(f32[4,32]{0,1:T(8,128)S(1)} %fusion.70), channel_id=1, source_target_pairs={{0,2},{1,3},{2,0},{3,1},{4,6},{5,7},{6,4},{7,5},{8,10},{9,11},{10,... | collective-permute-start | bytes 1544 | tf_op jit(solution)/shard_map/ppermute | solution.py:135
  59.2 3.7 %collective-permute-start.6 = (f32[4,32]{0,1:T(8,128)S(1)}, f32[4,32]{0,1:T(8,128)S(1)}, u32[]{:S(2)}, u32[]{:S(2)}) collective-permute-start(f32[4,32]{0,1:T(8,128)S(1)} %fusion.84), channel_id=1, source_target_pairs={{0,4},{1,5},{2,6},{3,7},{4,0},{5,1},{6,2},{7,3},{8,12},{9,13},{10,... | collective-permute-start | bytes 1544 | tf_op jit(solution)/shard_map/ppermute | solution.py:135
  63.0 3.7 %collective-permute-start.7 = (f32[4,32]{0,1:T(8,128)S(1)}, f32[4,32]{0,1:T(8,128)S(1)}, u32[]{:S(2)}, u32[]{:S(2)}) collective-permute-start(f32[4,32]{0,1:T(8,128)S(1)} %max.17), channel_id=1, source_target_pairs={{0,8},{1,9},{2,10},{3,11},{4,12},{5,13},{6,14},{7,15},{8,0},{9,1},... | collective-permute-start | bytes 1544 | tf_op jit(solution)/shard_map/ppermute | solution.py:135
  66.7 4.7 %collective-permute-start.8 = (f32[4,32]{0,1:T(8,128)S(1)}, f32[4,32]{0,1:T(8,128)S(1)}, u32[]{:S(2)}, u32[]{:S(2)}) collective-permute-start(f32[4,32]{0,1:T(8,128)S(1)} %max.18), channel_id=1, source_target_pairs={{0,16},{1,17},{2,18},{3,19},{4,20},{5,21},{6,22},{7,23},{8,24},{9,... | collective-permute-start | bytes 1544 | tf_op jit(solution)/shard_map/ppermute | solution.py:135

commit v16 on v12

--- a/solution.py
+++ b/solution.py
@@ -87,17 +87,17 @@
     plane = jnp.einsum("ntxc,hcq->nthxq", grid, box_table, precision=HIGH)
     rot_count, terms = plane.shape[0], plane.shape[1]
     plane = plane.reshape(rot_count, terms, 2 * LB, WIDTH)
-    return jnp.einsum("pk,ntkq->tnpq", mix_tables(LB), plane, precision=HIGH)
+    return jnp.einsum("pk,ntkq->ntpq", mix_tables(LB), plane, precision=HIGH)
 
 
 def correlate(rec_spec, lig_spec):
-    rr = rec_spec[:, :, None, :G]
-    ri = rec_spec[:, :, None, G:]
-    lr = lig_spec[:, None, :, :G]
-    li = lig_spec[:, None, :, G:]
-    prod_re = jnp.sum(lr * rr + li * ri, axis=0)
-    prod_im = jnp.sum(lr * ri - li * rr, axis=0)
-    return jnp.stack([prod_re, prod_im], axis=0)
+    rr = rec_spec[None, :, 0, :G]
+    ri = rec_spec[None, :, 0, G:]
+    lr = lig_spec[:, :, :G]
+    li = lig_spec[:, :, G:]
+    prod_re = jnp.sum(lr * rr + li * ri, axis=1)
+    prod_im = jnp.sum(lr * ri - li * rr, axis=1)
+    return jnp.stack([prod_re, prod_im], axis=0)[:, None]
 
 
 def inverse_scores(products, table_hi, table_lo):
@@ -186,7 +186,7 @@
             with jax.named_scope("receptor_spectra"):
                 rec_spec = receptor_mixed(grids, table_hi)
             with jax.named_scope("correlate"):
-                products = products + correlate(rec_spec, lig_spec[lo : lo + terms_here])
+                products = products + correlate(rec_spec, lig_spec[:, lo : lo + terms_here])
         with jax.named_scope("inverse_scores"):
             scores = inverse_scores(products, table_hi, table_lo)
             best_here = jnp.max(scores, axis=(2, 3))[0]

time: 70.6 us -> 70.6 us (level)
  no operation moved by 1% of the time
where the time goes in v16:
time: 70.6 us; the launch traced here: 70.3 us
  matrix products  21.5 us (30%)
  starting transfers between devices  16 us (23%)
  other arithmetic  10.3 us (15%)
  waiting for transfers between devices  8.73 us (12%)
  blocking collectives  8.44 us (12%)
  local copies, waits for them, and re-layouts  4.39 us (6%)
  between operations  0.95 us (1%)
    all_gather x1, blocking collectives, body(): own_rows = lax.all_gather(receptor_grids, 'inner', axis=1, tiled=True)  8.44 us
    ppermute x7, starting transfers between devices, butterfly_max(): received.append(lax.ppermute(values, axes, pairs))  8.23 us
    ppermute x7, waiting for transfers between devices, butterfly_max(): received.append(lax.ppermute(values, axes, pairs))  6.72 us
    dot_general x1, matrix products, ligand_spectra(): return jnp.einsum('pk,ntkq->ntpq', mix_tables(LB), plane, precision=HIGH)  5.81 us
    ppermute x2, starting transfers between devices, body(): moved = lax.ppermute(cells_here, 'plane', pairs)  5.76 us
    dot_general x2, matrix products, receptor_mixed(): return jnp.einsum('pk,trkq->trpq', mix_tables(G), plane, precision=HIGH)  3.43 us
    dot_general x2, matrix products, receptor_mixed(): jnp.einsum('trxc,hcq->trhxq', grids, table_hi, preferred_element_type=jnp...  3.31 us
    dot_general x1, matrix products, ligand_spectra(): plane = jnp.einsum('ntxc,hcq->nthxq', grid, box_table, precision=HIGH)  3.27 us
  transfers between devices with their start and end apart: 11, of which 7 were waited for; matrix products, arithmetic and copies ran while one was open for 34% of the time, Pallas kernels for 0%

profile of v16, /device:TPU:0, one launch (start us, length us, event | category | flops | bytes accessed | tf_op | source)
XLA Modules:
  0.0 70.3 jit_solution(7312025514103496550)
XLA Ops:
  0.6 3.1 %collective-permute-start.1 = (s32[3,2,256]{2,1,0:T(2,128)}, s32[3,2,256]{2,1,0:T(2,128)S(1)}, u32[]{:S(2)}, u32[]{:S(2)}) collective-permute-start(s32[3,2,256]{2,1,0:T(2,128)} %param.16), channel_id=1, source_target_pairs={{0,8},{8,0},{16,24},{24,16},{1,9},{9,1},{17,25},{25,17},{2,10},{10... | collective-permute-start | bytes 18440 | tf_op jit(solution)/shard_map/ppermute | solution.py:164
  3.7 0.8 %broadcast_multiply_fusion = f32[11,256]{1,0:T(8,128)S(1)} fusion(f32[11,256]{1,0:T(8,128)} %param.15, f32[11]{0:T(128)} %param.14), kind=kLoop, calls=%fused_computation.88 | loop fusion | flops 2816 | bytes 22572 | tf_op jit(solution)/shard_map/mul | solution.py:173
  4.5 1.5 %collective-permute-start = (f32[11,256]{1,0:T(8,128)S(1)}, f32[11,256]{1,0:T(8,128)S(1)}, u32[]{:S(2)}, u32[]{:S(2)}) collective-permute-start(f32[11,256]{1,0:T(8,128)S(1)} %broadcast_multiply_fusion), channel_id=1, source_target_pairs={{0,1},{1,0},{2,3},{3,2},{4,5},{5,4},{6,7},{7,6},{8,9},{9,8},{10,11... | collective-permute-start | bytes 33800 | tf_op jit(solution)/shard_map/ppermute | solution.py:124
  6.0 8.4 %all_gather.3 = bf16[11,32,1024]{2,1,0:T(8,128)(2,1)S(1)} all-gather(bf16[11,8,1024]{2,1,0:T(8,128)(2,1)} %param.13), channel_id=1, replica_groups=mesh['plane'=4,'inner'=4,'term'=2] {'inner'}, dimensions={1}, use_global_device_ids=true | all-gather | bytes 901120 | tf_op jit(solution)/shard_map/all_gather | solution.py:152
  15.0 2.0 %multiply_add_fusion = f32[2,32,32,640]{3,2,1,0:T(8,128)S(1)} fusion(f32[2,32,640]{2,1,0:T(8,128)} %constant.101, f32[2,32,640]{2,1,0:T(8,128)} %constant.99, f32[2,32,640]{2,1,0:T(8,128)} %constant.97, f32[2,32,640]{2,1,0:T(8,128)} %constant.95), kind=kLoop, calls=%fused_computation.4 | loop fusion | flops 3932160 | bytes 5898240 | tf_op jit(solution)/shard_map/twiddle_tables/add | solution.py:45
  17.1 2.4 %fusion = (bf16[2,1024,640]{2,1,0:T(8,128)(2,1)}, bf16[2,1024,640]{2,1,0:T(8,128)(2,1)S(1)}) fusion(f32[2,32,32,640]{3,2,1,0:T(8,128)S(1)} %multiply_add_fusion), kind=kLoop, calls=%fused_computation.3 | loop fusion | flops 5242880 | bytes 10485760 | tf_op jit(solution)/shard_map/twiddle_tables/convert_element_type | solution.py:52
  19.4 1.2 %multiply_add_fusion.1 = f32[2,16,16,640]{3,2,1,0:T(8,128)} fusion(f32[2,16,640]{2,1,0:T(8,128)S(1)} %copy-done.6, f32[2,16,640]{2,1,0:T(8,128)S(1)} %copy-done.5, f32[2,16,640]{2,1,0:T(8,128)S(1)} %copy-done.4, f32[2,16,640]{2,1,0:T(8,128)S(1)} %copy-done.3), kind=kLoop, calls=%fused_computation.30 | loop fusion | flops 983040 | bytes 1638400 | tf_op jit(solution)/shard_map/twiddle_tables/add | solution.py:45
  20.7 1.1 %fusion.13 = f32[11,1,2,32,640]{4,3,0,2,1:T(8,128)S(1)} fusion(bf16[2,1024,640]{2,1,0:T(8,128)(2,1)S(1)} %get-tuple-element.8, bf16[11,32,1024]{2,1,0:T(8,128)(2,1)S(1)} %all_gather.3), kind=kOutput, calls=%fused_computation.24 | convolution fusion | flops 922746880 | bytes 5144576 | tf_op jit(solution)/shard_map/receptor_spectra/trxc,hcq->trhxq/dot_general | solution.py:71
  21.8 1.3 %copy.21 = f32[11,1,2,32,640]{4,3,2,0,1:T(8,128)} copy(f32[11,1,2,32,640]{4,3,0,2,1:T(8,128)S(1)} %fusion.13) | data formatting | bytes 3604480 | tf_op jit(solution)/shard_map/receptor_spectra/trxc,hcq->trhxq/transpose | solution.py:71
  23.2 2.3 %convolution_bitcast_fusion.3 = f32[11,1,64,640]{3,2,0,1:T(8,128)S(1)} fusion(f32[11,64,640]{2,1,0:T(8,128)} %bitcast.152, f32[64,64,1]{1,0,2:T(8,128)S(1)} %copy-done.2), kind=kOutput, calls=%fused_computation.27 | convolution fusion | flops 173015040 | bytes 3620864 | tf_op jit(solution)/shard_map/receptor_spectra/pk,trkq->trpq/dot_general | solution.py:73
  25.6 2.7 %collective-permute-start.2 = (s32[3,4,256]{2,1,0:T(4,128)S(1)}, s32[3,4,256]{2,1,0:T(4,128)S(1)}, u32[]{:S(2)}, u32[]{:S(2)}) collective-permute-start(s32[3,4,256]{2,1,0:T(4,128)S(1)} %pad_add_fusion), channel_id=1, source_target_pairs={{0,16},{8,24},{16,0},{24,8},{1,17},{9,25},{17,1},{25,9},{2,18},{10... | collective-permute-start | bytes 36872 | tf_op jit(solution)/shard_map/ppermute | solution.py:164
  28.3 2.0 %collective-permute-done.2 = s32[3,4,256]{2,1,0:T(4,128)S(1)} collective-permute-done((s32[3,4,256]{2,1,0:T(4,128)S(1)}, s32[3,4,256]{2,1,0:T(4,128)S(1)}, u32[]{:S(2)}, u32[]{:S(2)}) %collective-permute-start.2) | collective-permute-done | bytes 12320 | tf_op jit(solution)/shard_map/ppermute | solution.py:164
  30.6 0.8 %fusion.40 = f32[4,22,16,256]{3,1,2,0:T(8,128)S(1)} fusion(bf16[4,22,16,256]{3,2,1,0:T(8,128)(2,1)S(1)} %get-tuple-element.28, s32[4,256]{1,0:T(4,128)S(1)} %get-tuple-element.30), kind=kOutput, calls=%fused_computation.39 | convolution fusion | flops 184811520 | bytes 2166784 | tf_op jit(solution)/shard_map/ligand_spectra/ntxa,nac->ntxc/dot_general | solution.py:86
  31.5 1.0 %fusion.42 = f32[4,22,16,256]{3,1,2,0:T(8,128)S(1)} fusion(bf16[4,22,16,256]{3,2,1,0:T(8,128)(2,1)S(1)} %get-tuple-element.29, s32[4,256]{1,0:T(4,128)S(1)} %get-tuple-element.30), kind=kOutput, calls=%fused_computation.40 | convolution fusion | flops 184811520 | bytes 2166784 | tf_op jit(solution)/shard_map/ligand_spectra/ntxa,nac->ntxc/dot_general | solution.py:85
  32.5 3.3 %convolution_bitcast_fusion.1 = f32[4,22,2,16,640]{4,1,3,0,2:T(8,128)S(1)} fusion(f32[4,22,16,256]{3,1,2,0:T(8,128)S(1)} %fusion.42, f32[4,22,16,256]{3,1,2,0:T(8,128)S(1)} %fusion.40, f32[2,256,640]{2,1,0:T(8,128)S(1)} %bitcast.156), kind=kOutput, calls=%fused_computation.9 | convolution fusion | flops 2768601088 | bytes 11403264 | tf_op jit(solution)/shard_map/ligand_spectra/ntxc,hcq->nthxq/dot_general | solution.py:87
  35.8 1.3 %copy.20 = f32[4,22,2,16,640]{4,3,2,1,0:T(8,128)S(1)} copy(f32[4,22,2,16,640]{4,1,3,0,2:T(8,128)S(1)} %convolution_bitcast_fusion.1) | data formatting | bytes 14417920 | tf_op jit(solution)/shard_map/ligand_spectra/ntxc,hcq->nthxq/transpose | solution.py:87
  37.1 5.8 %convolution_bitcast_fusion = f32[4,22,64,640]{3,2,1,0:T(8,128)S(1)} fusion(f32[4,22,32,640]{3,2,1,0:T(8,128)S(1)} %bitcast.151, f32[64,32,1,1]{0,1,3,2:T(8,128)S(1)} %copy-done.9), kind=kOutput, calls=%fused_computation | convolution fusion | flops 692060160 | bytes 21635072 | tf_op jit(solution)/shard_map/ligand_spectra/pk,ntkq->ntpq/dot_general | solution.py:90
  42.9 2.2 %fusion.16 = f32[11,1,2,32,640]{4,3,0,2,1:T(8,128)S(1)} fusion(bf16[2,1024,640]{2,1,0:T(8,128)(2,1)S(1)} %get-tuple-element.8, bf16[11,32,1024]{2,1,0:T(8,128)(2,1)} %collective-permute-done.3), kind=kOutput, calls=%fused_computation.25 | convolution fusion | flops 922746880 | bytes 5144576 | tf_op jit(solution)/shard_map/receptor_spectra/trxc,hcq->trhxq/dot_general | solution.py:71
  45.3 1.1 %convolution_bitcast_fusion.2 = f32[11,1,64,640]{3,2,0,1:T(8,128)S(1)} fusion(f32[11,64,640]{2,1,0:T(8,128)S(1)} %bitcast.153, f32[64,64,1]{1,0,2:T(8,128)S(1)} %copy-done.2), kind=kOutput, calls=%fused_computation.26 | convolution fusion | flops 173015040 | bytes 3620864 | tf_op jit(solution)/shard_map/receptor_spectra/pk,trkq->trpq/dot_general | solution.py:73
  46.7 2.5 %add_reduce_fusion = (f32[4,32,640]{2,1,0:T(8,128)S(1)}, f32[4,32,640]{2,1,0:T(8,128)S(1)}, f32[4,32,640]{2,1,0:T(8,128)S(1)}, f32[4,32,640]{2,1,0:T(8,128)S(1)}) fusion(f32[4,22,64,640]{3,2,1,0:T(8,128)S(1)} %convolution_bitcast_fusion, f32[11,32,640]{2,1,0:T(8,128)S(1)} %get-tuple-element.25, f32[11,32,640]{2,1,0:T(8,128)S(1)} %get-tuple-element.24, ...), kind=kLoop, calls=%fused_computation.6 | loop fusion | flops 14090240 | bytes 19333120 | tf_op jit(solution)/shard_map/correlate/reduce_sum | solution.py:98
  49.2 0.7 %fusion.49 = f32[2,4,640,64]{2,3,1,0:T(8,128)S(1)} fusion(f32[64,32,1,1]{0,1,3,2:T(8,128)S(1)} %copy-done.8, f32[1,4,32,640]{3,2,1,0:T(8,128)S(1)} %bitcast.159, f32[1,4,32,640]{3,2,1,0:T(8,128)S(1)} %bitcast.160, f32[1,4,32,640]{3,2,1,0:T(8,128)S(1)} %bitcast.158, f32[1,4,32,640]{3,2,1,0:T(8,128)S(1)} %bitcast.157), kind=kOutput, calls=%fused_computation.53 | convolution fusion | flops 63406080 | bytes 2629632 | tf_op jit(solution)/shard_map/inverse_scores/xp,srnpq->srnxq/dot_general | solution.py:104
  50.1 1.0 %fusion.21 = f32[4,32,1024]{2,1,0:T(8,128)S(1)} fusion(bf16[2,1024,640]{2,1,0:T(8,128)(2,1)S(1)} %get-tuple-element.8, bf16[1,4,32,2,640]{4,2,1,3,0:T(8,128)(2,1)S(1)} %get-tuple-element.9), kind=kOutput, calls=%fused_computation.31 | convolution fusion | flops 335544320 | bytes 3473408 | tf_op jit(solution)/shard_map/inverse_scores/rnxhq,hcq->rnxc/dot_general | solution.py:115
  51.1 1.0 %fusion.33 = f32[4,32,1024]{2,1,0:T(8,128)S(1)} fusion(f32[4,32,1024]{2,1,0:T(8,128)S(1)} %fusion.21, bf16[2,1024,640]{2,1,0:T(8,128)(2,1)S(1)} %get-tuple-element.8, bf16[1,4,32,2,640]{4,2,1,3,0:T(8,128)(2,1)S(1)} %get-tuple-element.10), kind=kOutput, calls=%fused_computation.35 | convolution fusion | flops 335675392 | bytes 3997696 | tf_op jit(solution)/shard_map/inverse_scores/rnxhq,hcq->rnxc/dot_general | solution.py:116
  52.1 0.7 %copy-done = bf16[2,1024,640]{2,1,0:T(8,128)(2,1)S(1)} copy-done((bf16[2,1024,640]{2,1,0:T(8,128)(2,1)S(1)}, bf16[2,1024,640]{2,1,0:T(8,128)(2,1)}, u32[]{:S(2)}) %copy-start) | copy-done | bytes 2621464
  52.9 1.1 %fusion.36 = f32[4]{0:T(128)S(1)} fusion(f32[4,32,1024]{2,1,0:T(8,128)S(1)} %fusion.33, bf16[2,1024,640]{2,1,0:T(8,128)(2,1)S(1)} %copy-done, bf16[1,4,32,2,640]{4,2,1,3,0:T(8,128)(2,1)S(1)} %get-tuple-element.9), kind=kOutput, calls=%fused_computation.36 | convolution fusion | flops 335806464 | bytes 3473424 | tf_op jit(solution)/shard_map/inverse_scores/rnxhq,hcq->rnxc/dot_general | solution.py:117
  54.1 1.5 %collective-permute-start.4 = (f32[4,32]{0,1:T(8,128)S(1)}, f32[4,32]{0,1:T(8,128)S(1)}, u32[]{:S(2)}, u32[]{:S(2)}) collective-permute-start(f32[4,32]{0,1:T(8,128)S(1)} %broadcast_select_fusion), channel_id=1, source_target_pairs={{0,1},{1,0},{2,3},{3,2},{4,5},{5,4},{6,7},{7,6},{8,9},{9,8},{10,11... | collective-permute-start | bytes 1544 | tf_op jit(solution)/shard_map/ppermute | solution.py:135
  56.3 1.6 %collective-permute-done.4 = f32[4,32]{0,1:T(8,128)S(1)} collective-permute-done((f32[4,32]{0,1:T(8,128)S(1)}, f32[4,32]{0,1:T(8,128)S(1)}, u32[]{:S(2)}, u32[]{:S(2)}) %collective-permute-start.4) | collective-permute-done | bytes 544 | tf_op jit(solution)/shard_map/ppermute | solution.py:135
  57.9 1.0 %collective-permute-done.6 = f32[4,32]{0,1:T(8,128)S(1)} collective-permute-done((f32[4,32]{0,1:T(8,128)S(1)}, f32[4,32]{0,1:T(8,128)S(1)}, u32[]{:S(2)}, u32[]{:S(2)}) %collective-permute-start.6) | collective-permute-done | bytes 544 | tf_op jit(solution)/shard_map/ppermute | solution.py:135
  59.9 2.5 %collective-permute-start.9 = (f32[4,32]{0,1:T(8,128)S(1)}, f32[4,32]{0,1:T(8,128)S(1)}, u32[]{:S(2)}, u32[]{:S(2)}) collective-permute-start(f32[4,32]{0,1:T(8,128)S(1)} %maximum_maximum_fusion.1), channel_id=1, source_target_pairs={{0,12},{1,13},{2,14},{3,15},{4,8},{5,9},{6,10},{7,11},{8,4},{9,5},... | collective-permute-start | bytes 1544 | tf_op jit(solution)/shard_map/ppermute | solution.py:135
  63.2 1.3 %collective-permute-done.9 = f32[4,32]{0,1:T(8,128)S(1)} collective-permute-done((f32[4,32]{0,1:T(8,128)S(1)}, f32[4,32]{0,1:T(8,128)S(1)}, u32[]{:S(2)}, u32[]{:S(2)}) %collective-permute-start.9) | collective-permute-done | bytes 544 | tf_op jit(solution)/shard_map/ppermute | solution.py:135
  64.5 2.6 %collective-permute-start.10 = (f32[4,32]{0,1:T(8,128)S(1)}, f32[4,32]{0,1:T(8,128)S(1)}, u32[]{:S(2)}, u32[]{:S(2)}) collective-permute-start(f32[4,32]{0,1:T(8,128)S(1)} %maximum_maximum_fusion), channel_id=1, source_target_pairs={{0,16},{1,17},{2,18},{3,19},{4,20},{5,21},{6,22},{7,23},{8,24},{9,... | collective-permute-start | bytes 1544 | tf_op jit(solution)/shard_map/ppermute | solution.py:135
  67.1 2.0 %collective-permute-done.10 = f32[4,32]{0,1:T(8,128)S(1)} collective-permute-done((f32[4,32]{0,1:T(8,128)S(1)}, f32[4,32]{0,1:T(8,128)S(1)}, u32[]{:S(2)}, u32[]{:S(2)}) %collective-permute-start.10) | collective-permute-done | bytes 544 | tf_op jit(solution)/shard_map/ppermute | solution.py:135
  (51 shorter events, 5.3 us)
Async XLA Ops:
  0.6 25.0 %collective-permute-start.1 = (s32[3,2,256]{2,1,0:T(2,128)}, s32[3,2,256]{2,1,0:T(2,128)S(1)}, u32[]{:S(2)}, u32[]{:S(2)}) collective-permute-start(s32[3,2,256]{2,1,0:T(2,128)} %param.16), channel_id=1, source_target_pairs={{0,8},{8,0},{16,24},{24,16},{1,9},{9,1},{17,25},{25,17},{2,10},{10... | collective-permute-start | bytes 18440 | tf_op jit(solution)/shard_map/ppermute | solution.py:164
  4.5 23.8 %collective-permute-start = (f32[11,256]{1,0:T(8,128)S(1)}, f32[11,256]{1,0:T(8,128)S(1)}, u32[]{:S(2)}, u32[]{:S(2)}) collective-permute-start(f32[11,256]{1,0:T(8,128)S(1)} %broadcast_multiply_fusion), channel_id=1, source_target_pairs={{0,1},{1,0},{2,3},{3,2},{4,5},{5,4},{6,7},{7,6},{8,9},{9,8},{10,11... | collective-permute-start | bytes 33800 | tf_op jit(solution)/shard_map/ppermute | solution.py:124
  14.5 28.5 %collective-permute-start.3 = (bf16[11,32,1024]{2,1,0:T(8,128)(2,1)S(1)}, bf16[11,32,1024]{2,1,0:T(8,128)(2,1)}, u32[]{:S(2)}, u32[]{:S(2)}) collective-permute-start(bf16[11,32,1024]{2,1,0:T(8,128)(2,1)S(1)} %all_gather.3), channel_id=1, source_target_pairs={{0,1},{1,0},{2,3},{3,2},{4,5},{5,4},{6,7},{7,6},{8,9},{9,8},{10,11... | collective-permute-start | bytes 2162696 | tf_op jit(solution)/shard_map/ppermute | solution.py:124
  17.0 2.4 %copy-start.3 = (f32[2,16,640]{2,1,0:T(8,128)S(1)}, f32[2,16,640]{2,1,0:T(8,128)}, u32[]{:S(2)}) copy-start(f32[2,16,640]{2,1,0:T(8,128)} %constant.84) | copy-start | bytes 245764
  17.0 2.4 %copy-start.4 = (f32[2,16,640]{2,1,0:T(8,128)S(1)}, f32[2,16,640]{2,1,0:T(8,128)}, u32[]{:S(2)}) copy-start(f32[2,16,640]{2,1,0:T(8,128)} %constant.87) | copy-start | bytes 245764
  17.0 2.4 %copy-start.5 = (f32[2,16,640]{2,1,0:T(8,128)S(1)}, f32[2,16,640]{2,1,0:T(8,128)}, u32[]{:S(2)}) copy-start(f32[2,16,640]{2,1,0:T(8,128)} %constant.90) | copy-start | bytes 245764
  17.1 2.4 %copy-start.6 = (f32[2,16,640]{2,1,0:T(8,128)S(1)}, f32[2,16,640]{2,1,0:T(8,128)}, u32[]{:S(2)}) copy-start(f32[2,16,640]{2,1,0:T(8,128)} %constant.93) | copy-start | bytes 245764
  21.8 1.4 %copy-start.2 = (f32[64,64,1]{1,0,2:T(8,128)S(1)}, f32[64,64,1]{1,0,2:T(8,128)}, u32[]{:S(2)}) copy-start(f32[64,64,1]{1,0,2:T(8,128)} %constant.103) | copy-start | bytes 49156
  23.2 2.4 %copy-start.7 = (s32[3,2,256]{2,1,0:T(2,128)S(1)}, s32[3,2,256]{2,1,0:T(2,128)}, u32[]{:S(2)}) copy-start(s32[3,2,256]{2,1,0:T(2,128)} %param.16) | copy-start | bytes 18436
  25.6 4.7 %collective-permute-start.2 = (s32[3,4,256]{2,1,0:T(4,128)S(1)}, s32[3,4,256]{2,1,0:T(4,128)S(1)}, u32[]{:S(2)}, u32[]{:S(2)}) collective-permute-start(s32[3,4,256]{2,1,0:T(4,128)S(1)} %pad_add_fusion), channel_id=1, source_target_pairs={{0,16},{8,24},{16,0},{24,8},{1,17},{9,25},{17,1},{25,9},{2,18},{10... | collective-permute-start | bytes 36872 | tf_op jit(solution)/shard_map/ppermute | solution.py:164
  30.6 1.9 %copy-start.1 = (f32[2,16,16,640]{3,2,1,0:T(8,128)S(1)}, f32[2,16,16,640]{3,2,1,0:T(8,128)}, u32[]{:S(2)}) copy-start(f32[2,16,16,640]{3,2,1,0:T(8,128)} %multiply_add_fusion.1) | copy-start | bytes 3932164
  35.8 1.3 %copy-start.9 = (f32[64,32,1,1]{0,1,3,2:T(8,128)S(1)}, f32[64,32,1,1]{0,1,3,2:T(8,128)}, u32[]{:S(2)}) copy-start(f32[64,32,1,1]{0,1,3,2:T(8,128)} %constant.102) | copy-start | bytes 24580
  46.7 2.5 %copy-start.8 = (f32[64,32,1,1]{0,1,3,2:T(8,128)S(1)}, f32[64,32,1,1]{0,1,3,2:T(8,128)}, u32[]{:S(2)}) copy-start(f32[64,32,1,1]{0,1,3,2:T(8,128)} %constant.104) | copy-start | bytes 24580
  49.2 0.8 %copy-start.10 = (f32[640]{0:T(1024)S(1)}, f32[640]{0:T(1024)}, u32[]{:S(2)}) copy-start(f32[640]{0:T(1024)} %constant.77.clone) | copy-start | bytes 7684
  51.1 1.7 %copy-start = (bf16[2,1024,640]{2,1,0:T(8,128)(2,1)S(1)}, bf16[2,1024,640]{2,1,0:T(8,128)(2,1)}, u32[]{:S(2)}) copy-start(bf16[2,1024,640]{2,1,0:T(8,128)(2,1)} %get-tuple-element.11) | copy-start | bytes 7864324
  54.1 3.7 %collective-permute-start.4 = (f32[4,32]{0,1:T(8,128)S(1)}, f32[4,32]{0,1:T(8,128)S(1)}, u32[]{:S(2)}, u32[]{:S(2)}) collective-permute-start(f32[4,32]{0,1:T(8,128)S(1)} %broadcast_select_fusion), channel_id=1, source_target_pairs={{0,1},{1,0},{2,3},{3,2},{4,5},{5,4},{6,7},{7,6},{8,9},{9,8},{10,11... | collective-permute-start | bytes 1544 | tf_op jit(solution)/shard_map/ppermute | solution.py:135
  55.7 2.2 %collective-permute-start.5 = (f32[4,32]{0,1:T(8,128)S(1)}, f32[4,32]{0,1:T(8,128)S(1)}, u32[]{:S(2)}, u32[]{:S(2)}) collective-permute-start(f32[4,32]{0,1:T(8,128)S(1)} %broadcast_select_fusion), channel_id=1, source_target_pairs={{0,2},{1,3},{2,0},{3,1},{4,6},{5,7},{6,4},{7,5},{8,10},{9,11},{10,... | collective-permute-start | bytes 1544 | tf_op jit(solution)/shard_map/ppermute | solution.py:135
  55.7 3.2 %collective-permute-start.6 = (f32[4,32]{0,1:T(8,128)S(1)}, f32[4,32]{0,1:T(8,128)S(1)}, u32[]{:S(2)}, u32[]{:S(2)}) collective-permute-start(f32[4,32]{0,1:T(8,128)S(1)} %broadcast_select_fusion), channel_id=1, source_target_pairs={{0,3},{1,2},{2,1},{3,0},{4,7},{5,6},{6,5},{7,4},{8,11},{9,10},{10,... | collective-permute-start | bytes 1544 | tf_op jit(solution)/shard_map/ppermute | solution.py:135
  58.9 3.7 %collective-permute-start.7 = (f32[4,32]{0,1:T(8,128)S(1)}, f32[4,32]{0,1:T(8,128)S(1)}, u32[]{:S(2)}, u32[]{:S(2)}) collective-permute-start(f32[4,32]{0,1:T(8,128)S(1)} %maximum_maximum_fusion.1), channel_id=1, source_target_pairs={{0,4},{1,5},{2,6},{3,7},{4,0},{5,1},{6,2},{7,3},{8,12},{9,13},{10,... | collective-permute-start | bytes 1544 | tf_op jit(solution)/shard_map/ppermute | solution.py:135
  59.4 3.7 %collective-permute-start.8 = (f32[4,32]{0,1:T(8,128)S(1)}, f32[4,32]{0,1:T(8,128)S(1)}, u32[]{:S(2)}, u32[]{:S(2)}) collective-permute-start(f32[4,32]{0,1:T(8,128)S(1)} %maximum_maximum_fusion.1), channel_id=1, source_target_pairs={{0,8},{1,9},{2,10},{3,11},{4,12},{5,13},{6,14},{7,15},{8,0},{9,1},... | collective-permute-start | bytes 1544 | tf_op jit(solution)/shard_map/ppermute | solution.py:135
  59.9 4.6 %collective-permute-start.9 = (f32[4,32]{0,1:T(8,128)S(1)}, f32[4,32]{0,1:T(8,128)S(1)}, u32[]{:S(2)}, u32[]{:S(2)}) collective-permute-start(f32[4,32]{0,1:T(8,128)S(1)} %maximum_maximum_fusion.1), channel_id=1, source_target_pairs={{0,12},{1,13},{2,14},{3,15},{4,8},{5,9},{6,10},{7,11},{8,4},{9,5},... | collective-permute-start | bytes 1544 | tf_op jit(solution)/shard_map/ppermute | solution.py:135
  64.5 4.6 %collective-permute-start.10 = (f32[4,32]{0,1:T(8,128)S(1)}, f32[4,32]{0,1:T(8,128)S(1)}, u32[]{:S(2)}, u32[]{:S(2)}) collective-permute-start(f32[4,32]{0,1:T(8,128)S(1)} %maximum_maximum_fusion), channel_id=1, source_target_pairs={{0,16},{1,17},{2,18},{3,19},{4,20},{5,21},{6,22},{7,23},{8,24},{9,... | collective-permute-start | bytes 1544 | tf_op jit(solution)/shard_map/ppermute | solution.py:135

commit v17 on v15

--- a/solution.py
+++ b/solution.py
@@ -128,7 +128,7 @@
 def butterfly_max(values, axes, device_count):
     stride = 1
     while stride < device_count:
-        radix = 2
+        radix = 4 if stride > 1 and stride * 4 <= device_count else 2
         received = []
         for digit in range(1, radix):
             pairs = [(k, k ^ (digit * stride)) for k in range(device_count)]

time: 72.8 us -> 71.2 us (0.978)
  waiting for transfers between devices: 14.1 us -> 9.68 us
  starting transfers between devices: 12.8 us -> 15.6 us
    ppermute x5 -> x7, waiting for transfers between devices: 12 us -> 7.68 us  [butterfly_max(): received.append(lax.ppermute(values, axes, pairs))]
    ppermute x5 -> x7, starting transfers between devices: 5.04 us -> 7.79 us  [butterfly_max(): received.append(lax.ppermute(values, axes, pairs))]
  transfers between devices with their start and end apart: 9 -> 11, of which waited for: 6 -> 6; matrix products, arithmetic and copies ran while one was open for 33% -> 34% of each run, Pallas kernels for 0% -> 0%
where the time goes in v17:
time: 71.2 us; the launch traced here: 70.9 us
  matrix products  21.5 us (30%)
  starting transfers between devices  15.6 us (22%)
  other arithmetic  10.4 us (15%)
  waiting for transfers between devices  9.68 us (14%)
  blocking collectives  8.44 us (12%)
  local copies, waits for them, and re-layouts  4.39 us (6%)
  between operations  0.95 us (1%)
    all_gather x1, blocking collectives, body(): own_rows = lax.all_gather(receptor_grids, 'inner', axis=1, tiled=True)  8.44 us
    ppermute x7, starting transfers between devices, butterfly_max(): received.append(lax.ppermute(values, axes, pairs))  7.79 us
    ppermute x7, waiting for transfers between devices, butterfly_max(): received.append(lax.ppermute(values, axes, pairs))  7.68 us
    dot_general x1, matrix products, ligand_spectra(): return jnp.einsum('pk,ntkq->tnpq', mix_tables(LB), plane, precision=HIGH)  5.81 us
    ppermute x2, starting transfers between devices, body(): moved = lax.ppermute(cells_here, 'plane', pairs)  5.76 us
    dot_general x2, matrix products, receptor_mixed(): return jnp.einsum('pk,trkq->trpq', mix_tables(G), plane, precision=HIGH)  3.43 us
    dot_general x2, matrix products, receptor_mixed(): jnp.einsum('trxc,hcq->trhxq', grids, table_hi, preferred_element_type=jnp...  3.31 us
    dot_general x1, matrix products, ligand_spectra(): plane = jnp.einsum('ntxc,hcq->nthxq', grid, box_table, precision=HIGH)  3.27 us
  transfers between devices with their start and end apart: 11, of which 6 were waited for; matrix products, arithmetic and copies ran while one was open for 34% of the time, Pallas kernels for 0%

profile of v17, /device:TPU:0, one launch (start us, length us, event | category | flops | bytes accessed | tf_op | source)
XLA Modules:
  0.0 70.9 jit_solution(15404758626309142945)
XLA Ops:
  0.6 3.1 %collective-permute-start.1 = (s32[3,2,256]{2,1,0:T(2,128)}, s32[3,2,256]{2,1,0:T(2,128)S(1)}, u32[]{:S(2)}, u32[]{:S(2)}) collective-permute-start(s32[3,2,256]{2,1,0:T(2,128)} %param.16), channel_id=1, source_target_pairs={{0,8},{8,0},{16,24},{24,16},{1,9},{9,1},{17,25},{25,17},{2,10},{10... | collective-permute-start | bytes 18440 | tf_op jit(solution)/shard_map/ppermute | solution.py:164
  3.7 0.8 %broadcast_multiply_fusion = f32[11,256]{1,0:T(8,128)S(1)} fusion(f32[11,256]{1,0:T(8,128)} %param.15, f32[11]{0:T(128)} %param.14), kind=kLoop, calls=%fused_computation.88 | loop fusion | flops 2816 | bytes 22572 | tf_op jit(solution)/shard_map/mul | solution.py:173
  4.5 1.5 %collective-permute-start = (f32[11,256]{1,0:T(8,128)S(1)}, f32[11,256]{1,0:T(8,128)S(1)}, u32[]{:S(2)}, u32[]{:S(2)}) collective-permute-start(f32[11,256]{1,0:T(8,128)S(1)} %broadcast_multiply_fusion), channel_id=1, source_target_pairs={{0,1},{1,0},{2,3},{3,2},{4,5},{5,4},{6,7},{7,6},{8,9},{9,8},{10,11... | collective-permute-start | bytes 33800 | tf_op jit(solution)/shard_map/ppermute | solution.py:124
  6.0 8.4 %all_gather.3 = bf16[11,32,1024]{2,1,0:T(8,128)(2,1)S(1)} all-gather(bf16[11,8,1024]{2,1,0:T(8,128)(2,1)} %param.13), channel_id=1, replica_groups=mesh['plane'=4,'inner'=4,'term'=2] {'inner'}, dimensions={1}, use_global_device_ids=true | all-gather | bytes 901120 | tf_op jit(solution)/shard_map/all_gather | solution.py:152
  15.0 2.0 %multiply_add_fusion = f32[2,32,32,640]{3,2,1,0:T(8,128)S(1)} fusion(f32[2,32,640]{2,1,0:T(8,128)} %constant.101, f32[2,32,640]{2,1,0:T(8,128)} %constant.99, f32[2,32,640]{2,1,0:T(8,128)} %constant.97, f32[2,32,640]{2,1,0:T(8,128)} %constant.95), kind=kLoop, calls=%fused_computation.4 | loop fusion | flops 3932160 | bytes 5898240 | tf_op jit(solution)/shard_map/twiddle_tables/add | solution.py:45
  17.1 2.4 %fusion = (bf16[2,1024,640]{2,1,0:T(8,128)(2,1)}, bf16[2,1024,640]{2,1,0:T(8,128)(2,1)S(1)}) fusion(f32[2,32,32,640]{3,2,1,0:T(8,128)S(1)} %multiply_add_fusion), kind=kLoop, calls=%fused_computation.3 | loop fusion | flops 5242880 | bytes 10485760 | tf_op jit(solution)/shard_map/twiddle_tables/convert_element_type | solution.py:52
  19.4 1.2 %multiply_add_fusion.1 = f32[2,16,16,640]{3,2,1,0:T(8,128)} fusion(f32[2,16,640]{2,1,0:T(8,128)S(1)} %copy-done.6, f32[2,16,640]{2,1,0:T(8,128)S(1)} %copy-done.5, f32[2,16,640]{2,1,0:T(8,128)S(1)} %copy-done.4, f32[2,16,640]{2,1,0:T(8,128)S(1)} %copy-done.3), kind=kLoop, calls=%fused_computation.30 | loop fusion | flops 983040 | bytes 1638400 | tf_op jit(solution)/shard_map/twiddle_tables/add | solution.py:45
  20.7 1.1 %fusion.13 = f32[11,1,2,32,640]{4,3,0,2,1:T(8,128)S(1)} fusion(bf16[2,1024,640]{2,1,0:T(8,128)(2,1)S(1)} %get-tuple-element.8, bf16[11,32,1024]{2,1,0:T(8,128)(2,1)S(1)} %all_gather.3), kind=kOutput, calls=%fused_computation.24 | convolution fusion | flops 922746880 | bytes 5144576 | tf_op jit(solution)/shard_map/receptor_spectra/trxc,hcq->trhxq/dot_general | solution.py:71
  21.8 1.3 %copy.21 = f32[11,1,2,32,640]{4,3,2,0,1:T(8,128)} copy(f32[11,1,2,32,640]{4,3,0,2,1:T(8,128)S(1)} %fusion.13) | data formatting | bytes 3604480 | tf_op jit(solution)/shard_map/receptor_spectra/trxc,hcq->trhxq/transpose | solution.py:71
  23.2 2.3 %convolution_bitcast_fusion.3 = f32[11,1,64,640]{3,2,0,1:T(8,128)S(1)} fusion(f32[11,64,640]{2,1,0:T(8,128)} %bitcast.152, f32[64,64,1]{1,0,2:T(8,128)S(1)} %copy-done.2), kind=kOutput, calls=%fused_computation.27 | convolution fusion | flops 173015040 | bytes 3620864 | tf_op jit(solution)/shard_map/receptor_spectra/pk,trkq->trpq/dot_general | solution.py:73
  25.6 2.7 %collective-permute-start.2 = (s32[3,4,256]{2,1,0:T(4,128)S(1)}, s32[3,4,256]{2,1,0:T(4,128)S(1)}, u32[]{:S(2)}, u32[]{:S(2)}) collective-permute-start(s32[3,4,256]{2,1,0:T(4,128)S(1)} %pad_add_fusion), channel_id=1, source_target_pairs={{0,16},{8,24},{16,0},{24,8},{1,17},{9,25},{17,1},{25,9},{2,18},{10... | collective-permute-start | bytes 36872 | tf_op jit(solution)/shard_map/ppermute | solution.py:164
  28.3 2.0 %collective-permute-done.2 = s32[3,4,256]{2,1,0:T(4,128)S(1)} collective-permute-done((s32[3,4,256]{2,1,0:T(4,128)S(1)}, s32[3,4,256]{2,1,0:T(4,128)S(1)}, u32[]{:S(2)}, u32[]{:S(2)}) %collective-permute-start.2) | collective-permute-done | bytes 12320 | tf_op jit(solution)/shard_map/ppermute | solution.py:164
  30.6 0.8 %fusion.40 = f32[4,22,16,256]{3,1,2,0:T(8,128)S(1)} fusion(bf16[4,22,16,256]{3,2,1,0:T(8,128)(2,1)S(1)} %get-tuple-element.28, s32[4,256]{1,0:T(4,128)S(1)} %get-tuple-element.30), kind=kOutput, calls=%fused_computation.39 | convolution fusion | flops 184811520 | bytes 2166784 | tf_op jit(solution)/shard_map/ligand_spectra/ntxa,nac->ntxc/dot_general | solution.py:86
  31.5 1.0 %fusion.42 = f32[4,22,16,256]{3,1,2,0:T(8,128)S(1)} fusion(bf16[4,22,16,256]{3,2,1,0:T(8,128)(2,1)S(1)} %get-tuple-element.29, s32[4,256]{1,0:T(4,128)S(1)} %get-tuple-element.30), kind=kOutput, calls=%fused_computation.40 | convolution fusion | flops 184811520 | bytes 2166784 | tf_op jit(solution)/shard_map/ligand_spectra/ntxa,nac->ntxc/dot_general | solution.py:85
  32.5 3.3 %convolution_bitcast_fusion.1 = f32[4,22,2,16,640]{4,1,3,0,2:T(8,128)S(1)} fusion(f32[4,22,16,256]{3,1,2,0:T(8,128)S(1)} %fusion.42, f32[4,22,16,256]{3,1,2,0:T(8,128)S(1)} %fusion.40, f32[2,256,640]{2,1,0:T(8,128)S(1)} %bitcast.156), kind=kOutput, calls=%fused_computation.9 | convolution fusion | flops 2768601088 | bytes 11403264 | tf_op jit(solution)/shard_map/ligand_spectra/ntxc,hcq->nthxq/dot_general | solution.py:87
  35.8 1.3 %copy.20 = f32[4,22,2,16,640]{4,3,2,1,0:T(8,128)S(1)} copy(f32[4,22,2,16,640]{4,1,3,0,2:T(8,128)S(1)} %convolution_bitcast_fusion.1) | data formatting | bytes 14417920 | tf_op jit(solution)/shard_map/ligand_spectra/ntxc,hcq->nthxq/transpose | solution.py:87
  37.1 5.8 %convolution_bitcast_fusion = f32[22,4,64,640]{3,2,0,1:T(8,128)S(1)} fusion(f32[4,22,32,640]{3,2,1,0:T(8,128)S(1)} %bitcast.151, f32[64,32,1,1]{0,1,3,2:T(8,128)S(1)} %copy-done.9), kind=kOutput, calls=%fused_computation | convolution fusion | flops 692060160 | bytes 21635072 | tf_op jit(solution)/shard_map/ligand_spectra/pk,ntkq->tnpq/dot_general | solution.py:90
  42.9 2.2 %fusion.16 = f32[11,1,2,32,640]{4,3,0,2,1:T(8,128)S(1)} fusion(bf16[2,1024,640]{2,1,0:T(8,128)(2,1)S(1)} %get-tuple-element.8, bf16[11,32,1024]{2,1,0:T(8,128)(2,1)} %collective-permute-done.3), kind=kOutput, calls=%fused_computation.25 | convolution fusion | flops 922746880 | bytes 5144576 | tf_op jit(solution)/shard_map/receptor_spectra/trxc,hcq->trhxq/dot_general | solution.py:71
  45.3 1.1 %convolution_bitcast_fusion.2 = f32[11,1,64,640]{3,2,0,1:T(8,128)S(1)} fusion(f32[11,64,640]{2,1,0:T(8,128)S(1)} %bitcast.153, f32[64,64,1]{1,0,2:T(8,128)S(1)} %copy-done.2), kind=kOutput, calls=%fused_computation.26 | convolution fusion | flops 173015040 | bytes 3620864 | tf_op jit(solution)/shard_map/receptor_spectra/pk,trkq->trpq/dot_general | solution.py:73
  46.7 2.5 %add_reduce_fusion = (f32[4,32,640]{2,1,0:T(8,128)S(1)}, f32[4,32,640]{2,1,0:T(8,128)S(1)}, f32[4,32,640]{2,1,0:T(8,128)S(1)}, f32[4,32,640]{2,1,0:T(8,128)S(1)}) fusion(f32[22,4,64,640]{3,2,0,1:T(8,128)S(1)} %convolution_bitcast_fusion, f32[11,32,640]{2,1,0:T(8,128)S(1)} %get-tuple-element.25, f32[11,32,640]{2,1,0:T(8,128)S(1)} %get-tuple-element.24, ...), kind=kLoop, calls=%fused_computation.6 | loop fusion | flops 14090240 | bytes 19333120 | tf_op jit(solution)/shard_map/correlate/reduce_sum | solution.py:98
  50.1 1.0 %fusion.21 = f32[4,32,1024]{2,1,0:T(8,128)S(1)} fusion(bf16[2,1024,640]{2,1,0:T(8,128)(2,1)S(1)} %get-tuple-element.8, bf16[1,4,32,2,640]{4,2,1,3,0:T(8,128)(2,1)S(1)} %get-tuple-element.9), kind=kOutput, calls=%fused_computation.31 | convolution fusion | flops 335544320 | bytes 3473408 | tf_op jit(solution)/shard_map/inverse_scores/rnxhq,hcq->rnxc/dot_general | solution.py:115
  51.1 1.0 %fusion.33 = f32[4,32,1024]{2,1,0:T(8,128)S(1)} fusion(f32[4,32,1024]{2,1,0:T(8,128)S(1)} %fusion.21, bf16[2,1024,640]{2,1,0:T(8,128)(2,1)S(1)} %get-tuple-element.8, bf16[1,4,32,2,640]{4,2,1,3,0:T(8,128)(2,1)S(1)} %get-tuple-element.10), kind=kOutput, calls=%fused_computation.35 | convolution fusion | flops 335675392 | bytes 3997696 | tf_op jit(solution)/shard_map/inverse_scores/rnxhq,hcq->rnxc/dot_general | solution.py:116
  52.1 0.7 %copy-done = bf16[2,1024,640]{2,1,0:T(8,128)(2,1)S(1)} copy-done((bf16[2,1024,640]{2,1,0:T(8,128)(2,1)S(1)}, bf16[2,1024,640]{2,1,0:T(8,128)(2,1)}, u32[]{:S(2)}) %copy-start) | copy-done | bytes 2621464
  52.9 1.1 %fusion.36 = f32[4]{0:T(128)S(1)} fusion(f32[4,32,1024]{2,1,0:T(8,128)S(1)} %fusion.33, bf16[2,1024,640]{2,1,0:T(8,128)(2,1)S(1)} %copy-done, bf16[1,4,32,2,640]{4,2,1,3,0:T(8,128)(2,1)S(1)} %get-tuple-element.9), kind=kOutput, calls=%fused_computation.36 | convolution fusion | flops 335806464 | bytes 3473424 | tf_op jit(solution)/shard_map/inverse_scores/rnxhq,hcq->rnxc/dot_general | solution.py:117
  54.1 1.5 %collective-permute-start.4 = (f32[4,32]{0,1:T(8,128)S(1)}, f32[4,32]{0,1:T(8,128)S(1)}, u32[]{:S(2)}, u32[]{:S(2)}) collective-permute-start(f32[4,32]{0,1:T(8,128)S(1)} %broadcast_select_fusion), channel_id=1, source_target_pairs={{0,1},{1,0},{2,3},{3,2},{4,5},{5,4},{6,7},{7,6},{8,9},{9,8},{10,11... | collective-permute-start | bytes 1544 | tf_op jit(solution)/shard_map/ppermute | solution.py:135
  55.7 2.2 %collective-permute-done.4 = f32[4,32]{0,1:T(8,128)S(1)} collective-permute-done((f32[4,32]{0,1:T(8,128)S(1)}, f32[4,32]{0,1:T(8,128)S(1)}, u32[]{:S(2)}, u32[]{:S(2)}) %collective-permute-start.4) | collective-permute-done | bytes 544 | tf_op jit(solution)/shard_map/ppermute | solution.py:135
  58.6 1.2 %collective-permute-start.7 = (f32[4,32]{0,1:T(8,128)S(1)}, f32[4,32]{0,1:T(8,128)S(1)}, u32[]{:S(2)}, u32[]{:S(2)}) collective-permute-start(f32[4,32]{0,1:T(8,128)S(1)} %fusion.70), channel_id=1, source_target_pairs={{0,6},{1,7},{2,4},{3,5},{4,2},{5,3},{6,0},{7,1},{8,14},{9,15},{10,... | collective-permute-start | bytes 1544 | tf_op jit(solution)/shard_map/ppermute | solution.py:135
  59.8 2.1 %collective-permute-done.6 = f32[4,32]{0,1:T(8,128)S(1)} collective-permute-done((f32[4,32]{0,1:T(8,128)S(1)}, f32[4,32]{0,1:T(8,128)S(1)}, u32[]{:S(2)}, u32[]{:S(2)}) %collective-permute-start.6) | collective-permute-done | bytes 544 | tf_op jit(solution)/shard_map/ppermute | solution.py:135
  62.0 2.4 %collective-permute-start.10 = (f32[4,32]{0,1:T(8,128)S(1)}, f32[4,32]{0,1:T(8,128)S(1)}, u32[]{:S(2)}, u32[]{:S(2)}) collective-permute-start(f32[4,32]{0,1:T(8,128)S(1)} %maximum_maximum_fusion.1), channel_id=1, source_target_pairs={{0,24},{1,25},{2,26},{3,27},{4,28},{5,29},{6,30},{7,31},{8,16},{9,... | collective-permute-start | bytes 1544 | tf_op jit(solution)/shard_map/ppermute | solution.py:135
  65.1 1.3 %collective-permute-start.9 = (f32[4,32]{0,1:T(8,128)S(1)}, f32[4,32]{0,1:T(8,128)S(1)}, u32[]{:S(2)}, u32[]{:S(2)}) collective-permute-start(f32[4,32]{0,1:T(8,128)S(1)} %maximum_maximum_fusion.1), channel_id=1, source_target_pairs={{0,16},{1,17},{2,18},{3,19},{4,20},{5,21},{6,22},{7,23},{8,24},{9,... | collective-permute-start | bytes 1544 | tf_op jit(solution)/shard_map/ppermute | solution.py:135
  66.4 1.1 %collective-permute-done.10 = f32[4,32]{0,1:T(8,128)S(1)} collective-permute-done((f32[4,32]{0,1:T(8,128)S(1)}, f32[4,32]{0,1:T(8,128)S(1)}, u32[]{:S(2)}, u32[]{:S(2)}) %collective-permute-start.10) | collective-permute-done | bytes 544 | tf_op jit(solution)/shard_map/ppermute | solution.py:135
  68.2 1.6 %collective-permute-done.9 = f32[4,32]{0,1:T(8,128)S(1)} collective-permute-done((f32[4,32]{0,1:T(8,128)S(1)}, f32[4,32]{0,1:T(8,128)S(1)}, u32[]{:S(2)}, u32[]{:S(2)}) %collective-permute-start.9) | collective-permute-done | bytes 544 | tf_op jit(solution)/shard_map/ppermute | solution.py:135
  (51 shorter events, 5.7 us)
Async XLA Ops:
  0.6 25.0 %collective-permute-start.1 = (s32[3,2,256]{2,1,0:T(2,128)}, s32[3,2,256]{2,1,0:T(2,128)S(1)}, u32[]{:S(2)}, u32[]{:S(2)}) collective-permute-start(s32[3,2,256]{2,1,0:T(2,128)} %param.16), channel_id=1, source_target_pairs={{0,8},{8,0},{16,24},{24,16},{1,9},{9,1},{17,25},{25,17},{2,10},{10... | collective-permute-start | bytes 18440 | tf_op jit(solution)/shard_map/ppermute | solution.py:164
  4.5 23.8 %collective-permute-start = (f32[11,256]{1,0:T(8,128)S(1)}, f32[11,256]{1,0:T(8,128)S(1)}, u32[]{:S(2)}, u32[]{:S(2)}) collective-permute-start(f32[11,256]{1,0:T(8,128)S(1)} %broadcast_multiply_fusion), channel_id=1, source_target_pairs={{0,1},{1,0},{2,3},{3,2},{4,5},{5,4},{6,7},{7,6},{8,9},{9,8},{10,11... | collective-permute-start | bytes 33800 | tf_op jit(solution)/shard_map/ppermute | solution.py:124
  14.5 28.5 %collective-permute-start.3 = (bf16[11,32,1024]{2,1,0:T(8,128)(2,1)S(1)}, bf16[11,32,1024]{2,1,0:T(8,128)(2,1)}, u32[]{:S(2)}, u32[]{:S(2)}) collective-permute-start(bf16[11,32,1024]{2,1,0:T(8,128)(2,1)S(1)} %all_gather.3), channel_id=1, source_target_pairs={{0,1},{1,0},{2,3},{3,2},{4,5},{5,4},{6,7},{7,6},{8,9},{9,8},{10,11... | collective-permute-start | bytes 2162696 | tf_op jit(solution)/shard_map/ppermute | solution.py:124
  17.0 2.4 %copy-start.3 = (f32[2,16,640]{2,1,0:T(8,128)S(1)}, f32[2,16,640]{2,1,0:T(8,128)}, u32[]{:S(2)}) copy-start(f32[2,16,640]{2,1,0:T(8,128)} %constant.84) | copy-start | bytes 245764
  17.0 2.4 %copy-start.4 = (f32[2,16,640]{2,1,0:T(8,128)S(1)}, f32[2,16,640]{2,1,0:T(8,128)}, u32[]{:S(2)}) copy-start(f32[2,16,640]{2,1,0:T(8,128)} %constant.87) | copy-start | bytes 245764
  17.0 2.4 %copy-start.5 = (f32[2,16,640]{2,1,0:T(8,128)S(1)}, f32[2,16,640]{2,1,0:T(8,128)}, u32[]{:S(2)}) copy-start(f32[2,16,640]{2,1,0:T(8,128)} %constant.90) | copy-start | bytes 245764
  17.1 2.4 %copy-start.6 = (f32[2,16,640]{2,1,0:T(8,128)S(1)}, f32[2,16,640]{2,1,0:T(8,128)}, u32[]{:S(2)}) copy-start(f32[2,16,640]{2,1,0:T(8,128)} %constant.93) | copy-start | bytes 245764
  21.8 1.4 %copy-start.2 = (f32[64,64,1]{1,0,2:T(8,128)S(1)}, f32[64,64,1]{1,0,2:T(8,128)}, u32[]{:S(2)}) copy-start(f32[64,64,1]{1,0,2:T(8,128)} %constant.103) | copy-start | bytes 49156
  23.2 2.4 %copy-start.7 = (s32[3,2,256]{2,1,0:T(2,128)S(1)}, s32[3,2,256]{2,1,0:T(2,128)}, u32[]{:S(2)}) copy-start(s32[3,2,256]{2,1,0:T(2,128)} %param.16) | copy-start | bytes 18436
  25.6 4.7 %collective-permute-start.2 = (s32[3,4,256]{2,1,0:T(4,128)S(1)}, s32[3,4,256]{2,1,0:T(4,128)S(1)}, u32[]{:S(2)}, u32[]{:S(2)}) collective-permute-start(s32[3,4,256]{2,1,0:T(4,128)S(1)} %pad_add_fusion), channel_id=1, source_target_pairs={{0,16},{8,24},{16,0},{24,8},{1,17},{9,25},{17,1},{25,9},{2,18},{10... | collective-permute-start | bytes 36872 | tf_op jit(solution)/shard_map/ppermute | solution.py:164
  30.6 1.9 %copy-start.1 = (f32[2,16,16,640]{3,2,1,0:T(8,128)S(1)}, f32[2,16,16,640]{3,2,1,0:T(8,128)}, u32[]{:S(2)}) copy-start(f32[2,16,16,640]{3,2,1,0:T(8,128)} %multiply_add_fusion.1) | copy-start | bytes 3932164
  35.8 1.3 %copy-start.9 = (f32[64,32,1,1]{0,1,3,2:T(8,128)S(1)}, f32[64,32,1,1]{0,1,3,2:T(8,128)}, u32[]{:S(2)}) copy-start(f32[64,32,1,1]{0,1,3,2:T(8,128)} %constant.102) | copy-start | bytes 24580
  46.7 2.5 %copy-start.8 = (f32[64,32,1,1]{0,1,3,2:T(8,128)S(1)}, f32[64,32,1,1]{0,1,3,2:T(8,128)}, u32[]{:S(2)}) copy-start(f32[64,32,1,1]{0,1,3,2:T(8,128)} %constant.104) | copy-start | bytes 24580
  49.2 0.8 %copy-start.10 = (f32[640]{0:T(1024)S(1)}, f32[640]{0:T(1024)}, u32[]{:S(2)}) copy-start(f32[640]{0:T(1024)} %constant.77.clone) | copy-start | bytes 7684
  51.1 1.7 %copy-start = (bf16[2,1024,640]{2,1,0:T(8,128)(2,1)S(1)}, bf16[2,1024,640]{2,1,0:T(8,128)(2,1)}, u32[]{:S(2)}) copy-start(bf16[2,1024,640]{2,1,0:T(8,128)(2,1)} %get-tuple-element.11) | copy-start | bytes 7864324
  54.1 3.7 %collective-permute-start.4 = (f32[4,32]{0,1:T(8,128)S(1)}, f32[4,32]{0,1:T(8,128)S(1)}, u32[]{:S(2)}, u32[]{:S(2)}) collective-permute-start(f32[4,32]{0,1:T(8,128)S(1)} %broadcast_select_fusion), channel_id=1, source_target_pairs={{0,1},{1,0},{2,3},{3,2},{4,5},{5,4},{6,7},{7,6},{8,9},{9,8},{10,11... | collective-permute-start | bytes 1544 | tf_op jit(solution)/shard_map/ppermute | solution.py:135
  57.9 1.9 %collective-permute-start.5 = (f32[4,32]{0,1:T(8,128)S(1)}, f32[4,32]{0,1:T(8,128)S(1)}, u32[]{:S(2)}, u32[]{:S(2)}) collective-permute-start(f32[4,32]{0,1:T(8,128)S(1)} %fusion.70), channel_id=1, source_target_pairs={{0,2},{1,3},{2,0},{3,1},{4,6},{5,7},{6,4},{7,5},{8,10},{9,11},{10,... | collective-permute-start | bytes 1544 | tf_op jit(solution)/shard_map/ppermute | solution.py:135
  57.9 4.0 %collective-permute-start.6 = (f32[4,32]{0,1:T(8,128)S(1)}, f32[4,32]{0,1:T(8,128)S(1)}, u32[]{:S(2)}, u32[]{:S(2)}) collective-permute-start(f32[4,32]{0,1:T(8,128)S(1)} %fusion.70), channel_id=1, source_target_pairs={{0,4},{1,5},{2,6},{3,7},{4,0},{5,1},{6,2},{7,3},{8,12},{9,13},{10,... | collective-permute-start | bytes 1544 | tf_op jit(solution)/shard_map/ppermute | solution.py:135
  58.6 3.3 %collective-permute-start.7 = (f32[4,32]{0,1:T(8,128)S(1)}, f32[4,32]{0,1:T(8,128)S(1)}, u32[]{:S(2)}, u32[]{:S(2)}) collective-permute-start(f32[4,32]{0,1:T(8,128)S(1)} %fusion.70), channel_id=1, source_target_pairs={{0,6},{1,7},{2,4},{3,5},{4,2},{5,3},{6,0},{7,1},{8,14},{9,15},{10,... | collective-permute-start | bytes 1544 | tf_op jit(solution)/shard_map/ppermute | solution.py:135
  62.0 5.5 %collective-permute-start.10 = (f32[4,32]{0,1:T(8,128)S(1)}, f32[4,32]{0,1:T(8,128)S(1)}, u32[]{:S(2)}, u32[]{:S(2)}) collective-permute-start(f32[4,32]{0,1:T(8,128)S(1)} %maximum_maximum_fusion.1), channel_id=1, source_target_pairs={{0,24},{1,25},{2,26},{3,27},{4,28},{5,29},{6,30},{7,31},{8,16},{9,... | collective-permute-start | bytes 1544 | tf_op jit(solution)/shard_map/ppermute | solution.py:135
  64.4 3.8 %collective-permute-start.8 = (f32[4,32]{0,1:T(8,128)S(1)}, f32[4,32]{0,1:T(8,128)S(1)}, u32[]{:S(2)}, u32[]{:S(2)}) collective-permute-start(f32[4,32]{0,1:T(8,128)S(1)} %maximum_maximum_fusion.1), channel_id=1, source_target_pairs={{0,8},{1,9},{2,10},{3,11},{4,12},{5,13},{6,14},{7,15},{8,0},{9,1},... | collective-permute-start | bytes 1544 | tf_op jit(solution)/shard_map/ppermute | solution.py:135
  65.1 4.6 %collective-permute-start.9 = (f32[4,32]{0,1:T(8,128)S(1)}, f32[4,32]{0,1:T(8,128)S(1)}, u32[]{:S(2)}, u32[]{:S(2)}) collective-permute-start(f32[4,32]{0,1:T(8,128)S(1)} %maximum_maximum_fusion.1), channel_id=1, source_target_pairs={{0,16},{1,17},{2,18},{3,19},{4,20},{5,21},{6,22},{7,23},{8,24},{9,... | collective-permute-start | bytes 1544 | tf_op jit(solution)/shard_map/ppermute | solution.py:135
